TPU v7x, 128 devices: a whole 4x4x4 slice. The times are simulated.
128 devices in a mesh: slab: 8 (over y, core), tile: 16 (over z, x).
Axes of the slice: x: 4, y: 4, z: 4, core: 2. Of those that a mesh axis runs over, the one named last changes fastest.
Arguments:
- positions: float32 [3, 262144], P(None, ('slab', 'tile')), may hold values from -6 to 6
- radius: float32 [262144], P(('slab', 'tile')), may hold values from 0.7 to 1.4
- uptake_rate: float32 [262144], P(('slab', 'tile')), may hold values from 0.3 to 3
- voxel_local: int32 [262144], P(('slab', 'tile')), may hold values from 0 to 262143
- cell_counts: int32 [128], P(('slab', 'tile')), may hold values from 512 to 2048, as said below
- send_counts: int32 [128, 16], P(('slab', 'tile')), may hold values from 0 to 256, as said below
- neighbor_blocks: int32 [2048, 8], P(('slab', 'tile')), may hold values from 0 to 23, as said below
- field: float32 [2, 64, 256, 2048], P(None, 'slab', 'tile'), may hold values from 0.2 to 2
Outputs:
- velocity: float32 [3, 262144], P(None, ('slab', 'tile'))
- field_next: float32 [2, 64, 256, 2048], P(None, 'slab', 'tile')
Inputs may be any that keep to these rules, and one draw needn't show every extreme that they name: `cell_counts`: A multiple of 128; in every slab one tile holds 2048 live cells and another 2048 // 4. `send_counts`: row g sums to cell_counts[g]; in every slab all tiles send exactly 256 cells to one common destination tile. `neighbor_blocks`: row g * 16 + b names 8 different blocks of tile g's extended table, the first being 4 + b.
All inputs are finite; a program needn't handle non-finite values.
Results may differ from a plain program's by a relative error of at most 0.0003.
Values sent between devices are 32-bit elements; how exact they have to be, the bound alone decides.
No kernel may reach another device: no remote copies, remote signals or barrier semaphores. Data moves between devices by JAX's collectives and lax.ppermute only.
A program may use at most 64 MiB of HBM per device.

v0:
```python
import jax
import jax.numpy as jnp
from jax import lax
from jax.sharding import PartitionSpec as P

HB = 4
K = 8
ITERS = 4


MICHAELIS_HALF = 0.5
HYPOXIA_HALF = 0.6
SECRETION = 0.4
STEP_TIME = 0.5
DIFFUSION = (0.16, 0.12)
DECAY = (0.0, 0.03)
REPULSION = 1.0
ADHESION = 0.35
REPEL_RANGE = 1.0
ADHERE_RANGE = 4.0
FORCE_SCALE = 0.08
CHEMOTAXIS = 1.5
SLOT_BLOCK = 512


def with_halo(block, sides, width):
    for axis, dim in sides:
        count = lax.axis_size(axis)
        forward = [(i, i + 1) for i in range(count - 1)]
        backward = [(target, source) for source, target in forward]
        low = lax.ppermute(
            lax.slice_in_dim(block, block.shape[dim] - width, None, axis=dim), axis, forward
        )
        high = lax.ppermute(lax.slice_in_dim(block, 0, width, axis=dim), axis, backward)
        block = jnp.concatenate([low, block, high], axis=dim)
    return block


def block_force(mine, others):
    offset = mine[:3, :, :, None, None] - others[:3, :, None, :, :]
    distance = jnp.sum(offset * offset, axis=0)
    strength = REPULSION * jnp.exp(-distance / REPEL_RANGE) - ADHESION * jnp.exp(
        -distance / ADHERE_RANGE
    )
    weight = mine[3][:, :, None, None] * others[3][:, None, :, :] * strength
    return jnp.sum(offset * weight[None], axis=(3, 4))


def relax(padded):
    center = padded[:, 1:-1, 1:-1]
    sideways = jnp.pad(center, ((0, 0), (0, 0), (0, 0), (1, 1)))
    beside_all = padded[:, 2:, 1:-1] + padded[:, :-2, 1:-1]
    beside_all = beside_all + padded[:, 1:-1, 2:] + padded[:, 1:-1, :-2]
    beside_all = beside_all + sideways[..., 2:] + sideways[..., :-2]
    spread = jnp.array(DIFFUSION, jnp.float32)[:, None, None, None]
    losses = jnp.array(DECAY, jnp.float32)[:, None, None, None]
    return center + spread * (beside_all - 6.0 * center) - losses * center


def routing(sends, length):
    ends = jnp.cumsum(sends)
    starts = ends - sends
    cell = jnp.arange(length, dtype=jnp.int32)
    target = jnp.sum((ends[:, None] <= cell[None, :]).astype(jnp.int32), axis=0)
    routed = target < sends.shape[0]
    target = jnp.minimum(target, sends.shape[0] - 1)
    lanes = jnp.arange(sends.shape[0], dtype=jnp.int32)
    first = jnp.sum(jnp.where(lanes[:, None] == target[None, :], starts[:, None], 0), axis=0)
    return (target, cell - first, routed)


def hot_tables(piece, planes, columns):
    row_hot = (piece[:, None] // columns == jnp.arange(planes, dtype=jnp.int32)[None, :]).astype(
        jnp.float32
    )
    column_hot = (piece[:, None] % columns == jnp.arange(columns, dtype=jnp.int32)[None, :]).astype(
        jnp.float32
    )
    return (row_hot, column_hot)


def pick_voxels(fields, reached):
    species, planes, columns = fields.shape
    pieces = reached.reshape(-1, SLOT_BLOCK)

    def one_piece(piece):
        row_hot, column_hot = hot_tables(piece, planes, columns)
        picked = jnp.einsum("srx,mx->srm", fields, column_hot, precision=lax.Precision.HIGHEST)
        return jnp.sum(picked * jnp.transpose(row_hot)[None], axis=1)

    found = lax.map(one_piece, pieces)
    return jnp.moveaxis(found, 1, 0).reshape(species, -1)


def spread_voxels(amounts, reached, planes, columns):
    species = amounts.shape[0]
    pieces = reached.reshape(-1, SLOT_BLOCK)
    shares = jnp.moveaxis(amounts.reshape(species, -1, SLOT_BLOCK), 1, 0)

    def add_piece(total, item):
        piece, share = item
        row_hot, column_hot = hot_tables(piece, planes, columns)
        weighted = share[:, :, None] * row_hot[None]
        return (
            total
            + jnp.einsum("smr,mx->srx", weighted, column_hot, precision=lax.Precision.HIGHEST),
            None,
        )

    empty = jnp.zeros((species, planes, columns), jnp.float32)
    total, unused = lax.scan(add_piece, empty, (pieces, shares))
    return total


def local(
    positions, radius, uptake_rate, voxel_local, cell_counts, send_counts, neighbor_blocks, field
):
    tiles = lax.axis_size("tile")
    capacity = positions.shape[1]
    blocks = capacity // 128
    slot_size = 2 * capacity // tiles
    cell = jnp.arange(capacity, dtype=jnp.int32)
    count = cell_counts[0]
    kept = jnp.where(cell < count, radius, 0.0)
    table = jnp.concatenate([positions, kept[None]], axis=0)
    extended = with_halo(table, (("tile", 1),), HB * 128)
    extended = extended.reshape(4, blocks + 2 * HB, 128)
    group = 4
    turns = (count // 128 + group - 1) // group

    def one_turn(turn, total):
        first = turn * group
        chosen = lax.dynamic_slice_in_dim(neighbor_blocks, first, group, 0)
        mine = lax.dynamic_slice_in_dim(extended, first + HB, group, 1)
        others = jnp.take(extended, chosen.reshape(-1), axis=1).reshape(4, group, K, 128)
        return lax.dynamic_update_slice_in_dim(total, block_force(mine, others), first, 1)

    forces = lax.fori_loop(0, turns, one_turn, jnp.zeros((3, blocks, 128), jnp.float32))
    forces = forces.reshape(3, capacity)
    sends = send_counts[0]
    ends = jnp.cumsum(sends)
    starts = ends - sends
    ranks = jnp.arange(slot_size, dtype=jnp.int32)
    valid = ranks[None, :] < sends[:, None]
    source = jnp.where(valid, starts[:, None] + ranks[None, :], 0)
    wanted = jnp.where(valid, jnp.take(voxel_local, source), 0)
    rates = jnp.where(valid, jnp.take(uptake_rate, source), 0.0)
    species, depth, rows, columns = field.shape
    planes = depth * rows
    oxygen_rows = field[0].reshape(1, planes, columns)
    incoming = lax.all_to_all(wanted, "tile", split_axis=0, concat_axis=0, tiled=True)
    reached = incoming.reshape(-1)
    found = pick_voxels(oxygen_rows, reached).reshape(tiles, slot_size)
    oxygen = lax.all_to_all(found, "tile", split_axis=0, concat_axis=0, tiled=True)
    consume = rates * oxygen / (MICHAELIS_HALF + oxygen)
    secrete = SECRETION * rates * HYPOXIA_HALF / (HYPOXIA_HALF + oxygen)
    amounts = jnp.stack([-STEP_TIME * consume, STEP_TIME * secrete])
    arrived = lax.all_to_all(amounts, "tile", split_axis=1, concat_axis=1, tiled=True)
    added = spread_voxels(arrived.reshape(species, -1), reached, planes, columns)
    state = field + added.reshape(species, depth, rows, columns)
    for step in range(ITERS):
        state = relax(with_halo(state, (("slab", 1), ("tile", 2)), 1))
    border = with_halo(state[1], (("slab", 0), ("tile", 1)), 1)
    rise_z = 0.5 * (border[2:, 1:-1] - border[:-2, 1:-1])
    rise_y = 0.5 * (border[1:-1, 2:] - border[1:-1, :-2])
    middle = jnp.pad(border[1:-1, 1:-1], ((0, 0), (0, 0), (1, 1)))
    rise_x = 0.5 * (middle[..., 2:] - middle[..., :-2])
    rises = jnp.stack([rise_z, rise_y, rise_x]).reshape(3, planes, columns)
    slopes = pick_voxels(rises, reached).reshape(3, tiles, slot_size)
    returned = lax.all_to_all(slopes, "tile", split_axis=1, concat_axis=1, tiled=True)
    target, rank, routed = routing(sends, capacity)
    where_back = jnp.clip(target * slot_size + rank, 0, tiles * slot_size - 1)
    slope = jnp.take(returned.reshape(3, tiles * slot_size), where_back, axis=1)
    slope = jnp.where(routed[None, :], slope, 0.0)
    velocity = FORCE_SCALE * forces + CHEMOTAXIS * slope
    return (velocity, state)


def solution(mesh):
    placed = (
        P(None, ("slab", "tile")),
        P(("slab", "tile")),
        P(("slab", "tile")),
        P(("slab", "tile")),
        P(("slab", "tile")),
        P(("slab", "tile"), None),
        P(("slab", "tile"), None),
        P(None, "slab", "tile", None),
    )
    return jax.shard_map(
        local,
        mesh=mesh,
        in_specs=placed,
        out_specs=(P(None, ("slab", "tile")), P(None, "slab", "tile", None)),
        check_vma=False,
    )
```

profile of v0, /device:TPU:26, one launch (start us, length us, event | category | flops | bytes accessed | tf_op | source)
XLA Modules:
  0.0 391.6 jit_solution(4688570988103458770)
XLA Ops:
  3.0 23.0 %gather_fusion.1 = s32[4096]{0:T(1024)S(1)} fusion(s32[2048]{0:T(1024)S(1)} %copy-done, s32[4096]{0:T(1024)S(1)} %broadcast_clamp_fusion), kind=kCustom, calls=%fused_computation.1 | custom fusion | bytes 49152 | tf_op jit(solution)/shard_map/jit(_take)/gather | solution.py:146
  26.8 8.3 %all-to-all-start = ((s32[16,1,256]{2,1,0:T(1,128)}), s32[16,1,256]{2,1,0:T(1,128)S(1)}, u32[]{:S(2)}, u32[]{:S(2)}) async-start(s32[16,1,256]{2,1,0:T(1,128)} %compare_select_fusion.8), calls=%async_computation | async-start | bytes 32768 | tf_op jit(solution)/shard_map/all_to_all | solution.py:151
  35.1 6.2 %all-to-all-done = s32[16,1,256]{2,1,0:T(1,128)S(1)} async-done(((s32[16,1,256]{2,1,0:T(1,128)}), s32[16,1,256]{2,1,0:T(1,128)S(1)}, u32[]{:S(2)}, u32[]{:S(2)}) %all-to-all-start) | async-done | bytes 16416 | tf_op jit(solution)/shard_map/all_to_all | solution.py:151
  41.4 25.0 %while.50 = (s32[]{:T(128)}, f32[8,1,512]{2,1,0:T(1,128)}, s32[8,512]{1,0:T(8,128)S(1)}, f32[1,128,2048]{2,1,0:T(8,128)S(1)}, s32[]{:T(128)}) while((s32[]{:T(128)}, f32[8,1,512]{2,1,0:T(1,128)}, s32[8,512]{1,0:T(8,128)S(1)}, f32[1,128,2048]{2,1,0:T(8,128)S(1)}, s32[]{:T(128)}) %tuple.148), condition=%wide.region_9.10_spmd, body=%wide.region_7.9_spmd.sunk | while | flops 1611867136 | bytes 1069633 | solution.py:91
  41.4 2.5 fusion.107
  44.6 2.5 fusion.107
  47.7 2.5 fusion.107
  50.8 2.5 fusion.107
  53.9 2.5 fusion.107
  57.1 2.5 fusion.107
  60.2 2.5 fusion.107
  63.3 2.5 fusion.107
  66.4 4.9 %all-to-all-start.1 = ((f32[16,1,256]{2,1,0:T(1,128)}), f32[16,1,256]{2,1,0:T(1,128)S(1)}, u32[]{:S(2)}, u32[]{:S(2)}) async-start(f32[16,1,256]{2,1,0:T(1,128)} %bitcast.22), calls=%async_computation.1 | async-start | bytes 32768 | tf_op jit(solution)/shard_map/all_to_all | solution.py:154
  71.3 23.0 %gather_fusion.2 = f32[4096]{0:T(1024)S(1)} fusion(f32[2048]{0:T(1024)S(1)} %copy-done.1, s32[4096]{0:T(1024)S(1)} %broadcast_clamp_fusion), kind=kCustom, calls=%fused_computation.2 | custom fusion | bytes 49152 | tf_op jit(solution)/shard_map/jit(_take)/gather | solution.py:147
  95.2 7.3 %all-to-all-start.2 = ((f32[2,16,256]{2,0,1:T(2,128)}), f32[2,16,256]{2,0,1:T(2,128)S(1)}, u32[]{:S(2)}, u32[]{:S(2)}) async-start(f32[2,16,256]{2,0,1:T(2,128)} %pad_maximum_fusion.56), calls=%async_computation.2 | async-start | bytes 65536 | tf_op jit(solution)/shard_map/all_to_all | solution.py:158
  102.5 6.2 %all-to-all-done.2 = f32[2,16,256]{2,0,1:T(2,128)S(1)} async-done(((f32[2,16,256]{2,0,1:T(2,128)}), f32[2,16,256]{2,0,1:T(2,128)S(1)}, u32[]{:S(2)}, u32[]{:S(2)}) %all-to-all-start.2) | async-done | bytes 32800 | tf_op jit(solution)/shard_map/all_to_all | solution.py:158
  108.7 25.1 %while.52 = (s32[]{:T(128)}, f32[2,128,2048]{2,1,0:T(8,128)S(1)}, f32[8,2,512]{2,0,1:T(8,128)S(1)}, s32[8,512]{1,0:T(8,128)S(1)}, s32[]{:T(128)}, /*index=5*/s32[]{:T(128)}) while((s32[]{:T(128)}, f32[2,128,2048]{2,1,0:T(8,128)S(1)}, f32[8,2,512]{2,0,1:T(8,128)S(1)}, s32[8,512]{1,0:T(8,128)S(1)}, s32[]{:T(128)}, ...), condition=%wide.region_11.12_spmd.clone, body=%wide.region_10.11_spmd.clone.sunk | while | flops 3223594496 | bytes 4753495 | solution.py:111
  108.9 3.0 fusion.115
  112.0 3.0 fusion.115
  115.1 3.0 fusion.115
  118.3 3.0 fusion.115
  121.4 3.0 fusion.115
  124.5 3.0 fusion.115
  127.7 3.0 fusion.115
  130.8 3.0 fusion.115
  137.8 2.4 collective-permute-start.3
  141.7 3.8 collective-permute-done.3
  145.8 3.4 collective-permute-start.4
  149.3 2.5 collective-permute-start.5
  154.3 3.3 collective-permute-done.5
  157.7 2.7 fusion.42
  162.4 2.4 collective-permute-start.7
  166.2 3.8 collective-permute-done.7
  172.4 4.1 %collective-permute-start.9 = (f32[2,10,1,2048]{3,1,2,0:T(8,128)S(1)}, f32[2,10,1,2048]{3,1,2,0:T(8,128)S(1)}, u32[]{:S(2)}, u32[]{:S(2)}) collective-permute-start(f32[2,10,1,2048]{3,1,2,0:T(8,128)S(1)} %copy.84), channel_id=1, source_target_pairs={{0,1},{1,2},{2,3},{3,4},{4,5},{5,6},{6,7},{7,8},{8,9},{9,10},{10,1... | collective-permute-start | bytes 491528 | tf_op jit(solution)/shard_map/ppermute | solution.py:31
  180.8 2.7 fusion.48
  185.5 2.4 collective-permute-start.11
  187.9 3.9 %collective-permute-start = (f32[4,512]{1,0:T(4,128)S(1)}, f32[4,512]{1,0:T(4,128)S(1)}, u32[]{:S(2)}, u32[]{:S(2)}) collective-permute-start(f32[4,512]{1,0:T(4,128)S(1)} %get-tuple-element.373), channel_id=1, source_target_pairs={{0,1},{1,2},{2,3},{3,4},{4,5},{5,6},{6,7},{7,8},{8,9},{9,10},{10,1... | collective-permute-start | bytes 24584 | tf_op jit(solution)/shard_map/ppermute | solution.py:31
  196.2 4.2 %collective-permute-start.13 = (f32[2,10,1,2048]{3,1,2,0:T(8,128)S(1)}, f32[2,10,1,2048]{3,1,2,0:T(8,128)S(1)}, u32[]{:S(2)}, u32[]{:S(2)}) collective-permute-start(f32[2,10,1,2048]{3,1,2,0:T(8,128)S(1)} %copy.88), channel_id=1, source_target_pairs={{0,1},{1,2},{2,3},{3,4},{4,5},{5,6},{6,7},{7,8},{8,9},{9,10},{10,1... | collective-permute-start | bytes 491528 | tf_op jit(solution)/shard_map/ppermute | solution.py:31
  200.6 3.5 collective-permute-done.12
  205.6 2.7 fusion.54
  208.3 2.8 collective-permute-start.14
  215.0 3.8 collective-permute-done.15
  221.8 6.3 %collective-permute-start.17 = (f32[2,10,1,2048]{3,1,2,0:T(8,128)}, f32[2,10,1,2048]{3,1,2,0:T(8,128)}, u32[]{:S(2)}, u32[]{:S(2)}) collective-permute-start(f32[2,10,1,2048]{3,1,2,0:T(8,128)} %copy.92), channel_id=1, source_target_pairs={{0,1},{1,2},{2,3},{3,4},{4,5},{5,6},{6,7},{7,8},{8,9},{9,10},{10,1... | collective-permute-start | bytes 491528 | tf_op jit(solution)/shard_map/ppermute | solution.py:31
  233.5 2.7 fusion.60
  240.6 3.9 collective-permute-done.19
  247.2 5.5 %collective-permute-start.21 = (f32[10,1,2048]{2,1,0:T(1,128)}, f32[10,1,2048]{2,1,0:T(1,128)}, u32[]{:S(2)}, u32[]{:S(2)}) collective-permute-start(f32[10,1,2048]{2,1,0:T(1,128)} %get-tuple-element.371), channel_id=1, source_target_pairs={{0,1},{1,2},{2,3},{3,4},{4,5},{5,6},{6,7},{7,8},{8,9},{9,10},{10,1... | collective-permute-start | bytes 245768 | tf_op jit(solution)/shard_map/ppermute | solution.py:31
  252.7 76.0 %while.49 = (s32[]{:T(128)}, f32[3,16,128]{2,1,0:T(8,128)S(1)}, s32[]{:T(128)}, f32[4,24,128]{2,0,1:T(4,128)S(1)}, s32[16,8]{1,0:T(8,128)S(1)}, /*index=5*/s32[]...) while((s32[]{:T(128)}, f32[3,16,128]{2,1,0:T(8,128)S(1)}, s32[]{:T(128)}, ...), condition=%wide.region_3.4_spmd, body=%wide.region_0.3_spmd.sunk | while | flops 12074795 | bytes 8963753 | solution.py:138
  256.6 15.0 %fusion.105 = f32[3,4,128]{2,1,0:T(4,128)S(1)} fusion(f32[4,128,8,128]{3,2,1,0:T(8,128)S(1)} %subtract_multiply_fusion.4, f32[3,4,8,128]{3,2,1,0:T(8,128)S(1)} %copy.105, f32[3,4,128]{2,1,0:T(4,128)S(1)} %copy.106), kind=kLoop, calls=%fused_computation.44.clone.1 | loop fusion | flops 4717056 | bytes 2158592 | tf_op jit(solution)/shard_map/while/body/reduce_sum | solution.py:46
  275.6 15.0 %fusion.105 = f32[3,4,128]{2,1,0:T(4,128)S(1)} fusion(f32[4,128,8,128]{3,2,1,0:T(8,128)S(1)} %subtract_multiply_fusion.4, f32[3,4,8,128]{3,2,1,0:T(8,128)S(1)} %copy.105, f32[3,4,128]{2,1,0:T(4,128)S(1)} %copy.106), kind=kLoop, calls=%fused_computation.44.clone.1 | loop fusion | flops 4717056 | bytes 2158592 | tf_op jit(solution)/shard_map/while/body/reduce_sum | solution.py:46
  294.5 15.0 %fusion.105 = f32[3,4,128]{2,1,0:T(4,128)S(1)} fusion(f32[4,128,8,128]{3,2,1,0:T(8,128)S(1)} %subtract_multiply_fusion.4, f32[3,4,8,128]{3,2,1,0:T(8,128)S(1)} %copy.105, f32[3,4,128]{2,1,0:T(4,128)S(1)} %copy.106), kind=kLoop, calls=%fused_computation.44.clone.1 | loop fusion | flops 4717056 | bytes 2158592 | tf_op jit(solution)/shard_map/while/body/reduce_sum | solution.py:46
  313.4 15.0 %fusion.105 = f32[3,4,128]{2,1,0:T(4,128)S(1)} fusion(f32[4,128,8,128]{3,2,1,0:T(8,128)S(1)} %subtract_multiply_fusion.4, f32[3,4,8,128]{3,2,1,0:T(8,128)S(1)} %copy.105, f32[3,4,128]{2,1,0:T(4,128)S(1)} %copy.106), kind=kLoop, calls=%fused_computation.44.clone.1 | loop fusion | flops 4717056 | bytes 2158592 | tf_op jit(solution)/shard_map/while/body/reduce_sum | solution.py:46
  330.8 30.7 %while.51 = (s32[]{:T(128)}, f32[8,3,512]{2,1,0:T(4,128)}, s32[8,512]{1,0:T(8,128)S(1)}, f32[3,128,2048]{2,1,0:T(8,128)S(1)}, s32[]{:T(128)}) while((s32[]{:T(128)}, f32[8,3,512]{2,1,0:T(4,128)}, s32[8,512]{1,0:T(8,128)S(1)}, f32[3,128,2048]{2,1,0:T(8,128)S(1)}, s32[]{:T(128)}) %tuple.150), condition=%wide.region_14.15_spmd, body=%wide.region_12.14_spmd.sunk | while | flops 4833419264 | bytes 3705409 | solution.py:91
  330.9 3.2 fusion.111
  334.7 3.2 fusion.111
  338.5 3.2 fusion.111
  342.4 3.2 fusion.111
  346.2 3.2 fusion.111
  350.1 3.2 fusion.111
  353.9 3.2 fusion.111
  357.7 3.2 fusion.111
  361.5 11.7 %all-to-all-start.3 = ((f32[3,16,256]{2,0,1:T(4,128)}), f32[3,16,256]{2,0,1:T(4,128)S(1)}, u32[]{:S(2)}, u32[]{:S(2)}) async-start(f32[3,16,256]{2,0,1:T(4,128)} %bitcast.33), calls=%async_computation.3 | async-start | bytes 131072 | tf_op jit(solution)/shard_map/all_to_all | solution.py:170
  373.6 5.9 %all-to-all-done.3 = f32[3,16,256]{2,0,1:T(4,128)S(1)} async-done(((f32[3,16,256]{2,0,1:T(4,128)}), f32[3,16,256]{2,0,1:T(4,128)S(1)}, u32[]{:S(2)}, u32[]{:S(2)}) %all-to-all-start.3) | async-done | bytes 49184 | tf_op jit(solution)/shard_map/all_to_all | solution.py:170
  380.2 7.6 %gather_fusion.3 = f32[2048,3]{1,0:T(8,128)} fusion(f32[3,4096]{0,1:T(8,128)S(1)} %bitcast.145, s32[2048]{0:T(1024)S(1)} %broadcast_clamp_fusion.1), kind=kCustom, calls=%fused_computation.3 | custom fusion | bytes 57344 | tf_op jit(solution)/shard_map/jit(_take)/gather | solution.py:173
  387.7 2.9 bitcast_add_fusion
  (273 shorter events, 78.7 us)
Async XLA Ops:
  0.6 2.3 copy-start
  3.0 23.1 %copy-start.7 = (s32[1,16]{1,0:T(1,128)S(1)}, s32[1,16]{1,0:T(1,128)}, u32[]{:S(2)}) copy-start(s32[1,16]{1,0:T(1,128)} %param.29) | copy-start | bytes 196
  26.0 15.4 %slice-start = ((f32[2,8,16,2048]{3,2,1,0:T(8,128)}), f32[1,8,16,2048]{3,2,1,0:T(8,128)S(1)}, s32[]{:S(2)}) async-start(f32[2,8,16,2048]{3,2,1,0:T(8,128)} %param.31), calls=%async_computation.4 | async-start | bytes 2097152 | tf_op jit(solution)/shard_map/slice | solution.py:150
  26.8 14.5 %all-to-all-start = ((s32[16,1,256]{2,1,0:T(1,128)}), s32[16,1,256]{2,1,0:T(1,128)S(1)}, u32[]{:S(2)}, u32[]{:S(2)}) async-start(s32[16,1,256]{2,1,0:T(1,128)} %compare_select_fusion.8), calls=%async_computation | async-start | bytes 32768 | tf_op jit(solution)/shard_map/all_to_all | solution.py:151
  66.4 4.9 %copy-start.1 = (f32[2048]{0:T(1024)S(1)}, f32[2048]{0:T(1024)}, u32[]{:S(2)}) copy-start(f32[2048]{0:T(1024)} %param.26) | copy-start | bytes 24580
  66.4 27.9 %all-to-all-start.1 = ((f32[16,1,256]{2,1,0:T(1,128)}), f32[16,1,256]{2,1,0:T(1,128)S(1)}, u32[]{:S(2)}, u32[]{:S(2)}) async-start(f32[16,1,256]{2,1,0:T(1,128)} %bitcast.22), calls=%async_computation.1 | async-start | bytes 32768 | tf_op jit(solution)/shard_map/all_to_all | solution.py:154
  95.2 13.5 %all-to-all-start.2 = ((f32[2,16,256]{2,0,1:T(2,128)}), f32[2,16,256]{2,0,1:T(2,128)S(1)}, u32[]{:S(2)}, u32[]{:S(2)}) async-start(f32[2,16,256]{2,0,1:T(2,128)} %pad_maximum_fusion.56), calls=%async_computation.2 | async-start | bytes 65536 | tf_op jit(solution)/shard_map/all_to_all | solution.py:158
  135.9 5.8 %collective-permute-start.2 = (f32[2,1,16,2048]{3,2,1,0:T(8,128)S(1)}, f32[2,1,16,2048]{3,2,1,0:T(8,128)S(1)}, u32[]{:S(2)}, u32[]{:S(2)}) collective-permute-start(f32[2,1,16,2048]{3,2,1,0:T(8,128)S(1)} %get-tuple-element.367), channel_id=1, source_target_pairs={{16,0},{32,16},{48,32},{64,48},{80,64},{96,80},{112,96},{17,1},{33... | collective-permute-start | bytes 786440 | tf_op jit(solution)/shard_map/ppermute | solution.py:34
  137.8 19.9 %copy-start.5 = (f32[2]{0:T(128)S(1)}, f32[2]{0:T(128)}, u32[]{:S(2)}) copy-start(f32[2]{0:T(128)} %constant.346.clone) | copy-start | bytes 28
  137.8 19.9 %copy-start.6 = (f32[2]{0:T(128)S(1)}, f32[2]{0:T(128)}, u32[]{:S(2)}) copy-start(f32[2]{0:T(128)} %constant.347.clone) | copy-start | bytes 28
  137.8 7.7 %collective-permute-start.3 = (f32[2,1,16,2048]{3,2,1,0:T(8,128)S(1)}, f32[2,1,16,2048]{3,2,1,0:T(8,128)S(1)}, u32[]{:S(2)}, u32[]{:S(2)}) collective-permute-start(f32[2,1,16,2048]{3,2,1,0:T(8,128)S(1)} %get-tuple-element.366), channel_id=1, source_target_pairs={{0,16},{16,32},{32,48},{48,64},{64,80},{80,96},{96,112},{1,17},{17... | collective-permute-start | bytes 786440 | tf_op jit(solution)/shard_map/ppermute | solution.py:31
  145.8 8.3 %collective-permute-start.4 = (f32[2,10,1,2048]{3,1,2,0:T(8,128)S(1)}, f32[2,10,1,2048]{3,1,2,0:T(8,128)S(1)}, u32[]{:S(2)}, u32[]{:S(2)}) collective-permute-start(f32[2,10,1,2048]{3,1,2,0:T(8,128)S(1)} %copy.78), channel_id=1, source_target_pairs={{1,0},{2,1},{3,2},{4,3},{5,4},{6,5},{7,6},{8,7},{9,8},{10,9},{11,1... | collective-permute-start | bytes 491528 | tf_op jit(solution)/shard_map/ppermute | solution.py:34
  149.3 8.3 %collective-permute-start.5 = (f32[2,10,1,2048]{3,1,2,0:T(8,128)S(1)}, f32[2,10,1,2048]{3,1,2,0:T(8,128)S(1)}, u32[]{:S(2)}, u32[]{:S(2)}) collective-permute-start(f32[2,10,1,2048]{3,1,2,0:T(8,128)S(1)} %copy.80), channel_id=1, source_target_pairs={{0,1},{1,2},{2,3},{3,4},{4,5},{5,6},{6,7},{7,8},{8,9},{9,10},{10,1... | collective-permute-start | bytes 491528 | tf_op jit(solution)/shard_map/ppermute | solution.py:31
  160.4 5.8 %collective-permute-start.6 = (f32[2,1,16,2048]{3,2,1,0:T(8,128)S(1)}, f32[2,1,16,2048]{3,2,1,0:T(8,128)S(1)}, u32[]{:S(2)}, u32[]{:S(2)}) collective-permute-start(f32[2,1,16,2048]{3,2,1,0:T(8,128)S(1)} %get-tuple-element.365), channel_id=1, source_target_pairs={{16,0},{32,16},{48,32},{64,48},{80,64},{96,80},{112,96},{17,1},{33... | collective-permute-start | bytes 786440 | tf_op jit(solution)/shard_map/ppermute | solution.py:34
  162.4 7.7 %collective-permute-start.7 = (f32[2,1,16,2048]{3,2,1,0:T(8,128)S(1)}, f32[2,1,16,2048]{3,2,1,0:T(8,128)S(1)}, u32[]{:S(2)}, u32[]{:S(2)}) collective-permute-start(f32[2,1,16,2048]{3,2,1,0:T(8,128)S(1)} %get-tuple-element.364), channel_id=1, source_target_pairs={{0,16},{16,32},{32,48},{48,64},{64,80},{80,96},{96,112},{1,17},{17... | collective-permute-start | bytes 786440 | tf_op jit(solution)/shard_map/ppermute | solution.py:31
  170.4 8.3 %collective-permute-start.8 = (f32[2,10,1,2048]{3,1,2,0:T(8,128)S(1)}, f32[2,10,1,2048]{3,1,2,0:T(8,128)S(1)}, u32[]{:S(2)}, u32[]{:S(2)}) collective-permute-start(f32[2,10,1,2048]{3,1,2,0:T(8,128)S(1)} %copy.82), channel_id=1, source_target_pairs={{1,0},{2,1},{3,2},{4,3},{5,4},{6,5},{7,6},{8,7},{9,8},{10,9},{11,1... | collective-permute-start | bytes 491528 | tf_op jit(solution)/shard_map/ppermute | solution.py:34
  172.4 8.3 %collective-permute-start.9 = (f32[2,10,1,2048]{3,1,2,0:T(8,128)S(1)}, f32[2,10,1,2048]{3,1,2,0:T(8,128)S(1)}, u32[]{:S(2)}, u32[]{:S(2)}) collective-permute-start(f32[2,10,1,2048]{3,1,2,0:T(8,128)S(1)} %copy.84), channel_id=1, source_target_pairs={{0,1},{1,2},{2,3},{3,4},{4,5},{5,6},{6,7},{7,8},{8,9},{9,10},{10,1... | collective-permute-start | bytes 491528 | tf_op jit(solution)/shard_map/ppermute | solution.py:31
  180.8 7.1 %copy-start.8 = (f32[2048]{0:T(1024)S(1)}, f32[2048]{0:T(1024)}, u32[]{:S(2)}) copy-start(f32[2048]{0:T(1024)} %param.25) | copy-start | bytes 24580
  180.8 7.1 %copy-start.4 = (f32[3,2048]{1,0:T(4,128)S(1)}, f32[3,2048]{1,0:T(4,128)}, u32[]{:S(2)}) copy-start(f32[3,2048]{1,0:T(4,128)} %param.24) | copy-start | bytes 73732
  183.5 10.4 %collective-permute-start.10 = (f32[2,1,16,2048]{3,2,1,0:T(8,128)S(1)}, f32[2,1,16,2048]{3,2,1,0:T(8,128)S(1)}, u32[]{:S(2)}, u32[]{:S(2)}) collective-permute-start(f32[2,1,16,2048]{3,2,1,0:T(8,128)S(1)} %get-tuple-element.363), channel_id=1, source_target_pairs={{16,0},{32,16},{48,32},{64,48},{80,64},{96,80},{112,96},{17,1},{33... | collective-permute-start | bytes 786440 | tf_op jit(solution)/shard_map/ppermute | solution.py:34
  185.5 8.5 %collective-permute-start.11 = (f32[2,1,16,2048]{3,2,1,0:T(8,128)S(1)}, f32[2,1,16,2048]{3,2,1,0:T(8,128)S(1)}, u32[]{:S(2)}, u32[]{:S(2)}) collective-permute-start(f32[2,1,16,2048]{3,2,1,0:T(8,128)S(1)} %get-tuple-element.362), channel_id=1, source_target_pairs={{0,16},{16,32},{32,48},{48,64},{64,80},{80,96},{96,112},{1,17},{17... | collective-permute-start | bytes 786440 | tf_op jit(solution)/shard_map/ppermute | solution.py:31
  187.9 40.4 %collective-permute-start = (f32[4,512]{1,0:T(4,128)S(1)}, f32[4,512]{1,0:T(4,128)S(1)}, u32[]{:S(2)}, u32[]{:S(2)}) collective-permute-start(f32[4,512]{1,0:T(4,128)S(1)} %get-tuple-element.373), channel_id=1, source_target_pairs={{0,1},{1,2},{2,3},{3,4},{4,5},{5,6},{6,7},{7,8},{8,9},{9,10},{10,1... | collective-permute-start | bytes 24584 | tf_op jit(solution)/shard_map/ppermute | solution.py:31
  191.9 36.4 %collective-permute-start.1 = (f32[4,512]{1,0:T(4,128)S(1)}, f32[4,512]{1,0:T(4,128)S(1)}, u32[]{:S(2)}, u32[]{:S(2)}) collective-permute-start(f32[4,512]{1,0:T(4,128)S(1)} %get-tuple-element.374), channel_id=1, source_target_pairs={{1,0},{2,1},{3,2},{4,3},{5,4},{6,5},{7,6},{8,7},{9,8},{10,9},{11,1... | collective-permute-start | bytes 24584 | tf_op jit(solution)/shard_map/ppermute | solution.py:34
  194.2 9.8 %collective-permute-start.12 = (f32[2,10,1,2048]{3,1,2,0:T(8,128)S(1)}, f32[2,10,1,2048]{3,1,2,0:T(8,128)S(1)}, u32[]{:S(2)}, u32[]{:S(2)}) collective-permute-start(f32[2,10,1,2048]{3,1,2,0:T(8,128)S(1)} %copy.86), channel_id=1, source_target_pairs={{1,0},{2,1},{3,2},{4,3},{5,4},{6,5},{7,6},{8,7},{9,8},{10,9},{11,1... | collective-permute-start | bytes 491528 | tf_op jit(solution)/shard_map/ppermute | solution.py:34
  196.2 9.2 %collective-permute-start.13 = (f32[2,10,1,2048]{3,1,2,0:T(8,128)S(1)}, f32[2,10,1,2048]{3,1,2,0:T(8,128)S(1)}, u32[]{:S(2)}, u32[]{:S(2)}) collective-permute-start(f32[2,10,1,2048]{3,1,2,0:T(8,128)S(1)} %copy.88), channel_id=1, source_target_pairs={{0,1},{1,2},{2,3},{3,4},{4,5},{5,6},{6,7},{7,8},{8,9},{9,10},{10,1... | collective-permute-start | bytes 491528 | tf_op jit(solution)/shard_map/ppermute | solution.py:31
  208.3 19.9 %copy-start.9 = (s32[16,8]{0,1:T(8,128)S(1)}, s32[16,8]{0,1:T(8,128)}, u32[]{:S(2)}) copy-start(s32[16,8]{0,1:T(8,128)} %param.30) | copy-start | bytes 1540
  208.3 6.7 %collective-permute-start.14 = (f32[2,1,16,2048]{3,2,1,0:T(8,128)S(1)}, f32[2,1,16,2048]{3,2,1,0:T(8,128)S(1)}, u32[]{:S(2)}, u32[]{:S(2)}) collective-permute-start(f32[2,1,16,2048]{3,2,1,0:T(8,128)S(1)} %get-tuple-element.361), channel_id=1, source_target_pairs={{16,0},{32,16},{48,32},{64,48},{80,64},{96,80},{112,96},{17,1},{33... | collective-permute-start | bytes 786440 | tf_op jit(solution)/shard_map/ppermute | solution.py:34
  211.1 7.7 %collective-permute-start.15 = (f32[2,1,16,2048]{3,2,1,0:T(8,128)S(1)}, f32[2,1,16,2048]{3,2,1,0:T(8,128)S(1)}, u32[]{:S(2)}, u32[]{:S(2)}) collective-permute-start(f32[2,1,16,2048]{3,2,1,0:T(8,128)S(1)} %get-tuple-element.360), channel_id=1, source_target_pairs={{0,16},{16,32},{32,48},{48,64},{64,80},{80,96},{96,112},{1,17},{17... | collective-permute-start | bytes 786440 | tf_op jit(solution)/shard_map/ppermute | solution.py:31
  219.1 10.7 %collective-permute-start.16 = (f32[2,10,1,2048]{3,1,2,0:T(8,128)S(1)}, f32[2,10,1,2048]{3,1,2,0:T(8,128)S(1)}, u32[]{:S(2)}, u32[]{:S(2)}) collective-permute-start(f32[2,10,1,2048]{3,1,2,0:T(8,128)S(1)} %copy.90), channel_id=1, source_target_pairs={{1,0},{2,1},{3,2},{4,3},{5,4},{6,5},{7,6},{8,7},{9,8},{10,9},{11,1... | collective-permute-start | bytes 491528 | tf_op jit(solution)/shard_map/ppermute | solution.py:34
  221.8 10.5 %collective-permute-start.17 = (f32[2,10,1,2048]{3,1,2,0:T(8,128)}, f32[2,10,1,2048]{3,1,2,0:T(8,128)}, u32[]{:S(2)}, u32[]{:S(2)}) collective-permute-start(f32[2,10,1,2048]{3,1,2,0:T(8,128)} %copy.92), channel_id=1, source_target_pairs={{0,1},{1,2},{2,3},{3,4},{4,5},{5,6},{6,7},{7,8},{8,9},{9,10},{10,1... | collective-permute-start | bytes 491528 | tf_op jit(solution)/shard_map/ppermute | solution.py:31
  236.1 4.4 %copy-start.2 = (f32[2,8,16,2048]{3,2,1,0:T(8,128)}, f32[2,8,16,2048]{3,2,1,0:T(8,128)S(1)}, u32[]{:S(2)}) copy-start(f32[2,8,16,2048]{3,2,1,0:T(8,128)S(1)} %fusion.60) | copy-start | bytes 6291460
  236.2 4.5 %collective-permute-start.18 = (f32[1,16,2048]{2,1,0:T(8,128)S(1)}, f32[1,16,2048]{2,1,0:T(8,128)S(1)}, u32[]{:S(2)}, u32[]{:S(2)}) collective-permute-start(f32[1,16,2048]{2,1,0:T(8,128)S(1)} %get-tuple-element.359), channel_id=1, source_target_pairs={{16,0},{32,16},{48,32},{64,48},{80,64},{96,80},{112,96},{17,1},{33... | collective-permute-start | bytes 393224 | tf_op jit(solution)/shard_map/ppermute | solution.py:34
  238.1 6.4 %collective-permute-start.19 = (f32[1,16,2048]{2,1,0:T(8,128)S(1)}, f32[1,16,2048]{2,1,0:T(8,128)S(1)}, u32[]{:S(2)}, u32[]{:S(2)}) collective-permute-start(f32[1,16,2048]{2,1,0:T(8,128)S(1)} %get-tuple-element.358), channel_id=1, source_target_pairs={{0,16},{16,32},{32,48},{48,64},{64,80},{80,96},{96,112},{1,17},{17... | collective-permute-start | bytes 393224 | tf_op jit(solution)/shard_map/ppermute | solution.py:31
  244.5 8.2 %copy-start.3 = (f32[1,16,2048]{2,1,0:T(8,128)}, f32[1,16,2048]{2,1,0:T(8,128)S(1)}, u32[]{:S(2)}) copy-start(f32[1,16,2048]{2,1,0:T(8,128)S(1)} %collective-permute-done.19) | copy-start | bytes 393220
  245.3 83.4 %collective-permute-start.20 = (f32[10,1,2048]{2,1,0:T(1,128)}, f32[10,1,2048]{2,1,0:T(1,128)}, u32[]{:S(2)}, u32[]{:S(2)}) collective-permute-start(f32[10,1,2048]{2,1,0:T(1,128)} %get-tuple-element.370), channel_id=1, source_target_pairs={{1,0},{2,1},{3,2},{4,3},{5,4},{6,5},{7,6},{8,7},{9,8},{10,9},{11,1... | collective-permute-start | bytes 245768 | tf_op jit(solution)/shard_map/ppermute | solution.py:34
  247.2 81.5 %collective-permute-start.21 = (f32[10,1,2048]{2,1,0:T(1,128)}, f32[10,1,2048]{2,1,0:T(1,128)}, u32[]{:S(2)}, u32[]{:S(2)}) collective-permute-start(f32[10,1,2048]{2,1,0:T(1,128)} %get-tuple-element.371), channel_id=1, source_target_pairs={{0,1},{1,2},{2,3},{3,4},{4,5},{5,6},{6,7},{7,8},{8,9},{9,10},{10,1... | collective-permute-start | bytes 245768 | tf_op jit(solution)/shard_map/ppermute | solution.py:31
  361.5 18.0 %all-to-all-start.3 = ((f32[3,16,256]{2,0,1:T(4,128)}), f32[3,16,256]{2,0,1:T(4,128)S(1)}, u32[]{:S(2)}, u32[]{:S(2)}) async-start(f32[3,16,256]{2,0,1:T(4,128)} %bitcast.33), calls=%async_computation.3 | async-start | bytes 131072 | tf_op jit(solution)/shard_map/all_to_all | solution.py:170
where the time goes:
time: 394 us; the launch traced here: 392 us
  other arithmetic  95.4 us (24%)
  starting transfers between devices  93.7 us (24%)
  local copies, waits for them, and re-layouts  73.4 us (19%)
  matrix products  69.6 us (18%)
  waiting for transfers between devices  56 us (14%)
    reduce_sum x4, other arithmetic, block_force(): return jnp.sum(offset * weight[None], axis=(3, 4))  60 us
    dot_general x16, matrix products, one_piece(): jnp.einsum('srx,mx->srm', fields, column_hot, precision=lax.Precision.HIG...  45.5 us
    ppermute x11, starting transfers between devices, with_halo(): lax.ppermute(lax.slice_in_dim(block, block.shape[dim] - width, None, axis...  38.1 us
    dot_general x8, matrix products, add_piece(): jnp.einsum('smr,mx->srx', weighted, column_hot, precision=lax.Precision.H...  24.1 us
    ppermute x11, waiting for transfers between devices, with_halo(): lax.ppermute(lax.slice_in_dim(block, block.shape[dim] - width, None, axis...  24.1 us
    ppermute x11, starting transfers between devices, with_halo(): lax.ppermute(lax.slice_in_dim(block, 0, width, axis=dim), axis, backward)  23.4 us
    gather x1, local copies, waits for them, and re-layouts, local(): wanted = jnp.where(valid, jnp.take(voxel_local, source), 0)  23 us
    gather x1, local copies, waits for them, and re-layouts, local(): rates = jnp.where(valid, jnp.take(uptake_rate, source), 0.0)  23 us
  transfers between devices with their start and end apart: 26, of which 18 were waited for; matrix products, arithmetic and copies ran while one was open for 27% of the time, Pallas kernels for 0%

commit v1 on v0

--- a/solution.py
+++ b/solution.py
@@ -110,6 +110,64 @@
     empty = jnp.zeros((species, planes, columns), jnp.float32)
     total, unused = lax.scan(add_piece, empty, (pieces, shares))
     return total
+
+
+def neighbours(block, axis, dim):
+    count = lax.axis_size(axis)
+    forward = [(i, i + 1) for i in range(count - 1)]
+    backward = [(target, source) for source, target in forward]
+    low = lax.ppermute(lax.slice_in_dim(block, block.shape[dim] - 1, None, axis=dim), axis, forward)
+    high = lax.ppermute(lax.slice_in_dim(block, 0, 1, axis=dim), axis, backward)
+    return (low, high)
+
+
+def shifted(block, low, high, dim):
+    size = block.shape[dim]
+    up = jnp.concatenate([lax.slice_in_dim(block, 1, size, axis=dim), high], axis=dim)
+    down = jnp.concatenate([low, lax.slice_in_dim(block, 0, size - 1, axis=dim)], axis=dim)
+    return (up, down)
+
+
+def relax_step(center):
+    z_low, z_high = neighbours(center, "slab", 1)
+    y_low, y_high = neighbours(center, "tile", 2)
+    z_up, z_down = shifted(center, z_low, z_high, 1)
+    y_up, y_down = shifted(center, y_low, y_high, 2)
+    sideways = jnp.pad(center, ((0, 0), (0, 0), (0, 0), (1, 1)))
+    beside_all = z_up + z_down
+    beside_all = beside_all + y_up + y_down
+    beside_all = beside_all + sideways[..., 2:] + sideways[..., :-2]
+    spread = jnp.array(DIFFUSION, jnp.float32)[:, None, None, None]
+    losses = jnp.array(DECAY, jnp.float32)[:, None, None, None]
+    return center + spread * (beside_all - 6.0 * center) - losses * center
+
+
+def bits_of(width):
+    return max(1, (width - 1).bit_length())
+
+
+def gather_windows(values, starts, length):
+    channels, cells = values.shape
+    width = cells + length
+    rows = starts.shape[0]
+    padded = jnp.pad(values, ((0, 0), (0, length)))
+    held = jnp.broadcast_to(padded[:, None, :], (channels, rows, width))
+    for bit in range(bits_of(width)):
+        step = 1 << bit
+        take = ((starts >> bit) & 1 == 1)[None, :, None]
+        held = jnp.where(take, jnp.roll(held, -step, axis=2), held)
+    return held[:, :, :length]
+
+
+def scatter_windows(windows, starts, cells):
+    channels, rows, length = windows.shape
+    width = cells + length
+    held = jnp.pad(windows, ((0, 0), (0, 0), (0, width - length)))
+    for bit in range(bits_of(width)):
+        step = 1 << bit
+        take = ((starts >> bit) & 1 == 1)[None, :, None]
+        held = jnp.where(take, jnp.roll(held, step, axis=2), held)
+    return jnp.sum(held[:, :, :cells], axis=1)
 
 
 def local(
@@ -126,52 +184,49 @@
     extended = with_halo(table, (("tile", 1),), HB * 128)
     extended = extended.reshape(4, blocks + 2 * HB, 128)
     group = 4
-    turns = (count // 128 + group - 1) // group
-
-    def one_turn(turn, total):
-        first = turn * group
-        chosen = lax.dynamic_slice_in_dim(neighbor_blocks, first, group, 0)
-        mine = lax.dynamic_slice_in_dim(extended, first + HB, group, 1)
+    parts = []
+    for first in range(0, blocks, group):
+        chosen = neighbor_blocks[first:first + group]
+        mine = extended[:, first + HB:first + HB + group]
         others = jnp.take(extended, chosen.reshape(-1), axis=1).reshape(4, group, K, 128)
-        return lax.dynamic_update_slice_in_dim(total, block_force(mine, others), first, 1)
-
-    forces = lax.fori_loop(0, turns, one_turn, jnp.zeros((3, blocks, 128), jnp.float32))
-    forces = forces.reshape(3, capacity)
+        parts.append(block_force(mine, others))
+    forces = jnp.concatenate(parts, axis=1).reshape(3, capacity)
     sends = send_counts[0]
     ends = jnp.cumsum(sends)
     starts = ends - sends
     ranks = jnp.arange(slot_size, dtype=jnp.int32)
     valid = ranks[None, :] < sends[:, None]
-    source = jnp.where(valid, starts[:, None] + ranks[None, :], 0)
-    wanted = jnp.where(valid, jnp.take(voxel_local, source), 0)
-    rates = jnp.where(valid, jnp.take(uptake_rate, source), 0.0)
+    payload = jnp.stack([voxel_local.astype(jnp.float32), uptake_rate])
+    windows = gather_windows(payload, starts, slot_size)
+    windows = jnp.where(valid[None], windows, 0.0)
+    arrived = lax.all_to_all(windows, "tile", split_axis=1, concat_axis=1, tiled=True)
+    reached = arrived[0].reshape(-1).astype(jnp.int32)
+    rates = arrived[1].reshape(-1)
     species, depth, rows, columns = field.shape
     planes = depth * rows
     oxygen_rows = field[0].reshape(1, planes, columns)
-    incoming = lax.all_to_all(wanted, "tile", split_axis=0, concat_axis=0, tiled=True)
-    reached = incoming.reshape(-1)
-    found = pick_voxels(oxygen_rows, reached).reshape(tiles, slot_size)
-    oxygen = lax.all_to_all(found, "tile", split_axis=0, concat_axis=0, tiled=True)
+    oxygen = pick_voxels(oxygen_rows, reached)[0]
     consume = rates * oxygen / (MICHAELIS_HALF + oxygen)
     secrete = SECRETION * rates * HYPOXIA_HALF / (HYPOXIA_HALF + oxygen)
     amounts = jnp.stack([-STEP_TIME * consume, STEP_TIME * secrete])
-    arrived = lax.all_to_all(amounts, "tile", split_axis=1, concat_axis=1, tiled=True)
-    added = spread_voxels(arrived.reshape(species, -1), reached, planes, columns)
+    added = spread_voxels(amounts, reached, planes, columns)
     state = field + added.reshape(species, depth, rows, columns)
     for step in range(ITERS):
-        state = relax(with_halo(state, (("slab", 1), ("tile", 2)), 1))
-    border = with_halo(state[1], (("slab", 0), ("tile", 1)), 1)
-    rise_z = 0.5 * (border[2:, 1:-1] - border[:-2, 1:-1])
-    rise_y = 0.5 * (border[1:-1, 2:] - border[1:-1, :-2])
-    middle = jnp.pad(border[1:-1, 1:-1], ((0, 0), (0, 0), (1, 1)))
+        state = relax_step(state)
+    vegf = state[1]
+    z_low, z_high = neighbours(vegf, "slab", 0)
+    y_low, y_high = neighbours(vegf, "tile", 1)
+    z_up, z_down = shifted(vegf, z_low, z_high, 0)
+    y_up, y_down = shifted(vegf, y_low, y_high, 1)
+    rise_z = 0.5 * (z_up - z_down)
+    rise_y = 0.5 * (y_up - y_down)
+    middle = jnp.pad(vegf, ((0, 0), (0, 0), (1, 1)))
     rise_x = 0.5 * (middle[..., 2:] - middle[..., :-2])
     rises = jnp.stack([rise_z, rise_y, rise_x]).reshape(3, planes, columns)
     slopes = pick_voxels(rises, reached).reshape(3, tiles, slot_size)
     returned = lax.all_to_all(slopes, "tile", split_axis=1, concat_axis=1, tiled=True)
-    target, rank, routed = routing(sends, capacity)
-    where_back = jnp.clip(target * slot_size + rank, 0, tiles * slot_size - 1)
-    slope = jnp.take(returned.reshape(3, tiles * slot_size), where_back, axis=1)
-    slope = jnp.where(routed[None, :], slope, 0.0)
+    returned = jnp.where(valid[None], returned, 0.0)
+    slope = scatter_windows(returned, starts, capacity)
     velocity = FORCE_SCALE * forces + CHEMOTAXIS * slope
     return (velocity, state)
 

time: 394 us -> 332 us (0.84)
  local copies, waits for them, and re-layouts: 73.4 us -> 21 us
  waiting for transfers between devices: 56 us -> 21.1 us
  other arithmetic: 95.4 us -> 120 us
  starting transfers between devices: 93.7 us -> 89.7 us
    ppermute x0 -> x20, starting transfers between devices: none -> 62.4 us  [the longest x10 36 us: neighbours(): lax.ppermute(lax.slice_in_dim(block, block.shape[dim] - 1, None, axis=dim...]
    gather x7 -> x4, local copies, waits for them, and re-layouts: 56.1 us -> 2.43 us  [local(): jnp.take(extended, chosen.reshape(-1), axis=1).reshape(4, group, K, 128)]
    ppermute x11 -> x1, starting transfers between devices: 38.1 us -> 3.37 us  [with_halo(): lax.ppermute(lax.slice_in_dim(block, block.shape[dim] - width, None, axis...]
    reduce_sum x4 -> x2, other arithmetic: 60 us -> 85 us  [block_force(): return jnp.sum(offset * weight[None], axis=(3, 4))]
    ppermute x11 -> x1, waiting for transfers between devices: 24.1 us -> 0.01 us  [with_halo(): lax.ppermute(lax.slice_in_dim(block, block.shape[dim] - width, None, axis...]
    ppermute x11 -> x1, starting transfers between devices: 23.4 us -> 2.64 us  [with_halo(): lax.ppermute(lax.slice_in_dim(block, 0, width, axis=dim), axis, backward)]
    ppermute x0 -> x20, waiting for transfers between devices: none -> 12.8 us  [the longest x10 10.6 us: neighbours(): lax.ppermute(lax.slice_in_dim(block, block.shape[dim] - 1, None, axis=dim...]
    all_to_all x3 -> x1, waiting for transfers between devices: 12.5 us -> 0.01 us  [local(): lax.all_to_all(windows, 'tile', split_axis=1, concat_axis=1, tiled=True)]
  transfers between devices with their start and end apart: 26 -> 24, of which waited for: 18 -> 12; matrix products, arithmetic and copies ran while one was open for 27% -> 32% of each run, Pallas kernels for 0% -> 0%
where the time goes in v1:
time: 332 us; the launch traced here: 326 us
  other arithmetic  120 us (36%)
  starting transfers between devices  89.7 us (27%)
  matrix products  69.6 us (21%)
  waiting for transfers between devices  21.1 us (6%)
  local copies, waits for them, and re-layouts  21 us (6%)
    reduce_sum x2, other arithmetic, block_force(): return jnp.sum(offset * weight[None], axis=(3, 4))  85 us
    dot_general x16, matrix products, one_piece(): jnp.einsum('srx,mx->srm', fields, column_hot, precision=lax.Precision.HIG...  45.5 us
    ppermute x10, starting transfers between devices, neighbours(): lax.ppermute(lax.slice_in_dim(block, block.shape[dim] - 1, None, axis=dim...  36 us
    ppermute x10, starting transfers between devices, neighbours(): high = lax.ppermute(lax.slice_in_dim(block, 0, 1, axis=dim), axis, backward)  26.4 us
    dot_general x8, matrix products, add_piece(): jnp.einsum('smr,mx->srx', weighted, column_hot, precision=lax.Precision.H...  24.1 us
    all_to_all x1, starting transfers between devices, local(): lax.all_to_all(slopes, 'tile', split_axis=1, concat_axis=1, tiled=True)  13 us
    ppermute x10, waiting for transfers between devices, neighbours(): lax.ppermute(lax.slice_in_dim(block, block.shape[dim] - 1, None, axis=dim...  10.6 us
    sub x4, other arithmetic, relax_step(): return center + spread * (beside_all - 6.0 * center) - losses * center  8.72 us
  transfers between devices with their start and end apart: 24, of which 12 were waited for; matrix products, arithmetic and copies ran while one was open for 32% of the time, Pallas kernels for 0%

profile of v1, /device:TPU:26, one launch (start us, length us, event | category | flops | bytes accessed | tf_op | source)
XLA Modules:
  0.0 326.1 jit_solution(5200408682347082856)
XLA Ops:
  10.7 8.3 %all-to-all-start = ((f32[2,16,256]{2,0,1:T(2,128)}), f32[2,16,256]{2,0,1:T(2,128)S(1)}, u32[]{:S(2)}, u32[]{:S(2)}) async-start(f32[2,16,256]{2,0,1:T(2,128)} %fusion.79), calls=%async_computation | async-start | bytes 65536 | tf_op jit(solution)/shard_map/all_to_all | solution.py:202
  19.7 3.4 %collective-permute-start = (f32[4,512]{1,0:T(4,128)S(1)}, f32[4,512]{1,0:T(4,128)S(1)}, u32[]{:S(2)}, u32[]{:S(2)}) collective-permute-start(f32[4,512]{1,0:T(4,128)S(1)} %get-tuple-element.275), channel_id=1, source_target_pairs={{0,1},{1,2},{2,3},{3,4},{4,5},{5,6},{6,7},{7,8},{8,9},{9,10},{10,1... | collective-permute-start | bytes 24584 | tf_op jit(solution)/shard_map/ppermute | solution.py:31
  23.1 2.6 collective-permute-start.1
  26.6 2.0 collective-permute-done.1
  31.7 2.1 fusion.36
  33.8 2.1 fusion.34
  37.4 42.5 %fusion.35 = (f32[3,4,128]{2,1,0:T(4,128)S(1)}, f32[3,4,128]{2,1,0:T(4,128)S(1)}) fusion(f32[4,128,8,128]{3,2,1,0:T(8,128)S(1)} %subtract_multiply_fusion.11, f32[3,4,8,128]{3,2,1,0:T(8,128)S(1)} %copy.142, f32[3,4,128]{2,1,0:T(4,128)S(1)} %copy.140, f32[4,128,8,128]{3,2,1,0:T(8,128)S(1)} %subtract_multiply_fusion.10, f32[3,4,8,128]{3,2,1,0:T(8,128)S(1)} %copy.145, ...), kind=kLoop, calls=%fused_computation.70 | loop fusion | flops 9434112 | bytes 4317184 | tf_op jit(solution)/shard_map/reduce_sum | solution.py:46
  79.9 2.1 fusion.40
  82.0 2.1 fusion.38
  85.7 42.5 %fusion.39 = (f32[3,4,128]{2,1,0:T(4,128)S(1)}, f32[3,4,128]{2,1,0:T(4,128)S(1)}) fusion(f32[4,128,8,128]{3,2,1,0:T(8,128)S(1)} %subtract_multiply_fusion.9, f32[3,4,8,128]{3,2,1,0:T(8,128)S(1)} %copy.148, f32[3,4,128]{2,1,0:T(4,128)S(1)} %copy.146, f32[4,128,8,128]{3,2,1,0:T(8,128)S(1)} %subtract_multiply_fusion.8, f32[3,4,8,128]{3,2,1,0:T(8,128)S(1)} %copy.151, ...), kind=kLoop, calls=%fused_computation.74 | loop fusion | flops 9434112 | bytes 4317184 | tf_op jit(solution)/shard_map/reduce_sum | solution.py:46
  128.3 21.0 %while.37 = (s32[]{:T(128)}, f32[8,1,512]{2,0,1:T(8,128)S(1)}, s32[8,512]{1,0:T(8,128)S(1)}, f32[1,128,2048]{2,1,0:T(8,128)S(1)}, s32[]{:T(128)}, /*index=5*/s32[]{:T(128)}) while((s32[]{:T(128)}, f32[8,1,512]{2,0,1:T(8,128)S(1)}, s32[8,512]{1,0:T(8,128)S(1)}, f32[1,128,2048]{2,1,0:T(8,128)S(1)}, s32[]{:T(128)}, /*index=5*/s32[]{:T(128)}) %tuple.141), condition=%wide.region_11.13_spmd, body=%wide.region_9.12_spmd.sunk | while | flops 1611867136 | bytes 1069133 | solution.py:91
  128.3 2.5 fusion.122
  130.9 2.5 fusion.122
  133.6 2.5 fusion.122
  136.2 2.5 fusion.122
  138.8 2.5 fusion.122
  141.4 2.5 fusion.122
  144.1 2.5 fusion.122
  146.7 2.5 fusion.122
  149.4 25.3 %while.39 = (s32[]{:T(128)}, f32[2,128,2048]{2,1,0:T(8,128)S(1)}, f32[8,2,512]{2,0,1:T(8,128)S(1)}, s32[8,512]{1,0:T(8,128)S(1)}, s32[]{:T(128)}, /*index=5*/s32[]{:T(128)}) while((s32[]{:T(128)}, f32[2,128,2048]{2,1,0:T(8,128)S(1)}, f32[8,2,512]{2,0,1:T(8,128)S(1)}, s32[8,512]{1,0:T(8,128)S(1)}, s32[]{:T(128)}, ...), condition=%wide.region_13.15_spmd.clone, body=%wide.region_12.14_spmd.clone.sunk | while | flops 3223594496 | bytes 4753495 | solution.py:111
  149.7 3.0 fusion.130
  152.8 3.0 fusion.130
  156.0 3.0 fusion.130
  159.1 3.0 fusion.130
  162.2 3.0 fusion.130
  165.4 3.0 fusion.130
  168.5 3.0 fusion.130
  171.6 3.0 fusion.130
  177.2 1.9 collective-permute-start.2
  179.2 2.4 collective-permute-start.3
  181.6 2.5 collective-permute-start.4
  184.2 3.4 %collective-permute-start.5 = (f32[2,8,1,2048]{3,1,2,0:T(8,128)S(1)}, f32[2,8,1,2048]{3,1,2,0:T(8,128)S(1)}, u32[]{:S(2)}, u32[]{:S(2)}) collective-permute-start(f32[2,8,1,2048]{3,1,2,0:T(8,128)S(1)} %copy.156), channel_id=1, source_target_pairs={{0,1},{1,2},{2,3},{3,4},{4,5},{5,6},{6,7},{7,8},{8,9},{9,10},{10,1... | collective-permute-start | bytes 393224 | tf_op jit(solution)/shard_map/ppermute | solution.py:119
  188.6 2.4 collective-permute-done.5
  191.2 2.2 fusion.47
  194.1 3.1 collective-permute-start.6
  197.2 1.9 collective-permute-start.7
  199.2 1.9 collective-permute-start.8
  201.2 4.2 %collective-permute-start.9 = (f32[2,8,1,2048]{3,1,2,0:T(8,128)S(1)}, f32[2,8,1,2048]{3,1,2,0:T(8,128)S(1)}, u32[]{:S(2)}, u32[]{:S(2)}) collective-permute-start(f32[2,8,1,2048]{3,1,2,0:T(8,128)S(1)} %copy.160), channel_id=1, source_target_pairs={{0,1},{1,2},{2,3},{3,4},{4,5},{5,6},{6,7},{7,8},{8,9},{9,10},{10,1... | collective-permute-start | bytes 393224 | tf_op jit(solution)/shard_map/ppermute | solution.py:119
  208.2 2.2 fusion.53
  211.1 4.1 %collective-permute-start.10 = (f32[2,1,16,2048]{3,2,1,0:T(8,128)S(1)}, f32[2,1,16,2048]{3,2,1,0:T(8,128)S(1)}, u32[]{:S(2)}, u32[]{:S(2)}) collective-permute-start(f32[2,1,16,2048]{3,2,1,0:T(8,128)S(1)} %get-tuple-element.244), channel_id=1, source_target_pairs={{16,0},{32,16},{48,32},{64,48},{80,64},{96,80},{112,96},{17,1},{33... | collective-permute-start | bytes 786440 | tf_op jit(solution)/shard_map/ppermute | solution.py:120
  215.2 1.9 collective-permute-start.11
  217.2 1.9 collective-permute-start.12
  219.2 5.3 %collective-permute-start.13 = (f32[2,8,1,2048]{3,1,2,0:T(8,128)S(1)}, f32[2,8,1,2048]{3,1,2,0:T(8,128)S(1)}, u32[]{:S(2)}, u32[]{:S(2)}) collective-permute-start(f32[2,8,1,2048]{3,1,2,0:T(8,128)S(1)} %copy.164), channel_id=1, source_target_pairs={{0,1},{1,2},{2,3},{3,4},{4,5},{5,6},{6,7},{7,8},{8,9},{9,10},{10,1... | collective-permute-start | bytes 393224 | tf_op jit(solution)/shard_map/ppermute | solution.py:119
  227.2 2.2 fusion.59
  230.1 3.7 %collective-permute-start.14 = (f32[2,1,16,2048]{3,2,1,0:T(8,128)S(1)}, f32[2,1,16,2048]{3,2,1,0:T(8,128)S(1)}, u32[]{:S(2)}, u32[]{:S(2)}) collective-permute-start(f32[2,1,16,2048]{3,2,1,0:T(8,128)S(1)} %get-tuple-element.236), channel_id=1, source_target_pairs={{16,0},{32,16},{48,32},{64,48},{80,64},{96,80},{112,96},{17,1},{33... | collective-permute-start | bytes 786440 | tf_op jit(solution)/shard_map/ppermute | solution.py:120
  233.8 1.9 collective-permute-start.15
  235.8 2.2 collective-permute-start.16
  238.0 6.5 %collective-permute-start.17 = (f32[2,8,1,2048]{3,1,2,0:T(8,128)S(1)}, f32[2,8,1,2048]{3,1,2,0:T(8,128)S(1)}, u32[]{:S(2)}, u32[]{:S(2)}) collective-permute-start(f32[2,8,1,2048]{3,1,2,0:T(8,128)S(1)} %copy.168), channel_id=1, source_target_pairs={{0,1},{1,2},{2,3},{3,4},{4,5},{5,6},{6,7},{7,8},{8,9},{9,10},{10,1... | collective-permute-start | bytes 393224 | tf_op jit(solution)/shard_map/ppermute | solution.py:119
  247.2 2.2 fusion.65
  250.9 1.9 collective-permute-start.20
  252.9 6.5 %collective-permute-start.21 = (f32[8,1,2048]{2,1,0:T(1,128)S(1)}, f32[8,1,2048]{2,1,0:T(1,128)S(1)}, u32[]{:S(2)}, u32[]{:S(2)}) collective-permute-start(f32[8,1,2048]{2,1,0:T(1,128)S(1)} %get-tuple-element.263), channel_id=1, source_target_pairs={{0,1},{1,2},{2,3},{3,4},{4,5},{5,6},{6,7},{7,8},{8,9},{9,10},{10,1... | collective-permute-start | bytes 196616 | tf_op jit(solution)/shard_map/ppermute | solution.py:119
  260.0 3.2 collective-permute-start.18
  265.7 3.8 %collective-permute-done.19 = f32[1,16,2048]{2,1,0:T(8,128)S(1)} collective-permute-done((f32[1,16,2048]{2,1,0:T(8,128)S(1)}, f32[1,16,2048]{2,1,0:T(8,128)S(1)}, u32[]{:S(2)}, u32[]{:S(2)}) %collective-permute-start.19) | collective-permute-done | bytes 131104 | tf_op jit(solution)/shard_map/ppermute | solution.py:119
  269.8 30.7 %while.38 = (s32[]{:T(128)}, f32[8,3,512]{2,1,0:T(4,128)}, s32[8,512]{1,0:T(8,128)S(1)}, f32[3,128,2048]{2,1,0:T(8,128)S(1)}, s32[]{:T(128)}) while((s32[]{:T(128)}, f32[8,3,512]{2,1,0:T(4,128)}, s32[8,512]{1,0:T(8,128)S(1)}, f32[3,128,2048]{2,1,0:T(8,128)S(1)}, s32[]{:T(128)}) %tuple.143), condition=%wide.region_16.18_spmd, body=%wide.region_14.17_spmd.sunk | while | flops 4833419264 | bytes 3705409 | solution.py:91
  269.9 3.2 fusion.126
  273.7 3.2 fusion.126
  277.6 3.2 fusion.126
  281.4 3.2 fusion.126
  285.2 3.2 fusion.126
  289.1 3.2 fusion.126
  292.9 3.2 fusion.126
  296.7 3.2 fusion.126
  300.5 13.0 %all-to-all-start.1 = ((f32[3,16,256]{2,0,1:T(4,128)}), f32[3,16,256]{2,0,1:T(4,128)S(1)}, u32[]{:S(2)}, u32[]{:S(2)}) async-start(f32[3,16,256]{2,0,1:T(4,128)} %bitcast.47), calls=%async_computation.1 | async-start | bytes 131072 | tf_op jit(solution)/shard_map/all_to_all | solution.py:227
  313.5 6.3 %all-to-all-done.1 = f32[3,16,256]{2,0,1:T(4,128)S(1)} async-done(((f32[3,16,256]{2,0,1:T(4,128)}), f32[3,16,256]{2,0,1:T(4,128)S(1)}, u32[]{:S(2)}, u32[]{:S(2)}) %all-to-all-start.1) | async-done | bytes 49184 | tf_op jit(solution)/shard_map/all_to_all | solution.py:227
  (317 shorter events, 47.9 us)
Async XLA Ops:
  4.4 2.1 copy-start.7
  9.0 0.9 copy-start.6
  9.2 10.4 %copy-start.5 = (f32[2048]{0:T(1024)S(1)}, f32[2048]{0:T(1024)}, u32[]{:S(2)}) copy-start(f32[2048]{0:T(1024)} %param.25) | copy-start | bytes 24580
  9.3 10.4 %copy-start.1 = (f32[3,2048]{1,0:T(4,128)S(1)}, f32[3,2048]{1,0:T(4,128)}, u32[]{:S(2)}) copy-start(f32[3,2048]{1,0:T(4,128)} %param.24) | copy-start | bytes 73732
  9.3 16.4 %copy-start.2 = (s32[16,8]{0,1:T(8,128)S(1)}, s32[16,8]{0,1:T(8,128)}, u32[]{:S(2)}) copy-start(s32[16,8]{0,1:T(8,128)} %param.30) | copy-start | bytes 1540
  10.7 117.5 %all-to-all-start = ((f32[2,16,256]{2,0,1:T(2,128)}), f32[2,16,256]{2,0,1:T(2,128)S(1)}, u32[]{:S(2)}, u32[]{:S(2)}) async-start(f32[2,16,256]{2,0,1:T(2,128)} %fusion.79), calls=%async_computation | async-start | bytes 65536 | tf_op jit(solution)/shard_map/all_to_all | solution.py:202
  19.7 6.9 %collective-permute-start = (f32[4,512]{1,0:T(4,128)S(1)}, f32[4,512]{1,0:T(4,128)S(1)}, u32[]{:S(2)}, u32[]{:S(2)}) collective-permute-start(f32[4,512]{1,0:T(4,128)S(1)} %get-tuple-element.275), channel_id=1, source_target_pairs={{0,1},{1,2},{2,3},{3,4},{4,5},{5,6},{6,7},{7,8},{8,9},{9,10},{10,1... | collective-permute-start | bytes 24584 | tf_op jit(solution)/shard_map/ppermute | solution.py:31
  23.1 5.5 %collective-permute-start.1 = (f32[4,512]{1,0:T(4,128)S(1)}, f32[4,512]{1,0:T(4,128)S(1)}, u32[]{:S(2)}, u32[]{:S(2)}) collective-permute-start(f32[4,512]{1,0:T(4,128)S(1)} %get-tuple-element.276), channel_id=1, source_target_pairs={{1,0},{2,1},{3,2},{4,3},{5,4},{6,5},{7,6},{8,7},{9,8},{10,9},{11,1... | collective-permute-start | bytes 24584 | tf_op jit(solution)/shard_map/ppermute | solution.py:34
  85.6 42.6 %slice-start = ((f32[2,8,16,2048]{3,2,1,0:T(8,128)}), f32[1,8,16,2048]{3,2,1,0:T(8,128)S(1)}, s32[]{:S(2)}) async-start(f32[2,8,16,2048]{3,2,1,0:T(8,128)} %param.31), calls=%async_computation.2 | async-start | bytes 2097152 | tf_op jit(solution)/shard_map/slice | solution.py:207
  177.2 14.0 %collective-permute-start.2 = (f32[2,1,16,2048]{3,2,1,0:T(8,128)S(1)}, f32[2,1,16,2048]{3,2,1,0:T(8,128)S(1)}, u32[]{:S(2)}, u32[]{:S(2)}) collective-permute-start(f32[2,1,16,2048]{3,2,1,0:T(8,128)S(1)} %get-tuple-element.260), channel_id=1, source_target_pairs={{16,0},{32,16},{48,32},{64,48},{80,64},{96,80},{112,96},{17,1},{33... | collective-permute-start | bytes 786440 | tf_op jit(solution)/shard_map/ppermute | solution.py:120
  179.2 12.0 %collective-permute-start.3 = (f32[2,1,16,2048]{3,2,1,0:T(8,128)S(1)}, f32[2,1,16,2048]{3,2,1,0:T(8,128)S(1)}, u32[]{:S(2)}, u32[]{:S(2)}) collective-permute-start(f32[2,1,16,2048]{3,2,1,0:T(8,128)S(1)} %get-tuple-element.259), channel_id=1, source_target_pairs={{0,16},{16,32},{32,48},{48,64},{64,80},{80,96},{96,112},{1,17},{17... | collective-permute-start | bytes 786440 | tf_op jit(solution)/shard_map/ppermute | solution.py:119
  181.6 6.9 %collective-permute-start.4 = (f32[2,8,1,2048]{3,1,2,0:T(8,128)S(1)}, f32[2,8,1,2048]{3,1,2,0:T(8,128)S(1)}, u32[]{:S(2)}, u32[]{:S(2)}) collective-permute-start(f32[2,8,1,2048]{3,1,2,0:T(8,128)S(1)} %copy.154), channel_id=1, source_target_pairs={{1,0},{2,1},{3,2},{4,3},{5,4},{6,5},{7,6},{8,7},{9,8},{10,9},{11,1... | collective-permute-start | bytes 393224 | tf_op jit(solution)/shard_map/ppermute | solution.py:120
  184.2 7.0 %copy-start.3 = (f32[2]{0:T(128)S(1)}, f32[2]{0:T(128)}, u32[]{:S(2)}) copy-start(f32[2]{0:T(128)} %constant.241.clone) | copy-start | bytes 28
  184.2 7.0 %copy-start.4 = (f32[2]{0:T(128)S(1)}, f32[2]{0:T(128)}, u32[]{:S(2)}) copy-start(f32[2]{0:T(128)} %constant.242.clone) | copy-start | bytes 28
  184.2 6.9 %collective-permute-start.5 = (f32[2,8,1,2048]{3,1,2,0:T(8,128)S(1)}, f32[2,8,1,2048]{3,1,2,0:T(8,128)S(1)}, u32[]{:S(2)}, u32[]{:S(2)}) collective-permute-start(f32[2,8,1,2048]{3,1,2,0:T(8,128)S(1)} %copy.156), channel_id=1, source_target_pairs={{0,1},{1,2},{2,3},{3,4},{4,5},{5,6},{6,7},{7,8},{8,9},{9,10},{10,1... | collective-permute-start | bytes 393224 | tf_op jit(solution)/shard_map/ppermute | solution.py:119
  194.1 14.0 %collective-permute-start.6 = (f32[2,1,16,2048]{3,2,1,0:T(8,128)S(1)}, f32[2,1,16,2048]{3,2,1,0:T(8,128)S(1)}, u32[]{:S(2)}, u32[]{:S(2)}) collective-permute-start(f32[2,1,16,2048]{3,2,1,0:T(8,128)S(1)} %get-tuple-element.252), channel_id=1, source_target_pairs={{16,0},{32,16},{48,32},{64,48},{80,64},{96,80},{112,96},{17,1},{33... | collective-permute-start | bytes 786440 | tf_op jit(solution)/shard_map/ppermute | solution.py:120
  197.2 11.0 %collective-permute-start.7 = (f32[2,1,16,2048]{3,2,1,0:T(8,128)S(1)}, f32[2,1,16,2048]{3,2,1,0:T(8,128)S(1)}, u32[]{:S(2)}, u32[]{:S(2)}) collective-permute-start(f32[2,1,16,2048]{3,2,1,0:T(8,128)S(1)} %get-tuple-element.251), channel_id=1, source_target_pairs={{0,16},{16,32},{32,48},{48,64},{64,80},{80,96},{96,112},{1,17},{17... | collective-permute-start | bytes 786440 | tf_op jit(solution)/shard_map/ppermute | solution.py:119
  199.2 7.1 %collective-permute-start.8 = (f32[2,8,1,2048]{3,1,2,0:T(8,128)S(1)}, f32[2,8,1,2048]{3,1,2,0:T(8,128)S(1)}, u32[]{:S(2)}, u32[]{:S(2)}) collective-permute-start(f32[2,8,1,2048]{3,1,2,0:T(8,128)S(1)} %copy.158), channel_id=1, source_target_pairs={{1,0},{2,1},{3,2},{4,3},{5,4},{6,5},{7,6},{8,7},{9,8},{10,9},{11,1... | collective-permute-start | bytes 393224 | tf_op jit(solution)/shard_map/ppermute | solution.py:120
  201.2 6.9 %collective-permute-start.9 = (f32[2,8,1,2048]{3,1,2,0:T(8,128)S(1)}, f32[2,8,1,2048]{3,1,2,0:T(8,128)S(1)}, u32[]{:S(2)}, u32[]{:S(2)}) collective-permute-start(f32[2,8,1,2048]{3,1,2,0:T(8,128)S(1)} %copy.160), channel_id=1, source_target_pairs={{0,1},{1,2},{2,3},{3,4},{4,5},{5,6},{6,7},{7,8},{8,9},{9,10},{10,1... | collective-permute-start | bytes 393224 | tf_op jit(solution)/shard_map/ppermute | solution.py:119
  211.1 16.1 %collective-permute-start.10 = (f32[2,1,16,2048]{3,2,1,0:T(8,128)S(1)}, f32[2,1,16,2048]{3,2,1,0:T(8,128)S(1)}, u32[]{:S(2)}, u32[]{:S(2)}) collective-permute-start(f32[2,1,16,2048]{3,2,1,0:T(8,128)S(1)} %get-tuple-element.244), channel_id=1, source_target_pairs={{16,0},{32,16},{48,32},{64,48},{80,64},{96,80},{112,96},{17,1},{33... | collective-permute-start | bytes 786440 | tf_op jit(solution)/shard_map/ppermute | solution.py:120
  215.2 11.9 %collective-permute-start.11 = (f32[2,1,16,2048]{3,2,1,0:T(8,128)S(1)}, f32[2,1,16,2048]{3,2,1,0:T(8,128)S(1)}, u32[]{:S(2)}, u32[]{:S(2)}) collective-permute-start(f32[2,1,16,2048]{3,2,1,0:T(8,128)S(1)} %get-tuple-element.243), channel_id=1, source_target_pairs={{0,16},{16,32},{32,48},{48,64},{64,80},{80,96},{96,112},{1,17},{17... | collective-permute-start | bytes 786440 | tf_op jit(solution)/shard_map/ppermute | solution.py:119
  217.2 8.3 %collective-permute-start.12 = (f32[2,8,1,2048]{3,1,2,0:T(8,128)S(1)}, f32[2,8,1,2048]{3,1,2,0:T(8,128)S(1)}, u32[]{:S(2)}, u32[]{:S(2)}) collective-permute-start(f32[2,8,1,2048]{3,1,2,0:T(8,128)S(1)} %copy.162), channel_id=1, source_target_pairs={{1,0},{2,1},{3,2},{4,3},{5,4},{6,5},{7,6},{8,7},{9,8},{10,9},{11,1... | collective-permute-start | bytes 393224 | tf_op jit(solution)/shard_map/ppermute | solution.py:120
  219.2 7.8 %collective-permute-start.13 = (f32[2,8,1,2048]{3,1,2,0:T(8,128)S(1)}, f32[2,8,1,2048]{3,1,2,0:T(8,128)S(1)}, u32[]{:S(2)}, u32[]{:S(2)}) collective-permute-start(f32[2,8,1,2048]{3,1,2,0:T(8,128)S(1)} %copy.164), channel_id=1, source_target_pairs={{0,1},{1,2},{2,3},{3,4},{4,5},{5,6},{6,7},{7,8},{8,9},{9,10},{10,1... | collective-permute-start | bytes 393224 | tf_op jit(solution)/shard_map/ppermute | solution.py:119
  230.1 17.1 %collective-permute-start.14 = (f32[2,1,16,2048]{3,2,1,0:T(8,128)S(1)}, f32[2,1,16,2048]{3,2,1,0:T(8,128)S(1)}, u32[]{:S(2)}, u32[]{:S(2)}) collective-permute-start(f32[2,1,16,2048]{3,2,1,0:T(8,128)S(1)} %get-tuple-element.236), channel_id=1, source_target_pairs={{16,0},{32,16},{48,32},{64,48},{80,64},{96,80},{112,96},{17,1},{33... | collective-permute-start | bytes 786440 | tf_op jit(solution)/shard_map/ppermute | solution.py:120
  233.8 13.4 %collective-permute-start.15 = (f32[2,1,16,2048]{3,2,1,0:T(8,128)S(1)}, f32[2,1,16,2048]{3,2,1,0:T(8,128)S(1)}, u32[]{:S(2)}, u32[]{:S(2)}) collective-permute-start(f32[2,1,16,2048]{3,2,1,0:T(8,128)S(1)} %get-tuple-element.235), channel_id=1, source_target_pairs={{0,16},{16,32},{32,48},{48,64},{64,80},{80,96},{96,112},{1,17},{17... | collective-permute-start | bytes 786440 | tf_op jit(solution)/shard_map/ppermute | solution.py:119
  235.8 9.7 %collective-permute-start.16 = (f32[2,8,1,2048]{3,1,2,0:T(8,128)S(1)}, f32[2,8,1,2048]{3,1,2,0:T(8,128)S(1)}, u32[]{:S(2)}, u32[]{:S(2)}) collective-permute-start(f32[2,8,1,2048]{3,1,2,0:T(8,128)S(1)} %copy.166), channel_id=1, source_target_pairs={{1,0},{2,1},{3,2},{4,3},{5,4},{6,5},{7,6},{8,7},{9,8},{10,9},{11,1... | collective-permute-start | bytes 393224 | tf_op jit(solution)/shard_map/ppermute | solution.py:120
  238.0 9.0 %collective-permute-start.17 = (f32[2,8,1,2048]{3,1,2,0:T(8,128)S(1)}, f32[2,8,1,2048]{3,1,2,0:T(8,128)S(1)}, u32[]{:S(2)}, u32[]{:S(2)}) collective-permute-start(f32[2,8,1,2048]{3,1,2,0:T(8,128)S(1)} %copy.168), channel_id=1, source_target_pairs={{0,1},{1,2},{2,3},{3,4},{4,5},{5,6},{6,7},{7,8},{8,9},{9,10},{10,1... | collective-permute-start | bytes 393224 | tf_op jit(solution)/shard_map/ppermute | solution.py:119
  249.3 1.3 copy-start
  250.9 14.2 %collective-permute-start.20 = (f32[8,1,2048]{2,1,0:T(1,128)S(1)}, f32[8,1,2048]{2,1,0:T(1,128)S(1)}, u32[]{:S(2)}, u32[]{:S(2)}) collective-permute-start(f32[8,1,2048]{2,1,0:T(1,128)S(1)} %get-tuple-element.264), channel_id=1, source_target_pairs={{1,0},{2,1},{3,2},{4,3},{5,4},{6,5},{7,6},{8,7},{9,8},{10,9},{11,1... | collective-permute-start | bytes 196616 | tf_op jit(solution)/shard_map/ppermute | solution.py:120
  252.9 12.2 %collective-permute-start.21 = (f32[8,1,2048]{2,1,0:T(1,128)S(1)}, f32[8,1,2048]{2,1,0:T(1,128)S(1)}, u32[]{:S(2)}, u32[]{:S(2)}) collective-permute-start(f32[8,1,2048]{2,1,0:T(1,128)S(1)} %get-tuple-element.263), channel_id=1, source_target_pairs={{0,1},{1,2},{2,3},{3,4},{4,5},{5,6},{6,7},{7,8},{8,9},{9,10},{10,1... | collective-permute-start | bytes 196616 | tf_op jit(solution)/shard_map/ppermute | solution.py:119
  260.0 5.7 %collective-permute-start.18 = (f32[1,16,2048]{2,1,0:T(8,128)S(1)}, f32[1,16,2048]{2,1,0:T(8,128)S(1)}, u32[]{:S(2)}, u32[]{:S(2)}) collective-permute-start(f32[1,16,2048]{2,1,0:T(8,128)S(1)} %get-tuple-element.228), channel_id=1, source_target_pairs={{16,0},{32,16},{48,32},{64,48},{80,64},{96,80},{112,96},{17,1},{33... | collective-permute-start | bytes 393224 | tf_op jit(solution)/shard_map/ppermute | solution.py:120
  263.2 6.3 %collective-permute-start.19 = (f32[1,16,2048]{2,1,0:T(8,128)S(1)}, f32[1,16,2048]{2,1,0:T(8,128)S(1)}, u32[]{:S(2)}, u32[]{:S(2)}) collective-permute-start(f32[1,16,2048]{2,1,0:T(8,128)S(1)} %get-tuple-element.227), channel_id=1, source_target_pairs={{0,16},{16,32},{32,48},{48,64},{64,80},{80,96},{96,112},{1,17},{17... | collective-permute-start | bytes 393224 | tf_op jit(solution)/shard_map/ppermute | solution.py:119
  300.5 19.9 %copy-start.8 = (pred[16]{0:T(512)(128)(4,1)S(1)}, pred[16]{0:T(512)(128)(4,1)}, u32[]{:S(2)}) copy-start(pred[16]{0:T(512)(128)(4,1)} %copy-done.7) | copy-start | bytes 52
  300.5 19.3 %all-to-all-start.1 = ((f32[3,16,256]{2,0,1:T(4,128)}), f32[3,16,256]{2,0,1:T(4,128)S(1)}, u32[]{:S(2)}, u32[]{:S(2)}) async-start(f32[3,16,256]{2,0,1:T(4,128)} %bitcast.47), calls=%async_computation.1 | async-start | bytes 131072 | tf_op jit(solution)/shard_map/all_to_all | solution.py:227

commit v2 on v1

--- a/solution.py
+++ b/solution.py
@@ -1,6 +1,8 @@
 import jax
 import jax.numpy as jnp
 from jax import lax
+from jax.experimental import pallas as pl
+from jax.experimental.pallas import tpu as pltpu
 from jax.sharding import PartitionSpec as P
 
 HB = 4
@@ -112,6 +114,63 @@
     return total
 
 
+def force_kernel(chosen_ref, rows_ref, cols_ref, out_ref):
+    blocks = out_ref.shape[0]
+    picks = chosen_ref.shape[0] // blocks
+    chunks = cols_ref.shape[2] // 8
+    shape = (8, cols_ref.shape[3])
+
+    def one_block(block, carry):
+        own = rows_ref[block + HB]
+        mine = [jnp.broadcast_to(own[axis:axis + 1, :], shape) for axis in range(4)]
+
+        def one_pick(pick, totals):
+            other = chosen_ref[block * picks + pick]
+            totals = list(totals)
+            for chunk in range(chunks):
+                part = pl.ds(chunk * 8, 8)
+                offset = [mine[axis] - cols_ref[other, axis, part, :] for axis in range(3)]
+                distance = offset[0] * offset[0] + offset[1] * offset[1] + offset[2] * offset[2]
+                strength = REPULSION * jnp.exp(-distance / REPEL_RANGE) - ADHESION * jnp.exp(
+                    -distance / ADHERE_RANGE
+                )
+                weight = mine[3] * cols_ref[other, 3, part, :] * strength
+                for axis in range(3):
+                    totals[axis] = totals[axis] + offset[axis] * weight
+            return tuple(totals)
+
+        zero = jnp.zeros(shape, jnp.float32)
+        totals = lax.fori_loop(0, picks, one_pick, (zero, zero, zero))
+        out_ref[block] = jnp.concatenate(
+            [jnp.sum(total, axis=0, keepdims=True) for total in totals], axis=0
+        )
+        return carry
+
+    lax.fori_loop(0, blocks, one_block, 0)
+
+
+def pair_forces(extended, neighbor_blocks):
+    coords, span, lanes = extended.shape
+    blocks, picks = neighbor_blocks.shape
+    rows = jnp.transpose(extended, (1, 0, 2))
+    cols = jnp.broadcast_to(rows[:, :, :, None], (span, coords, lanes, lanes))
+    pairs = blocks * picks * lanes * lanes
+    out = pl.pallas_call(
+        force_kernel,
+        out_shape=jax.ShapeDtypeStruct((blocks, 3, lanes), jnp.float32),
+        in_specs=[
+            pl.BlockSpec(memory_space=pltpu.SMEM),
+            pl.BlockSpec(memory_space=pltpu.VMEM),
+            pl.BlockSpec(memory_space=pltpu.VMEM),
+        ],
+        out_specs=pl.BlockSpec(memory_space=pltpu.VMEM),
+        cost_estimate=pl.CostEstimate(
+            flops=26 * pairs, transcendentals=2 * pairs, bytes_accessed=4 * cols.size
+        ),
+    )(neighbor_blocks.reshape(-1), rows, cols)
+    return jnp.transpose(out, (1, 0, 2))
+
+
 def neighbours(block, axis, dim):
     count = lax.axis_size(axis)
     forward = [(i, i + 1) for i in range(count - 1)]
@@ -183,14 +242,7 @@
     table = jnp.concatenate([positions, kept[None]], axis=0)
     extended = with_halo(table, (("tile", 1),), HB * 128)
     extended = extended.reshape(4, blocks + 2 * HB, 128)
-    group = 4
-    parts = []
-    for first in range(0, blocks, group):
-        chosen = neighbor_blocks[first:first + group]
-        mine = extended[:, first + HB:first + HB + group]
-        others = jnp.take(extended, chosen.reshape(-1), axis=1).reshape(4, group, K, 128)
-        parts.append(block_force(mine, others))
-    forces = jnp.concatenate(parts, axis=1).reshape(3, capacity)
+    forces = pair_forces(extended, neighbor_blocks).reshape(3, capacity)
     sends = send_counts[0]
     ends = jnp.cumsum(sends)
     starts = ends - sends

time: 332 us -> 229 us (0.69); the launches traced: 326 us -> 228 us
  other arithmetic: 120 us -> 23.5 us
  Pallas kernels: 0 us -> 11.9 us
  waiting for transfers between devices: 21.1 us -> 14 us
  starting transfers between devices: 89.7 us -> 83.4 us
    reduce_sum x6 -> x0, other arithmetic: 93.4 us -> none  [the longest x2 85 us: block_force(): return jnp.sum(offset * weight[None], axis=(3, 4))]
    pallas_call x0 -> x1, Pallas kernels: none -> 11.9 us  [pair_forces(): pl.pallas_call(force_kernel, out_shape=jax.ShapeDtypeStruct((blocks, 3, l...]
    all_to_all x1, waiting for transfers between devices: 6.29 us -> 0.01 us  [local(): lax.all_to_all(slopes, 'tile', split_axis=1, concat_axis=1, tiled=True)]
    ppermute x10, starting transfers between devices: 36 us -> 31.4 us  [neighbours(): lax.ppermute(lax.slice_in_dim(block, block.shape[dim] - 1, None, axis=dim...]
    broadcast_in_dim x0 -> x1, local copies, waits for them, and re-layouts: none -> 3.83 us  [pair_forces(): cols = jnp.broadcast_to(rows[:, :, :, None], (span, coords, lanes, lanes))]
  transfers between devices with their start and end apart: 24 -> 24, of which waited for: 12 -> 9; matrix products, arithmetic and copies ran while one was open for 32% -> 43% of each run, Pallas kernels for 0% -> 5%
where the time goes in v2:
time: 229 us; the launch traced here: 228 us
  starting transfers between devices  83.4 us (36%)
  matrix products  69.5 us (30%)
  other arithmetic  23.5 us (10%)
  local copies, waits for them, and re-layouts  22.6 us (10%)
  waiting for transfers between devices  14 us (6%)
  Pallas kernels  11.9 us (5%)
  between operations  2.46 us (1%)
    dot_general x16, matrix products, one_piece(): jnp.einsum('srx,mx->srm', fields, column_hot, precision=lax.Precision.HIG...  45.5 us
    ppermute x10, starting transfers between devices, neighbours(): lax.ppermute(lax.slice_in_dim(block, block.shape[dim] - 1, None, axis=dim...  31.4 us
    ppermute x10, starting transfers between devices, neighbours(): high = lax.ppermute(lax.slice_in_dim(block, 0, 1, axis=dim), axis, backward)  26.6 us
    dot_general x8, matrix products, add_piece(): jnp.einsum('smr,mx->srx', weighted, column_hot, precision=lax.Precision.H...  24.1 us
    pallas_call x1, Pallas kernels, pair_forces(): pl.pallas_call(force_kernel, out_shape=jax.ShapeDtypeStruct((blocks, 3, l...  11.9 us
    all_to_all x1, starting transfers between devices, local(): lax.all_to_all(slopes, 'tile', split_axis=1, concat_axis=1, tiled=True)  11.8 us
    ppermute x10, waiting for transfers between devices, neighbours(): lax.ppermute(lax.slice_in_dim(block, block.shape[dim] - 1, None, axis=dim...  10.8 us
    sub x4, other arithmetic, relax_step(): return center + spread * (beside_all - 6.0 * center) - losses * center  8.72 us
  transfers between devices with their start and end apart: 24, of which 9 were waited for; matrix products, arithmetic and copies ran while one was open for 43% of the time, Pallas kernels for 5%

profile of v2, /device:TPU:26, one launch (start us, length us, event | category | flops | bytes accessed | tf_op | source)
XLA Modules:
  0.0 228.3 jit_solution(2484305575992404658)
XLA Ops:
  10.7 8.3 %all-to-all-start = ((f32[2,16,256]{2,0,1:T(2,128)}), f32[2,16,256]{2,0,1:T(2,128)S(1)}, u32[]{:S(2)}, u32[]{:S(2)}) async-start(f32[2,16,256]{2,0,1:T(2,128)} %fusion.71), calls=%async_computation | async-start | bytes 65536 | tf_op jit(solution)/shard_map/all_to_all | solution.py:254
  19.7 3.4 %collective-permute-start = (f32[4,512]{1,0:T(4,128)S(1)}, f32[4,512]{1,0:T(4,128)S(1)}, u32[]{:S(2)}, u32[]{:S(2)}) collective-permute-start(f32[4,512]{1,0:T(4,128)S(1)} %get-tuple-element.266), channel_id=1, source_target_pairs={{0,1},{1,2},{2,3},{3,4},{4,5},{5,6},{6,7},{7,8},{8,9},{9,10},{10,1... | collective-permute-start | bytes 24584 | tf_op jit(solution)/shard_map/ppermute | solution.py:33
  23.9 1.4 all-to-all-done
  25.3 21.0 %while.37 = (s32[]{:T(128)}, f32[8,1,512]{2,0,1:T(8,128)S(1)}, s32[8,512]{1,0:T(8,128)S(1)}, f32[1,128,2048]{2,1,0:T(8,128)S(1)}, s32[]{:T(128)}, /*index=5*/s32[]{:T(128)}) while((s32[]{:T(128)}, f32[8,1,512]{2,0,1:T(8,128)S(1)}, s32[8,512]{1,0:T(8,128)S(1)}, f32[1,128,2048]{2,1,0:T(8,128)S(1)}, s32[]{:T(128)}, /*index=5*/s32[]{:T(128)}) %tuple.129), condition=%wide.region_3.4_spmd, body=%wide.region_1.3_spmd.sunk | while | flops 1611867136 | bytes 1069133 | solution.py:93
  25.3 2.5 %fusion.110 = f32[512]{0:T(512)S(1)} fusion(s32[512]{0:T(512)S(1)} %get-tuple-element.354, f32[1,128,2048]{2,1,0:T(8,128)S(1)} %get-tuple-element.383, s32[512]{0:T(512)S(1)} %get-tuple-element.355), kind=kOutput, calls=%fused_computation.5.clone.1 | convolution fusion | flops 1611857408 | bytes 1054720 | tf_op jit(solution)/shard_map/while/body/eval_jaxpr/srx,mx->srm/dot_general | solution.py:90
  28.0 2.5 %fusion.110 = f32[512]{0:T(512)S(1)} fusion(s32[512]{0:T(512)S(1)} %get-tuple-element.354, f32[1,128,2048]{2,1,0:T(8,128)S(1)} %get-tuple-element.383, s32[512]{0:T(512)S(1)} %get-tuple-element.355), kind=kOutput, calls=%fused_computation.5.clone.1 | convolution fusion | flops 1611857408 | bytes 1054720 | tf_op jit(solution)/shard_map/while/body/eval_jaxpr/srx,mx->srm/dot_general | solution.py:90
  30.6 2.5 %fusion.110 = f32[512]{0:T(512)S(1)} fusion(s32[512]{0:T(512)S(1)} %get-tuple-element.354, f32[1,128,2048]{2,1,0:T(8,128)S(1)} %get-tuple-element.383, s32[512]{0:T(512)S(1)} %get-tuple-element.355), kind=kOutput, calls=%fused_computation.5.clone.1 | convolution fusion | flops 1611857408 | bytes 1054720 | tf_op jit(solution)/shard_map/while/body/eval_jaxpr/srx,mx->srm/dot_general | solution.py:90
  33.2 2.5 %fusion.110 = f32[512]{0:T(512)S(1)} fusion(s32[512]{0:T(512)S(1)} %get-tuple-element.354, f32[1,128,2048]{2,1,0:T(8,128)S(1)} %get-tuple-element.383, s32[512]{0:T(512)S(1)} %get-tuple-element.355), kind=kOutput, calls=%fused_computation.5.clone.1 | convolution fusion | flops 1611857408 | bytes 1054720 | tf_op jit(solution)/shard_map/while/body/eval_jaxpr/srx,mx->srm/dot_general | solution.py:90
  35.8 2.5 %fusion.110 = f32[512]{0:T(512)S(1)} fusion(s32[512]{0:T(512)S(1)} %get-tuple-element.354, f32[1,128,2048]{2,1,0:T(8,128)S(1)} %get-tuple-element.383, s32[512]{0:T(512)S(1)} %get-tuple-element.355), kind=kOutput, calls=%fused_computation.5.clone.1 | convolution fusion | flops 1611857408 | bytes 1054720 | tf_op jit(solution)/shard_map/while/body/eval_jaxpr/srx,mx->srm/dot_general | solution.py:90
  38.5 2.5 %fusion.110 = f32[512]{0:T(512)S(1)} fusion(s32[512]{0:T(512)S(1)} %get-tuple-element.354, f32[1,128,2048]{2,1,0:T(8,128)S(1)} %get-tuple-element.383, s32[512]{0:T(512)S(1)} %get-tuple-element.355), kind=kOutput, calls=%fused_computation.5.clone.1 | convolution fusion | flops 1611857408 | bytes 1054720 | tf_op jit(solution)/shard_map/while/body/eval_jaxpr/srx,mx->srm/dot_general | solution.py:90
  41.1 2.5 %fusion.110 = f32[512]{0:T(512)S(1)} fusion(s32[512]{0:T(512)S(1)} %get-tuple-element.354, f32[1,128,2048]{2,1,0:T(8,128)S(1)} %get-tuple-element.383, s32[512]{0:T(512)S(1)} %get-tuple-element.355), kind=kOutput, calls=%fused_computation.5.clone.1 | convolution fusion | flops 1611857408 | bytes 1054720 | tf_op jit(solution)/shard_map/while/body/eval_jaxpr/srx,mx->srm/dot_general | solution.py:90
  43.7 2.5 %fusion.110 = f32[512]{0:T(512)S(1)} fusion(s32[512]{0:T(512)S(1)} %get-tuple-element.354, f32[1,128,2048]{2,1,0:T(8,128)S(1)} %get-tuple-element.383, s32[512]{0:T(512)S(1)} %get-tuple-element.355), kind=kOutput, calls=%fused_computation.5.clone.1 | convolution fusion | flops 1611857408 | bytes 1054720 | tf_op jit(solution)/shard_map/while/body/eval_jaxpr/srx,mx->srm/dot_general | solution.py:90
  46.4 25.0 %while.39 = (s32[]{:T(128)}, f32[2,128,2048]{2,1,0:T(8,128)S(1)}, f32[8,2,512]{2,0,1:T(8,128)S(1)}, s32[8,512]{1,0:T(8,128)S(1)}, s32[]{:T(128)}, /*index=5*/s32[]{:T(128)}) while((s32[]{:T(128)}, f32[2,128,2048]{2,1,0:T(8,128)S(1)}, f32[8,2,512]{2,0,1:T(8,128)S(1)}, s32[8,512]{1,0:T(8,128)S(1)}, s32[]{:T(128)}, ...), condition=%wide.region_5.6_spmd.clone, body=%wide.region_4.5_spmd.clone.sunk | while | flops 3223594496 | bytes 4753495 | solution.py:113
  46.5 3.0 %fusion.118 = f32[2,128,2048]{2,1,0:T(8,128)S(1)} fusion(f32[2,128,2048]{2,1,0:T(8,128)S(1)} %get-tuple-element.393, s32[512]{0:T(512)S(1)} %get-tuple-element.366, pred[]{:T(512)S(6)} %compare.53, f32[512,128]{0,1:T(8,128)S(1)} %fusion.117, f32[2,512]{1,0:T(2,128)S(1)} %bitcast.137), kind=kOutput, calls=%fused_computation.39.clone.1 | convolution fusion | flops 3223453696 | bytes 4462593 | tf_op jit(solution)/shard_map/while/body/eval_jaxpr/smr,mx->srx/dot_general | solution.py:108
  49.7 3.0 %fusion.118 = f32[2,128,2048]{2,1,0:T(8,128)S(1)} fusion(f32[2,128,2048]{2,1,0:T(8,128)S(1)} %get-tuple-element.393, s32[512]{0:T(512)S(1)} %get-tuple-element.366, pred[]{:T(512)S(6)} %compare.53, f32[512,128]{0,1:T(8,128)S(1)} %fusion.117, f32[2,512]{1,0:T(2,128)S(1)} %bitcast.137), kind=kOutput, calls=%fused_computation.39.clone.1 | convolution fusion | flops 3223453696 | bytes 4462593 | tf_op jit(solution)/shard_map/while/body/eval_jaxpr/smr,mx->srx/dot_general | solution.py:108
  52.8 3.0 %fusion.118 = f32[2,128,2048]{2,1,0:T(8,128)S(1)} fusion(f32[2,128,2048]{2,1,0:T(8,128)S(1)} %get-tuple-element.393, s32[512]{0:T(512)S(1)} %get-tuple-element.366, pred[]{:T(512)S(6)} %compare.53, f32[512,128]{0,1:T(8,128)S(1)} %fusion.117, f32[2,512]{1,0:T(2,128)S(1)} %bitcast.137), kind=kOutput, calls=%fused_computation.39.clone.1 | convolution fusion | flops 3223453696 | bytes 4462593 | tf_op jit(solution)/shard_map/while/body/eval_jaxpr/smr,mx->srx/dot_general | solution.py:108
  55.9 3.0 %fusion.118 = f32[2,128,2048]{2,1,0:T(8,128)S(1)} fusion(f32[2,128,2048]{2,1,0:T(8,128)S(1)} %get-tuple-element.393, s32[512]{0:T(512)S(1)} %get-tuple-element.366, pred[]{:T(512)S(6)} %compare.53, f32[512,128]{0,1:T(8,128)S(1)} %fusion.117, f32[2,512]{1,0:T(2,128)S(1)} %bitcast.137), kind=kOutput, calls=%fused_computation.39.clone.1 | convolution fusion | flops 3223453696 | bytes 4462593 | tf_op jit(solution)/shard_map/while/body/eval_jaxpr/smr,mx->srx/dot_general | solution.py:108
  59.0 3.0 %fusion.118 = f32[2,128,2048]{2,1,0:T(8,128)S(1)} fusion(f32[2,128,2048]{2,1,0:T(8,128)S(1)} %get-tuple-element.393, s32[512]{0:T(512)S(1)} %get-tuple-element.366, pred[]{:T(512)S(6)} %compare.53, f32[512,128]{0,1:T(8,128)S(1)} %fusion.117, f32[2,512]{1,0:T(2,128)S(1)} %bitcast.137), kind=kOutput, calls=%fused_computation.39.clone.1 | convolution fusion | flops 3223453696 | bytes 4462593 | tf_op jit(solution)/shard_map/while/body/eval_jaxpr/smr,mx->srx/dot_general | solution.py:108
  62.2 3.0 %fusion.118 = f32[2,128,2048]{2,1,0:T(8,128)S(1)} fusion(f32[2,128,2048]{2,1,0:T(8,128)S(1)} %get-tuple-element.393, s32[512]{0:T(512)S(1)} %get-tuple-element.366, pred[]{:T(512)S(6)} %compare.53, f32[512,128]{0,1:T(8,128)S(1)} %fusion.117, f32[2,512]{1,0:T(2,128)S(1)} %bitcast.137), kind=kOutput, calls=%fused_computation.39.clone.1 | convolution fusion | flops 3223453696 | bytes 4462593 | tf_op jit(solution)/shard_map/while/body/eval_jaxpr/smr,mx->srx/dot_general | solution.py:108
  65.3 3.0 %fusion.118 = f32[2,128,2048]{2,1,0:T(8,128)S(1)} fusion(f32[2,128,2048]{2,1,0:T(8,128)S(1)} %get-tuple-element.393, s32[512]{0:T(512)S(1)} %get-tuple-element.366, pred[]{:T(512)S(6)} %compare.53, f32[512,128]{0,1:T(8,128)S(1)} %fusion.117, f32[2,512]{1,0:T(2,128)S(1)} %bitcast.137), kind=kOutput, calls=%fused_computation.39.clone.1 | convolution fusion | flops 3223453696 | bytes 4462593 | tf_op jit(solution)/shard_map/while/body/eval_jaxpr/smr,mx->srx/dot_general | solution.py:108
  68.4 3.0 %fusion.118 = f32[2,128,2048]{2,1,0:T(8,128)S(1)} fusion(f32[2,128,2048]{2,1,0:T(8,128)S(1)} %get-tuple-element.393, s32[512]{0:T(512)S(1)} %get-tuple-element.366, pred[]{:T(512)S(6)} %compare.53, f32[512,128]{0,1:T(8,128)S(1)} %fusion.117, f32[2,512]{1,0:T(2,128)S(1)} %bitcast.137), kind=kOutput, calls=%fused_computation.39.clone.1 | convolution fusion | flops 3223453696 | bytes 4462593 | tf_op jit(solution)/shard_map/while/body/eval_jaxpr/smr,mx->srx/dot_general | solution.py:108
  71.5 1.8 add.207
  74.0 1.9 collective-permute-start.2
  76.0 2.4 %collective-permute-start.3 = (f32[2,1,16,2048]{3,2,1,0:T(8,128)S(1)}, f32[2,1,16,2048]{3,2,1,0:T(8,128)S(1)}, u32[]{:S(2)}, u32[]{:S(2)}) collective-permute-start(f32[2,1,16,2048]{3,2,1,0:T(8,128)S(1)} %get-tuple-element.258), channel_id=1, source_target_pairs={{0,16},{16,32},{32,48},{48,64},{64,80},{80,96},{96,112},{1,17},{17... | collective-permute-start | bytes 786440 | tf_op jit(solution)/shard_map/ppermute | solution.py:178
  78.4 3.4 %collective-permute-start.4 = (f32[2,8,1,2048]{3,1,2,0:T(8,128)S(1)}, f32[2,8,1,2048]{3,1,2,0:T(8,128)S(1)}, u32[]{:S(2)}, u32[]{:S(2)}) collective-permute-start(f32[2,8,1,2048]{3,1,2,0:T(8,128)S(1)} %copy.63), channel_id=1, source_target_pairs={{1,0},{2,1},{3,2},{4,3},{5,4},{6,5},{7,6},{8,7},{9,8},{10,9},{11,1... | collective-permute-start | bytes 393224 | tf_op jit(solution)/shard_map/ppermute | solution.py:179
  81.9 2.7 %collective-permute-start.5 = (f32[2,8,1,2048]{3,1,2,0:T(8,128)S(1)}, f32[2,8,1,2048]{3,1,2,0:T(8,128)S(1)}, u32[]{:S(2)}, u32[]{:S(2)}) collective-permute-start(f32[2,8,1,2048]{3,1,2,0:T(8,128)S(1)} %copy.65), channel_id=1, source_target_pairs={{0,1},{1,2},{2,3},{3,4},{4,5},{5,6},{6,7},{7,8},{8,9},{9,10},{10,1... | collective-permute-start | bytes 393224 | tf_op jit(solution)/shard_map/ppermute | solution.py:178
  85.4 3.3 %collective-permute-done.5 = f32[2,8,1,2048]{3,1,2,0:T(8,128)S(1)} collective-permute-done((f32[2,8,1,2048]{3,1,2,0:T(8,128)S(1)}, f32[2,8,1,2048]{3,1,2,0:T(8,128)S(1)}, u32[]{:S(2)}, u32[]{:S(2)}) %collective-permute-start.5) | collective-permute-done | bytes 131104 | tf_op jit(solution)/shard_map/ppermute | solution.py:178
  88.9 2.2 fusion.39
  91.8 3.1 %collective-permute-start.6 = (f32[2,1,16,2048]{3,2,1,0:T(8,128)S(1)}, f32[2,1,16,2048]{3,2,1,0:T(8,128)S(1)}, u32[]{:S(2)}, u32[]{:S(2)}) collective-permute-start(f32[2,1,16,2048]{3,2,1,0:T(8,128)S(1)} %get-tuple-element.251), channel_id=1, source_target_pairs={{16,0},{32,16},{48,32},{64,48},{80,64},{96,80},{112,96},{17,1},{33... | collective-permute-start | bytes 786440 | tf_op jit(solution)/shard_map/ppermute | solution.py:179
  94.9 1.9 collective-permute-start.7
  96.9 1.9 collective-permute-start.8
  98.9 3.9 %collective-permute-start.9 = (f32[2,8,1,2048]{3,1,2,0:T(8,128)S(1)}, f32[2,8,1,2048]{3,1,2,0:T(8,128)S(1)}, u32[]{:S(2)}, u32[]{:S(2)}) collective-permute-start(f32[2,8,1,2048]{3,1,2,0:T(8,128)S(1)} %copy.69), channel_id=1, source_target_pairs={{0,1},{1,2},{2,3},{3,4},{4,5},{5,6},{6,7},{7,8},{8,9},{9,10},{10,1... | collective-permute-start | bytes 393224 | tf_op jit(solution)/shard_map/ppermute | solution.py:178
  103.9 1.8 collective-permute-done.9
  105.9 2.2 fusion.45
  108.8 4.1 %collective-permute-start.10 = (f32[2,1,16,2048]{3,2,1,0:T(8,128)S(1)}, f32[2,1,16,2048]{3,2,1,0:T(8,128)S(1)}, u32[]{:S(2)}, u32[]{:S(2)}) collective-permute-start(f32[2,1,16,2048]{3,2,1,0:T(8,128)S(1)} %get-tuple-element.243), channel_id=1, source_target_pairs={{16,0},{32,16},{48,32},{64,48},{80,64},{96,80},{112,96},{17,1},{33... | collective-permute-start | bytes 786440 | tf_op jit(solution)/shard_map/ppermute | solution.py:179
  112.9 1.9 collective-permute-start.11
  114.9 1.9 collective-permute-start.12
  116.9 3.9 %collective-permute-start.13 = (f32[2,8,1,2048]{3,1,2,0:T(8,128)S(1)}, f32[2,8,1,2048]{3,1,2,0:T(8,128)S(1)}, u32[]{:S(2)}, u32[]{:S(2)}) collective-permute-start(f32[2,8,1,2048]{3,1,2,0:T(8,128)S(1)} %copy.73), channel_id=1, source_target_pairs={{0,1},{1,2},{2,3},{3,4},{4,5},{5,6},{6,7},{7,8},{8,9},{9,10},{10,1... | collective-permute-start | bytes 393224 | tf_op jit(solution)/shard_map/ppermute | solution.py:178
  121.9 1.8 collective-permute-done.13
  123.9 2.2 fusion.51
  126.8 3.5 %collective-permute-start.14 = (f32[2,1,16,2048]{3,2,1,0:T(8,128)S(1)}, f32[2,1,16,2048]{3,2,1,0:T(8,128)S(1)}, u32[]{:S(2)}, u32[]{:S(2)}) collective-permute-start(f32[2,1,16,2048]{3,2,1,0:T(8,128)S(1)} %get-tuple-element.235), channel_id=1, source_target_pairs={{16,0},{32,16},{48,32},{64,48},{80,64},{96,80},{112,96},{17,1},{33... | collective-permute-start | bytes 786440 | tf_op jit(solution)/shard_map/ppermute | solution.py:179
  130.3 1.9 collective-permute-start.15
  132.3 1.9 collective-permute-start.16
  134.3 4.1 %collective-permute-start.17 = (f32[2,8,1,2048]{3,1,2,0:T(8,128)S(1)}, f32[2,8,1,2048]{3,1,2,0:T(8,128)S(1)}, u32[]{:S(2)}, u32[]{:S(2)}) collective-permute-start(f32[2,8,1,2048]{3,1,2,0:T(8,128)S(1)} %copy.77), channel_id=1, source_target_pairs={{0,1},{1,2},{2,3},{3,4},{4,5},{5,6},{6,7},{7,8},{8,9},{9,10},{10,1... | collective-permute-start | bytes 393224 | tf_op jit(solution)/shard_map/ppermute | solution.py:178
  139.4 1.9 collective-permute-start.1
  141.6 2.2 fusion.57
  144.0 1.1 copy-done
  145.4 1.9 collective-permute-start.20
  147.4 6.5 %collective-permute-start.21 = (f32[8,1,2048]{2,1,0:T(1,128)S(1)}, f32[8,1,2048]{2,1,0:T(1,128)S(1)}, u32[]{:S(2)}, u32[]{:S(2)}) collective-permute-start(f32[8,1,2048]{2,1,0:T(1,128)S(1)} %get-tuple-element.262), channel_id=1, source_target_pairs={{0,1},{1,2},{2,3},{3,4},{4,5},{5,6},{6,7},{7,8},{8,9},{9,10},{10,1... | collective-permute-start | bytes 196616 | tf_op jit(solution)/shard_map/ppermute | solution.py:178
  154.5 2.9 %collective-permute-start.18 = (f32[1,16,2048]{2,1,0:T(8,128)S(1)}, f32[1,16,2048]{2,1,0:T(8,128)S(1)}, u32[]{:S(2)}, u32[]{:S(2)}) collective-permute-start(f32[1,16,2048]{2,1,0:T(8,128)S(1)} %get-tuple-element.227), channel_id=1, source_target_pairs={{16,0},{32,16},{48,32},{64,48},{80,64},{96,80},{112,96},{17,1},{33... | collective-permute-start | bytes 393224 | tf_op jit(solution)/shard_map/ppermute | solution.py:179
  157.4 2.1 collective-permute-start.19
  159.9 3.8 %collective-permute-done.19 = f32[1,16,2048]{2,1,0:T(8,128)S(1)} collective-permute-done((f32[1,16,2048]{2,1,0:T(8,128)S(1)}, f32[1,16,2048]{2,1,0:T(8,128)S(1)}, u32[]{:S(2)}, u32[]{:S(2)}) %collective-permute-start.19) | collective-permute-done | bytes 131104 | tf_op jit(solution)/shard_map/ppermute | solution.py:178
  164.0 30.7 %while.38 = (s32[]{:T(128)}, f32[8,3,512]{2,1,0:T(4,128)}, s32[8,512]{1,0:T(8,128)S(1)}, f32[3,128,2048]{2,1,0:T(8,128)S(1)}, s32[]{:T(128)}) while((s32[]{:T(128)}, f32[8,3,512]{2,1,0:T(4,128)}, s32[8,512]{1,0:T(8,128)S(1)}, f32[3,128,2048]{2,1,0:T(8,128)S(1)}, s32[]{:T(128)}) %tuple.131), condition=%wide.region_8.9_spmd, body=%wide.region_6.8_spmd.sunk | while | flops 4833419264 | bytes 3705409 | solution.py:93
  164.1 3.2 %fusion.114 = f32[3,512]{1,0:T(4,128)S(1)} fusion(f32[3,128,2048]{2,1,0:T(8,128)S(1)} %get-tuple-element.417, s32[512]{0:T(512)S(1)} %get-tuple-element.360, f32[128,512]{1,0:T(8,128)S(1)} %fusion.113), kind=kOutput, calls=%fused_computation.23.clone.1 | convolution fusion | flops 4833278464 | bytes 3416064 | tf_op jit(solution)/shard_map/while/body/eval_jaxpr/srx,mx->srm/dot_general | solution.py:90
  167.9 3.2 %fusion.114 = f32[3,512]{1,0:T(4,128)S(1)} fusion(f32[3,128,2048]{2,1,0:T(8,128)S(1)} %get-tuple-element.417, s32[512]{0:T(512)S(1)} %get-tuple-element.360, f32[128,512]{1,0:T(8,128)S(1)} %fusion.113), kind=kOutput, calls=%fused_computation.23.clone.1 | convolution fusion | flops 4833278464 | bytes 3416064 | tf_op jit(solution)/shard_map/while/body/eval_jaxpr/srx,mx->srm/dot_general | solution.py:90
  171.8 3.2 %fusion.114 = f32[3,512]{1,0:T(4,128)S(1)} fusion(f32[3,128,2048]{2,1,0:T(8,128)S(1)} %get-tuple-element.417, s32[512]{0:T(512)S(1)} %get-tuple-element.360, f32[128,512]{1,0:T(8,128)S(1)} %fusion.113), kind=kOutput, calls=%fused_computation.23.clone.1 | convolution fusion | flops 4833278464 | bytes 3416064 | tf_op jit(solution)/shard_map/while/body/eval_jaxpr/srx,mx->srm/dot_general | solution.py:90
  175.6 3.2 %fusion.114 = f32[3,512]{1,0:T(4,128)S(1)} fusion(f32[3,128,2048]{2,1,0:T(8,128)S(1)} %get-tuple-element.417, s32[512]{0:T(512)S(1)} %get-tuple-element.360, f32[128,512]{1,0:T(8,128)S(1)} %fusion.113), kind=kOutput, calls=%fused_computation.23.clone.1 | convolution fusion | flops 4833278464 | bytes 3416064 | tf_op jit(solution)/shard_map/while/body/eval_jaxpr/srx,mx->srm/dot_general | solution.py:90
  179.4 3.2 %fusion.114 = f32[3,512]{1,0:T(4,128)S(1)} fusion(f32[3,128,2048]{2,1,0:T(8,128)S(1)} %get-tuple-element.417, s32[512]{0:T(512)S(1)} %get-tuple-element.360, f32[128,512]{1,0:T(8,128)S(1)} %fusion.113), kind=kOutput, calls=%fused_computation.23.clone.1 | convolution fusion | flops 4833278464 | bytes 3416064 | tf_op jit(solution)/shard_map/while/body/eval_jaxpr/srx,mx->srm/dot_general | solution.py:90
  183.3 3.2 %fusion.114 = f32[3,512]{1,0:T(4,128)S(1)} fusion(f32[3,128,2048]{2,1,0:T(8,128)S(1)} %get-tuple-element.417, s32[512]{0:T(512)S(1)} %get-tuple-element.360, f32[128,512]{1,0:T(8,128)S(1)} %fusion.113), kind=kOutput, calls=%fused_computation.23.clone.1 | convolution fusion | flops 4833278464 | bytes 3416064 | tf_op jit(solution)/shard_map/while/body/eval_jaxpr/srx,mx->srm/dot_general | solution.py:90
  187.1 3.2 %fusion.114 = f32[3,512]{1,0:T(4,128)S(1)} fusion(f32[3,128,2048]{2,1,0:T(8,128)S(1)} %get-tuple-element.417, s32[512]{0:T(512)S(1)} %get-tuple-element.360, f32[128,512]{1,0:T(8,128)S(1)} %fusion.113), kind=kOutput, calls=%fused_computation.23.clone.1 | convolution fusion | flops 4833278464 | bytes 3416064 | tf_op jit(solution)/shard_map/while/body/eval_jaxpr/srx,mx->srm/dot_general | solution.py:90
  191.0 3.2 %fusion.114 = f32[3,512]{1,0:T(4,128)S(1)} fusion(f32[3,128,2048]{2,1,0:T(8,128)S(1)} %get-tuple-element.417, s32[512]{0:T(512)S(1)} %get-tuple-element.360, f32[128,512]{1,0:T(8,128)S(1)} %fusion.113), kind=kOutput, calls=%fused_computation.23.clone.1 | convolution fusion | flops 4833278464 | bytes 3416064 | tf_op jit(solution)/shard_map/while/body/eval_jaxpr/srx,mx->srm/dot_general | solution.py:90
  194.7 11.8 %all-to-all-start.1 = ((f32[3,16,256]{2,0,1:T(4,128)}), f32[3,16,256]{2,0,1:T(4,128)S(1)}, u32[]{:S(2)}, u32[]{:S(2)}) async-start(f32[3,16,256]{2,0,1:T(4,128)} %bitcast.35), calls=%async_computation.1 | async-start | bytes 131072 | tf_op jit(solution)/shard_map/all_to_all | solution.py:279
  206.6 3.8 %broadcast_in_dim.255.cols_ref = f32[24,4,128,128]{3,2,1,0:T(8,128)} broadcast(f32[24,4,128]{2,1,0:T(4,128)S(1)} %maximum_bitcast_fusion.rows_ref), dimensions={0,1,2} | broadcast | bytes 6340608 | tf_op jit(solution)/shard_map/broadcast_in_dim | solution.py:156
  210.4 11.9 %shard_map.167 = f32[16,3,128]{2,1,0:T(4,128)} custom-call(s32[128]{0:T(128)} %reshape.650.chosen_ref, f32[24,4,128]{2,1,0:T(4,128)} %copy-done.1, f32[24,4,128,128]{3,2,1,0:T(8,128)} %broadcast_in_dim.255.cols_ref), custom_call_target="tpu_custom_call" | custom-call | flops 54525952 | bytes 6291456 | tf_op jit(solution)/shard_map/pallas_call | solution.py:158
  (267 shorter events, 32.5 us)
Async XLA Ops:
  9.0 0.9 copy-start.7
  9.2 10.4 %copy-start.6 = (f32[2048]{0:T(1024)S(1)}, f32[2048]{0:T(1024)}, u32[]{:S(2)}) copy-start(f32[2048]{0:T(1024)} %param.23) | copy-start | bytes 24580
  9.2 10.4 %copy-start.2 = (f32[3,2048]{1,0:T(4,128)S(1)}, f32[3,2048]{1,0:T(4,128)}, u32[]{:S(2)}) copy-start(f32[3,2048]{1,0:T(4,128)} %param.22) | copy-start | bytes 73732
  9.6 13.5 %copy-start.8 = (s32[16,8]{0,1:T(8,128)S(1)}, s32[16,8]{0,1:T(8,128)}, u32[]{:S(2)}) copy-start(s32[16,8]{0,1:T(8,128)} %param.28) | copy-start | bytes 1540
  9.6 15.7 %slice-start = ((f32[2,8,16,2048]{3,2,1,0:T(8,128)}), f32[1,8,16,2048]{3,2,1,0:T(8,128)S(1)}, s32[]{:S(2)}) async-start(f32[2,8,16,2048]{3,2,1,0:T(8,128)} %param.29), calls=%async_computation.2 | async-start | bytes 2097152 | tf_op jit(solution)/shard_map/slice | solution.py:259
  10.7 14.6 %all-to-all-start = ((f32[2,16,256]{2,0,1:T(2,128)}), f32[2,16,256]{2,0,1:T(2,128)S(1)}, u32[]{:S(2)}, u32[]{:S(2)}) async-start(f32[2,16,256]{2,0,1:T(2,128)} %fusion.71), calls=%async_computation | async-start | bytes 65536 | tf_op jit(solution)/shard_map/all_to_all | solution.py:254
  19.7 186.9 %collective-permute-start = (f32[4,512]{1,0:T(4,128)S(1)}, f32[4,512]{1,0:T(4,128)S(1)}, u32[]{:S(2)}, u32[]{:S(2)}) collective-permute-start(f32[4,512]{1,0:T(4,128)S(1)} %get-tuple-element.266), channel_id=1, source_target_pairs={{0,1},{1,2},{2,3},{3,4},{4,5},{5,6},{6,7},{7,8},{8,9},{9,10},{10,1... | collective-permute-start | bytes 24584 | tf_op jit(solution)/shard_map/ppermute | solution.py:33
  74.0 14.9 %collective-permute-start.2 = (f32[2,1,16,2048]{3,2,1,0:T(8,128)S(1)}, f32[2,1,16,2048]{3,2,1,0:T(8,128)S(1)}, u32[]{:S(2)}, u32[]{:S(2)}) collective-permute-start(f32[2,1,16,2048]{3,2,1,0:T(8,128)S(1)} %get-tuple-element.259), channel_id=1, source_target_pairs={{16,0},{32,16},{48,32},{64,48},{80,64},{96,80},{112,96},{17,1},{33... | collective-permute-start | bytes 786440 | tf_op jit(solution)/shard_map/ppermute | solution.py:179
  76.0 12.9 %collective-permute-start.3 = (f32[2,1,16,2048]{3,2,1,0:T(8,128)S(1)}, f32[2,1,16,2048]{3,2,1,0:T(8,128)S(1)}, u32[]{:S(2)}, u32[]{:S(2)}) collective-permute-start(f32[2,1,16,2048]{3,2,1,0:T(8,128)S(1)} %get-tuple-element.258), channel_id=1, source_target_pairs={{0,16},{16,32},{32,48},{48,64},{64,80},{80,96},{96,112},{1,17},{17... | collective-permute-start | bytes 786440 | tf_op jit(solution)/shard_map/ppermute | solution.py:178
  78.4 6.9 %collective-permute-start.4 = (f32[2,8,1,2048]{3,1,2,0:T(8,128)S(1)}, f32[2,8,1,2048]{3,1,2,0:T(8,128)S(1)}, u32[]{:S(2)}, u32[]{:S(2)}) collective-permute-start(f32[2,8,1,2048]{3,1,2,0:T(8,128)S(1)} %copy.63), channel_id=1, source_target_pairs={{1,0},{2,1},{3,2},{4,3},{5,4},{6,5},{7,6},{8,7},{9,8},{10,9},{11,1... | collective-permute-start | bytes 393224 | tf_op jit(solution)/shard_map/ppermute | solution.py:179
  81.9 7.0 %copy-start.4 = (f32[2]{0:T(128)S(1)}, f32[2]{0:T(128)}, u32[]{:S(2)}) copy-start(f32[2]{0:T(128)} %constant.222.clone) | copy-start | bytes 28
  81.9 7.0 %copy-start.5 = (f32[2]{0:T(128)S(1)}, f32[2]{0:T(128)}, u32[]{:S(2)}) copy-start(f32[2]{0:T(128)} %constant.223.clone) | copy-start | bytes 28
  81.9 6.9 %collective-permute-start.5 = (f32[2,8,1,2048]{3,1,2,0:T(8,128)S(1)}, f32[2,8,1,2048]{3,1,2,0:T(8,128)S(1)}, u32[]{:S(2)}, u32[]{:S(2)}) collective-permute-start(f32[2,8,1,2048]{3,1,2,0:T(8,128)S(1)} %copy.65), channel_id=1, source_target_pairs={{0,1},{1,2},{2,3},{3,4},{4,5},{5,6},{6,7},{7,8},{8,9},{9,10},{10,1... | collective-permute-start | bytes 393224 | tf_op jit(solution)/shard_map/ppermute | solution.py:178
  91.8 14.0 %collective-permute-start.6 = (f32[2,1,16,2048]{3,2,1,0:T(8,128)S(1)}, f32[2,1,16,2048]{3,2,1,0:T(8,128)S(1)}, u32[]{:S(2)}, u32[]{:S(2)}) collective-permute-start(f32[2,1,16,2048]{3,2,1,0:T(8,128)S(1)} %get-tuple-element.251), channel_id=1, source_target_pairs={{16,0},{32,16},{48,32},{64,48},{80,64},{96,80},{112,96},{17,1},{33... | collective-permute-start | bytes 786440 | tf_op jit(solution)/shard_map/ppermute | solution.py:179
  94.9 11.0 %collective-permute-start.7 = (f32[2,1,16,2048]{3,2,1,0:T(8,128)S(1)}, f32[2,1,16,2048]{3,2,1,0:T(8,128)S(1)}, u32[]{:S(2)}, u32[]{:S(2)}) collective-permute-start(f32[2,1,16,2048]{3,2,1,0:T(8,128)S(1)} %get-tuple-element.250), channel_id=1, source_target_pairs={{0,16},{16,32},{32,48},{48,64},{64,80},{80,96},{96,112},{1,17},{17... | collective-permute-start | bytes 786440 | tf_op jit(solution)/shard_map/ppermute | solution.py:178
  96.9 6.9 %collective-permute-start.8 = (f32[2,8,1,2048]{3,1,2,0:T(8,128)S(1)}, f32[2,8,1,2048]{3,1,2,0:T(8,128)S(1)}, u32[]{:S(2)}, u32[]{:S(2)}) collective-permute-start(f32[2,8,1,2048]{3,1,2,0:T(8,128)S(1)} %copy.67), channel_id=1, source_target_pairs={{1,0},{2,1},{3,2},{4,3},{5,4},{6,5},{7,6},{8,7},{9,8},{10,9},{11,1... | collective-permute-start | bytes 393224 | tf_op jit(solution)/shard_map/ppermute | solution.py:179
  98.9 6.9 %collective-permute-start.9 = (f32[2,8,1,2048]{3,1,2,0:T(8,128)S(1)}, f32[2,8,1,2048]{3,1,2,0:T(8,128)S(1)}, u32[]{:S(2)}, u32[]{:S(2)}) collective-permute-start(f32[2,8,1,2048]{3,1,2,0:T(8,128)S(1)} %copy.69), channel_id=1, source_target_pairs={{0,1},{1,2},{2,3},{3,4},{4,5},{5,6},{6,7},{7,8},{8,9},{9,10},{10,1... | collective-permute-start | bytes 393224 | tf_op jit(solution)/shard_map/ppermute | solution.py:178
  108.8 15.1 %collective-permute-start.10 = (f32[2,1,16,2048]{3,2,1,0:T(8,128)S(1)}, f32[2,1,16,2048]{3,2,1,0:T(8,128)S(1)}, u32[]{:S(2)}, u32[]{:S(2)}) collective-permute-start(f32[2,1,16,2048]{3,2,1,0:T(8,128)S(1)} %get-tuple-element.243), channel_id=1, source_target_pairs={{16,0},{32,16},{48,32},{64,48},{80,64},{96,80},{112,96},{17,1},{33... | collective-permute-start | bytes 786440 | tf_op jit(solution)/shard_map/ppermute | solution.py:179
  112.9 11.0 %collective-permute-start.11 = (f32[2,1,16,2048]{3,2,1,0:T(8,128)S(1)}, f32[2,1,16,2048]{3,2,1,0:T(8,128)S(1)}, u32[]{:S(2)}, u32[]{:S(2)}) collective-permute-start(f32[2,1,16,2048]{3,2,1,0:T(8,128)S(1)} %get-tuple-element.242), channel_id=1, source_target_pairs={{0,16},{16,32},{32,48},{48,64},{64,80},{80,96},{96,112},{1,17},{17... | collective-permute-start | bytes 786440 | tf_op jit(solution)/shard_map/ppermute | solution.py:178
  114.9 6.9 %collective-permute-start.12 = (f32[2,8,1,2048]{3,1,2,0:T(8,128)S(1)}, f32[2,8,1,2048]{3,1,2,0:T(8,128)S(1)}, u32[]{:S(2)}, u32[]{:S(2)}) collective-permute-start(f32[2,8,1,2048]{3,1,2,0:T(8,128)S(1)} %copy.71), channel_id=1, source_target_pairs={{1,0},{2,1},{3,2},{4,3},{5,4},{6,5},{7,6},{8,7},{9,8},{10,9},{11,1... | collective-permute-start | bytes 393224 | tf_op jit(solution)/shard_map/ppermute | solution.py:179
  116.9 6.9 %collective-permute-start.13 = (f32[2,8,1,2048]{3,1,2,0:T(8,128)S(1)}, f32[2,8,1,2048]{3,1,2,0:T(8,128)S(1)}, u32[]{:S(2)}, u32[]{:S(2)}) collective-permute-start(f32[2,8,1,2048]{3,1,2,0:T(8,128)S(1)} %copy.73), channel_id=1, source_target_pairs={{0,1},{1,2},{2,3},{3,4},{4,5},{5,6},{6,7},{7,8},{8,9},{9,10},{10,1... | collective-permute-start | bytes 393224 | tf_op jit(solution)/shard_map/ppermute | solution.py:178
  126.8 14.8 %collective-permute-start.14 = (f32[2,1,16,2048]{3,2,1,0:T(8,128)S(1)}, f32[2,1,16,2048]{3,2,1,0:T(8,128)S(1)}, u32[]{:S(2)}, u32[]{:S(2)}) collective-permute-start(f32[2,1,16,2048]{3,2,1,0:T(8,128)S(1)} %get-tuple-element.235), channel_id=1, source_target_pairs={{16,0},{32,16},{48,32},{64,48},{80,64},{96,80},{112,96},{17,1},{33... | collective-permute-start | bytes 786440 | tf_op jit(solution)/shard_map/ppermute | solution.py:179
  130.3 11.3 %collective-permute-start.15 = (f32[2,1,16,2048]{3,2,1,0:T(8,128)S(1)}, f32[2,1,16,2048]{3,2,1,0:T(8,128)S(1)}, u32[]{:S(2)}, u32[]{:S(2)}) collective-permute-start(f32[2,1,16,2048]{3,2,1,0:T(8,128)S(1)} %get-tuple-element.234), channel_id=1, source_target_pairs={{0,16},{16,32},{32,48},{48,64},{64,80},{80,96},{96,112},{1,17},{17... | collective-permute-start | bytes 786440 | tf_op jit(solution)/shard_map/ppermute | solution.py:178
  132.3 7.1 %collective-permute-start.16 = (f32[2,8,1,2048]{3,1,2,0:T(8,128)S(1)}, f32[2,8,1,2048]{3,1,2,0:T(8,128)S(1)}, u32[]{:S(2)}, u32[]{:S(2)}) collective-permute-start(f32[2,8,1,2048]{3,1,2,0:T(8,128)S(1)} %copy.75), channel_id=1, source_target_pairs={{1,0},{2,1},{3,2},{4,3},{5,4},{6,5},{7,6},{8,7},{9,8},{10,9},{11,1... | collective-permute-start | bytes 393224 | tf_op jit(solution)/shard_map/ppermute | solution.py:179
  134.3 7.1 %collective-permute-start.17 = (f32[2,8,1,2048]{3,1,2,0:T(8,128)S(1)}, f32[2,8,1,2048]{3,1,2,0:T(8,128)S(1)}, u32[]{:S(2)}, u32[]{:S(2)}) collective-permute-start(f32[2,8,1,2048]{3,1,2,0:T(8,128)S(1)} %copy.77), channel_id=1, source_target_pairs={{0,1},{1,2},{2,3},{3,4},{4,5},{5,6},{6,7},{7,8},{8,9},{9,10},{10,1... | collective-permute-start | bytes 393224 | tf_op jit(solution)/shard_map/ppermute | solution.py:178
  139.4 67.2 %collective-permute-start.1 = (f32[4,512]{1,0:T(4,128)S(1)}, f32[4,512]{1,0:T(4,128)S(1)}, u32[]{:S(2)}, u32[]{:S(2)}) collective-permute-start(f32[4,512]{1,0:T(4,128)S(1)} %get-tuple-element.267), channel_id=1, source_target_pairs={{1,0},{2,1},{3,2},{4,3},{5,4},{6,5},{7,6},{8,7},{9,8},{10,9},{11,1... | collective-permute-start | bytes 24584 | tf_op jit(solution)/shard_map/ppermute | solution.py:36
  143.8 1.3 copy-start
  145.4 11.9 %collective-permute-start.20 = (f32[8,1,2048]{2,1,0:T(1,128)S(1)}, f32[8,1,2048]{2,1,0:T(1,128)S(1)}, u32[]{:S(2)}, u32[]{:S(2)}) collective-permute-start(f32[8,1,2048]{2,1,0:T(1,128)S(1)} %get-tuple-element.263), channel_id=1, source_target_pairs={{1,0},{2,1},{3,2},{4,3},{5,4},{6,5},{7,6},{8,7},{9,8},{10,9},{11,1... | collective-permute-start | bytes 196616 | tf_op jit(solution)/shard_map/ppermute | solution.py:179
  147.4 12.2 %collective-permute-start.21 = (f32[8,1,2048]{2,1,0:T(1,128)S(1)}, f32[8,1,2048]{2,1,0:T(1,128)S(1)}, u32[]{:S(2)}, u32[]{:S(2)}) collective-permute-start(f32[8,1,2048]{2,1,0:T(1,128)S(1)} %get-tuple-element.262), channel_id=1, source_target_pairs={{0,1},{1,2},{2,3},{3,4},{4,5},{5,6},{6,7},{7,8},{8,9},{9,10},{10,1... | collective-permute-start | bytes 196616 | tf_op jit(solution)/shard_map/ppermute | solution.py:178
  154.5 5.4 %collective-permute-start.18 = (f32[1,16,2048]{2,1,0:T(8,128)S(1)}, f32[1,16,2048]{2,1,0:T(8,128)S(1)}, u32[]{:S(2)}, u32[]{:S(2)}) collective-permute-start(f32[1,16,2048]{2,1,0:T(8,128)S(1)} %get-tuple-element.227), channel_id=1, source_target_pairs={{16,0},{32,16},{48,32},{64,48},{80,64},{96,80},{112,96},{17,1},{33... | collective-permute-start | bytes 393224 | tf_op jit(solution)/shard_map/ppermute | solution.py:179
  157.4 6.3 %collective-permute-start.19 = (f32[1,16,2048]{2,1,0:T(8,128)S(1)}, f32[1,16,2048]{2,1,0:T(8,128)S(1)}, u32[]{:S(2)}, u32[]{:S(2)}) collective-permute-start(f32[1,16,2048]{2,1,0:T(8,128)S(1)} %get-tuple-element.226), channel_id=1, source_target_pairs={{0,16},{16,32},{32,48},{48,64},{64,80},{80,96},{96,112},{1,17},{17... | collective-permute-start | bytes 393224 | tf_op jit(solution)/shard_map/ppermute | solution.py:178
  194.7 27.6 %all-to-all-start.1 = ((f32[3,16,256]{2,0,1:T(4,128)}), f32[3,16,256]{2,0,1:T(4,128)S(1)}, u32[]{:S(2)}, u32[]{:S(2)}) async-start(f32[3,16,256]{2,0,1:T(4,128)} %bitcast.35), calls=%async_computation.1 | async-start | bytes 131072 | tf_op jit(solution)/shard_map/all_to_all | solution.py:279
  206.6 3.8 %copy-start.1 = (f32[24,4,128]{2,1,0:T(4,128)}, f32[24,4,128]{2,1,0:T(4,128)S(1)}, u32[]{:S(2)}) copy-start(f32[24,4,128]{2,1,0:T(4,128)S(1)} %maximum_bitcast_fusion.rows_ref) | copy-start | bytes 147460
  226.9 0.8 copy-start.3

commit v3 on v2

--- a/solution.py
+++ b/solution.py
@@ -22,7 +22,7 @@
 ADHERE_RANGE = 4.0
 FORCE_SCALE = 0.08
 CHEMOTAXIS = 1.5
-SLOT_BLOCK = 512
+SLOT_BLOCK = 1024
 
 
 def with_halo(block, sides, width):
@@ -71,24 +71,35 @@
     return (target, cell - first, routed)
 
 
-def hot_tables(piece, planes, columns):
+def hot_tables(piece, planes, columns, kind=jnp.float32):
     row_hot = (piece[:, None] // columns == jnp.arange(planes, dtype=jnp.int32)[None, :]).astype(
-        jnp.float32
+        kind
     )
     column_hot = (piece[:, None] % columns == jnp.arange(columns, dtype=jnp.int32)[None, :]).astype(
-        jnp.float32
+        kind
     )
     return (row_hot, column_hot)
+
+
+def split_three(values):
+    high = lax.reduce_precision(values, exponent_bits=8, mantissa_bits=7)
+    rest = values - high
+    middle = lax.reduce_precision(rest, exponent_bits=8, mantissa_bits=7)
+    return jnp.stack([high, middle, rest - middle]).astype(jnp.bfloat16)
 
 
 def pick_voxels(fields, reached):
     species, planes, columns = fields.shape
+    parts = split_three(fields)
     pieces = reached.reshape(-1, SLOT_BLOCK)
 
     def one_piece(piece):
-        row_hot, column_hot = hot_tables(piece, planes, columns)
-        picked = jnp.einsum("srx,mx->srm", fields, column_hot, precision=lax.Precision.HIGHEST)
-        return jnp.sum(picked * jnp.transpose(row_hot)[None], axis=1)
+        row_hot, column_hot = hot_tables(piece, planes, columns, jnp.bfloat16)
+        picked = jnp.einsum(
+            "psrx,mx->psrm", parts, column_hot, preferred_element_type=jnp.float32
+        )
+        picked = picked[0] + picked[1] + picked[2]
+        return jnp.sum(picked * jnp.transpose(row_hot).astype(jnp.float32)[None], axis=1)
 
     found = lax.map(one_piece, pieces)
     return jnp.moveaxis(found, 1, 0).reshape(species, -1)

time: 229 us -> 229 us (level)
  other arithmetic: 23.5 us -> 30 us
  matrix products: 69.5 us -> 64.4 us
    dot_general x16 -> x8, matrix products: 45.5 us -> 38.2 us  [one_piece(): jnp.einsum('psrx,mx->psrm', parts, column_hot, preferred_element_type=jnp...]
    another operation x3 -> x6, other arithmetic: 0.36 us -> 3.97 us  [the longest x2 2.62 us: split_three(): return jnp.stack([high, middle, rest - middle]).astype(jnp.bfloat16)]
    reduce_sum x0 -> x8, other arithmetic: none -> 3.08 us  [one_piece(): jnp.sum(picked * jnp.transpose(row_hot).astype(jnp.float32)[None], axis=1)]
    dynamic_update_slice x16 -> x8, local copies, waits for them, and re-layouts: 5.3 us -> 2.72 us  [pick_voxels(): found = lax.map(one_piece, pieces)]
    dot_general x8 -> x4, matrix products: 24.1 us -> 26.2 us  [add_piece(): jnp.einsum('smr,mx->srx', weighted, column_hot, precision=lax.Precision.H...]
where the time goes in v3:
time: 229 us; the launch traced here: 228 us
  starting transfers between devices  84.2 us (37%)
  matrix products  64.4 us (28%)
  other arithmetic  30 us (13%)
  local copies, waits for them, and re-layouts  20.7 us (9%)
  waiting for transfers between devices  13.4 us (6%)
  Pallas kernels  11.9 us (5%)
  between operations  2.78 us (1%)
    dot_general x8, matrix products, one_piece(): jnp.einsum('psrx,mx->psrm', parts, column_hot, preferred_element_type=jnp...  38.2 us
    ppermute x10, starting transfers between devices, neighbours(): lax.ppermute(lax.slice_in_dim(block, block.shape[dim] - 1, None, axis=dim...  31.3 us
    ppermute x10, starting transfers between devices, neighbours(): high = lax.ppermute(lax.slice_in_dim(block, 0, 1, axis=dim), axis, backward)  26.8 us
    dot_general x4, matrix products, add_piece(): jnp.einsum('smr,mx->srx', weighted, column_hot, precision=lax.Precision.H...  26.2 us
    all_to_all x1, starting transfers between devices, local(): lax.all_to_all(slopes, 'tile', split_axis=1, concat_axis=1, tiled=True)  12.5 us
    pallas_call x1, Pallas kernels, pair_forces(): pl.pallas_call(force_kernel, out_shape=jax.ShapeDtypeStruct((blocks, 3, l...  11.9 us
    ppermute x10, waiting for transfers between devices, neighbours(): lax.ppermute(lax.slice_in_dim(block, block.shape[dim] - 1, None, axis=dim...  11 us
    sub x4, other arithmetic, relax_step(): return center + spread * (beside_all - 6.0 * center) - losses * center  8.71 us
  transfers between devices with their start and end apart: 24, of which 9 were waited for; matrix products, arithmetic and copies ran while one was open for 43% of the time, Pallas kernels for 5%

profile of v3, /device:TPU:26, one launch (start us, length us, event | category | flops | bytes accessed | tf_op | source)
XLA Modules:
  0.0 227.7 jit_solution(17567815816942538461)
XLA Ops:
  0.6 0.7 convert_element_type.92
  1.3 0.7 pad_maximum_fusion.5
  2.0 0.8 fusion.89
  2.8 0.7 copy.71
  3.7 0.7 and_compare_fusion.11
  10.2 0.7 fusion.81
  10.9 8.3 %all-to-all-start = ((f32[2,16,256]{2,0,1:T(2,128)}), f32[2,16,256]{2,0,1:T(2,128)S(1)}, u32[]{:S(2)}, u32[]{:S(2)}) async-start(f32[2,16,256]{2,0,1:T(2,128)} %fusion.81), calls=%async_computation | async-start | bytes 65536 | tf_op jit(solution)/shard_map/all_to_all | solution.py:265
  19.9 3.4 %collective-permute-start = (f32[4,512]{1,0:T(4,128)S(1)}, f32[4,512]{1,0:T(4,128)S(1)}, u32[]{:S(2)}, u32[]{:S(2)}) collective-permute-start(f32[4,512]{1,0:T(4,128)S(1)} %get-tuple-element.272), channel_id=1, source_target_pairs={{0,1},{1,2},{2,3},{3,4},{4,5},{5,6},{6,7},{7,8},{8,9},{9,10},{10,1... | collective-permute-start | bytes 24584 | tf_op jit(solution)/shard_map/ppermute | solution.py:33
  25.5 9.5 %while.37 = (s32[]{:T(128)}, f32[4,1,1024]{2,0,1:T(4,128)S(1)}, s32[4,1024]{1,0:T(4,128)S(1)}, bf16[3,1,128,2048]{3,2,0,1:T(8,128)(2,1)S(1)}, s32[]{:T(128)}, /*index=5*/s32[]{:T(128)}) while((s32[]{:T(128)}, f32[4,1,1024]{2,0,1:T(4,128)S(1)}, s32[4,1024]{1,0:T(4,128)S(1)}, bf16[3,1,128,2048]{3,2,0,1:T(8,128)(2,1)S(1)}, s32[]{:T(128)}, ...), condition=%wide.region_3.4_spmd, body=%wide.region_1.3_spmd.sunk | while | flops 1613645824 | bytes 4759629 | solution.py:104
  25.5 2.1 fusion.124
  27.9 2.1 fusion.124
  30.3 2.1 fusion.124
  32.7 2.1 fusion.124
  35.2 26.7 %while.39 = (s32[]{:T(128)}, f32[2,128,2048]{2,1,0:T(8,128)}, f32[4,2,1024]{2,0,1:T(4,128)S(1)}, s32[4,1024]{1,0:T(4,128)S(1)}, s32[]{:T(128)}, /*index=5*/s32[]{:T(128)}) while((s32[]{:T(128)}, f32[2,128,2048]{2,1,0:T(8,128)}, f32[4,2,1024]{2,0,1:T(4,128)S(1)}, s32[4,1024]{1,0:T(4,128)S(1)}, s32[]{:T(128)}, ...), condition=%wide.region_5.6_spmd.clone, body=%wide.region_4.5_spmd.clone.sunk | while | flops 6446140416 | bytes 5312599 | solution.py:124
  35.3 5.7 %fusion.134 = f32[2,128,2048]{2,1,0:T(8,128)} fusion(s32[1024]{0:T(1024)S(1)} %get-tuple-element.372, f32[2,128,2048]{2,1,0:T(8,128)} %get-tuple-element.399, pred[]{:T(512)S(6)} %compare.53, f32[1024,128]{0,1:T(8,128)S(1)} %fusion.133, f32[2,1024]{1,0:T(2,128)S(1)} %bitcast.163), kind=kOutput, calls=%fused_computation.48.clone.1 | convolution fusion | flops 6445858816 | bytes 4730881 | tf_op jit(solution)/shard_map/while/body/eval_jaxpr/smr,mx->srx/dot_general | solution.py:119
  41.1 6.8 %fusion.134 = f32[2,128,2048]{2,1,0:T(8,128)} fusion(s32[1024]{0:T(1024)S(1)} %get-tuple-element.372, f32[2,128,2048]{2,1,0:T(8,128)} %get-tuple-element.399, pred[]{:T(512)S(6)} %compare.53, f32[1024,128]{0,1:T(8,128)S(1)} %fusion.133, f32[2,1024]{1,0:T(2,128)S(1)} %bitcast.163), kind=kOutput, calls=%fused_computation.48.clone.1 | convolution fusion | flops 6445858816 | bytes 4730881 | tf_op jit(solution)/shard_map/while/body/eval_jaxpr/smr,mx->srx/dot_general | solution.py:119
  48.1 6.8 %fusion.134 = f32[2,128,2048]{2,1,0:T(8,128)} fusion(s32[1024]{0:T(1024)S(1)} %get-tuple-element.372, f32[2,128,2048]{2,1,0:T(8,128)} %get-tuple-element.399, pred[]{:T(512)S(6)} %compare.53, f32[1024,128]{0,1:T(8,128)S(1)} %fusion.133, f32[2,1024]{1,0:T(2,128)S(1)} %bitcast.163), kind=kOutput, calls=%fused_computation.48.clone.1 | convolution fusion | flops 6445858816 | bytes 4730881 | tf_op jit(solution)/shard_map/while/body/eval_jaxpr/smr,mx->srx/dot_general | solution.py:119
  55.1 6.8 %fusion.134 = f32[2,128,2048]{2,1,0:T(8,128)} fusion(s32[1024]{0:T(1024)S(1)} %get-tuple-element.372, f32[2,128,2048]{2,1,0:T(8,128)} %get-tuple-element.399, pred[]{:T(512)S(6)} %compare.53, f32[1024,128]{0,1:T(8,128)S(1)} %fusion.133, f32[2,1024]{1,0:T(2,128)S(1)} %bitcast.163), kind=kOutput, calls=%fused_computation.48.clone.1 | convolution fusion | flops 6445858816 | bytes 4730881 | tf_op jit(solution)/shard_map/while/body/eval_jaxpr/smr,mx->srx/dot_general | solution.py:119
  61.9 1.8 add.239
  64.5 1.9 collective-permute-start.2
  66.4 2.4 %collective-permute-start.3 = (f32[2,1,16,2048]{3,2,1,0:T(8,128)S(1)}, f32[2,1,16,2048]{3,2,1,0:T(8,128)S(1)}, u32[]{:S(2)}, u32[]{:S(2)}) collective-permute-start(f32[2,1,16,2048]{3,2,1,0:T(8,128)S(1)} %get-tuple-element.261), channel_id=1, source_target_pairs={{0,16},{16,32},{32,48},{48,64},{64,80},{80,96},{96,112},{1,17},{17... | collective-permute-start | bytes 786440 | tf_op jit(solution)/shard_map/ppermute | solution.py:189
  68.9 3.5 %collective-permute-start.4 = (f32[2,8,1,2048]{3,1,2,0:T(8,128)S(1)}, f32[2,8,1,2048]{3,1,2,0:T(8,128)S(1)}, u32[]{:S(2)}, u32[]{:S(2)}) collective-permute-start(f32[2,8,1,2048]{3,1,2,0:T(8,128)S(1)} %copy.75), channel_id=1, source_target_pairs={{1,0},{2,1},{3,2},{4,3},{5,4},{6,5},{7,6},{8,7},{9,8},{10,9},{11,1... | collective-permute-start | bytes 393224 | tf_op jit(solution)/shard_map/ppermute | solution.py:190
  72.5 2.5 %collective-permute-start.5 = (f32[2,8,1,2048]{3,1,2,0:T(8,128)S(1)}, f32[2,8,1,2048]{3,1,2,0:T(8,128)S(1)}, u32[]{:S(2)}, u32[]{:S(2)}) collective-permute-start(f32[2,8,1,2048]{3,1,2,0:T(8,128)S(1)} %copy.77), channel_id=1, source_target_pairs={{0,1},{1,2},{2,3},{3,4},{4,5},{5,6},{6,7},{7,8},{8,9},{9,10},{10,1... | collective-permute-start | bytes 393224 | tf_op jit(solution)/shard_map/ppermute | solution.py:189
  75.9 3.5 %collective-permute-done.5 = f32[2,8,1,2048]{3,1,2,0:T(8,128)S(1)} collective-permute-done((f32[2,8,1,2048]{3,1,2,0:T(8,128)S(1)}, f32[2,8,1,2048]{3,1,2,0:T(8,128)S(1)}, u32[]{:S(2)}, u32[]{:S(2)}) %collective-permute-start.5) | collective-permute-done | bytes 131104 | tf_op jit(solution)/shard_map/ppermute | solution.py:189
  79.6 2.2 fusion.48
  82.5 3.1 %collective-permute-start.6 = (f32[2,1,16,2048]{3,2,1,0:T(8,128)S(1)}, f32[2,1,16,2048]{3,2,1,0:T(8,128)S(1)}, u32[]{:S(2)}, u32[]{:S(2)}) collective-permute-start(f32[2,1,16,2048]{3,2,1,0:T(8,128)S(1)} %get-tuple-element.254), channel_id=1, source_target_pairs={{16,0},{32,16},{48,32},{64,48},{80,64},{96,80},{112,96},{17,1},{33... | collective-permute-start | bytes 786440 | tf_op jit(solution)/shard_map/ppermute | solution.py:190
  85.5 1.9 collective-permute-start.7
  87.5 1.9 collective-permute-start.8
  89.5 3.9 %collective-permute-start.9 = (f32[2,8,1,2048]{3,1,2,0:T(8,128)S(1)}, f32[2,8,1,2048]{3,1,2,0:T(8,128)S(1)}, u32[]{:S(2)}, u32[]{:S(2)}) collective-permute-start(f32[2,8,1,2048]{3,1,2,0:T(8,128)S(1)} %copy.81), channel_id=1, source_target_pairs={{0,1},{1,2},{2,3},{3,4},{4,5},{5,6},{6,7},{7,8},{8,9},{9,10},{10,1... | collective-permute-start | bytes 393224 | tf_op jit(solution)/shard_map/ppermute | solution.py:189
  94.5 1.8 collective-permute-done.9
  96.5 2.2 fusion.54
  99.4 4.1 %collective-permute-start.10 = (f32[2,1,16,2048]{3,2,1,0:T(8,128)S(1)}, f32[2,1,16,2048]{3,2,1,0:T(8,128)S(1)}, u32[]{:S(2)}, u32[]{:S(2)}) collective-permute-start(f32[2,1,16,2048]{3,2,1,0:T(8,128)S(1)} %get-tuple-element.246), channel_id=1, source_target_pairs={{16,0},{32,16},{48,32},{64,48},{80,64},{96,80},{112,96},{17,1},{33... | collective-permute-start | bytes 786440 | tf_op jit(solution)/shard_map/ppermute | solution.py:190
  103.5 1.9 collective-permute-start.11
  105.5 1.9 collective-permute-start.12
  107.5 3.9 %collective-permute-start.13 = (f32[2,8,1,2048]{3,1,2,0:T(8,128)S(1)}, f32[2,8,1,2048]{3,1,2,0:T(8,128)S(1)}, u32[]{:S(2)}, u32[]{:S(2)}) collective-permute-start(f32[2,8,1,2048]{3,1,2,0:T(8,128)S(1)} %copy.85), channel_id=1, source_target_pairs={{0,1},{1,2},{2,3},{3,4},{4,5},{5,6},{6,7},{7,8},{8,9},{9,10},{10,1... | collective-permute-start | bytes 393224 | tf_op jit(solution)/shard_map/ppermute | solution.py:189
  112.5 1.8 collective-permute-done.13
  114.5 2.2 fusion.60
  117.4 3.5 %collective-permute-start.14 = (f32[2,1,16,2048]{3,2,1,0:T(8,128)S(1)}, f32[2,1,16,2048]{3,2,1,0:T(8,128)S(1)}, u32[]{:S(2)}, u32[]{:S(2)}) collective-permute-start(f32[2,1,16,2048]{3,2,1,0:T(8,128)S(1)} %get-tuple-element.238), channel_id=1, source_target_pairs={{16,0},{32,16},{48,32},{64,48},{80,64},{96,80},{112,96},{17,1},{33... | collective-permute-start | bytes 786440 | tf_op jit(solution)/shard_map/ppermute | solution.py:190
  120.9 1.9 collective-permute-start.15
  122.9 1.9 collective-permute-start.16
  124.9 4.2 %collective-permute-start.17 = (f32[2,8,1,2048]{3,1,2,0:T(8,128)S(1)}, f32[2,8,1,2048]{3,1,2,0:T(8,128)S(1)}, u32[]{:S(2)}, u32[]{:S(2)}) collective-permute-start(f32[2,8,1,2048]{3,1,2,0:T(8,128)S(1)} %copy.89), channel_id=1, source_target_pairs={{0,1},{1,2},{2,3},{3,4},{4,5},{5,6},{6,7},{7,8},{8,9},{9,10},{10,1... | collective-permute-start | bytes 393224 | tf_op jit(solution)/shard_map/ppermute | solution.py:189
  130.0 1.9 collective-permute-start.1
  132.3 2.2 fusion.66
  134.7 1.1 copy-done
  136.1 1.9 collective-permute-start.20
  138.1 6.5 %collective-permute-start.21 = (f32[8,1,2048]{2,1,0:T(1,128)S(1)}, f32[8,1,2048]{2,1,0:T(1,128)S(1)}, u32[]{:S(2)}, u32[]{:S(2)}) collective-permute-start(f32[8,1,2048]{2,1,0:T(1,128)S(1)} %get-tuple-element.265), channel_id=1, source_target_pairs={{0,1},{1,2},{2,3},{3,4},{4,5},{5,6},{6,7},{7,8},{8,9},{9,10},{10,1... | collective-permute-start | bytes 196616 | tf_op jit(solution)/shard_map/ppermute | solution.py:189
  145.2 2.9 %collective-permute-start.18 = (f32[1,16,2048]{2,1,0:T(8,128)S(1)}, f32[1,16,2048]{2,1,0:T(8,128)S(1)}, u32[]{:S(2)}, u32[]{:S(2)}) collective-permute-start(f32[1,16,2048]{2,1,0:T(8,128)S(1)} %get-tuple-element.230), channel_id=1, source_target_pairs={{16,0},{32,16},{48,32},{64,48},{80,64},{96,80},{112,96},{17,1},{33... | collective-permute-start | bytes 393224 | tf_op jit(solution)/shard_map/ppermute | solution.py:190
  148.1 2.1 collective-permute-start.19
  150.6 3.8 %collective-permute-done.19 = f32[1,16,2048]{2,1,0:T(8,128)S(1)} collective-permute-done((f32[1,16,2048]{2,1,0:T(8,128)S(1)}, f32[1,16,2048]{2,1,0:T(8,128)S(1)}, u32[]{:S(2)}, u32[]{:S(2)}) %collective-permute-start.19) | collective-permute-done | bytes 131104 | tf_op jit(solution)/shard_map/ppermute | solution.py:189
  154.5 0.9 reduce-precision_convert_fusion.1
  155.5 2.4 %pad_maximum_fusion = bf16[3,3,128,2048]{3,2,1,0:T(8,128)(2,1)} fusion(bf16[1,3,128,2048]{3,2,1,0:T(8,128)(2,1)S(1)} %get-tuple-element.228, bf16[1,3,128,2048]{3,2,1,0:T(8,128)(2,1)S(1)} %get-tuple-element.227, bf16[1,3,128,2048]{3,2,1,0:T(8,128)(2,1)S(1)} %get-tuple-element.226), kind=kLoop, calls=%fused_computation.65 | loop fusion | flops 4718592 | bytes 9437184 | tf_op jit(solution)/shard_map/stack | solution.py:88
  157.9 35.1 %while.38 = (s32[]{:T(128)}, f32[4,3,1024]{2,1,0:T(4,128)}, s32[4,1024]{1,0:T(4,128)S(1)}, bf16[3,3,128,2048]{3,2,1,0:T(8,128)(2,1)}, s32[]{:T(128)}) while((s32[]{:T(128)}, f32[4,3,1024]{2,1,0:T(4,128)}, s32[4,1024]{1,0:T(4,128)S(1)}, bf16[3,3,128,2048]{3,2,1,0:T(8,128)(2,1)}, s32[]{:T(128)}) %tuple.134), condition=%wide.region_8.9_spmd, body=%wide.region_6.8_spmd.sunk | while | flops 4835917824 | bytes 15274561 | solution.py:104
  157.9 7.4 %fusion.128 = f32[3,3,128,1024]{3,2,1,0:T(8,128)S(1)} fusion(bf16[3,3,128,2048]{3,2,1,0:T(8,128)(2,1)} %get-tuple-element.423, s32[1024]{0:T(1024)S(1)} %get-tuple-element.366), kind=kOutput, calls=%fused_computation.25.clone.1 | convolution fusion | flops 4833935360 | bytes 9441280 | tf_op jit(solution)/shard_map/while/body/eval_jaxpr/psrx,mx->psrm/dot_general | solution.py:98
  165.5 0.6 fusion.130
  166.7 7.5 %fusion.128 = f32[3,3,128,1024]{3,2,1,0:T(8,128)S(1)} fusion(bf16[3,3,128,2048]{3,2,1,0:T(8,128)(2,1)} %get-tuple-element.423, s32[1024]{0:T(1024)S(1)} %get-tuple-element.366), kind=kOutput, calls=%fused_computation.25.clone.1 | convolution fusion | flops 4833935360 | bytes 9441280 | tf_op jit(solution)/shard_map/while/body/eval_jaxpr/psrx,mx->psrm/dot_general | solution.py:98
  174.2 0.6 fusion.130
  174.8 0.6 bitcast_dynamic-update-slice_fusion.2
  175.5 7.4 %fusion.128 = f32[3,3,128,1024]{3,2,1,0:T(8,128)S(1)} fusion(bf16[3,3,128,2048]{3,2,1,0:T(8,128)(2,1)} %get-tuple-element.423, s32[1024]{0:T(1024)S(1)} %get-tuple-element.366), kind=kOutput, calls=%fused_computation.25.clone.1 | convolution fusion | flops 4833935360 | bytes 9441280 | tf_op jit(solution)/shard_map/while/body/eval_jaxpr/psrx,mx->psrm/dot_general | solution.py:98
  183.0 0.6 fusion.130
  184.2 7.4 %fusion.128 = f32[3,3,128,1024]{3,2,1,0:T(8,128)S(1)} fusion(bf16[3,3,128,2048]{3,2,1,0:T(8,128)(2,1)} %get-tuple-element.423, s32[1024]{0:T(1024)S(1)} %get-tuple-element.366), kind=kOutput, calls=%fused_computation.25.clone.1 | convolution fusion | flops 4833935360 | bytes 9441280 | tf_op jit(solution)/shard_map/while/body/eval_jaxpr/psrx,mx->psrm/dot_general | solution.py:98
  193.0 12.5 %all-to-all-start.1 = ((f32[3,16,256]{2,0,1:T(4,128)}), f32[3,16,256]{2,0,1:T(4,128)S(1)}, u32[]{:S(2)}, u32[]{:S(2)}) async-start(f32[3,16,256]{2,0,1:T(4,128)} %bitcast.43), calls=%async_computation.1 | async-start | bytes 131072 | tf_op jit(solution)/shard_map/all_to_all | solution.py:290
  205.6 3.8 %broadcast_in_dim.255.cols_ref = f32[24,4,128,128]{3,2,1,0:T(8,128)} broadcast(f32[24,4,128]{2,1,0:T(4,128)S(1)} %maximum_bitcast_fusion.rows_ref), dimensions={0,1,2} | broadcast | bytes 6340608 | tf_op jit(solution)/shard_map/broadcast_in_dim | solution.py:167
  209.4 11.9 %shard_map.167 = f32[16,3,128]{2,1,0:T(4,128)} custom-call(s32[128]{0:T(128)} %reshape.962.chosen_ref, f32[24,4,128]{2,1,0:T(4,128)} %copy-done.2, f32[24,4,128,128]{3,2,1,0:T(8,128)} %broadcast_in_dim.255.cols_ref), custom_call_target="tpu_custom_call" | custom-call | flops 54525952 | bytes 6291456 | tf_op jit(solution)/shard_map/pallas_call | solution.py:169
  227.1 0.6 bitcast_add_fusion
  (272 shorter events, 26.8 us)
Async XLA Ops:
  4.4 5.8 %copy-start.12 = (pred[16]{0:T(512)(128)(4,1)}, pred[16]{0:T(512)(128)(4,1)S(1)}, u32[]{:S(2)}) copy-start(pred[16]{0:T(512)(128)(4,1)S(1)} %get-tuple-element.218) | copy-start | bytes 52
  4.4 2.2 copy-start.10
  4.4 2.2 copy-start.31
  4.4 2.2 copy-start.33
  4.4 2.2 copy-start.29
  4.4 2.9 %copy-start.27 = (pred[16]{0:T(512)(128)(4,1)}, pred[16]{0:T(512)(128)(4,1)S(1)}, u32[]{:S(2)}) copy-start(pred[16]{0:T(512)(128)(4,1)S(1)} %get-tuple-element.280) | copy-start | bytes 52
  4.4 3.5 %copy-start.25 = (pred[16]{0:T(512)(128)(4,1)}, pred[16]{0:T(512)(128)(4,1)S(1)}, u32[]{:S(2)}) copy-start(pred[16]{0:T(512)(128)(4,1)S(1)} %get-tuple-element.281) | copy-start | bytes 52
  4.5 4.1 %copy-start.23 = (pred[16]{0:T(512)(128)(4,1)}, pred[16]{0:T(512)(128)(4,1)S(1)}, u32[]{:S(2)}) copy-start(pred[16]{0:T(512)(128)(4,1)S(1)} %get-tuple-element.282) | copy-start | bytes 52
  4.5 4.4 %copy-start.21 = (pred[16]{0:T(512)(128)(4,1)}, pred[16]{0:T(512)(128)(4,1)S(1)}, u32[]{:S(2)}) copy-start(pred[16]{0:T(512)(128)(4,1)S(1)} %get-tuple-element.283) | copy-start | bytes 52
  4.5 4.7 %copy-start.19 = (pred[16]{0:T(512)(128)(4,1)}, pred[16]{0:T(512)(128)(4,1)S(1)}, u32[]{:S(2)}) copy-start(pred[16]{0:T(512)(128)(4,1)S(1)} %get-tuple-element.284) | copy-start | bytes 52
  4.5 5.0 %copy-start.17 = (pred[16]{0:T(512)(128)(4,1)}, pred[16]{0:T(512)(128)(4,1)S(1)}, u32[]{:S(2)}) copy-start(pred[16]{0:T(512)(128)(4,1)S(1)} %get-tuple-element.285) | copy-start | bytes 52
  4.5 5.3 %copy-start.15 = (pred[16]{0:T(512)(128)(4,1)}, pred[16]{0:T(512)(128)(4,1)S(1)}, u32[]{:S(2)}) copy-start(pred[16]{0:T(512)(128)(4,1)S(1)} %get-tuple-element.276) | copy-start | bytes 52
  9.2 0.9 copy-start.14
  9.4 10.4 %copy-start.9 = (f32[2048]{0:T(1024)S(1)}, f32[2048]{0:T(1024)}, u32[]{:S(2)}) copy-start(f32[2048]{0:T(1024)} %param.23) | copy-start | bytes 24580
  9.4 10.4 %copy-start.3 = (f32[3,2048]{1,0:T(4,128)S(1)}, f32[3,2048]{1,0:T(4,128)}, u32[]{:S(2)}) copy-start(f32[3,2048]{1,0:T(4,128)} %param.22) | copy-start | bytes 73732
  9.8 13.5 %slice-start = ((f32[2,8,16,2048]{3,2,1,0:T(8,128)}), f32[1,8,16,2048]{3,2,1,0:T(8,128)S(1)}, s32[]{:S(2)}) async-start(f32[2,8,16,2048]{3,2,1,0:T(8,128)} %param.29), calls=%async_computation.2 | async-start | bytes 2097152 | tf_op jit(solution)/shard_map/slice | solution.py:270
  10.2 13.4 %copy-start.4 = (pred[16,256]{1,0:T(8,128)(4,1)}, pred[16,256]{1,0:T(8,128)(4,1)S(1)}, u32[]{:S(2)}) copy-start(pred[16,256]{1,0:T(8,128)(4,1)S(1)} %iota_compare_fusion.6) | copy-start | bytes 12292
  10.9 14.6 %all-to-all-start = ((f32[2,16,256]{2,0,1:T(2,128)}), f32[2,16,256]{2,0,1:T(2,128)S(1)}, u32[]{:S(2)}, u32[]{:S(2)}) async-start(f32[2,16,256]{2,0,1:T(2,128)} %fusion.81), calls=%async_computation | async-start | bytes 65536 | tf_op jit(solution)/shard_map/all_to_all | solution.py:265
  19.9 185.6 %collective-permute-start = (f32[4,512]{1,0:T(4,128)S(1)}, f32[4,512]{1,0:T(4,128)S(1)}, u32[]{:S(2)}, u32[]{:S(2)}) collective-permute-start(f32[4,512]{1,0:T(4,128)S(1)} %get-tuple-element.272), channel_id=1, source_target_pairs={{0,1},{1,2},{2,3},{3,4},{4,5},{5,6},{6,7},{7,8},{8,9},{9,10},{10,1... | collective-permute-start | bytes 24584 | tf_op jit(solution)/shard_map/ppermute | solution.py:33
  23.6 0.7 copy-start.35
  35.2 26.7 %copy-start.1 = (f32[2,8,16,2048]{3,2,1,0:T(8,128)S(1)}, f32[2,8,16,2048]{3,2,1,0:T(8,128)}, u32[]{:S(2)}) copy-start(f32[2,8,16,2048]{3,2,1,0:T(8,128)} %param.29) | copy-start | bytes 6291460
  64.5 15.0 %collective-permute-start.2 = (f32[2,1,16,2048]{3,2,1,0:T(8,128)S(1)}, f32[2,1,16,2048]{3,2,1,0:T(8,128)S(1)}, u32[]{:S(2)}, u32[]{:S(2)}) collective-permute-start(f32[2,1,16,2048]{3,2,1,0:T(8,128)S(1)} %get-tuple-element.262), channel_id=1, source_target_pairs={{16,0},{32,16},{48,32},{64,48},{80,64},{96,80},{112,96},{17,1},{33... | collective-permute-start | bytes 786440 | tf_op jit(solution)/shard_map/ppermute | solution.py:190
  66.4 13.1 %collective-permute-start.3 = (f32[2,1,16,2048]{3,2,1,0:T(8,128)S(1)}, f32[2,1,16,2048]{3,2,1,0:T(8,128)S(1)}, u32[]{:S(2)}, u32[]{:S(2)}) collective-permute-start(f32[2,1,16,2048]{3,2,1,0:T(8,128)S(1)} %get-tuple-element.261), channel_id=1, source_target_pairs={{0,16},{16,32},{32,48},{48,64},{64,80},{80,96},{96,112},{1,17},{17... | collective-permute-start | bytes 786440 | tf_op jit(solution)/shard_map/ppermute | solution.py:189
  68.9 6.9 %collective-permute-start.4 = (f32[2,8,1,2048]{3,1,2,0:T(8,128)S(1)}, f32[2,8,1,2048]{3,1,2,0:T(8,128)S(1)}, u32[]{:S(2)}, u32[]{:S(2)}) collective-permute-start(f32[2,8,1,2048]{3,1,2,0:T(8,128)S(1)} %copy.75), channel_id=1, source_target_pairs={{1,0},{2,1},{3,2},{4,3},{5,4},{6,5},{7,6},{8,7},{9,8},{10,9},{11,1... | collective-permute-start | bytes 393224 | tf_op jit(solution)/shard_map/ppermute | solution.py:190
  72.5 7.0 %copy-start.7 = (f32[2]{0:T(128)S(1)}, f32[2]{0:T(128)}, u32[]{:S(2)}) copy-start(f32[2]{0:T(128)} %constant.220.clone) | copy-start | bytes 28
  72.5 7.0 %copy-start.8 = (f32[2]{0:T(128)S(1)}, f32[2]{0:T(128)}, u32[]{:S(2)}) copy-start(f32[2]{0:T(128)} %constant.221.clone) | copy-start | bytes 28
  72.5 6.9 %collective-permute-start.5 = (f32[2,8,1,2048]{3,1,2,0:T(8,128)S(1)}, f32[2,8,1,2048]{3,1,2,0:T(8,128)S(1)}, u32[]{:S(2)}, u32[]{:S(2)}) collective-permute-start(f32[2,8,1,2048]{3,1,2,0:T(8,128)S(1)} %copy.77), channel_id=1, source_target_pairs={{0,1},{1,2},{2,3},{3,4},{4,5},{5,6},{6,7},{7,8},{8,9},{9,10},{10,1... | collective-permute-start | bytes 393224 | tf_op jit(solution)/shard_map/ppermute | solution.py:189
  82.5 14.0 %collective-permute-start.6 = (f32[2,1,16,2048]{3,2,1,0:T(8,128)S(1)}, f32[2,1,16,2048]{3,2,1,0:T(8,128)S(1)}, u32[]{:S(2)}, u32[]{:S(2)}) collective-permute-start(f32[2,1,16,2048]{3,2,1,0:T(8,128)S(1)} %get-tuple-element.254), channel_id=1, source_target_pairs={{16,0},{32,16},{48,32},{64,48},{80,64},{96,80},{112,96},{17,1},{33... | collective-permute-start | bytes 786440 | tf_op jit(solution)/shard_map/ppermute | solution.py:190
  85.5 11.0 %collective-permute-start.7 = (f32[2,1,16,2048]{3,2,1,0:T(8,128)S(1)}, f32[2,1,16,2048]{3,2,1,0:T(8,128)S(1)}, u32[]{:S(2)}, u32[]{:S(2)}) collective-permute-start(f32[2,1,16,2048]{3,2,1,0:T(8,128)S(1)} %get-tuple-element.253), channel_id=1, source_target_pairs={{0,16},{16,32},{32,48},{48,64},{64,80},{80,96},{96,112},{1,17},{17... | collective-permute-start | bytes 786440 | tf_op jit(solution)/shard_map/ppermute | solution.py:189
  87.5 6.9 %collective-permute-start.8 = (f32[2,8,1,2048]{3,1,2,0:T(8,128)S(1)}, f32[2,8,1,2048]{3,1,2,0:T(8,128)S(1)}, u32[]{:S(2)}, u32[]{:S(2)}) collective-permute-start(f32[2,8,1,2048]{3,1,2,0:T(8,128)S(1)} %copy.79), channel_id=1, source_target_pairs={{1,0},{2,1},{3,2},{4,3},{5,4},{6,5},{7,6},{8,7},{9,8},{10,9},{11,1... | collective-permute-start | bytes 393224 | tf_op jit(solution)/shard_map/ppermute | solution.py:190
  89.5 6.9 %collective-permute-start.9 = (f32[2,8,1,2048]{3,1,2,0:T(8,128)S(1)}, f32[2,8,1,2048]{3,1,2,0:T(8,128)S(1)}, u32[]{:S(2)}, u32[]{:S(2)}) collective-permute-start(f32[2,8,1,2048]{3,1,2,0:T(8,128)S(1)} %copy.81), channel_id=1, source_target_pairs={{0,1},{1,2},{2,3},{3,4},{4,5},{5,6},{6,7},{7,8},{8,9},{9,10},{10,1... | collective-permute-start | bytes 393224 | tf_op jit(solution)/shard_map/ppermute | solution.py:189
  99.4 15.1 %collective-permute-start.10 = (f32[2,1,16,2048]{3,2,1,0:T(8,128)S(1)}, f32[2,1,16,2048]{3,2,1,0:T(8,128)S(1)}, u32[]{:S(2)}, u32[]{:S(2)}) collective-permute-start(f32[2,1,16,2048]{3,2,1,0:T(8,128)S(1)} %get-tuple-element.246), channel_id=1, source_target_pairs={{16,0},{32,16},{48,32},{64,48},{80,64},{96,80},{112,96},{17,1},{33... | collective-permute-start | bytes 786440 | tf_op jit(solution)/shard_map/ppermute | solution.py:190
  103.5 11.0 %collective-permute-start.11 = (f32[2,1,16,2048]{3,2,1,0:T(8,128)S(1)}, f32[2,1,16,2048]{3,2,1,0:T(8,128)S(1)}, u32[]{:S(2)}, u32[]{:S(2)}) collective-permute-start(f32[2,1,16,2048]{3,2,1,0:T(8,128)S(1)} %get-tuple-element.245), channel_id=1, source_target_pairs={{0,16},{16,32},{32,48},{48,64},{64,80},{80,96},{96,112},{1,17},{17... | collective-permute-start | bytes 786440 | tf_op jit(solution)/shard_map/ppermute | solution.py:189
  105.5 6.9 %collective-permute-start.12 = (f32[2,8,1,2048]{3,1,2,0:T(8,128)S(1)}, f32[2,8,1,2048]{3,1,2,0:T(8,128)S(1)}, u32[]{:S(2)}, u32[]{:S(2)}) collective-permute-start(f32[2,8,1,2048]{3,1,2,0:T(8,128)S(1)} %copy.83), channel_id=1, source_target_pairs={{1,0},{2,1},{3,2},{4,3},{5,4},{6,5},{7,6},{8,7},{9,8},{10,9},{11,1... | collective-permute-start | bytes 393224 | tf_op jit(solution)/shard_map/ppermute | solution.py:190
  107.5 6.9 %collective-permute-start.13 = (f32[2,8,1,2048]{3,1,2,0:T(8,128)S(1)}, f32[2,8,1,2048]{3,1,2,0:T(8,128)S(1)}, u32[]{:S(2)}, u32[]{:S(2)}) collective-permute-start(f32[2,8,1,2048]{3,1,2,0:T(8,128)S(1)} %copy.85), channel_id=1, source_target_pairs={{0,1},{1,2},{2,3},{3,4},{4,5},{5,6},{6,7},{7,8},{8,9},{9,10},{10,1... | collective-permute-start | bytes 393224 | tf_op jit(solution)/shard_map/ppermute | solution.py:189
  117.4 14.8 %collective-permute-start.14 = (f32[2,1,16,2048]{3,2,1,0:T(8,128)S(1)}, f32[2,1,16,2048]{3,2,1,0:T(8,128)S(1)}, u32[]{:S(2)}, u32[]{:S(2)}) collective-permute-start(f32[2,1,16,2048]{3,2,1,0:T(8,128)S(1)} %get-tuple-element.238), channel_id=1, source_target_pairs={{16,0},{32,16},{48,32},{64,48},{80,64},{96,80},{112,96},{17,1},{33... | collective-permute-start | bytes 786440 | tf_op jit(solution)/shard_map/ppermute | solution.py:190
  120.9 11.3 %collective-permute-start.15 = (f32[2,1,16,2048]{3,2,1,0:T(8,128)S(1)}, f32[2,1,16,2048]{3,2,1,0:T(8,128)S(1)}, u32[]{:S(2)}, u32[]{:S(2)}) collective-permute-start(f32[2,1,16,2048]{3,2,1,0:T(8,128)S(1)} %get-tuple-element.237), channel_id=1, source_target_pairs={{0,16},{16,32},{32,48},{48,64},{64,80},{80,96},{96,112},{1,17},{17... | collective-permute-start | bytes 786440 | tf_op jit(solution)/shard_map/ppermute | solution.py:189
  122.9 7.1 %collective-permute-start.16 = (f32[2,8,1,2048]{3,1,2,0:T(8,128)S(1)}, f32[2,8,1,2048]{3,1,2,0:T(8,128)S(1)}, u32[]{:S(2)}, u32[]{:S(2)}) collective-permute-start(f32[2,8,1,2048]{3,1,2,0:T(8,128)S(1)} %copy.87), channel_id=1, source_target_pairs={{1,0},{2,1},{3,2},{4,3},{5,4},{6,5},{7,6},{8,7},{9,8},{10,9},{11,1... | collective-permute-start | bytes 393224 | tf_op jit(solution)/shard_map/ppermute | solution.py:190
  124.9 7.2 %collective-permute-start.17 = (f32[2,8,1,2048]{3,1,2,0:T(8,128)S(1)}, f32[2,8,1,2048]{3,1,2,0:T(8,128)S(1)}, u32[]{:S(2)}, u32[]{:S(2)}) collective-permute-start(f32[2,8,1,2048]{3,1,2,0:T(8,128)S(1)} %copy.89), channel_id=1, source_target_pairs={{0,1},{1,2},{2,3},{3,4},{4,5},{5,6},{6,7},{7,8},{8,9},{9,10},{10,1... | collective-permute-start | bytes 393224 | tf_op jit(solution)/shard_map/ppermute | solution.py:189
  130.0 75.5 %collective-permute-start.1 = (f32[4,512]{1,0:T(4,128)S(1)}, f32[4,512]{1,0:T(4,128)S(1)}, u32[]{:S(2)}, u32[]{:S(2)}) collective-permute-start(f32[4,512]{1,0:T(4,128)S(1)} %get-tuple-element.273), channel_id=1, source_target_pairs={{1,0},{2,1},{3,2},{4,3},{5,4},{6,5},{7,6},{8,7},{9,8},{10,9},{11,1... | collective-permute-start | bytes 24584 | tf_op jit(solution)/shard_map/ppermute | solution.py:36
  134.4 1.3 copy-start
  136.1 12.0 %collective-permute-start.20 = (f32[8,1,2048]{2,1,0:T(1,128)S(1)}, f32[8,1,2048]{2,1,0:T(1,128)S(1)}, u32[]{:S(2)}, u32[]{:S(2)}) collective-permute-start(f32[8,1,2048]{2,1,0:T(1,128)S(1)} %get-tuple-element.266), channel_id=1, source_target_pairs={{1,0},{2,1},{3,2},{4,3},{5,4},{6,5},{7,6},{8,7},{9,8},{10,9},{11,1... | collective-permute-start | bytes 196616 | tf_op jit(solution)/shard_map/ppermute | solution.py:190
  138.1 12.2 %collective-permute-start.21 = (f32[8,1,2048]{2,1,0:T(1,128)S(1)}, f32[8,1,2048]{2,1,0:T(1,128)S(1)}, u32[]{:S(2)}, u32[]{:S(2)}) collective-permute-start(f32[8,1,2048]{2,1,0:T(1,128)S(1)} %get-tuple-element.265), channel_id=1, source_target_pairs={{0,1},{1,2},{2,3},{3,4},{4,5},{5,6},{6,7},{7,8},{8,9},{9,10},{10,1... | collective-permute-start | bytes 196616 | tf_op jit(solution)/shard_map/ppermute | solution.py:189
  145.2 5.4 %collective-permute-start.18 = (f32[1,16,2048]{2,1,0:T(8,128)S(1)}, f32[1,16,2048]{2,1,0:T(8,128)S(1)}, u32[]{:S(2)}, u32[]{:S(2)}) collective-permute-start(f32[1,16,2048]{2,1,0:T(8,128)S(1)} %get-tuple-element.230), channel_id=1, source_target_pairs={{16,0},{32,16},{48,32},{64,48},{80,64},{96,80},{112,96},{17,1},{33... | collective-permute-start | bytes 393224 | tf_op jit(solution)/shard_map/ppermute | solution.py:190
  148.1 6.3 %collective-permute-start.19 = (f32[1,16,2048]{2,1,0:T(8,128)S(1)}, f32[1,16,2048]{2,1,0:T(8,128)S(1)}, u32[]{:S(2)}, u32[]{:S(2)}) collective-permute-start(f32[1,16,2048]{2,1,0:T(8,128)S(1)} %get-tuple-element.229), channel_id=1, source_target_pairs={{0,16},{16,32},{32,48},{48,64},{64,80},{80,96},{96,112},{1,17},{17... | collective-permute-start | bytes 393224 | tf_op jit(solution)/shard_map/ppermute | solution.py:189
  193.0 28.3 %all-to-all-start.1 = ((f32[3,16,256]{2,0,1:T(4,128)}), f32[3,16,256]{2,0,1:T(4,128)S(1)}, u32[]{:S(2)}, u32[]{:S(2)}) async-start(f32[3,16,256]{2,0,1:T(4,128)} %bitcast.43), calls=%async_computation.1 | async-start | bytes 131072 | tf_op jit(solution)/shard_map/all_to_all | solution.py:290
  205.6 3.8 %copy-start.2 = (f32[24,4,128]{2,1,0:T(4,128)}, f32[24,4,128]{2,1,0:T(4,128)S(1)}, u32[]{:S(2)}) copy-start(f32[24,4,128]{2,1,0:T(4,128)S(1)} %maximum_bitcast_fusion.rows_ref) | copy-start | bytes 147460
  209.4 11.9 %copy-start.5 = (pred[16,256]{1,0:T(8,128)(4,1)S(1)}, pred[16,256]{1,0:T(8,128)(4,1)}, u32[]{:S(2)}) copy-start(pred[16,256]{1,0:T(8,128)(4,1)} %copy-done.4) | copy-start | bytes 12292
  209.4 12.0 %copy-start.11 = (pred[16]{0:T(512)(128)(4,1)S(1)}, pred[16]{0:T(512)(128)(4,1)}, u32[]{:S(2)}) copy-start(pred[16]{0:T(512)(128)(4,1)} %copy-done.10) | copy-start | bytes 52
  221.3 0.7 copy-start.34
  221.3 1.2 copy-start.32
  221.8 1.1 copy-start.30
  222.4 1.1 copy-start.28
  222.9 1.1 copy-start.26
  223.3 1.1 copy-start.24
  223.9 1.0 copy-start.22
  224.8 0.6 copy-start.20
  225.2 0.6 copy-start.18
  225.7 0.7 copy-start.16
  226.0 0.7 copy-start.13
  226.3 0.8 copy-start.6

commit v4 on v3

--- a/solution.py
+++ b/solution.py
@@ -22,7 +22,7 @@
 ADHERE_RANGE = 4.0
 FORCE_SCALE = 0.08
 CHEMOTAXIS = 1.5
-SLOT_BLOCK = 1024
+SLOT_BLOCK = 512
 
 
 def with_halo(block, sides, width):
@@ -88,10 +88,10 @@
     return jnp.stack([high, middle, rest - middle]).astype(jnp.bfloat16)
 
 
-def pick_voxels(fields, reached):
+def pick_exact(fields, reached, block):
     species, planes, columns = fields.shape
     parts = split_three(fields)
-    pieces = reached.reshape(-1, SLOT_BLOCK)
+    pieces = reached.reshape(-1, block)
 
     def one_piece(piece):
         row_hot, column_hot = hot_tables(piece, planes, columns, jnp.bfloat16)
@@ -100,6 +100,19 @@
         )
         picked = picked[0] + picked[1] + picked[2]
         return jnp.sum(picked * jnp.transpose(row_hot).astype(jnp.float32)[None], axis=1)
+
+    found = lax.map(one_piece, pieces)
+    return jnp.moveaxis(found, 1, 0).reshape(species, -1)
+
+
+def pick_voxels(fields, reached):
+    species, planes, columns = fields.shape
+    pieces = reached.reshape(-1, SLOT_BLOCK)
+
+    def one_piece(piece):
+        row_hot, column_hot = hot_tables(piece, planes, columns)
+        picked = jnp.einsum("srx,mx->srm", fields, column_hot, precision=lax.Precision.HIGHEST)
+        return jnp.sum(picked * jnp.transpose(row_hot)[None], axis=1)
 
     found = lax.map(one_piece, pieces)
     return jnp.moveaxis(found, 1, 0).reshape(species, -1)
@@ -263,12 +276,13 @@
     windows = gather_windows(payload, starts, slot_size)
     windows = jnp.where(valid[None], windows, 0.0)
     arrived = lax.all_to_all(windows, "tile", split_axis=1, concat_axis=1, tiled=True)
+    forces, arrived = lax.optimization_barrier((forces, arrived))
     reached = arrived[0].reshape(-1).astype(jnp.int32)
     rates = arrived[1].reshape(-1)
     species, depth, rows, columns = field.shape
     planes = depth * rows
     oxygen_rows = field[0].reshape(1, planes, columns)
-    oxygen = pick_voxels(oxygen_rows, reached)[0]
+    oxygen = pick_exact(oxygen_rows, reached, 2 * SLOT_BLOCK)[0]
     consume = rates * oxygen / (MICHAELIS_HALF + oxygen)
     secrete = SECRETION * rates * HYPOXIA_HALF / (HYPOXIA_HALF + oxygen)
     amounts = jnp.stack([-STEP_TIME * consume, STEP_TIME * secrete])

time: 229 us -> 233 us (1.017)
  blocking collectives: 0 us -> 18.9 us
  starting transfers between devices: 84.2 us -> 76.7 us
  other arithmetic: 30 us -> 25.7 us
  local copies, waits for them, and re-layouts: 20.7 us -> 17.4 us
    dot_general x0 -> x8, matrix products: none -> 25.4 us  [one_piece(): jnp.einsum('srx,mx->srm', fields, column_hot, precision=lax.Precision.HIG...]
    dot_general x8 -> x4, matrix products: 38.2 us -> 13.8 us  [one_piece(): jnp.einsum('psrx,mx->psrm', parts, column_hot, preferred_element_type=jnp...]
    all_to_all x0 -> x1, blocking collectives: none -> 18.9 us  [local(): lax.all_to_all(slopes, 'tile', split_axis=1, concat_axis=1, tiled=True)]
    all_to_all x1 -> x0, starting transfers between devices: 12.5 us -> none  [local(): lax.all_to_all(slopes, 'tile', split_axis=1, concat_axis=1, tiled=True)]
    ppermute x10, starting transfers between devices: 31.3 us -> 36.2 us  [neighbours(): lax.ppermute(lax.slice_in_dim(block, block.shape[dim] - 1, None, axis=dim...]
    dynamic_update_slice x8, local copies, waits for them, and re-layouts: 2.72 us -> 0.11 us  [pick_voxels(): found = lax.map(one_piece, pieces)]
    reduce_sum x8 -> x4, other arithmetic: 3.08 us -> 0.64 us  [one_piece(): jnp.sum(picked * jnp.transpose(row_hot).astype(jnp.float32)[None], axis=1)]
    dot_general x4 -> x8, matrix products: 26.2 us -> 24.1 us  [add_piece(): jnp.einsum('smr,mx->srx', weighted, column_hot, precision=lax.Precision.H...]
  transfers between devices with their start and end apart: 24 -> 23, of which waited for: 9 -> 11; matrix products, arithmetic and copies ran while one was open for 43% -> 4% of each run, Pallas kernels for 5% -> 5%
where the time goes in v4:
time: 233 us; the launch traced here: 231 us
  starting transfers between devices  76.7 us (33%)
  matrix products  63.3 us (27%)
  other arithmetic  25.7 us (11%)
  blocking collectives  18.9 us (8%)
  local copies, waits for them, and re-layouts  17.4 us (7%)
  waiting for transfers between devices  13.2 us (6%)
  Pallas kernels  11.9 us (5%)
  between operations  2.43 us (1%)
    ppermute x10, starting transfers between devices, neighbours(): lax.ppermute(lax.slice_in_dim(block, block.shape[dim] - 1, None, axis=dim...  36.2 us
    ppermute x10, starting transfers between devices, neighbours(): high = lax.ppermute(lax.slice_in_dim(block, 0, 1, axis=dim), axis, backward)  26.1 us
    dot_general x8, matrix products, one_piece(): jnp.einsum('srx,mx->srm', fields, column_hot, precision=lax.Precision.HIG...  25.4 us
    dot_general x8, matrix products, add_piece(): jnp.einsum('smr,mx->srx', weighted, column_hot, precision=lax.Precision.H...  24.1 us
    all_to_all x1, blocking collectives, local(): lax.all_to_all(slopes, 'tile', split_axis=1, concat_axis=1, tiled=True)  18.9 us
    dot_general x4, matrix products, one_piece(): jnp.einsum('psrx,mx->psrm', parts, column_hot, preferred_element_type=jnp...  13.8 us
    pallas_call x1, Pallas kernels, pair_forces(): pl.pallas_call(force_kernel, out_shape=jax.ShapeDtypeStruct((blocks, 3, l...  11.9 us
    ppermute x10, waiting for transfers between devices, neighbours(): lax.ppermute(lax.slice_in_dim(block, block.shape[dim] - 1, None, axis=dim...  10.6 us
  transfers between devices with their start and end apart: 23, of which 11 were waited for; matrix products, arithmetic and copies ran while one was open for 4% of the time, Pallas kernels for 5%

profile of v4, /device:TPU:26, one launch (start us, length us, event | category | flops | bytes accessed | tf_op | source)
XLA Modules:
  0.0 230.5 jit_solution(2058930326716645062)
XLA Ops:
  1.3 0.7 pad_maximum_fusion.4
  2.0 0.8 fusion.83
  2.8 0.7 copy.71
  10.6 8.3 %all-to-all-start = ((f32[2,16,256]{2,0,1:T(2,128)}), f32[2,16,256]{2,0,1:T(2,128)S(1)}, u32[]{:S(2)}, u32[]{:S(2)}) async-start(f32[2,16,256]{2,0,1:T(2,128)} %fusion.80), calls=%async_computation | async-start | bytes 65536 | tf_op jit(solution)/shard_map/all_to_all | solution.py:278
  19.7 3.4 %collective-permute-start = (f32[4,512]{1,0:T(4,128)S(1)}, f32[4,512]{1,0:T(4,128)S(1)}, u32[]{:S(2)}, u32[]{:S(2)}) collective-permute-start(f32[4,512]{1,0:T(4,128)S(1)} %get-tuple-element.273), channel_id=1, source_target_pairs={{0,1},{1,2},{2,3},{3,4},{4,5},{5,6},{6,7},{7,8},{8,9},{9,10},{10,1... | collective-permute-start | bytes 24584 | tf_op jit(solution)/shard_map/ppermute | solution.py:33
  23.0 2.6 %collective-permute-start.1 = (f32[4,512]{1,0:T(4,128)S(1)}, f32[4,512]{1,0:T(4,128)S(1)}, u32[]{:S(2)}, u32[]{:S(2)}) collective-permute-start(f32[4,512]{1,0:T(4,128)S(1)} %get-tuple-element.274), channel_id=1, source_target_pairs={{1,0},{2,1},{3,2},{4,3},{5,4},{6,5},{7,6},{8,7},{9,8},{10,9},{11,1... | collective-permute-start | bytes 24584 | tf_op jit(solution)/shard_map/ppermute | solution.py:36
  26.0 1.3 pad_maximum_fusion.1
  28.6 3.9 %broadcast_in_dim.255.cols_ref = f32[24,4,128,128]{3,2,1,0:T(8,128)} broadcast(f32[24,4,128]{2,1,0:T(4,128)S(1)} %maximum_bitcast_fusion.rows_ref), dimensions={0,1,2} | broadcast | bytes 6340608 | tf_op jit(solution)/shard_map/broadcast_in_dim | solution.py:180
  32.5 11.9 %shard_map.167 = f32[16,3,128]{2,1,0:T(4,128)} custom-call(s32[128]{0:T(128)} %reshape.815.chosen_ref, f32[24,4,128]{2,1,0:T(4,128)} %copy-done.1, f32[24,4,128,128]{3,2,1,0:T(8,128)} %broadcast_in_dim.255.cols_ref), custom_call_target="tpu_custom_call" | custom-call | flops 54525952 | bytes 6291456 | tf_op jit(solution)/shard_map/pallas_call | solution.py:182
  44.5 14.8 %while.37 = (s32[]{:T(128)}, f32[4,1,1024]{2,1,0:T(1,128)S(1)}, s32[4,1024]{1,0:T(4,128)S(1)}, bf16[3,1,128,2048]{3,2,0,1:T(8,128)(2,1)}, s32[]{:T(128)}) while((s32[]{:T(128)}, f32[4,1,1024]{2,1,0:T(1,128)S(1)}, s32[4,1024]{1,0:T(4,128)S(1)}, bf16[3,1,128,2048]{3,2,0,1:T(8,128)(2,1)}, s32[]{:T(128)}) %tuple.124), condition=%wide.region_3.4_spmd, body=%wide.region_1.3_spmd.sunk | while | flops 1613645824 | bytes 4759621 | solution.py:104
  44.6 3.5 %fusion.117 = f32[3,128,1024]{2,1,0:T(8,128)S(1)} fusion(bf16[3,1,128,2048]{3,2,0,1:T(8,128)(2,1)} %get-tuple-element.388, s32[1024]{0:T(1024)S(1)} %get-tuple-element.361), kind=kOutput, calls=%fused_computation.5.clone.1 | convolution fusion | flops 1612709888 | bytes 3149824 | tf_op jit(solution)/shard_map/while/body/eval_jaxpr/psrx,mx->psrm/dot_general | solution.py:98
  48.2 3.5 %fusion.117 = f32[3,128,1024]{2,1,0:T(8,128)S(1)} fusion(bf16[3,1,128,2048]{3,2,0,1:T(8,128)(2,1)} %get-tuple-element.388, s32[1024]{0:T(1024)S(1)} %get-tuple-element.361), kind=kOutput, calls=%fused_computation.5.clone.1 | convolution fusion | flops 1612709888 | bytes 3149824 | tf_op jit(solution)/shard_map/while/body/eval_jaxpr/psrx,mx->psrm/dot_general | solution.py:98
  51.9 3.5 %fusion.117 = f32[3,128,1024]{2,1,0:T(8,128)S(1)} fusion(bf16[3,1,128,2048]{3,2,0,1:T(8,128)(2,1)} %get-tuple-element.388, s32[1024]{0:T(1024)S(1)} %get-tuple-element.361), kind=kOutput, calls=%fused_computation.5.clone.1 | convolution fusion | flops 1612709888 | bytes 3149824 | tf_op jit(solution)/shard_map/while/body/eval_jaxpr/psrx,mx->psrm/dot_general | solution.py:98
  55.6 3.5 %fusion.117 = f32[3,128,1024]{2,1,0:T(8,128)S(1)} fusion(bf16[3,1,128,2048]{3,2,0,1:T(8,128)(2,1)} %get-tuple-element.388, s32[1024]{0:T(1024)S(1)} %get-tuple-element.361), kind=kOutput, calls=%fused_computation.5.clone.1 | convolution fusion | flops 1612709888 | bytes 3149824 | tf_op jit(solution)/shard_map/while/body/eval_jaxpr/psrx,mx->psrm/dot_general | solution.py:98
  59.4 25.1 %while.39 = (s32[]{:T(128)}, f32[2,128,2048]{2,1,0:T(8,128)S(1)}, f32[8,2,512]{2,0,1:T(8,128)S(1)}, s32[8,512]{1,0:T(8,128)S(1)}, s32[]{:T(128)}, /*index=5*/s32[]{:T(128)}) while((s32[]{:T(128)}, f32[2,128,2048]{2,1,0:T(8,128)S(1)}, f32[8,2,512]{2,0,1:T(8,128)S(1)}, s32[8,512]{1,0:T(8,128)S(1)}, s32[]{:T(128)}, ...), condition=%wide.region_5.6_spmd.clone, body=%wide.region_4.5_spmd.clone.sunk | while | flops 3223594496 | bytes 4753495 | solution.py:137
  59.5 3.0 %fusion.126 = f32[2,128,2048]{2,1,0:T(8,128)S(1)} fusion(f32[2,128,2048]{2,1,0:T(8,128)S(1)} %get-tuple-element.397, s32[512]{0:T(512)S(1)} %get-tuple-element.373, pred[]{:T(512)S(6)} %compare.53, f32[512,128]{0,1:T(8,128)S(1)} %fusion.125, f32[2,512]{1,0:T(2,128)S(1)} %bitcast.140), kind=kOutput, calls=%fused_computation.44.clone.1 | convolution fusion | flops 3223453696 | bytes 4462593 | tf_op jit(solution)/shard_map/while/body/eval_jaxpr/smr,mx->srx/dot_general | solution.py:132
  62.6 3.0 %fusion.126 = f32[2,128,2048]{2,1,0:T(8,128)S(1)} fusion(f32[2,128,2048]{2,1,0:T(8,128)S(1)} %get-tuple-element.397, s32[512]{0:T(512)S(1)} %get-tuple-element.373, pred[]{:T(512)S(6)} %compare.53, f32[512,128]{0,1:T(8,128)S(1)} %fusion.125, f32[2,512]{1,0:T(2,128)S(1)} %bitcast.140), kind=kOutput, calls=%fused_computation.44.clone.1 | convolution fusion | flops 3223453696 | bytes 4462593 | tf_op jit(solution)/shard_map/while/body/eval_jaxpr/smr,mx->srx/dot_general | solution.py:132
  65.8 3.0 %fusion.126 = f32[2,128,2048]{2,1,0:T(8,128)S(1)} fusion(f32[2,128,2048]{2,1,0:T(8,128)S(1)} %get-tuple-element.397, s32[512]{0:T(512)S(1)} %get-tuple-element.373, pred[]{:T(512)S(6)} %compare.53, f32[512,128]{0,1:T(8,128)S(1)} %fusion.125, f32[2,512]{1,0:T(2,128)S(1)} %bitcast.140), kind=kOutput, calls=%fused_computation.44.clone.1 | convolution fusion | flops 3223453696 | bytes 4462593 | tf_op jit(solution)/shard_map/while/body/eval_jaxpr/smr,mx->srx/dot_general | solution.py:132
  68.9 3.0 %fusion.126 = f32[2,128,2048]{2,1,0:T(8,128)S(1)} fusion(f32[2,128,2048]{2,1,0:T(8,128)S(1)} %get-tuple-element.397, s32[512]{0:T(512)S(1)} %get-tuple-element.373, pred[]{:T(512)S(6)} %compare.53, f32[512,128]{0,1:T(8,128)S(1)} %fusion.125, f32[2,512]{1,0:T(2,128)S(1)} %bitcast.140), kind=kOutput, calls=%fused_computation.44.clone.1 | convolution fusion | flops 3223453696 | bytes 4462593 | tf_op jit(solution)/shard_map/while/body/eval_jaxpr/smr,mx->srx/dot_general | solution.py:132
  72.0 3.0 %fusion.126 = f32[2,128,2048]{2,1,0:T(8,128)S(1)} fusion(f32[2,128,2048]{2,1,0:T(8,128)S(1)} %get-tuple-element.397, s32[512]{0:T(512)S(1)} %get-tuple-element.373, pred[]{:T(512)S(6)} %compare.53, f32[512,128]{0,1:T(8,128)S(1)} %fusion.125, f32[2,512]{1,0:T(2,128)S(1)} %bitcast.140), kind=kOutput, calls=%fused_computation.44.clone.1 | convolution fusion | flops 3223453696 | bytes 4462593 | tf_op jit(solution)/shard_map/while/body/eval_jaxpr/smr,mx->srx/dot_general | solution.py:132
  75.2 3.0 %fusion.126 = f32[2,128,2048]{2,1,0:T(8,128)S(1)} fusion(f32[2,128,2048]{2,1,0:T(8,128)S(1)} %get-tuple-element.397, s32[512]{0:T(512)S(1)} %get-tuple-element.373, pred[]{:T(512)S(6)} %compare.53, f32[512,128]{0,1:T(8,128)S(1)} %fusion.125, f32[2,512]{1,0:T(2,128)S(1)} %bitcast.140), kind=kOutput, calls=%fused_computation.44.clone.1 | convolution fusion | flops 3223453696 | bytes 4462593 | tf_op jit(solution)/shard_map/while/body/eval_jaxpr/smr,mx->srx/dot_general | solution.py:132
  78.3 3.0 %fusion.126 = f32[2,128,2048]{2,1,0:T(8,128)S(1)} fusion(f32[2,128,2048]{2,1,0:T(8,128)S(1)} %get-tuple-element.397, s32[512]{0:T(512)S(1)} %get-tuple-element.373, pred[]{:T(512)S(6)} %compare.53, f32[512,128]{0,1:T(8,128)S(1)} %fusion.125, f32[2,512]{1,0:T(2,128)S(1)} %bitcast.140), kind=kOutput, calls=%fused_computation.44.clone.1 | convolution fusion | flops 3223453696 | bytes 4462593 | tf_op jit(solution)/shard_map/while/body/eval_jaxpr/smr,mx->srx/dot_general | solution.py:132
  81.4 3.0 %fusion.126 = f32[2,128,2048]{2,1,0:T(8,128)S(1)} fusion(f32[2,128,2048]{2,1,0:T(8,128)S(1)} %get-tuple-element.397, s32[512]{0:T(512)S(1)} %get-tuple-element.373, pred[]{:T(512)S(6)} %compare.53, f32[512,128]{0,1:T(8,128)S(1)} %fusion.125, f32[2,512]{1,0:T(2,128)S(1)} %bitcast.140), kind=kOutput, calls=%fused_computation.44.clone.1 | convolution fusion | flops 3223453696 | bytes 4462593 | tf_op jit(solution)/shard_map/while/body/eval_jaxpr/smr,mx->srx/dot_general | solution.py:132
  84.5 1.8 add.225
  87.0 1.9 collective-permute-start.2
  88.9 2.4 %collective-permute-start.3 = (f32[2,1,16,2048]{3,2,1,0:T(8,128)S(1)}, f32[2,1,16,2048]{3,2,1,0:T(8,128)S(1)}, u32[]{:S(2)}, u32[]{:S(2)}) collective-permute-start(f32[2,1,16,2048]{3,2,1,0:T(8,128)S(1)} %get-tuple-element.262), channel_id=1, source_target_pairs={{0,16},{16,32},{32,48},{48,64},{64,80},{80,96},{96,112},{1,17},{17... | collective-permute-start | bytes 786440 | tf_op jit(solution)/shard_map/ppermute | solution.py:202
  91.4 2.4 %collective-permute-start.4 = (f32[2,8,1,2048]{3,1,2,0:T(8,128)S(1)}, f32[2,8,1,2048]{3,1,2,0:T(8,128)S(1)}, u32[]{:S(2)}, u32[]{:S(2)}) collective-permute-start(f32[2,8,1,2048]{3,1,2,0:T(8,128)S(1)} %copy.75), channel_id=1, source_target_pairs={{1,0},{2,1},{3,2},{4,3},{5,4},{6,5},{7,6},{8,7},{9,8},{10,9},{11,1... | collective-permute-start | bytes 393224 | tf_op jit(solution)/shard_map/ppermute | solution.py:203
  94.0 3.4 %collective-permute-start.5 = (f32[2,8,1,2048]{3,1,2,0:T(8,128)S(1)}, f32[2,8,1,2048]{3,1,2,0:T(8,128)S(1)}, u32[]{:S(2)}, u32[]{:S(2)}) collective-permute-start(f32[2,8,1,2048]{3,1,2,0:T(8,128)S(1)} %copy.77), channel_id=1, source_target_pairs={{0,1},{1,2},{2,3},{3,4},{4,5},{5,6},{6,7},{7,8},{8,9},{9,10},{10,1... | collective-permute-start | bytes 393224 | tf_op jit(solution)/shard_map/ppermute | solution.py:202
  98.4 2.4 %collective-permute-done.5 = f32[2,8,1,2048]{3,1,2,0:T(8,128)S(1)} collective-permute-done((f32[2,8,1,2048]{3,1,2,0:T(8,128)S(1)}, f32[2,8,1,2048]{3,1,2,0:T(8,128)S(1)}, u32[]{:S(2)}, u32[]{:S(2)}) %collective-permute-start.5) | collective-permute-done | bytes 131104 | tf_op jit(solution)/shard_map/ppermute | solution.py:202
  101.0 2.2 fusion.47
  103.9 3.1 %collective-permute-start.6 = (f32[2,1,16,2048]{3,2,1,0:T(8,128)S(1)}, f32[2,1,16,2048]{3,2,1,0:T(8,128)S(1)}, u32[]{:S(2)}, u32[]{:S(2)}) collective-permute-start(f32[2,1,16,2048]{3,2,1,0:T(8,128)S(1)} %get-tuple-element.255), channel_id=1, source_target_pairs={{16,0},{32,16},{48,32},{64,48},{80,64},{96,80},{112,96},{17,1},{33... | collective-permute-start | bytes 786440 | tf_op jit(solution)/shard_map/ppermute | solution.py:203
  107.0 1.9 collective-permute-start.7
  108.9 1.9 collective-permute-start.8
  110.9 4.4 %collective-permute-start.9 = (f32[2,8,1,2048]{3,1,2,0:T(8,128)S(1)}, f32[2,8,1,2048]{3,1,2,0:T(8,128)S(1)}, u32[]{:S(2)}, u32[]{:S(2)}) collective-permute-start(f32[2,8,1,2048]{3,1,2,0:T(8,128)S(1)} %copy.81), channel_id=1, source_target_pairs={{0,1},{1,2},{2,3},{3,4},{4,5},{5,6},{6,7},{7,8},{8,9},{9,10},{10,1... | collective-permute-start | bytes 393224 | tf_op jit(solution)/shard_map/ppermute | solution.py:202
  116.2 1.6 collective-permute-done.9
  117.9 2.2 fusion.53
  120.8 4.1 %collective-permute-start.10 = (f32[2,1,16,2048]{3,2,1,0:T(8,128)S(1)}, f32[2,1,16,2048]{3,2,1,0:T(8,128)S(1)}, u32[]{:S(2)}, u32[]{:S(2)}) collective-permute-start(f32[2,1,16,2048]{3,2,1,0:T(8,128)S(1)} %get-tuple-element.247), channel_id=1, source_target_pairs={{16,0},{32,16},{48,32},{64,48},{80,64},{96,80},{112,96},{17,1},{33... | collective-permute-start | bytes 786440 | tf_op jit(solution)/shard_map/ppermute | solution.py:203
  125.0 1.9 collective-permute-start.11
  127.0 1.9 collective-permute-start.12
  128.9 5.3 %collective-permute-start.13 = (f32[2,8,1,2048]{3,1,2,0:T(8,128)S(1)}, f32[2,8,1,2048]{3,1,2,0:T(8,128)S(1)}, u32[]{:S(2)}, u32[]{:S(2)}) collective-permute-start(f32[2,8,1,2048]{3,1,2,0:T(8,128)S(1)} %copy.85), channel_id=1, source_target_pairs={{0,1},{1,2},{2,3},{3,4},{4,5},{5,6},{6,7},{7,8},{8,9},{9,10},{10,1... | collective-permute-start | bytes 393224 | tf_op jit(solution)/shard_map/ppermute | solution.py:202
  135.4 1.4 collective-permute-done.13
  136.9 2.2 fusion.59
  139.8 3.7 %collective-permute-start.14 = (f32[2,1,16,2048]{3,2,1,0:T(8,128)S(1)}, f32[2,1,16,2048]{3,2,1,0:T(8,128)S(1)}, u32[]{:S(2)}, u32[]{:S(2)}) collective-permute-start(f32[2,1,16,2048]{3,2,1,0:T(8,128)S(1)} %get-tuple-element.239), channel_id=1, source_target_pairs={{16,0},{32,16},{48,32},{64,48},{80,64},{96,80},{112,96},{17,1},{33... | collective-permute-start | bytes 786440 | tf_op jit(solution)/shard_map/ppermute | solution.py:203
  143.6 1.9 collective-permute-start.15
  145.6 1.9 collective-permute-start.16
  147.5 6.5 %collective-permute-start.17 = (f32[2,8,1,2048]{3,1,2,0:T(8,128)S(1)}, f32[2,8,1,2048]{3,1,2,0:T(8,128)S(1)}, u32[]{:S(2)}, u32[]{:S(2)}) collective-permute-start(f32[2,8,1,2048]{3,1,2,0:T(8,128)S(1)} %copy.89), channel_id=1, source_target_pairs={{0,1},{1,2},{2,3},{3,4},{4,5},{5,6},{6,7},{7,8},{8,9},{9,10},{10,1... | collective-permute-start | bytes 393224 | tf_op jit(solution)/shard_map/ppermute | solution.py:202
  155.1 1.4 collective-permute-done.17
  156.7 2.2 fusion.65
  159.1 1.1 copy-done
  160.5 1.9 collective-permute-start.20
  162.5 6.5 %collective-permute-start.21 = (f32[8,1,2048]{2,1,0:T(1,128)S(1)}, f32[8,1,2048]{2,1,0:T(1,128)S(1)}, u32[]{:S(2)}, u32[]{:S(2)}) collective-permute-start(f32[8,1,2048]{2,1,0:T(1,128)S(1)} %get-tuple-element.266), channel_id=1, source_target_pairs={{0,1},{1,2},{2,3},{3,4},{4,5},{5,6},{6,7},{7,8},{8,9},{9,10},{10,1... | collective-permute-start | bytes 196616 | tf_op jit(solution)/shard_map/ppermute | solution.py:202
  169.6 3.2 %collective-permute-start.18 = (f32[1,16,2048]{2,1,0:T(8,128)S(1)}, f32[1,16,2048]{2,1,0:T(8,128)S(1)}, u32[]{:S(2)}, u32[]{:S(2)}) collective-permute-start(f32[1,16,2048]{2,1,0:T(8,128)S(1)} %get-tuple-element.231), channel_id=1, source_target_pairs={{16,0},{32,16},{48,32},{64,48},{80,64},{96,80},{112,96},{17,1},{33... | collective-permute-start | bytes 393224 | tf_op jit(solution)/shard_map/ppermute | solution.py:203
  172.8 1.9 collective-permute-start.19
  175.3 3.8 %collective-permute-done.19 = f32[1,16,2048]{2,1,0:T(8,128)S(1)} collective-permute-done((f32[1,16,2048]{2,1,0:T(8,128)S(1)}, f32[1,16,2048]{2,1,0:T(8,128)S(1)}, u32[]{:S(2)}, u32[]{:S(2)}) %collective-permute-start.19) | collective-permute-done | bytes 131104 | tf_op jit(solution)/shard_map/ppermute | solution.py:202
  179.4 26.2 %while.38 = (s32[]{:T(128)}, f32[8,3,512]{2,1,0:T(4,128)S(1)}, s32[8,512]{1,0:T(8,128)S(1)}, f32[3,128,2048]{2,1,0:T(8,128)S(1)}, s32[]{:T(128)}) while((s32[]{:T(128)}, f32[8,3,512]{2,1,0:T(4,128)S(1)}, s32[8,512]{1,0:T(8,128)S(1)}, f32[3,128,2048]{2,1,0:T(8,128)S(1)}, s32[]{:T(128)}) %tuple.133), condition=%wide.region_8.9_spmd, body=%wide.region_6.8_spmd.sunk | while | flops 4833419264 | bytes 3706949 | solution.py:117
  179.5 3.2 %fusion.122 = f32[3,512]{1,0:T(4,128)S(1)} fusion(f32[3,128,2048]{2,1,0:T(8,128)S(1)} %get-tuple-element.421, s32[512]{0:T(512)S(1)} %get-tuple-element.367, f32[128,512]{1,0:T(8,128)S(1)} %fusion.121), kind=kOutput, calls=%fused_computation.28.clone.1 | convolution fusion | flops 4833278464 | bytes 3416064 | tf_op jit(solution)/shard_map/while/body/eval_jaxpr/srx,mx->srm/dot_general | solution.py:114
  182.8 3.2 %fusion.122 = f32[3,512]{1,0:T(4,128)S(1)} fusion(f32[3,128,2048]{2,1,0:T(8,128)S(1)} %get-tuple-element.421, s32[512]{0:T(512)S(1)} %get-tuple-element.367, f32[128,512]{1,0:T(8,128)S(1)} %fusion.121), kind=kOutput, calls=%fused_computation.28.clone.1 | convolution fusion | flops 4833278464 | bytes 3416064 | tf_op jit(solution)/shard_map/while/body/eval_jaxpr/srx,mx->srm/dot_general | solution.py:114
  186.0 3.2 %fusion.122 = f32[3,512]{1,0:T(4,128)S(1)} fusion(f32[3,128,2048]{2,1,0:T(8,128)S(1)} %get-tuple-element.421, s32[512]{0:T(512)S(1)} %get-tuple-element.367, f32[128,512]{1,0:T(8,128)S(1)} %fusion.121), kind=kOutput, calls=%fused_computation.28.clone.1 | convolution fusion | flops 4833278464 | bytes 3416064 | tf_op jit(solution)/shard_map/while/body/eval_jaxpr/srx,mx->srm/dot_general | solution.py:114
  189.3 3.2 %fusion.122 = f32[3,512]{1,0:T(4,128)S(1)} fusion(f32[3,128,2048]{2,1,0:T(8,128)S(1)} %get-tuple-element.421, s32[512]{0:T(512)S(1)} %get-tuple-element.367, f32[128,512]{1,0:T(8,128)S(1)} %fusion.121), kind=kOutput, calls=%fused_computation.28.clone.1 | convolution fusion | flops 4833278464 | bytes 3416064 | tf_op jit(solution)/shard_map/while/body/eval_jaxpr/srx,mx->srm/dot_general | solution.py:114
  192.6 3.2 %fusion.122 = f32[3,512]{1,0:T(4,128)S(1)} fusion(f32[3,128,2048]{2,1,0:T(8,128)S(1)} %get-tuple-element.421, s32[512]{0:T(512)S(1)} %get-tuple-element.367, f32[128,512]{1,0:T(8,128)S(1)} %fusion.121), kind=kOutput, calls=%fused_computation.28.clone.1 | convolution fusion | flops 4833278464 | bytes 3416064 | tf_op jit(solution)/shard_map/while/body/eval_jaxpr/srx,mx->srm/dot_general | solution.py:114
  195.9 3.2 %fusion.122 = f32[3,512]{1,0:T(4,128)S(1)} fusion(f32[3,128,2048]{2,1,0:T(8,128)S(1)} %get-tuple-element.421, s32[512]{0:T(512)S(1)} %get-tuple-element.367, f32[128,512]{1,0:T(8,128)S(1)} %fusion.121), kind=kOutput, calls=%fused_computation.28.clone.1 | convolution fusion | flops 4833278464 | bytes 3416064 | tf_op jit(solution)/shard_map/while/body/eval_jaxpr/srx,mx->srm/dot_general | solution.py:114
  199.1 3.2 %fusion.122 = f32[3,512]{1,0:T(4,128)S(1)} fusion(f32[3,128,2048]{2,1,0:T(8,128)S(1)} %get-tuple-element.421, s32[512]{0:T(512)S(1)} %get-tuple-element.367, f32[128,512]{1,0:T(8,128)S(1)} %fusion.121), kind=kOutput, calls=%fused_computation.28.clone.1 | convolution fusion | flops 4833278464 | bytes 3416064 | tf_op jit(solution)/shard_map/while/body/eval_jaxpr/srx,mx->srm/dot_general | solution.py:114
  202.4 3.2 %fusion.122 = f32[3,512]{1,0:T(4,128)S(1)} fusion(f32[3,128,2048]{2,1,0:T(8,128)S(1)} %get-tuple-element.421, s32[512]{0:T(512)S(1)} %get-tuple-element.367, f32[128,512]{1,0:T(8,128)S(1)} %fusion.121), kind=kOutput, calls=%fused_computation.28.clone.1 | convolution fusion | flops 4833278464 | bytes 3416064 | tf_op jit(solution)/shard_map/while/body/eval_jaxpr/srx,mx->srm/dot_general | solution.py:114
  205.6 18.9 %all_to_all.10 = f32[3,16,256]{2,0,1:T(4,128)S(1)} all-to-all(f32[3,16,256]{2,0,1:T(4,128)S(1)} %bitcast.153), channel_id=1, replica_groups=mesh['slab'=8,'tile'=16] {'tile'}, dimensions={1} | all-to-all | bytes 98304 | tf_op jit(solution)/shard_map/all_to_all | solution.py:304
  (259 shorter events, 26.7 us)
Async XLA Ops:
  9.0 0.9 copy-start.7
  9.2 10.4 %copy-start.6 = (f32[2048]{0:T(1024)S(1)}, f32[2048]{0:T(1024)}, u32[]{:S(2)}) copy-start(f32[2048]{0:T(1024)} %param.23) | copy-start | bytes 24580
  9.2 10.4 %copy-start.2 = (f32[3,2048]{1,0:T(4,128)S(1)}, f32[3,2048]{1,0:T(4,128)}, u32[]{:S(2)}) copy-start(f32[3,2048]{1,0:T(4,128)} %param.22) | copy-start | bytes 73732
  9.6 16.1 %slice-start = ((f32[2,8,16,2048]{3,2,1,0:T(8,128)}), f32[1,8,16,2048]{3,2,1,0:T(8,128)S(1)}, s32[]{:S(2)}) async-start(f32[2,8,16,2048]{3,2,1,0:T(8,128)} %param.29), calls=%async_computation.2 | async-start | bytes 2097152 | tf_op jit(solution)/shard_map/slice | solution.py:284
  10.6 33.7 %all-to-all-start = ((f32[2,16,256]{2,0,1:T(2,128)}), f32[2,16,256]{2,0,1:T(2,128)S(1)}, u32[]{:S(2)}, u32[]{:S(2)}) async-start(f32[2,16,256]{2,0,1:T(2,128)} %fusion.80), calls=%async_computation | async-start | bytes 65536 | tf_op jit(solution)/shard_map/all_to_all | solution.py:278
  19.7 8.3 %collective-permute-start = (f32[4,512]{1,0:T(4,128)S(1)}, f32[4,512]{1,0:T(4,128)S(1)}, u32[]{:S(2)}, u32[]{:S(2)}) collective-permute-start(f32[4,512]{1,0:T(4,128)S(1)} %get-tuple-element.273), channel_id=1, source_target_pairs={{0,1},{1,2},{2,3},{3,4},{4,5},{5,6},{6,7},{7,8},{8,9},{9,10},{10,1... | collective-permute-start | bytes 24584 | tf_op jit(solution)/shard_map/ppermute | solution.py:33
  23.0 5.5 %collective-permute-start.1 = (f32[4,512]{1,0:T(4,128)S(1)}, f32[4,512]{1,0:T(4,128)S(1)}, u32[]{:S(2)}, u32[]{:S(2)}) collective-permute-start(f32[4,512]{1,0:T(4,128)S(1)} %get-tuple-element.274), channel_id=1, source_target_pairs={{1,0},{2,1},{3,2},{4,3},{5,4},{6,5},{7,6},{8,7},{9,8},{10,9},{11,1... | collective-permute-start | bytes 24584 | tf_op jit(solution)/shard_map/ppermute | solution.py:36
  26.0 1.3 copy-start.8
  28.6 3.9 %copy-start.1 = (f32[24,4,128]{2,1,0:T(4,128)}, f32[24,4,128]{2,1,0:T(4,128)S(1)}, u32[]{:S(2)}) copy-start(f32[24,4,128]{2,1,0:T(4,128)S(1)} %maximum_bitcast_fusion.rows_ref) | copy-start | bytes 147460
  87.0 13.9 %collective-permute-start.2 = (f32[2,1,16,2048]{3,2,1,0:T(8,128)S(1)}, f32[2,1,16,2048]{3,2,1,0:T(8,128)S(1)}, u32[]{:S(2)}, u32[]{:S(2)}) collective-permute-start(f32[2,1,16,2048]{3,2,1,0:T(8,128)S(1)} %get-tuple-element.263), channel_id=1, source_target_pairs={{16,0},{32,16},{48,32},{64,48},{80,64},{96,80},{112,96},{17,1},{33... | collective-permute-start | bytes 786440 | tf_op jit(solution)/shard_map/ppermute | solution.py:203
  88.9 12.0 %collective-permute-start.3 = (f32[2,1,16,2048]{3,2,1,0:T(8,128)S(1)}, f32[2,1,16,2048]{3,2,1,0:T(8,128)S(1)}, u32[]{:S(2)}, u32[]{:S(2)}) collective-permute-start(f32[2,1,16,2048]{3,2,1,0:T(8,128)S(1)} %get-tuple-element.262), channel_id=1, source_target_pairs={{0,16},{16,32},{32,48},{48,64},{64,80},{80,96},{96,112},{1,17},{17... | collective-permute-start | bytes 786440 | tf_op jit(solution)/shard_map/ppermute | solution.py:202
  91.4 6.9 %collective-permute-start.4 = (f32[2,8,1,2048]{3,1,2,0:T(8,128)S(1)}, f32[2,8,1,2048]{3,1,2,0:T(8,128)S(1)}, u32[]{:S(2)}, u32[]{:S(2)}) collective-permute-start(f32[2,8,1,2048]{3,1,2,0:T(8,128)S(1)} %copy.75), channel_id=1, source_target_pairs={{1,0},{2,1},{3,2},{4,3},{5,4},{6,5},{7,6},{8,7},{9,8},{10,9},{11,1... | collective-permute-start | bytes 393224 | tf_op jit(solution)/shard_map/ppermute | solution.py:203
  93.9 7.0 %copy-start.4 = (f32[2]{0:T(128)S(1)}, f32[2]{0:T(128)}, u32[]{:S(2)}) copy-start(f32[2]{0:T(128)} %constant.226.clone) | copy-start | bytes 28
  93.9 7.0 %copy-start.5 = (f32[2]{0:T(128)S(1)}, f32[2]{0:T(128)}, u32[]{:S(2)}) copy-start(f32[2]{0:T(128)} %constant.227.clone) | copy-start | bytes 28
  94.0 6.9 %collective-permute-start.5 = (f32[2,8,1,2048]{3,1,2,0:T(8,128)S(1)}, f32[2,8,1,2048]{3,1,2,0:T(8,128)S(1)}, u32[]{:S(2)}, u32[]{:S(2)}) collective-permute-start(f32[2,8,1,2048]{3,1,2,0:T(8,128)S(1)} %copy.77), channel_id=1, source_target_pairs={{0,1},{1,2},{2,3},{3,4},{4,5},{5,6},{6,7},{7,8},{8,9},{9,10},{10,1... | collective-permute-start | bytes 393224 | tf_op jit(solution)/shard_map/ppermute | solution.py:202
  103.9 14.0 %collective-permute-start.6 = (f32[2,1,16,2048]{3,2,1,0:T(8,128)S(1)}, f32[2,1,16,2048]{3,2,1,0:T(8,128)S(1)}, u32[]{:S(2)}, u32[]{:S(2)}) collective-permute-start(f32[2,1,16,2048]{3,2,1,0:T(8,128)S(1)} %get-tuple-element.255), channel_id=1, source_target_pairs={{16,0},{32,16},{48,32},{64,48},{80,64},{96,80},{112,96},{17,1},{33... | collective-permute-start | bytes 786440 | tf_op jit(solution)/shard_map/ppermute | solution.py:203
  107.0 11.0 %collective-permute-start.7 = (f32[2,1,16,2048]{3,2,1,0:T(8,128)S(1)}, f32[2,1,16,2048]{3,2,1,0:T(8,128)S(1)}, u32[]{:S(2)}, u32[]{:S(2)}) collective-permute-start(f32[2,1,16,2048]{3,2,1,0:T(8,128)S(1)} %get-tuple-element.254), channel_id=1, source_target_pairs={{0,16},{16,32},{32,48},{48,64},{64,80},{80,96},{96,112},{1,17},{17... | collective-permute-start | bytes 786440 | tf_op jit(solution)/shard_map/ppermute | solution.py:202
  108.9 7.1 %collective-permute-start.8 = (f32[2,8,1,2048]{3,1,2,0:T(8,128)S(1)}, f32[2,8,1,2048]{3,1,2,0:T(8,128)S(1)}, u32[]{:S(2)}, u32[]{:S(2)}) collective-permute-start(f32[2,8,1,2048]{3,1,2,0:T(8,128)S(1)} %copy.79), channel_id=1, source_target_pairs={{1,0},{2,1},{3,2},{4,3},{5,4},{6,5},{7,6},{8,7},{9,8},{10,9},{11,1... | collective-permute-start | bytes 393224 | tf_op jit(solution)/shard_map/ppermute | solution.py:203
  110.9 6.9 %collective-permute-start.9 = (f32[2,8,1,2048]{3,1,2,0:T(8,128)S(1)}, f32[2,8,1,2048]{3,1,2,0:T(8,128)S(1)}, u32[]{:S(2)}, u32[]{:S(2)}) collective-permute-start(f32[2,8,1,2048]{3,1,2,0:T(8,128)S(1)} %copy.81), channel_id=1, source_target_pairs={{0,1},{1,2},{2,3},{3,4},{4,5},{5,6},{6,7},{7,8},{8,9},{9,10},{10,1... | collective-permute-start | bytes 393224 | tf_op jit(solution)/shard_map/ppermute | solution.py:202
  120.8 16.1 %collective-permute-start.10 = (f32[2,1,16,2048]{3,2,1,0:T(8,128)S(1)}, f32[2,1,16,2048]{3,2,1,0:T(8,128)S(1)}, u32[]{:S(2)}, u32[]{:S(2)}) collective-permute-start(f32[2,1,16,2048]{3,2,1,0:T(8,128)S(1)} %get-tuple-element.247), channel_id=1, source_target_pairs={{16,0},{32,16},{48,32},{64,48},{80,64},{96,80},{112,96},{17,1},{33... | collective-permute-start | bytes 786440 | tf_op jit(solution)/shard_map/ppermute | solution.py:203
  125.0 11.9 %collective-permute-start.11 = (f32[2,1,16,2048]{3,2,1,0:T(8,128)S(1)}, f32[2,1,16,2048]{3,2,1,0:T(8,128)S(1)}, u32[]{:S(2)}, u32[]{:S(2)}) collective-permute-start(f32[2,1,16,2048]{3,2,1,0:T(8,128)S(1)} %get-tuple-element.246), channel_id=1, source_target_pairs={{0,16},{16,32},{32,48},{48,64},{64,80},{80,96},{96,112},{1,17},{17... | collective-permute-start | bytes 786440 | tf_op jit(solution)/shard_map/ppermute | solution.py:202
  127.0 8.3 %collective-permute-start.12 = (f32[2,8,1,2048]{3,1,2,0:T(8,128)S(1)}, f32[2,8,1,2048]{3,1,2,0:T(8,128)S(1)}, u32[]{:S(2)}, u32[]{:S(2)}) collective-permute-start(f32[2,8,1,2048]{3,1,2,0:T(8,128)S(1)} %copy.83), channel_id=1, source_target_pairs={{1,0},{2,1},{3,2},{4,3},{5,4},{6,5},{7,6},{8,7},{9,8},{10,9},{11,1... | collective-permute-start | bytes 393224 | tf_op jit(solution)/shard_map/ppermute | solution.py:203
  128.9 7.8 %collective-permute-start.13 = (f32[2,8,1,2048]{3,1,2,0:T(8,128)S(1)}, f32[2,8,1,2048]{3,1,2,0:T(8,128)S(1)}, u32[]{:S(2)}, u32[]{:S(2)}) collective-permute-start(f32[2,8,1,2048]{3,1,2,0:T(8,128)S(1)} %copy.85), channel_id=1, source_target_pairs={{0,1},{1,2},{2,3},{3,4},{4,5},{5,6},{6,7},{7,8},{8,9},{9,10},{10,1... | collective-permute-start | bytes 393224 | tf_op jit(solution)/shard_map/ppermute | solution.py:202
  139.8 16.8 %collective-permute-start.14 = (f32[2,1,16,2048]{3,2,1,0:T(8,128)S(1)}, f32[2,1,16,2048]{3,2,1,0:T(8,128)S(1)}, u32[]{:S(2)}, u32[]{:S(2)}) collective-permute-start(f32[2,1,16,2048]{3,2,1,0:T(8,128)S(1)} %get-tuple-element.239), channel_id=1, source_target_pairs={{16,0},{32,16},{48,32},{64,48},{80,64},{96,80},{112,96},{17,1},{33... | collective-permute-start | bytes 786440 | tf_op jit(solution)/shard_map/ppermute | solution.py:203
  143.6 13.1 %collective-permute-start.15 = (f32[2,1,16,2048]{3,2,1,0:T(8,128)S(1)}, f32[2,1,16,2048]{3,2,1,0:T(8,128)S(1)}, u32[]{:S(2)}, u32[]{:S(2)}) collective-permute-start(f32[2,1,16,2048]{3,2,1,0:T(8,128)S(1)} %get-tuple-element.238), channel_id=1, source_target_pairs={{0,16},{16,32},{32,48},{48,64},{64,80},{80,96},{96,112},{1,17},{17... | collective-permute-start | bytes 786440 | tf_op jit(solution)/shard_map/ppermute | solution.py:202
  145.6 9.4 %collective-permute-start.16 = (f32[2,8,1,2048]{3,1,2,0:T(8,128)S(1)}, f32[2,8,1,2048]{3,1,2,0:T(8,128)S(1)}, u32[]{:S(2)}, u32[]{:S(2)}) collective-permute-start(f32[2,8,1,2048]{3,1,2,0:T(8,128)S(1)} %copy.87), channel_id=1, source_target_pairs={{1,0},{2,1},{3,2},{4,3},{5,4},{6,5},{7,6},{8,7},{9,8},{10,9},{11,1... | collective-permute-start | bytes 393224 | tf_op jit(solution)/shard_map/ppermute | solution.py:203
  147.5 9.0 %collective-permute-start.17 = (f32[2,8,1,2048]{3,1,2,0:T(8,128)S(1)}, f32[2,8,1,2048]{3,1,2,0:T(8,128)S(1)}, u32[]{:S(2)}, u32[]{:S(2)}) collective-permute-start(f32[2,8,1,2048]{3,1,2,0:T(8,128)S(1)} %copy.89), channel_id=1, source_target_pairs={{0,1},{1,2},{2,3},{3,4},{4,5},{5,6},{6,7},{7,8},{8,9},{9,10},{10,1... | collective-permute-start | bytes 393224 | tf_op jit(solution)/shard_map/ppermute | solution.py:202
  158.9 1.3 copy-start
  160.5 14.2 %collective-permute-start.20 = (f32[8,1,2048]{2,1,0:T(1,128)S(1)}, f32[8,1,2048]{2,1,0:T(1,128)S(1)}, u32[]{:S(2)}, u32[]{:S(2)}) collective-permute-start(f32[8,1,2048]{2,1,0:T(1,128)S(1)} %get-tuple-element.267), channel_id=1, source_target_pairs={{1,0},{2,1},{3,2},{4,3},{5,4},{6,5},{7,6},{8,7},{9,8},{10,9},{11,1... | collective-permute-start | bytes 196616 | tf_op jit(solution)/shard_map/ppermute | solution.py:203
  162.5 12.2 %collective-permute-start.21 = (f32[8,1,2048]{2,1,0:T(1,128)S(1)}, f32[8,1,2048]{2,1,0:T(1,128)S(1)}, u32[]{:S(2)}, u32[]{:S(2)}) collective-permute-start(f32[8,1,2048]{2,1,0:T(1,128)S(1)} %get-tuple-element.266), channel_id=1, source_target_pairs={{0,1},{1,2},{2,3},{3,4},{4,5},{5,6},{6,7},{7,8},{8,9},{9,10},{10,1... | collective-permute-start | bytes 196616 | tf_op jit(solution)/shard_map/ppermute | solution.py:202
  169.6 5.7 %collective-permute-start.18 = (f32[1,16,2048]{2,1,0:T(8,128)S(1)}, f32[1,16,2048]{2,1,0:T(8,128)S(1)}, u32[]{:S(2)}, u32[]{:S(2)}) collective-permute-start(f32[1,16,2048]{2,1,0:T(8,128)S(1)} %get-tuple-element.231), channel_id=1, source_target_pairs={{16,0},{32,16},{48,32},{64,48},{80,64},{96,80},{112,96},{17,1},{33... | collective-permute-start | bytes 393224 | tf_op jit(solution)/shard_map/ppermute | solution.py:203
  172.8 6.3 %collective-permute-start.19 = (f32[1,16,2048]{2,1,0:T(8,128)S(1)}, f32[1,16,2048]{2,1,0:T(8,128)S(1)}, u32[]{:S(2)}, u32[]{:S(2)}) collective-permute-start(f32[1,16,2048]{2,1,0:T(8,128)S(1)} %get-tuple-element.230), channel_id=1, source_target_pairs={{0,16},{16,32},{32,48},{48,64},{64,80},{80,96},{96,112},{1,17},{17... | collective-permute-start | bytes 393224 | tf_op jit(solution)/shard_map/ppermute | solution.py:202
  229.1 0.8 copy-start.3

commit v5 on v4

--- a/solution.py
+++ b/solution.py
@@ -276,7 +276,6 @@
     windows = gather_windows(payload, starts, slot_size)
     windows = jnp.where(valid[None], windows, 0.0)
     arrived = lax.all_to_all(windows, "tile", split_axis=1, concat_axis=1, tiled=True)
-    forces, arrived = lax.optimization_barrier((forces, arrived))
     reached = arrived[0].reshape(-1).astype(jnp.int32)
     rates = arrived[1].reshape(-1)
     species, depth, rows, columns = field.shape

time: 233 us -> 225 us (0.966)
  blocking collectives: 18.9 us -> 0 us
  starting transfers between devices: 76.7 us -> 85.1 us
  local copies, waits for them, and re-layouts: 17.4 us -> 22.1 us
    all_to_all x1 -> x0, blocking collectives: 18.9 us -> none  [local(): lax.all_to_all(slopes, 'tile', split_axis=1, concat_axis=1, tiled=True)]
    all_to_all x0 -> x1, starting transfers between devices: none -> 12.6 us  [local(): lax.all_to_all(slopes, 'tile', split_axis=1, concat_axis=1, tiled=True)]
    dynamic_update_slice x8, local copies, waits for them, and re-layouts: 0.11 us -> 4.81 us  [pick_voxels(): found = lax.map(one_piece, pieces)]
    ppermute x10, starting transfers between devices: 36.2 us -> 32.5 us  [neighbours(): lax.ppermute(lax.slice_in_dim(block, block.shape[dim] - 1, None, axis=dim...]
  transfers between devices with their start and end apart: 23 -> 24, of which waited for: 11 -> 9; matrix products, arithmetic and copies ran while one was open for 4% -> 42% of each run, Pallas kernels for 5% -> 5%
where the time goes in v5:
time: 225 us; the launch traced here: 224 us
  starting transfers between devices  85.1 us (38%)
  matrix products  63.3 us (28%)
  other arithmetic  25.7 us (11%)
  local copies, waits for them, and re-layouts  22.1 us (10%)
  waiting for transfers between devices  12.7 us (6%)
  Pallas kernels  11.9 us (5%)
  between operations  2.45 us (1%)
    ppermute x10, starting transfers between devices, neighbours(): lax.ppermute(lax.slice_in_dim(block, block.shape[dim] - 1, None, axis=dim...  32.5 us
    ppermute x10, starting transfers between devices, neighbours(): high = lax.ppermute(lax.slice_in_dim(block, 0, 1, axis=dim), axis, backward)  26.2 us
    dot_general x8, matrix products, one_piece(): jnp.einsum('srx,mx->srm', fields, column_hot, precision=lax.Precision.HIG...  25.4 us
    dot_general x8, matrix products, add_piece(): jnp.einsum('smr,mx->srx', weighted, column_hot, precision=lax.Precision.H...  24.1 us
    dot_general x4, matrix products, one_piece(): jnp.einsum('psrx,mx->psrm', parts, column_hot, preferred_element_type=jnp...  13.8 us
    all_to_all x1, starting transfers between devices, local(): lax.all_to_all(slopes, 'tile', split_axis=1, concat_axis=1, tiled=True)  12.6 us
    pallas_call x1, Pallas kernels, pair_forces(): pl.pallas_call(force_kernel, out_shape=jax.ShapeDtypeStruct((blocks, 3, l...  11.9 us
    ppermute x10, waiting for transfers between devices, neighbours(): lax.ppermute(lax.slice_in_dim(block, block.shape[dim] - 1, None, axis=dim...  10.5 us
  transfers between devices with their start and end apart: 24, of which 9 were waited for; matrix products, arithmetic and copies ran while one was open for 42% of the time, Pallas kernels for 5%

profile of v5, /device:TPU:26, one launch (start us, length us, event | category | flops | bytes accessed | tf_op | source)
XLA Modules:
  0.0 224.0 jit_solution(11696928915380407491)
XLA Ops:
  1.3 0.7 pad_maximum_fusion.4
  2.0 0.8 fusion.84
  2.8 0.7 copy.71
  9.9 0.7 fusion.80
  10.6 8.3 %all-to-all-start = ((f32[2,16,256]{2,0,1:T(2,128)}), f32[2,16,256]{2,0,1:T(2,128)S(1)}, u32[]{:S(2)}, u32[]{:S(2)}) async-start(f32[2,16,256]{2,0,1:T(2,128)} %fusion.80), calls=%async_computation | async-start | bytes 65536 | tf_op jit(solution)/shard_map/all_to_all | solution.py:278
  19.7 3.6 %collective-permute-start = (f32[4,512]{1,0:T(4,128)S(1)}, f32[4,512]{1,0:T(4,128)S(1)}, u32[]{:S(2)}, u32[]{:S(2)}) collective-permute-start(f32[4,512]{1,0:T(4,128)S(1)} %get-tuple-element.269), channel_id=1, source_target_pairs={{0,1},{1,2},{2,3},{3,4},{4,5},{5,6},{6,7},{7,8},{8,9},{9,10},{10,1... | collective-permute-start | bytes 24584 | tf_op jit(solution)/shard_map/ppermute | solution.py:33
  23.5 1.3 pad_maximum_fusion.1
  25.6 14.8 %while.37 = (s32[]{:T(128)}, f32[4,1,1024]{2,1,0:T(1,128)S(1)}, s32[4,1024]{1,0:T(4,128)S(1)}, bf16[3,1,128,2048]{3,2,0,1:T(8,128)(2,1)}, s32[]{:T(128)}) while((s32[]{:T(128)}, f32[4,1,1024]{2,1,0:T(1,128)S(1)}, s32[4,1024]{1,0:T(4,128)S(1)}, bf16[3,1,128,2048]{3,2,0,1:T(8,128)(2,1)}, s32[]{:T(128)}) %tuple.122), condition=%wide.region_3.4_spmd, body=%wide.region_1.3_spmd.sunk | while | flops 1613645824 | bytes 4759621 | solution.py:104
  25.7 3.5 %fusion.118 = f32[3,128,1024]{2,1,0:T(8,128)S(1)} fusion(bf16[3,1,128,2048]{3,2,0,1:T(8,128)(2,1)} %get-tuple-element.384, s32[1024]{0:T(1024)S(1)} %get-tuple-element.357), kind=kOutput, calls=%fused_computation.5.clone.1 | convolution fusion | flops 1612709888 | bytes 3149824 | tf_op jit(solution)/shard_map/while/body/eval_jaxpr/psrx,mx->psrm/dot_general | solution.py:98
  29.4 3.5 %fusion.118 = f32[3,128,1024]{2,1,0:T(8,128)S(1)} fusion(bf16[3,1,128,2048]{3,2,0,1:T(8,128)(2,1)} %get-tuple-element.384, s32[1024]{0:T(1024)S(1)} %get-tuple-element.357), kind=kOutput, calls=%fused_computation.5.clone.1 | convolution fusion | flops 1612709888 | bytes 3149824 | tf_op jit(solution)/shard_map/while/body/eval_jaxpr/psrx,mx->psrm/dot_general | solution.py:98
  33.0 3.5 %fusion.118 = f32[3,128,1024]{2,1,0:T(8,128)S(1)} fusion(bf16[3,1,128,2048]{3,2,0,1:T(8,128)(2,1)} %get-tuple-element.384, s32[1024]{0:T(1024)S(1)} %get-tuple-element.357), kind=kOutput, calls=%fused_computation.5.clone.1 | convolution fusion | flops 1612709888 | bytes 3149824 | tf_op jit(solution)/shard_map/while/body/eval_jaxpr/psrx,mx->psrm/dot_general | solution.py:98
  36.7 3.5 %fusion.118 = f32[3,128,1024]{2,1,0:T(8,128)S(1)} fusion(bf16[3,1,128,2048]{3,2,0,1:T(8,128)(2,1)} %get-tuple-element.384, s32[1024]{0:T(1024)S(1)} %get-tuple-element.357), kind=kOutput, calls=%fused_computation.5.clone.1 | convolution fusion | flops 1612709888 | bytes 3149824 | tf_op jit(solution)/shard_map/while/body/eval_jaxpr/psrx,mx->psrm/dot_general | solution.py:98
  40.6 25.0 %while.39 = (s32[]{:T(128)}, f32[2,128,2048]{2,1,0:T(8,128)S(1)}, f32[8,2,512]{2,0,1:T(8,128)S(1)}, s32[8,512]{1,0:T(8,128)S(1)}, s32[]{:T(128)}, /*index=5*/s32[]{:T(128)}) while((s32[]{:T(128)}, f32[2,128,2048]{2,1,0:T(8,128)S(1)}, f32[8,2,512]{2,0,1:T(8,128)S(1)}, s32[8,512]{1,0:T(8,128)S(1)}, s32[]{:T(128)}, ...), condition=%wide.region_5.6_spmd.clone, body=%wide.region_4.5_spmd.clone.sunk | while | flops 3223594496 | bytes 4753495 | solution.py:137
  40.7 3.0 %fusion.127 = f32[2,128,2048]{2,1,0:T(8,128)S(1)} fusion(f32[2,128,2048]{2,1,0:T(8,128)S(1)} %get-tuple-element.393, s32[512]{0:T(512)S(1)} %get-tuple-element.369, pred[]{:T(512)S(6)} %compare.53, f32[512,128]{0,1:T(8,128)S(1)} %fusion.126, f32[2,512]{1,0:T(2,128)S(1)} %bitcast.141), kind=kOutput, calls=%fused_computation.44.clone.1 | convolution fusion | flops 3223453696 | bytes 4462593 | tf_op jit(solution)/shard_map/while/body/eval_jaxpr/smr,mx->srx/dot_general | solution.py:132
  43.8 3.0 %fusion.127 = f32[2,128,2048]{2,1,0:T(8,128)S(1)} fusion(f32[2,128,2048]{2,1,0:T(8,128)S(1)} %get-tuple-element.393, s32[512]{0:T(512)S(1)} %get-tuple-element.369, pred[]{:T(512)S(6)} %compare.53, f32[512,128]{0,1:T(8,128)S(1)} %fusion.126, f32[2,512]{1,0:T(2,128)S(1)} %bitcast.141), kind=kOutput, calls=%fused_computation.44.clone.1 | convolution fusion | flops 3223453696 | bytes 4462593 | tf_op jit(solution)/shard_map/while/body/eval_jaxpr/smr,mx->srx/dot_general | solution.py:132
  46.9 3.0 %fusion.127 = f32[2,128,2048]{2,1,0:T(8,128)S(1)} fusion(f32[2,128,2048]{2,1,0:T(8,128)S(1)} %get-tuple-element.393, s32[512]{0:T(512)S(1)} %get-tuple-element.369, pred[]{:T(512)S(6)} %compare.53, f32[512,128]{0,1:T(8,128)S(1)} %fusion.126, f32[2,512]{1,0:T(2,128)S(1)} %bitcast.141), kind=kOutput, calls=%fused_computation.44.clone.1 | convolution fusion | flops 3223453696 | bytes 4462593 | tf_op jit(solution)/shard_map/while/body/eval_jaxpr/smr,mx->srx/dot_general | solution.py:132
  50.1 3.0 %fusion.127 = f32[2,128,2048]{2,1,0:T(8,128)S(1)} fusion(f32[2,128,2048]{2,1,0:T(8,128)S(1)} %get-tuple-element.393, s32[512]{0:T(512)S(1)} %get-tuple-element.369, pred[]{:T(512)S(6)} %compare.53, f32[512,128]{0,1:T(8,128)S(1)} %fusion.126, f32[2,512]{1,0:T(2,128)S(1)} %bitcast.141), kind=kOutput, calls=%fused_computation.44.clone.1 | convolution fusion | flops 3223453696 | bytes 4462593 | tf_op jit(solution)/shard_map/while/body/eval_jaxpr/smr,mx->srx/dot_general | solution.py:132
  53.2 3.0 %fusion.127 = f32[2,128,2048]{2,1,0:T(8,128)S(1)} fusion(f32[2,128,2048]{2,1,0:T(8,128)S(1)} %get-tuple-element.393, s32[512]{0:T(512)S(1)} %get-tuple-element.369, pred[]{:T(512)S(6)} %compare.53, f32[512,128]{0,1:T(8,128)S(1)} %fusion.126, f32[2,512]{1,0:T(2,128)S(1)} %bitcast.141), kind=kOutput, calls=%fused_computation.44.clone.1 | convolution fusion | flops 3223453696 | bytes 4462593 | tf_op jit(solution)/shard_map/while/body/eval_jaxpr/smr,mx->srx/dot_general | solution.py:132
  56.3 3.0 %fusion.127 = f32[2,128,2048]{2,1,0:T(8,128)S(1)} fusion(f32[2,128,2048]{2,1,0:T(8,128)S(1)} %get-tuple-element.393, s32[512]{0:T(512)S(1)} %get-tuple-element.369, pred[]{:T(512)S(6)} %compare.53, f32[512,128]{0,1:T(8,128)S(1)} %fusion.126, f32[2,512]{1,0:T(2,128)S(1)} %bitcast.141), kind=kOutput, calls=%fused_computation.44.clone.1 | convolution fusion | flops 3223453696 | bytes 4462593 | tf_op jit(solution)/shard_map/while/body/eval_jaxpr/smr,mx->srx/dot_general | solution.py:132
  59.5 3.0 %fusion.127 = f32[2,128,2048]{2,1,0:T(8,128)S(1)} fusion(f32[2,128,2048]{2,1,0:T(8,128)S(1)} %get-tuple-element.393, s32[512]{0:T(512)S(1)} %get-tuple-element.369, pred[]{:T(512)S(6)} %compare.53, f32[512,128]{0,1:T(8,128)S(1)} %fusion.126, f32[2,512]{1,0:T(2,128)S(1)} %bitcast.141), kind=kOutput, calls=%fused_computation.44.clone.1 | convolution fusion | flops 3223453696 | bytes 4462593 | tf_op jit(solution)/shard_map/while/body/eval_jaxpr/smr,mx->srx/dot_general | solution.py:132
  62.6 3.0 %fusion.127 = f32[2,128,2048]{2,1,0:T(8,128)S(1)} fusion(f32[2,128,2048]{2,1,0:T(8,128)S(1)} %get-tuple-element.393, s32[512]{0:T(512)S(1)} %get-tuple-element.369, pred[]{:T(512)S(6)} %compare.53, f32[512,128]{0,1:T(8,128)S(1)} %fusion.126, f32[2,512]{1,0:T(2,128)S(1)} %bitcast.141), kind=kOutput, calls=%fused_computation.44.clone.1 | convolution fusion | flops 3223453696 | bytes 4462593 | tf_op jit(solution)/shard_map/while/body/eval_jaxpr/smr,mx->srx/dot_general | solution.py:132
  65.6 1.8 add.225
  68.2 1.9 collective-permute-start.2
  70.1 2.4 %collective-permute-start.3 = (f32[2,1,16,2048]{3,2,1,0:T(8,128)S(1)}, f32[2,1,16,2048]{3,2,1,0:T(8,128)S(1)}, u32[]{:S(2)}, u32[]{:S(2)}) collective-permute-start(f32[2,1,16,2048]{3,2,1,0:T(8,128)S(1)} %get-tuple-element.258), channel_id=1, source_target_pairs={{0,16},{16,32},{32,48},{48,64},{64,80},{80,96},{96,112},{1,17},{17... | collective-permute-start | bytes 786440 | tf_op jit(solution)/shard_map/ppermute | solution.py:202
  72.6 3.0 %collective-permute-start.4 = (f32[2,8,1,2048]{3,1,2,0:T(8,128)S(1)}, f32[2,8,1,2048]{3,1,2,0:T(8,128)S(1)}, u32[]{:S(2)}, u32[]{:S(2)}) collective-permute-start(f32[2,8,1,2048]{3,1,2,0:T(8,128)S(1)} %copy.75), channel_id=1, source_target_pairs={{1,0},{2,1},{3,2},{4,3},{5,4},{6,5},{7,6},{8,7},{9,8},{10,9},{11,1... | collective-permute-start | bytes 393224 | tf_op jit(solution)/shard_map/ppermute | solution.py:203
  75.7 2.8 %collective-permute-start.5 = (f32[2,8,1,2048]{3,1,2,0:T(8,128)S(1)}, f32[2,8,1,2048]{3,1,2,0:T(8,128)S(1)}, u32[]{:S(2)}, u32[]{:S(2)}) collective-permute-start(f32[2,8,1,2048]{3,1,2,0:T(8,128)S(1)} %copy.77), channel_id=1, source_target_pairs={{0,1},{1,2},{2,3},{3,4},{4,5},{5,6},{6,7},{7,8},{8,9},{9,10},{10,1... | collective-permute-start | bytes 393224 | tf_op jit(solution)/shard_map/ppermute | solution.py:202
  79.6 3.0 %collective-permute-done.5 = f32[2,8,1,2048]{3,1,2,0:T(8,128)S(1)} collective-permute-done((f32[2,8,1,2048]{3,1,2,0:T(8,128)S(1)}, f32[2,8,1,2048]{3,1,2,0:T(8,128)S(1)}, u32[]{:S(2)}, u32[]{:S(2)}) %collective-permute-start.5) | collective-permute-done | bytes 131104 | tf_op jit(solution)/shard_map/ppermute | solution.py:202
  82.7 2.2 fusion.47
  85.6 3.1 %collective-permute-start.6 = (f32[2,1,16,2048]{3,2,1,0:T(8,128)S(1)}, f32[2,1,16,2048]{3,2,1,0:T(8,128)S(1)}, u32[]{:S(2)}, u32[]{:S(2)}) collective-permute-start(f32[2,1,16,2048]{3,2,1,0:T(8,128)S(1)} %get-tuple-element.251), channel_id=1, source_target_pairs={{16,0},{32,16},{48,32},{64,48},{80,64},{96,80},{112,96},{17,1},{33... | collective-permute-start | bytes 786440 | tf_op jit(solution)/shard_map/ppermute | solution.py:203
  88.7 1.9 collective-permute-start.7
  90.7 1.9 collective-permute-start.8
  92.7 3.9 %collective-permute-start.9 = (f32[2,8,1,2048]{3,1,2,0:T(8,128)S(1)}, f32[2,8,1,2048]{3,1,2,0:T(8,128)S(1)}, u32[]{:S(2)}, u32[]{:S(2)}) collective-permute-start(f32[2,8,1,2048]{3,1,2,0:T(8,128)S(1)} %copy.81), channel_id=1, source_target_pairs={{0,1},{1,2},{2,3},{3,4},{4,5},{5,6},{6,7},{7,8},{8,9},{9,10},{10,1... | collective-permute-start | bytes 393224 | tf_op jit(solution)/shard_map/ppermute | solution.py:202
  97.7 1.8 collective-permute-done.9
  99.7 2.2 fusion.53
  102.6 4.1 %collective-permute-start.10 = (f32[2,1,16,2048]{3,2,1,0:T(8,128)S(1)}, f32[2,1,16,2048]{3,2,1,0:T(8,128)S(1)}, u32[]{:S(2)}, u32[]{:S(2)}) collective-permute-start(f32[2,1,16,2048]{3,2,1,0:T(8,128)S(1)} %get-tuple-element.243), channel_id=1, source_target_pairs={{16,0},{32,16},{48,32},{64,48},{80,64},{96,80},{112,96},{17,1},{33... | collective-permute-start | bytes 786440 | tf_op jit(solution)/shard_map/ppermute | solution.py:203
  106.7 2.1 collective-permute-start.11
  108.9 1.9 collective-permute-start.12
  110.9 3.9 %collective-permute-start.13 = (f32[2,8,1,2048]{3,1,2,0:T(8,128)S(1)}, f32[2,8,1,2048]{3,1,2,0:T(8,128)S(1)}, u32[]{:S(2)}, u32[]{:S(2)}) collective-permute-start(f32[2,8,1,2048]{3,1,2,0:T(8,128)S(1)} %copy.85), channel_id=1, source_target_pairs={{0,1},{1,2},{2,3},{3,4},{4,5},{5,6},{6,7},{7,8},{8,9},{9,10},{10,1... | collective-permute-start | bytes 393224 | tf_op jit(solution)/shard_map/ppermute | solution.py:202
  115.9 1.8 collective-permute-done.13
  117.9 2.2 fusion.59
  120.8 3.5 %collective-permute-start.14 = (f32[2,1,16,2048]{3,2,1,0:T(8,128)S(1)}, f32[2,1,16,2048]{3,2,1,0:T(8,128)S(1)}, u32[]{:S(2)}, u32[]{:S(2)}) collective-permute-start(f32[2,1,16,2048]{3,2,1,0:T(8,128)S(1)} %get-tuple-element.235), channel_id=1, source_target_pairs={{16,0},{32,16},{48,32},{64,48},{80,64},{96,80},{112,96},{17,1},{33... | collective-permute-start | bytes 786440 | tf_op jit(solution)/shard_map/ppermute | solution.py:203
  124.3 1.9 collective-permute-start.15
  126.3 1.9 collective-permute-start.16
  128.3 5.0 %collective-permute-start.17 = (f32[2,8,1,2048]{3,1,2,0:T(8,128)S(1)}, f32[2,8,1,2048]{3,1,2,0:T(8,128)S(1)}, u32[]{:S(2)}, u32[]{:S(2)}) collective-permute-start(f32[2,8,1,2048]{3,1,2,0:T(8,128)S(1)} %copy.89), channel_id=1, source_target_pairs={{0,1},{1,2},{2,3},{3,4},{4,5},{5,6},{6,7},{7,8},{8,9},{9,10},{10,1... | collective-permute-start | bytes 393224 | tf_op jit(solution)/shard_map/ppermute | solution.py:202
  134.3 1.9 collective-permute-start.1
  136.5 2.2 fusion.65
  138.9 1.1 copy-done
  140.3 1.9 collective-permute-start.20
  142.3 6.5 %collective-permute-start.21 = (f32[8,1,2048]{2,1,0:T(1,128)S(1)}, f32[8,1,2048]{2,1,0:T(1,128)S(1)}, u32[]{:S(2)}, u32[]{:S(2)}) collective-permute-start(f32[8,1,2048]{2,1,0:T(1,128)S(1)} %get-tuple-element.262), channel_id=1, source_target_pairs={{0,1},{1,2},{2,3},{3,4},{4,5},{5,6},{6,7},{7,8},{8,9},{9,10},{10,1... | collective-permute-start | bytes 196616 | tf_op jit(solution)/shard_map/ppermute | solution.py:202
  149.4 2.9 %collective-permute-start.18 = (f32[1,16,2048]{2,1,0:T(8,128)S(1)}, f32[1,16,2048]{2,1,0:T(8,128)S(1)}, u32[]{:S(2)}, u32[]{:S(2)}) collective-permute-start(f32[1,16,2048]{2,1,0:T(8,128)S(1)} %get-tuple-element.227), channel_id=1, source_target_pairs={{16,0},{32,16},{48,32},{64,48},{80,64},{96,80},{112,96},{17,1},{33... | collective-permute-start | bytes 393224 | tf_op jit(solution)/shard_map/ppermute | solution.py:203
  152.3 1.9 collective-permute-start.19
  154.8 3.8 %collective-permute-done.19 = f32[1,16,2048]{2,1,0:T(8,128)S(1)} collective-permute-done((f32[1,16,2048]{2,1,0:T(8,128)S(1)}, f32[1,16,2048]{2,1,0:T(8,128)S(1)}, u32[]{:S(2)}, u32[]{:S(2)}) %collective-permute-start.19) | collective-permute-done | bytes 131104 | tf_op jit(solution)/shard_map/ppermute | solution.py:202
  159.0 30.7 %while.38 = (s32[]{:T(128)}, f32[8,3,512]{2,1,0:T(4,128)}, s32[8,512]{1,0:T(8,128)S(1)}, f32[3,128,2048]{2,1,0:T(8,128)S(1)}, s32[]{:T(128)}) while((s32[]{:T(128)}, f32[8,3,512]{2,1,0:T(4,128)}, s32[8,512]{1,0:T(8,128)S(1)}, f32[3,128,2048]{2,1,0:T(8,128)S(1)}, s32[]{:T(128)}) %tuple.131), condition=%wide.region_8.9_spmd, body=%wide.region_6.8_spmd.sunk | while | flops 4833419264 | bytes 3705409 | solution.py:117
  159.0 3.2 %fusion.123 = f32[3,512]{1,0:T(4,128)S(1)} fusion(f32[3,128,2048]{2,1,0:T(8,128)S(1)} %get-tuple-element.417, s32[512]{0:T(512)S(1)} %get-tuple-element.363, f32[128,512]{1,0:T(8,128)S(1)} %fusion.122), kind=kOutput, calls=%fused_computation.28.clone.1 | convolution fusion | flops 4833278464 | bytes 3416064 | tf_op jit(solution)/shard_map/while/body/eval_jaxpr/srx,mx->srm/dot_general | solution.py:114
  162.9 3.2 %fusion.123 = f32[3,512]{1,0:T(4,128)S(1)} fusion(f32[3,128,2048]{2,1,0:T(8,128)S(1)} %get-tuple-element.417, s32[512]{0:T(512)S(1)} %get-tuple-element.363, f32[128,512]{1,0:T(8,128)S(1)} %fusion.122), kind=kOutput, calls=%fused_computation.28.clone.1 | convolution fusion | flops 4833278464 | bytes 3416064 | tf_op jit(solution)/shard_map/while/body/eval_jaxpr/srx,mx->srm/dot_general | solution.py:114
  166.7 3.2 %fusion.123 = f32[3,512]{1,0:T(4,128)S(1)} fusion(f32[3,128,2048]{2,1,0:T(8,128)S(1)} %get-tuple-element.417, s32[512]{0:T(512)S(1)} %get-tuple-element.363, f32[128,512]{1,0:T(8,128)S(1)} %fusion.122), kind=kOutput, calls=%fused_computation.28.clone.1 | convolution fusion | flops 4833278464 | bytes 3416064 | tf_op jit(solution)/shard_map/while/body/eval_jaxpr/srx,mx->srm/dot_general | solution.py:114
  170.5 3.2 %fusion.123 = f32[3,512]{1,0:T(4,128)S(1)} fusion(f32[3,128,2048]{2,1,0:T(8,128)S(1)} %get-tuple-element.417, s32[512]{0:T(512)S(1)} %get-tuple-element.363, f32[128,512]{1,0:T(8,128)S(1)} %fusion.122), kind=kOutput, calls=%fused_computation.28.clone.1 | convolution fusion | flops 4833278464 | bytes 3416064 | tf_op jit(solution)/shard_map/while/body/eval_jaxpr/srx,mx->srm/dot_general | solution.py:114
  174.4 3.2 %fusion.123 = f32[3,512]{1,0:T(4,128)S(1)} fusion(f32[3,128,2048]{2,1,0:T(8,128)S(1)} %get-tuple-element.417, s32[512]{0:T(512)S(1)} %get-tuple-element.363, f32[128,512]{1,0:T(8,128)S(1)} %fusion.122), kind=kOutput, calls=%fused_computation.28.clone.1 | convolution fusion | flops 4833278464 | bytes 3416064 | tf_op jit(solution)/shard_map/while/body/eval_jaxpr/srx,mx->srm/dot_general | solution.py:114
  178.2 3.2 %fusion.123 = f32[3,512]{1,0:T(4,128)S(1)} fusion(f32[3,128,2048]{2,1,0:T(8,128)S(1)} %get-tuple-element.417, s32[512]{0:T(512)S(1)} %get-tuple-element.363, f32[128,512]{1,0:T(8,128)S(1)} %fusion.122), kind=kOutput, calls=%fused_computation.28.clone.1 | convolution fusion | flops 4833278464 | bytes 3416064 | tf_op jit(solution)/shard_map/while/body/eval_jaxpr/srx,mx->srm/dot_general | solution.py:114
  182.1 3.2 %fusion.123 = f32[3,512]{1,0:T(4,128)S(1)} fusion(f32[3,128,2048]{2,1,0:T(8,128)S(1)} %get-tuple-element.417, s32[512]{0:T(512)S(1)} %get-tuple-element.363, f32[128,512]{1,0:T(8,128)S(1)} %fusion.122), kind=kOutput, calls=%fused_computation.28.clone.1 | convolution fusion | flops 4833278464 | bytes 3416064 | tf_op jit(solution)/shard_map/while/body/eval_jaxpr/srx,mx->srm/dot_general | solution.py:114
  185.9 3.2 %fusion.123 = f32[3,512]{1,0:T(4,128)S(1)} fusion(f32[3,128,2048]{2,1,0:T(8,128)S(1)} %get-tuple-element.417, s32[512]{0:T(512)S(1)} %get-tuple-element.363, f32[128,512]{1,0:T(8,128)S(1)} %fusion.122), kind=kOutput, calls=%fused_computation.28.clone.1 | convolution fusion | flops 4833278464 | bytes 3416064 | tf_op jit(solution)/shard_map/while/body/eval_jaxpr/srx,mx->srm/dot_general | solution.py:114
  189.7 12.6 %all-to-all-start.1 = ((f32[3,16,256]{2,0,1:T(4,128)}), f32[3,16,256]{2,0,1:T(4,128)S(1)}, u32[]{:S(2)}, u32[]{:S(2)}) async-start(f32[3,16,256]{2,0,1:T(4,128)} %bitcast.41), calls=%async_computation.1 | async-start | bytes 131072 | tf_op jit(solution)/shard_map/all_to_all | solution.py:303
  202.3 3.8 %broadcast_in_dim.255.cols_ref = f32[24,4,128,128]{3,2,1,0:T(8,128)} broadcast(f32[24,4,128]{2,1,0:T(4,128)S(1)} %maximum_bitcast_fusion.rows_ref), dimensions={0,1,2} | broadcast | bytes 6340608 | tf_op jit(solution)/shard_map/broadcast_in_dim | solution.py:180
  206.1 11.9 %shard_map.167 = f32[16,3,128]{2,1,0:T(4,128)} custom-call(s32[128]{0:T(128)} %reshape.815.chosen_ref, f32[24,4,128]{2,1,0:T(4,128)} %copy-done.1, f32[24,4,128,128]{3,2,1,0:T(8,128)} %broadcast_in_dim.255.cols_ref), custom_call_target="tpu_custom_call" | custom-call | flops 54525952 | bytes 6291456 | tf_op jit(solution)/shard_map/pallas_call | solution.py:182
  (260 shorter events, 30.3 us)
Async XLA Ops:
  9.0 0.9 copy-start.7
  9.2 10.4 %copy-start.6 = (f32[2048]{0:T(1024)S(1)}, f32[2048]{0:T(1024)}, u32[]{:S(2)}) copy-start(f32[2048]{0:T(1024)} %param.23) | copy-start | bytes 24580
  9.2 10.4 %copy-start.2 = (f32[3,2048]{1,0:T(4,128)S(1)}, f32[3,2048]{1,0:T(4,128)}, u32[]{:S(2)}) copy-start(f32[3,2048]{1,0:T(4,128)} %param.22) | copy-start | bytes 73732
  9.6 13.7 %slice-start = ((f32[2,8,16,2048]{3,2,1,0:T(8,128)}), f32[1,8,16,2048]{3,2,1,0:T(8,128)S(1)}, s32[]{:S(2)}) async-start(f32[2,8,16,2048]{3,2,1,0:T(8,128)} %param.29), calls=%async_computation.2 | async-start | bytes 2097152 | tf_op jit(solution)/shard_map/slice | solution.py:283
  10.6 14.9 %all-to-all-start = ((f32[2,16,256]{2,0,1:T(2,128)}), f32[2,16,256]{2,0,1:T(2,128)S(1)}, u32[]{:S(2)}, u32[]{:S(2)}) async-start(f32[2,16,256]{2,0,1:T(2,128)} %fusion.80), calls=%async_computation | async-start | bytes 65536 | tf_op jit(solution)/shard_map/all_to_all | solution.py:278
  19.7 182.6 %collective-permute-start = (f32[4,512]{1,0:T(4,128)S(1)}, f32[4,512]{1,0:T(4,128)S(1)}, u32[]{:S(2)}, u32[]{:S(2)}) collective-permute-start(f32[4,512]{1,0:T(4,128)S(1)} %get-tuple-element.269), channel_id=1, source_target_pairs={{0,1},{1,2},{2,3},{3,4},{4,5},{5,6},{6,7},{7,8},{8,9},{9,10},{10,1... | collective-permute-start | bytes 24584 | tf_op jit(solution)/shard_map/ppermute | solution.py:33
  23.5 1.3 copy-start.8
  68.2 14.5 %collective-permute-start.2 = (f32[2,1,16,2048]{3,2,1,0:T(8,128)S(1)}, f32[2,1,16,2048]{3,2,1,0:T(8,128)S(1)}, u32[]{:S(2)}, u32[]{:S(2)}) collective-permute-start(f32[2,1,16,2048]{3,2,1,0:T(8,128)S(1)} %get-tuple-element.259), channel_id=1, source_target_pairs={{16,0},{32,16},{48,32},{64,48},{80,64},{96,80},{112,96},{17,1},{33... | collective-permute-start | bytes 786440 | tf_op jit(solution)/shard_map/ppermute | solution.py:203
  70.1 12.6 %collective-permute-start.3 = (f32[2,1,16,2048]{3,2,1,0:T(8,128)S(1)}, f32[2,1,16,2048]{3,2,1,0:T(8,128)S(1)}, u32[]{:S(2)}, u32[]{:S(2)}) collective-permute-start(f32[2,1,16,2048]{3,2,1,0:T(8,128)S(1)} %get-tuple-element.258), channel_id=1, source_target_pairs={{0,16},{16,32},{32,48},{48,64},{64,80},{80,96},{96,112},{1,17},{17... | collective-permute-start | bytes 786440 | tf_op jit(solution)/shard_map/ppermute | solution.py:202
  72.6 6.9 %collective-permute-start.4 = (f32[2,8,1,2048]{3,1,2,0:T(8,128)S(1)}, f32[2,8,1,2048]{3,1,2,0:T(8,128)S(1)}, u32[]{:S(2)}, u32[]{:S(2)}) collective-permute-start(f32[2,8,1,2048]{3,1,2,0:T(8,128)S(1)} %copy.75), channel_id=1, source_target_pairs={{1,0},{2,1},{3,2},{4,3},{5,4},{6,5},{7,6},{8,7},{9,8},{10,9},{11,1... | collective-permute-start | bytes 393224 | tf_op jit(solution)/shard_map/ppermute | solution.py:203
  75.7 7.0 %copy-start.4 = (f32[2]{0:T(128)S(1)}, f32[2]{0:T(128)}, u32[]{:S(2)}) copy-start(f32[2]{0:T(128)} %constant.226.clone) | copy-start | bytes 28
  75.7 7.0 %copy-start.5 = (f32[2]{0:T(128)S(1)}, f32[2]{0:T(128)}, u32[]{:S(2)}) copy-start(f32[2]{0:T(128)} %constant.227.clone) | copy-start | bytes 28
  75.7 6.9 %collective-permute-start.5 = (f32[2,8,1,2048]{3,1,2,0:T(8,128)S(1)}, f32[2,8,1,2048]{3,1,2,0:T(8,128)S(1)}, u32[]{:S(2)}, u32[]{:S(2)}) collective-permute-start(f32[2,8,1,2048]{3,1,2,0:T(8,128)S(1)} %copy.77), channel_id=1, source_target_pairs={{0,1},{1,2},{2,3},{3,4},{4,5},{5,6},{6,7},{7,8},{8,9},{9,10},{10,1... | collective-permute-start | bytes 393224 | tf_op jit(solution)/shard_map/ppermute | solution.py:202
  85.6 14.0 %collective-permute-start.6 = (f32[2,1,16,2048]{3,2,1,0:T(8,128)S(1)}, f32[2,1,16,2048]{3,2,1,0:T(8,128)S(1)}, u32[]{:S(2)}, u32[]{:S(2)}) collective-permute-start(f32[2,1,16,2048]{3,2,1,0:T(8,128)S(1)} %get-tuple-element.251), channel_id=1, source_target_pairs={{16,0},{32,16},{48,32},{64,48},{80,64},{96,80},{112,96},{17,1},{33... | collective-permute-start | bytes 786440 | tf_op jit(solution)/shard_map/ppermute | solution.py:203
  88.7 11.0 %collective-permute-start.7 = (f32[2,1,16,2048]{3,2,1,0:T(8,128)S(1)}, f32[2,1,16,2048]{3,2,1,0:T(8,128)S(1)}, u32[]{:S(2)}, u32[]{:S(2)}) collective-permute-start(f32[2,1,16,2048]{3,2,1,0:T(8,128)S(1)} %get-tuple-element.250), channel_id=1, source_target_pairs={{0,16},{16,32},{32,48},{48,64},{64,80},{80,96},{96,112},{1,17},{17... | collective-permute-start | bytes 786440 | tf_op jit(solution)/shard_map/ppermute | solution.py:202
  90.7 6.9 %collective-permute-start.8 = (f32[2,8,1,2048]{3,1,2,0:T(8,128)S(1)}, f32[2,8,1,2048]{3,1,2,0:T(8,128)S(1)}, u32[]{:S(2)}, u32[]{:S(2)}) collective-permute-start(f32[2,8,1,2048]{3,1,2,0:T(8,128)S(1)} %copy.79), channel_id=1, source_target_pairs={{1,0},{2,1},{3,2},{4,3},{5,4},{6,5},{7,6},{8,7},{9,8},{10,9},{11,1... | collective-permute-start | bytes 393224 | tf_op jit(solution)/shard_map/ppermute | solution.py:203
  92.7 6.9 %collective-permute-start.9 = (f32[2,8,1,2048]{3,1,2,0:T(8,128)S(1)}, f32[2,8,1,2048]{3,1,2,0:T(8,128)S(1)}, u32[]{:S(2)}, u32[]{:S(2)}) collective-permute-start(f32[2,8,1,2048]{3,1,2,0:T(8,128)S(1)} %copy.81), channel_id=1, source_target_pairs={{0,1},{1,2},{2,3},{3,4},{4,5},{5,6},{6,7},{7,8},{8,9},{9,10},{10,1... | collective-permute-start | bytes 393224 | tf_op jit(solution)/shard_map/ppermute | solution.py:202
  102.6 15.3 %collective-permute-start.10 = (f32[2,1,16,2048]{3,2,1,0:T(8,128)S(1)}, f32[2,1,16,2048]{3,2,1,0:T(8,128)S(1)}, u32[]{:S(2)}, u32[]{:S(2)}) collective-permute-start(f32[2,1,16,2048]{3,2,1,0:T(8,128)S(1)} %get-tuple-element.243), channel_id=1, source_target_pairs={{16,0},{32,16},{48,32},{64,48},{80,64},{96,80},{112,96},{17,1},{33... | collective-permute-start | bytes 786440 | tf_op jit(solution)/shard_map/ppermute | solution.py:203
  106.7 11.2 %collective-permute-start.11 = (f32[2,1,16,2048]{3,2,1,0:T(8,128)S(1)}, f32[2,1,16,2048]{3,2,1,0:T(8,128)S(1)}, u32[]{:S(2)}, u32[]{:S(2)}) collective-permute-start(f32[2,1,16,2048]{3,2,1,0:T(8,128)S(1)} %get-tuple-element.242), channel_id=1, source_target_pairs={{0,16},{16,32},{32,48},{48,64},{64,80},{80,96},{96,112},{1,17},{17... | collective-permute-start | bytes 786440 | tf_op jit(solution)/shard_map/ppermute | solution.py:202
  108.9 6.9 %collective-permute-start.12 = (f32[2,8,1,2048]{3,1,2,0:T(8,128)S(1)}, f32[2,8,1,2048]{3,1,2,0:T(8,128)S(1)}, u32[]{:S(2)}, u32[]{:S(2)}) collective-permute-start(f32[2,8,1,2048]{3,1,2,0:T(8,128)S(1)} %copy.83), channel_id=1, source_target_pairs={{1,0},{2,1},{3,2},{4,3},{5,4},{6,5},{7,6},{8,7},{9,8},{10,9},{11,1... | collective-permute-start | bytes 393224 | tf_op jit(solution)/shard_map/ppermute | solution.py:203
  110.9 6.9 %collective-permute-start.13 = (f32[2,8,1,2048]{3,1,2,0:T(8,128)S(1)}, f32[2,8,1,2048]{3,1,2,0:T(8,128)S(1)}, u32[]{:S(2)}, u32[]{:S(2)}) collective-permute-start(f32[2,8,1,2048]{3,1,2,0:T(8,128)S(1)} %copy.85), channel_id=1, source_target_pairs={{0,1},{1,2},{2,3},{3,4},{4,5},{5,6},{6,7},{7,8},{8,9},{9,10},{10,1... | collective-permute-start | bytes 393224 | tf_op jit(solution)/shard_map/ppermute | solution.py:202
  120.8 15.7 %collective-permute-start.14 = (f32[2,1,16,2048]{3,2,1,0:T(8,128)S(1)}, f32[2,1,16,2048]{3,2,1,0:T(8,128)S(1)}, u32[]{:S(2)}, u32[]{:S(2)}) collective-permute-start(f32[2,1,16,2048]{3,2,1,0:T(8,128)S(1)} %get-tuple-element.235), channel_id=1, source_target_pairs={{16,0},{32,16},{48,32},{64,48},{80,64},{96,80},{112,96},{17,1},{33... | collective-permute-start | bytes 786440 | tf_op jit(solution)/shard_map/ppermute | solution.py:203
  124.3 12.1 %collective-permute-start.15 = (f32[2,1,16,2048]{3,2,1,0:T(8,128)S(1)}, f32[2,1,16,2048]{3,2,1,0:T(8,128)S(1)}, u32[]{:S(2)}, u32[]{:S(2)}) collective-permute-start(f32[2,1,16,2048]{3,2,1,0:T(8,128)S(1)} %get-tuple-element.234), channel_id=1, source_target_pairs={{0,16},{16,32},{32,48},{48,64},{64,80},{80,96},{96,112},{1,17},{17... | collective-permute-start | bytes 786440 | tf_op jit(solution)/shard_map/ppermute | solution.py:202
  126.3 7.9 %collective-permute-start.16 = (f32[2,8,1,2048]{3,1,2,0:T(8,128)S(1)}, f32[2,8,1,2048]{3,1,2,0:T(8,128)S(1)}, u32[]{:S(2)}, u32[]{:S(2)}) collective-permute-start(f32[2,8,1,2048]{3,1,2,0:T(8,128)S(1)} %copy.87), channel_id=1, source_target_pairs={{1,0},{2,1},{3,2},{4,3},{5,4},{6,5},{7,6},{8,7},{9,8},{10,9},{11,1... | collective-permute-start | bytes 393224 | tf_op jit(solution)/shard_map/ppermute | solution.py:203
  128.3 8.0 %collective-permute-start.17 = (f32[2,8,1,2048]{3,1,2,0:T(8,128)S(1)}, f32[2,8,1,2048]{3,1,2,0:T(8,128)S(1)}, u32[]{:S(2)}, u32[]{:S(2)}) collective-permute-start(f32[2,8,1,2048]{3,1,2,0:T(8,128)S(1)} %copy.89), channel_id=1, source_target_pairs={{0,1},{1,2},{2,3},{3,4},{4,5},{5,6},{6,7},{7,8},{8,9},{9,10},{10,1... | collective-permute-start | bytes 393224 | tf_op jit(solution)/shard_map/ppermute | solution.py:202
  134.3 68.0 %collective-permute-start.1 = (f32[4,512]{1,0:T(4,128)S(1)}, f32[4,512]{1,0:T(4,128)S(1)}, u32[]{:S(2)}, u32[]{:S(2)}) collective-permute-start(f32[4,512]{1,0:T(4,128)S(1)} %get-tuple-element.270), channel_id=1, source_target_pairs={{1,0},{2,1},{3,2},{4,3},{5,4},{6,5},{7,6},{8,7},{9,8},{10,9},{11,1... | collective-permute-start | bytes 24584 | tf_op jit(solution)/shard_map/ppermute | solution.py:36
  138.7 1.3 copy-start
  140.3 12.0 %collective-permute-start.20 = (f32[8,1,2048]{2,1,0:T(1,128)S(1)}, f32[8,1,2048]{2,1,0:T(1,128)S(1)}, u32[]{:S(2)}, u32[]{:S(2)}) collective-permute-start(f32[8,1,2048]{2,1,0:T(1,128)S(1)} %get-tuple-element.263), channel_id=1, source_target_pairs={{1,0},{2,1},{3,2},{4,3},{5,4},{6,5},{7,6},{8,7},{9,8},{10,9},{11,1... | collective-permute-start | bytes 196616 | tf_op jit(solution)/shard_map/ppermute | solution.py:203
  142.3 12.0 %collective-permute-start.21 = (f32[8,1,2048]{2,1,0:T(1,128)S(1)}, f32[8,1,2048]{2,1,0:T(1,128)S(1)}, u32[]{:S(2)}, u32[]{:S(2)}) collective-permute-start(f32[8,1,2048]{2,1,0:T(1,128)S(1)} %get-tuple-element.262), channel_id=1, source_target_pairs={{0,1},{1,2},{2,3},{3,4},{4,5},{5,6},{6,7},{7,8},{8,9},{9,10},{10,1... | collective-permute-start | bytes 196616 | tf_op jit(solution)/shard_map/ppermute | solution.py:202
  149.4 5.4 %collective-permute-start.18 = (f32[1,16,2048]{2,1,0:T(8,128)S(1)}, f32[1,16,2048]{2,1,0:T(8,128)S(1)}, u32[]{:S(2)}, u32[]{:S(2)}) collective-permute-start(f32[1,16,2048]{2,1,0:T(8,128)S(1)} %get-tuple-element.227), channel_id=1, source_target_pairs={{16,0},{32,16},{48,32},{64,48},{80,64},{96,80},{112,96},{17,1},{33... | collective-permute-start | bytes 393224 | tf_op jit(solution)/shard_map/ppermute | solution.py:203
  152.3 6.3 %collective-permute-start.19 = (f32[1,16,2048]{2,1,0:T(8,128)S(1)}, f32[1,16,2048]{2,1,0:T(8,128)S(1)}, u32[]{:S(2)}, u32[]{:S(2)}) collective-permute-start(f32[1,16,2048]{2,1,0:T(8,128)S(1)} %get-tuple-element.226), channel_id=1, source_target_pairs={{0,16},{16,32},{32,48},{48,64},{64,80},{80,96},{96,112},{1,17},{17... | collective-permute-start | bytes 393224 | tf_op jit(solution)/shard_map/ppermute | solution.py:202
  189.7 28.3 %all-to-all-start.1 = ((f32[3,16,256]{2,0,1:T(4,128)}), f32[3,16,256]{2,0,1:T(4,128)S(1)}, u32[]{:S(2)}, u32[]{:S(2)}) async-start(f32[3,16,256]{2,0,1:T(4,128)} %bitcast.41), calls=%async_computation.1 | async-start | bytes 131072 | tf_op jit(solution)/shard_map/all_to_all | solution.py:303
  202.3 3.8 %copy-start.1 = (f32[24,4,128]{2,1,0:T(4,128)}, f32[24,4,128]{2,1,0:T(4,128)S(1)}, u32[]{:S(2)}) copy-start(f32[24,4,128]{2,1,0:T(4,128)S(1)} %maximum_bitcast_fusion.rows_ref) | copy-start | bytes 147460
  222.6 0.8 copy-start.3

commit v6 on v5

--- a/solution.py
+++ b/solution.py
@@ -193,6 +193,32 @@
         ),
     )(neighbor_blocks.reshape(-1), rows, cols)
     return jnp.transpose(out, (1, 0, 2))
+
+
+def deposit_voxels(oxygen_rows, reached, rates, planes, columns):
+    pieces = reached.reshape(-1, SLOT_BLOCK)
+    shares = rates.reshape(-1, SLOT_BLOCK)
+
+    def add_piece(total, item):
+        piece, rate = item
+        row_hot, column_hot = hot_tables(piece, planes, columns)
+        picked = jnp.einsum(
+            "srx,mx->srm", oxygen_rows, column_hot, precision=lax.Precision.HIGHEST
+        )
+        oxygen = jnp.sum(picked * jnp.transpose(row_hot)[None], axis=1)[0]
+        consume = rate * oxygen / (MICHAELIS_HALF + oxygen)
+        secrete = SECRETION * rate * HYPOXIA_HALF / (HYPOXIA_HALF + oxygen)
+        share = jnp.stack([-STEP_TIME * consume, STEP_TIME * secrete])
+        weighted = share[:, :, None] * row_hot[None]
+        return (
+            total
+            + jnp.einsum("smr,mx->srx", weighted, column_hot, precision=lax.Precision.HIGHEST),
+            None,
+        )
+
+    empty = jnp.zeros((2, planes, columns), jnp.float32)
+    total, unused = lax.scan(add_piece, empty, (pieces, shares))
+    return total
 
 
 def neighbours(block, axis, dim):
@@ -281,11 +307,7 @@
     species, depth, rows, columns = field.shape
     planes = depth * rows
     oxygen_rows = field[0].reshape(1, planes, columns)
-    oxygen = pick_exact(oxygen_rows, reached, 2 * SLOT_BLOCK)[0]
-    consume = rates * oxygen / (MICHAELIS_HALF + oxygen)
-    secrete = SECRETION * rates * HYPOXIA_HALF / (HYPOXIA_HALF + oxygen)
-    amounts = jnp.stack([-STEP_TIME * consume, STEP_TIME * secrete])
-    added = spread_voxels(amounts, reached, planes, columns)
+    added = deposit_voxels(oxygen_rows, reached, rates, planes, columns)
     state = field + added.reshape(species, depth, rows, columns)
     for step in range(ITERS):
         state = relax_step(state)

time: 225 us -> 229 us (1.018)
  matrix products: 63.3 us -> 69.5 us
    dot_general x4 -> x8, matrix products: 13.8 us -> 20.1 us  [add_piece(): jnp.einsum('srx,mx->srm', oxygen_rows, column_hot, precision=lax.Precisio...]
  transfers between devices with their start and end apart: 24 -> 24, of which waited for: 9 -> 9; matrix products, arithmetic and copies ran while one was open for 42% -> 43% of each run, Pallas kernels for 5% -> 5%
where the time goes in v6:
time: 229 us; the launch traced here: 227 us
  starting transfers between devices  83.3 us (36%)
  matrix products  69.5 us (30%)
  other arithmetic  23.6 us (10%)
  local copies, waits for them, and re-layouts  21.9 us (10%)
  waiting for transfers between devices  14.1 us (6%)
  Pallas kernels  11.9 us (5%)
  between operations  2.5 us (1%)
    ppermute x10, starting transfers between devices, neighbours(): lax.ppermute(lax.slice_in_dim(block, block.shape[dim] - 1, None, axis=dim...  31.4 us
    ppermute x10, starting transfers between devices, neighbours(): high = lax.ppermute(lax.slice_in_dim(block, 0, 1, axis=dim), axis, backward)  26.6 us
    dot_general x8, matrix products, one_piece(): jnp.einsum('srx,mx->srm', fields, column_hot, precision=lax.Precision.HIG...  25.4 us
    dot_general x8, matrix products, add_piece(): jnp.einsum('smr,mx->srx', weighted, column_hot, precision=lax.Precision.H...  24 us
    dot_general x8, matrix products, add_piece(): jnp.einsum('srx,mx->srm', oxygen_rows, column_hot, precision=lax.Precisio...  20.1 us
    pallas_call x1, Pallas kernels, pair_forces(): pl.pallas_call(force_kernel, out_shape=jax.ShapeDtypeStruct((blocks, 3, l...  11.9 us
    all_to_all x1, starting transfers between devices, local(): lax.all_to_all(slopes, 'tile', split_axis=1, concat_axis=1, tiled=True)  11.7 us
    ppermute x10, waiting for transfers between devices, neighbours(): lax.ppermute(lax.slice_in_dim(block, block.shape[dim] - 1, None, axis=dim...  10.8 us
  transfers between devices with their start and end apart: 24, of which 9 were waited for; matrix products, arithmetic and copies ran while one was open for 43% of the time, Pallas kernels for 5%

profile of v6, /device:TPU:26, one launch (start us, length us, event | category | flops | bytes accessed | tf_op | source)
XLA Modules:
  0.0 227.5 jit_solution(10947726695093264871)
XLA Ops:
  2.0 0.8 fusion.76
  10.7 8.3 %all-to-all-start = ((f32[2,16,256]{2,0,1:T(2,128)}), f32[2,16,256]{2,0,1:T(2,128)S(1)}, u32[]{:S(2)}, u32[]{:S(2)}) async-start(f32[2,16,256]{2,0,1:T(2,128)} %fusion.72), calls=%async_computation | async-start | bytes 65536 | tf_op jit(solution)/shard_map/all_to_all | solution.py:304
  19.7 3.4 %collective-permute-start = (f32[4,512]{1,0:T(4,128)S(1)}, f32[4,512]{1,0:T(4,128)S(1)}, u32[]{:S(2)}, u32[]{:S(2)}) collective-permute-start(f32[4,512]{1,0:T(4,128)S(1)} %get-tuple-element.215), channel_id=1, source_target_pairs={{0,1},{1,2},{2,3},{3,4},{4,5},{5,6},{6,7},{7,8},{8,9},{9,10},{10,1... | collective-permute-start | bytes 24584 | tf_op jit(solution)/shard_map/ppermute | solution.py:33
  23.9 1.4 all-to-all-done
  25.4 45.2 %while.26 = (s32[]{:T(128)}, f32[2,128,2048]{2,1,0:T(8,128)S(1)}, f32[8,512]{1,0:T(8,128)S(1)}, s32[8,512]{1,0:T(8,128)S(1)}, f32[1,128,2048]{2,1,0:T(8,128)S(1)}, /*index=5*/s32[]{:T(128)}, s32[]{:T(128)}) while((s32[]{:T(128)}, f32[2,128,2048]{2,1,0:T(8,128)S(1)}, f32[8,512]{1,0:T(8,128)S(1)}, s32[8,512]{1,0:T(8,128)S(1)}, ...), condition=%wide.region_3.4_spmd.clone, body=%wide.region_1.3_spmd.clone.sunk | while | flops 4835457024 | bytes 5808223 | solution.py:220
  25.5 2.5 %fusion.115 = f32[512]{0:T(512)S(1)} fusion(s32[512]{0:T(512)S(1)} %get-tuple-element.292, f32[1,128,2048]{2,1,0:T(8,128)S(1)} %get-tuple-element.314, s32[512]{0:T(512)S(1)} %get-tuple-element.293), kind=kOutput, calls=%fused_computation.28.clone.1 | convolution fusion | flops 1611857408 | bytes 1054720 | tf_op jit(solution)/shard_map/while/body/eval_jaxpr/srx,mx->srm/dot_general | solution.py:205
  28.1 3.0 %fusion.117 = f32[2,128,2048]{2,1,0:T(8,128)S(1)} fusion(f32[2,128,2048]{2,1,0:T(8,128)S(1)} %get-tuple-element.304, s32[512]{0:T(512)S(1)} %get-tuple-element.292, pred[]{:T(512)S(6)} %compare.39, f32[512,128]{0,1:T(8,128)S(1)} %fusion.114, f32[2,512]{1,0:T(2,128)S(1)} %pad_maximum_fusion.8), kind=kOutput, calls=%fused_computation.23.clone.1 | convolution fusion | flops 3223453696 | bytes 4462593 | tf_op jit(solution)/shard_map/while/body/eval_jaxpr/smr,mx->srx/dot_general | solution.py:215
  31.1 2.5 %fusion.115 = f32[512]{0:T(512)S(1)} fusion(s32[512]{0:T(512)S(1)} %get-tuple-element.292, f32[1,128,2048]{2,1,0:T(8,128)S(1)} %get-tuple-element.314, s32[512]{0:T(512)S(1)} %get-tuple-element.293), kind=kOutput, calls=%fused_computation.28.clone.1 | convolution fusion | flops 1611857408 | bytes 1054720 | tf_op jit(solution)/shard_map/while/body/eval_jaxpr/srx,mx->srm/dot_general | solution.py:205
  33.7 3.0 %fusion.117 = f32[2,128,2048]{2,1,0:T(8,128)S(1)} fusion(f32[2,128,2048]{2,1,0:T(8,128)S(1)} %get-tuple-element.304, s32[512]{0:T(512)S(1)} %get-tuple-element.292, pred[]{:T(512)S(6)} %compare.39, f32[512,128]{0,1:T(8,128)S(1)} %fusion.114, f32[2,512]{1,0:T(2,128)S(1)} %pad_maximum_fusion.8), kind=kOutput, calls=%fused_computation.23.clone.1 | convolution fusion | flops 3223453696 | bytes 4462593 | tf_op jit(solution)/shard_map/while/body/eval_jaxpr/smr,mx->srx/dot_general | solution.py:215
  36.8 2.5 %fusion.115 = f32[512]{0:T(512)S(1)} fusion(s32[512]{0:T(512)S(1)} %get-tuple-element.292, f32[1,128,2048]{2,1,0:T(8,128)S(1)} %get-tuple-element.314, s32[512]{0:T(512)S(1)} %get-tuple-element.293), kind=kOutput, calls=%fused_computation.28.clone.1 | convolution fusion | flops 1611857408 | bytes 1054720 | tf_op jit(solution)/shard_map/while/body/eval_jaxpr/srx,mx->srm/dot_general | solution.py:205
  39.4 3.0 %fusion.117 = f32[2,128,2048]{2,1,0:T(8,128)S(1)} fusion(f32[2,128,2048]{2,1,0:T(8,128)S(1)} %get-tuple-element.304, s32[512]{0:T(512)S(1)} %get-tuple-element.292, pred[]{:T(512)S(6)} %compare.39, f32[512,128]{0,1:T(8,128)S(1)} %fusion.114, f32[2,512]{1,0:T(2,128)S(1)} %pad_maximum_fusion.8), kind=kOutput, calls=%fused_computation.23.clone.1 | convolution fusion | flops 3223453696 | bytes 4462593 | tf_op jit(solution)/shard_map/while/body/eval_jaxpr/smr,mx->srx/dot_general | solution.py:215
  42.4 2.5 %fusion.115 = f32[512]{0:T(512)S(1)} fusion(s32[512]{0:T(512)S(1)} %get-tuple-element.292, f32[1,128,2048]{2,1,0:T(8,128)S(1)} %get-tuple-element.314, s32[512]{0:T(512)S(1)} %get-tuple-element.293), kind=kOutput, calls=%fused_computation.28.clone.1 | convolution fusion | flops 1611857408 | bytes 1054720 | tf_op jit(solution)/shard_map/while/body/eval_jaxpr/srx,mx->srm/dot_general | solution.py:205
  45.0 3.0 %fusion.117 = f32[2,128,2048]{2,1,0:T(8,128)S(1)} fusion(f32[2,128,2048]{2,1,0:T(8,128)S(1)} %get-tuple-element.304, s32[512]{0:T(512)S(1)} %get-tuple-element.292, pred[]{:T(512)S(6)} %compare.39, f32[512,128]{0,1:T(8,128)S(1)} %fusion.114, f32[2,512]{1,0:T(2,128)S(1)} %pad_maximum_fusion.8), kind=kOutput, calls=%fused_computation.23.clone.1 | convolution fusion | flops 3223453696 | bytes 4462593 | tf_op jit(solution)/shard_map/while/body/eval_jaxpr/smr,mx->srx/dot_general | solution.py:215
  48.1 2.5 %fusion.115 = f32[512]{0:T(512)S(1)} fusion(s32[512]{0:T(512)S(1)} %get-tuple-element.292, f32[1,128,2048]{2,1,0:T(8,128)S(1)} %get-tuple-element.314, s32[512]{0:T(512)S(1)} %get-tuple-element.293), kind=kOutput, calls=%fused_computation.28.clone.1 | convolution fusion | flops 1611857408 | bytes 1054720 | tf_op jit(solution)/shard_map/while/body/eval_jaxpr/srx,mx->srm/dot_general | solution.py:205
  50.7 3.0 %fusion.117 = f32[2,128,2048]{2,1,0:T(8,128)S(1)} fusion(f32[2,128,2048]{2,1,0:T(8,128)S(1)} %get-tuple-element.304, s32[512]{0:T(512)S(1)} %get-tuple-element.292, pred[]{:T(512)S(6)} %compare.39, f32[512,128]{0,1:T(8,128)S(1)} %fusion.114, f32[2,512]{1,0:T(2,128)S(1)} %pad_maximum_fusion.8), kind=kOutput, calls=%fused_computation.23.clone.1 | convolution fusion | flops 3223453696 | bytes 4462593 | tf_op jit(solution)/shard_map/while/body/eval_jaxpr/smr,mx->srx/dot_general | solution.py:215
  53.7 2.5 %fusion.115 = f32[512]{0:T(512)S(1)} fusion(s32[512]{0:T(512)S(1)} %get-tuple-element.292, f32[1,128,2048]{2,1,0:T(8,128)S(1)} %get-tuple-element.314, s32[512]{0:T(512)S(1)} %get-tuple-element.293), kind=kOutput, calls=%fused_computation.28.clone.1 | convolution fusion | flops 1611857408 | bytes 1054720 | tf_op jit(solution)/shard_map/while/body/eval_jaxpr/srx,mx->srm/dot_general | solution.py:205
  56.3 3.0 %fusion.117 = f32[2,128,2048]{2,1,0:T(8,128)S(1)} fusion(f32[2,128,2048]{2,1,0:T(8,128)S(1)} %get-tuple-element.304, s32[512]{0:T(512)S(1)} %get-tuple-element.292, pred[]{:T(512)S(6)} %compare.39, f32[512,128]{0,1:T(8,128)S(1)} %fusion.114, f32[2,512]{1,0:T(2,128)S(1)} %pad_maximum_fusion.8), kind=kOutput, calls=%fused_computation.23.clone.1 | convolution fusion | flops 3223453696 | bytes 4462593 | tf_op jit(solution)/shard_map/while/body/eval_jaxpr/smr,mx->srx/dot_general | solution.py:215
  59.4 2.5 %fusion.115 = f32[512]{0:T(512)S(1)} fusion(s32[512]{0:T(512)S(1)} %get-tuple-element.292, f32[1,128,2048]{2,1,0:T(8,128)S(1)} %get-tuple-element.314, s32[512]{0:T(512)S(1)} %get-tuple-element.293), kind=kOutput, calls=%fused_computation.28.clone.1 | convolution fusion | flops 1611857408 | bytes 1054720 | tf_op jit(solution)/shard_map/while/body/eval_jaxpr/srx,mx->srm/dot_general | solution.py:205
  62.0 3.0 %fusion.117 = f32[2,128,2048]{2,1,0:T(8,128)S(1)} fusion(f32[2,128,2048]{2,1,0:T(8,128)S(1)} %get-tuple-element.304, s32[512]{0:T(512)S(1)} %get-tuple-element.292, pred[]{:T(512)S(6)} %compare.39, f32[512,128]{0,1:T(8,128)S(1)} %fusion.114, f32[2,512]{1,0:T(2,128)S(1)} %pad_maximum_fusion.8), kind=kOutput, calls=%fused_computation.23.clone.1 | convolution fusion | flops 3223453696 | bytes 4462593 | tf_op jit(solution)/shard_map/while/body/eval_jaxpr/smr,mx->srx/dot_general | solution.py:215
  65.0 2.5 %fusion.115 = f32[512]{0:T(512)S(1)} fusion(s32[512]{0:T(512)S(1)} %get-tuple-element.292, f32[1,128,2048]{2,1,0:T(8,128)S(1)} %get-tuple-element.314, s32[512]{0:T(512)S(1)} %get-tuple-element.293), kind=kOutput, calls=%fused_computation.28.clone.1 | convolution fusion | flops 1611857408 | bytes 1054720 | tf_op jit(solution)/shard_map/while/body/eval_jaxpr/srx,mx->srm/dot_general | solution.py:205
  67.6 3.0 %fusion.117 = f32[2,128,2048]{2,1,0:T(8,128)S(1)} fusion(f32[2,128,2048]{2,1,0:T(8,128)S(1)} %get-tuple-element.304, s32[512]{0:T(512)S(1)} %get-tuple-element.292, pred[]{:T(512)S(6)} %compare.39, f32[512,128]{0,1:T(8,128)S(1)} %fusion.114, f32[2,512]{1,0:T(2,128)S(1)} %pad_maximum_fusion.8), kind=kOutput, calls=%fused_computation.23.clone.1 | convolution fusion | flops 3223453696 | bytes 4462593 | tf_op jit(solution)/shard_map/while/body/eval_jaxpr/smr,mx->srx/dot_general | solution.py:215
  70.6 1.8 add.182
  73.2 1.9 collective-permute-start.2
  75.1 2.4 %collective-permute-start.3 = (f32[2,1,16,2048]{3,2,1,0:T(8,128)S(1)}, f32[2,1,16,2048]{3,2,1,0:T(8,128)S(1)}, u32[]{:S(2)}, u32[]{:S(2)}) collective-permute-start(f32[2,1,16,2048]{3,2,1,0:T(8,128)S(1)} %get-tuple-element.207), channel_id=1, source_target_pairs={{0,16},{16,32},{32,48},{48,64},{64,80},{80,96},{96,112},{1,17},{17... | collective-permute-start | bytes 786440 | tf_op jit(solution)/shard_map/ppermute | solution.py:228
  77.6 3.4 %collective-permute-start.4 = (f32[2,8,1,2048]{3,1,2,0:T(8,128)S(1)}, f32[2,8,1,2048]{3,1,2,0:T(8,128)S(1)}, u32[]{:S(2)}, u32[]{:S(2)}) collective-permute-start(f32[2,8,1,2048]{3,1,2,0:T(8,128)S(1)} %copy.38), channel_id=1, source_target_pairs={{1,0},{2,1},{3,2},{4,3},{5,4},{6,5},{7,6},{8,7},{9,8},{10,9},{11,1... | collective-permute-start | bytes 393224 | tf_op jit(solution)/shard_map/ppermute | solution.py:229
  81.1 2.7 %collective-permute-start.5 = (f32[2,8,1,2048]{3,1,2,0:T(8,128)S(1)}, f32[2,8,1,2048]{3,1,2,0:T(8,128)S(1)}, u32[]{:S(2)}, u32[]{:S(2)}) collective-permute-start(f32[2,8,1,2048]{3,1,2,0:T(8,128)S(1)} %copy.40), channel_id=1, source_target_pairs={{0,1},{1,2},{2,3},{3,4},{4,5},{5,6},{6,7},{7,8},{8,9},{9,10},{10,1... | collective-permute-start | bytes 393224 | tf_op jit(solution)/shard_map/ppermute | solution.py:228
  84.6 3.3 %collective-permute-done.5 = f32[2,8,1,2048]{3,1,2,0:T(8,128)S(1)} collective-permute-done((f32[2,8,1,2048]{3,1,2,0:T(8,128)S(1)}, f32[2,8,1,2048]{3,1,2,0:T(8,128)S(1)}, u32[]{:S(2)}, u32[]{:S(2)}) %collective-permute-start.5) | collective-permute-done | bytes 131104 | tf_op jit(solution)/shard_map/ppermute | solution.py:228
  88.1 2.2 fusion.40
  91.0 3.1 %collective-permute-start.6 = (f32[2,1,16,2048]{3,2,1,0:T(8,128)S(1)}, f32[2,1,16,2048]{3,2,1,0:T(8,128)S(1)}, u32[]{:S(2)}, u32[]{:S(2)}) collective-permute-start(f32[2,1,16,2048]{3,2,1,0:T(8,128)S(1)} %get-tuple-element.200), channel_id=1, source_target_pairs={{16,0},{32,16},{48,32},{64,48},{80,64},{96,80},{112,96},{17,1},{33... | collective-permute-start | bytes 786440 | tf_op jit(solution)/shard_map/ppermute | solution.py:229
  94.1 1.9 collective-permute-start.7
  96.0 1.9 collective-permute-start.8
  98.0 3.9 %collective-permute-start.9 = (f32[2,8,1,2048]{3,1,2,0:T(8,128)S(1)}, f32[2,8,1,2048]{3,1,2,0:T(8,128)S(1)}, u32[]{:S(2)}, u32[]{:S(2)}) collective-permute-start(f32[2,8,1,2048]{3,1,2,0:T(8,128)S(1)} %copy.44), channel_id=1, source_target_pairs={{0,1},{1,2},{2,3},{3,4},{4,5},{5,6},{6,7},{7,8},{8,9},{9,10},{10,1... | collective-permute-start | bytes 393224 | tf_op jit(solution)/shard_map/ppermute | solution.py:228
  103.0 1.8 collective-permute-done.9
  105.0 2.2 fusion.46
  107.9 4.1 %collective-permute-start.10 = (f32[2,1,16,2048]{3,2,1,0:T(8,128)S(1)}, f32[2,1,16,2048]{3,2,1,0:T(8,128)S(1)}, u32[]{:S(2)}, u32[]{:S(2)}) collective-permute-start(f32[2,1,16,2048]{3,2,1,0:T(8,128)S(1)} %get-tuple-element.192), channel_id=1, source_target_pairs={{16,0},{32,16},{48,32},{64,48},{80,64},{96,80},{112,96},{17,1},{33... | collective-permute-start | bytes 786440 | tf_op jit(solution)/shard_map/ppermute | solution.py:229
  112.1 1.9 collective-permute-start.11
  114.1 1.9 collective-permute-start.12
  116.0 3.9 %collective-permute-start.13 = (f32[2,8,1,2048]{3,1,2,0:T(8,128)S(1)}, f32[2,8,1,2048]{3,1,2,0:T(8,128)S(1)}, u32[]{:S(2)}, u32[]{:S(2)}) collective-permute-start(f32[2,8,1,2048]{3,1,2,0:T(8,128)S(1)} %copy.48), channel_id=1, source_target_pairs={{0,1},{1,2},{2,3},{3,4},{4,5},{5,6},{6,7},{7,8},{8,9},{9,10},{10,1... | collective-permute-start | bytes 393224 | tf_op jit(solution)/shard_map/ppermute | solution.py:228
  121.1 1.8 collective-permute-done.13
  123.1 2.2 fusion.52
  126.0 3.5 %collective-permute-start.14 = (f32[2,1,16,2048]{3,2,1,0:T(8,128)S(1)}, f32[2,1,16,2048]{3,2,1,0:T(8,128)S(1)}, u32[]{:S(2)}, u32[]{:S(2)}) collective-permute-start(f32[2,1,16,2048]{3,2,1,0:T(8,128)S(1)} %get-tuple-element.184), channel_id=1, source_target_pairs={{16,0},{32,16},{48,32},{64,48},{80,64},{96,80},{112,96},{17,1},{33... | collective-permute-start | bytes 786440 | tf_op jit(solution)/shard_map/ppermute | solution.py:229
  129.5 1.9 collective-permute-start.15
  131.5 1.9 collective-permute-start.16
  133.4 4.1 %collective-permute-start.17 = (f32[2,8,1,2048]{3,1,2,0:T(8,128)S(1)}, f32[2,8,1,2048]{3,1,2,0:T(8,128)S(1)}, u32[]{:S(2)}, u32[]{:S(2)}) collective-permute-start(f32[2,8,1,2048]{3,1,2,0:T(8,128)S(1)} %copy.52), channel_id=1, source_target_pairs={{0,1},{1,2},{2,3},{3,4},{4,5},{5,6},{6,7},{7,8},{8,9},{9,10},{10,1... | collective-permute-start | bytes 393224 | tf_op jit(solution)/shard_map/ppermute | solution.py:228
  138.5 1.9 collective-permute-start.1
  140.8 2.2 fusion.58
  143.2 1.1 copy-done
  144.6 1.9 collective-permute-start.20
  146.5 6.5 %collective-permute-start.21 = (f32[8,1,2048]{2,1,0:T(1,128)S(1)}, f32[8,1,2048]{2,1,0:T(1,128)S(1)}, u32[]{:S(2)}, u32[]{:S(2)}) collective-permute-start(f32[8,1,2048]{2,1,0:T(1,128)S(1)} %get-tuple-element.211), channel_id=1, source_target_pairs={{0,1},{1,2},{2,3},{3,4},{4,5},{5,6},{6,7},{7,8},{8,9},{9,10},{10,1... | collective-permute-start | bytes 196616 | tf_op jit(solution)/shard_map/ppermute | solution.py:228
  153.6 2.9 %collective-permute-start.18 = (f32[1,16,2048]{2,1,0:T(8,128)S(1)}, f32[1,16,2048]{2,1,0:T(8,128)S(1)}, u32[]{:S(2)}, u32[]{:S(2)}) collective-permute-start(f32[1,16,2048]{2,1,0:T(8,128)S(1)} %get-tuple-element.176), channel_id=1, source_target_pairs={{16,0},{32,16},{48,32},{64,48},{80,64},{96,80},{112,96},{17,1},{33... | collective-permute-start | bytes 393224 | tf_op jit(solution)/shard_map/ppermute | solution.py:229
  156.6 2.1 collective-permute-start.19
  159.0 3.8 %collective-permute-done.19 = f32[1,16,2048]{2,1,0:T(8,128)S(1)} collective-permute-done((f32[1,16,2048]{2,1,0:T(8,128)S(1)}, f32[1,16,2048]{2,1,0:T(8,128)S(1)}, u32[]{:S(2)}, u32[]{:S(2)}) %collective-permute-start.19) | collective-permute-done | bytes 131104 | tf_op jit(solution)/shard_map/ppermute | solution.py:228
  163.2 30.7 %while.25 = (s32[]{:T(128)}, f32[8,3,512]{2,1,0:T(4,128)}, s32[8,512]{1,0:T(8,128)S(1)}, f32[3,128,2048]{2,1,0:T(8,128)S(1)}, s32[]{:T(128)}) while((s32[]{:T(128)}, f32[8,3,512]{2,1,0:T(4,128)}, s32[8,512]{1,0:T(8,128)S(1)}, f32[3,128,2048]{2,1,0:T(8,128)S(1)}, s32[]{:T(128)}) %tuple.104), condition=%wide.region_6.7_spmd, body=%wide.region_4.6_spmd.sunk | while | flops 4833419264 | bytes 3705409 | solution.py:117
  163.3 3.2 %fusion.110 = f32[3,512]{1,0:T(4,128)S(1)} fusion(f32[3,128,2048]{2,1,0:T(8,128)S(1)} %get-tuple-element.330, s32[512]{0:T(512)S(1)} %get-tuple-element.285, f32[128,512]{1,0:T(8,128)S(1)} %fusion.109), kind=kOutput, calls=%fused_computation.6.clone.1 | convolution fusion | flops 4833278464 | bytes 3416064 | tf_op jit(solution)/shard_map/while/body/eval_jaxpr/srx,mx->srm/dot_general | solution.py:114
  167.1 3.2 %fusion.110 = f32[3,512]{1,0:T(4,128)S(1)} fusion(f32[3,128,2048]{2,1,0:T(8,128)S(1)} %get-tuple-element.330, s32[512]{0:T(512)S(1)} %get-tuple-element.285, f32[128,512]{1,0:T(8,128)S(1)} %fusion.109), kind=kOutput, calls=%fused_computation.6.clone.1 | convolution fusion | flops 4833278464 | bytes 3416064 | tf_op jit(solution)/shard_map/while/body/eval_jaxpr/srx,mx->srm/dot_general | solution.py:114
  170.9 3.2 %fusion.110 = f32[3,512]{1,0:T(4,128)S(1)} fusion(f32[3,128,2048]{2,1,0:T(8,128)S(1)} %get-tuple-element.330, s32[512]{0:T(512)S(1)} %get-tuple-element.285, f32[128,512]{1,0:T(8,128)S(1)} %fusion.109), kind=kOutput, calls=%fused_computation.6.clone.1 | convolution fusion | flops 4833278464 | bytes 3416064 | tf_op jit(solution)/shard_map/while/body/eval_jaxpr/srx,mx->srm/dot_general | solution.py:114
  174.8 3.2 %fusion.110 = f32[3,512]{1,0:T(4,128)S(1)} fusion(f32[3,128,2048]{2,1,0:T(8,128)S(1)} %get-tuple-element.330, s32[512]{0:T(512)S(1)} %get-tuple-element.285, f32[128,512]{1,0:T(8,128)S(1)} %fusion.109), kind=kOutput, calls=%fused_computation.6.clone.1 | convolution fusion | flops 4833278464 | bytes 3416064 | tf_op jit(solution)/shard_map/while/body/eval_jaxpr/srx,mx->srm/dot_general | solution.py:114
  178.6 3.2 %fusion.110 = f32[3,512]{1,0:T(4,128)S(1)} fusion(f32[3,128,2048]{2,1,0:T(8,128)S(1)} %get-tuple-element.330, s32[512]{0:T(512)S(1)} %get-tuple-element.285, f32[128,512]{1,0:T(8,128)S(1)} %fusion.109), kind=kOutput, calls=%fused_computation.6.clone.1 | convolution fusion | flops 4833278464 | bytes 3416064 | tf_op jit(solution)/shard_map/while/body/eval_jaxpr/srx,mx->srm/dot_general | solution.py:114
  182.4 3.2 %fusion.110 = f32[3,512]{1,0:T(4,128)S(1)} fusion(f32[3,128,2048]{2,1,0:T(8,128)S(1)} %get-tuple-element.330, s32[512]{0:T(512)S(1)} %get-tuple-element.285, f32[128,512]{1,0:T(8,128)S(1)} %fusion.109), kind=kOutput, calls=%fused_computation.6.clone.1 | convolution fusion | flops 4833278464 | bytes 3416064 | tf_op jit(solution)/shard_map/while/body/eval_jaxpr/srx,mx->srm/dot_general | solution.py:114
  186.3 3.2 %fusion.110 = f32[3,512]{1,0:T(4,128)S(1)} fusion(f32[3,128,2048]{2,1,0:T(8,128)S(1)} %get-tuple-element.330, s32[512]{0:T(512)S(1)} %get-tuple-element.285, f32[128,512]{1,0:T(8,128)S(1)} %fusion.109), kind=kOutput, calls=%fused_computation.6.clone.1 | convolution fusion | flops 4833278464 | bytes 3416064 | tf_op jit(solution)/shard_map/while/body/eval_jaxpr/srx,mx->srm/dot_general | solution.py:114
  190.1 3.2 %fusion.110 = f32[3,512]{1,0:T(4,128)S(1)} fusion(f32[3,128,2048]{2,1,0:T(8,128)S(1)} %get-tuple-element.330, s32[512]{0:T(512)S(1)} %get-tuple-element.285, f32[128,512]{1,0:T(8,128)S(1)} %fusion.109), kind=kOutput, calls=%fused_computation.6.clone.1 | convolution fusion | flops 4833278464 | bytes 3416064 | tf_op jit(solution)/shard_map/while/body/eval_jaxpr/srx,mx->srm/dot_general | solution.py:114
  193.9 11.7 %all-to-all-start.1 = ((f32[3,16,256]{2,0,1:T(4,128)}), f32[3,16,256]{2,0,1:T(4,128)S(1)}, u32[]{:S(2)}, u32[]{:S(2)}) async-start(f32[3,16,256]{2,0,1:T(4,128)} %bitcast.30), calls=%async_computation.1 | async-start | bytes 131072 | tf_op jit(solution)/shard_map/all_to_all | solution.py:325
  205.7 3.8 %broadcast_in_dim.239.cols_ref = f32[24,4,128,128]{3,2,1,0:T(8,128)} broadcast(f32[24,4,128]{2,1,0:T(4,128)S(1)} %maximum_bitcast_fusion.rows_ref), dimensions={0,1,2} | broadcast | bytes 6340608 | tf_op jit(solution)/shard_map/broadcast_in_dim | solution.py:180
  209.5 11.9 %shard_map.167 = f32[16,3,128]{2,1,0:T(4,128)} custom-call(s32[128]{0:T(128)} %reshape.506.chosen_ref, f32[24,4,128]{2,1,0:T(4,128)} %copy-done.1, f32[24,4,128,128]{3,2,1,0:T(8,128)} %broadcast_in_dim.239.cols_ref), custom_call_target="tpu_custom_call" | custom-call | flops 54525952 | bytes 6291456 | tf_op jit(solution)/shard_map/pallas_call | solution.py:182
  (251 shorter events, 31.1 us)
Async XLA Ops:
  4.4 2.2 copy-start.10
  4.4 2.2 copy-start.12
  4.4 2.2 copy-start.8
  9.0 0.9 copy-start.7
  9.3 10.4 %copy-start.6 = (f32[2048]{0:T(1024)S(1)}, f32[2048]{0:T(1024)}, u32[]{:S(2)}) copy-start(f32[2048]{0:T(1024)} %param.21) | copy-start | bytes 24580
  9.3 10.4 %copy-start.2 = (f32[3,2048]{1,0:T(4,128)S(1)}, f32[3,2048]{1,0:T(4,128)}, u32[]{:S(2)}) copy-start(f32[3,2048]{1,0:T(4,128)} %param.20) | copy-start | bytes 73732
  9.6 13.5 %copy-start.14 = (s32[16,8]{0,1:T(8,128)S(1)}, s32[16,8]{0,1:T(8,128)}, u32[]{:S(2)}) copy-start(s32[16,8]{0,1:T(8,128)} %param.26) | copy-start | bytes 1540
  9.6 15.8 %slice-start = ((f32[2,8,16,2048]{3,2,1,0:T(8,128)}), f32[1,8,16,2048]{3,2,1,0:T(8,128)S(1)}, s32[]{:S(2)}) async-start(f32[2,8,16,2048]{3,2,1,0:T(8,128)} %param.27), calls=%async_computation.2 | async-start | bytes 2097152 | tf_op jit(solution)/shard_map/slice | solution.py:309
  10.7 14.6 %all-to-all-start = ((f32[2,16,256]{2,0,1:T(2,128)}), f32[2,16,256]{2,0,1:T(2,128)S(1)}, u32[]{:S(2)}, u32[]{:S(2)}) async-start(f32[2,16,256]{2,0,1:T(2,128)} %fusion.72), calls=%async_computation | async-start | bytes 65536 | tf_op jit(solution)/shard_map/all_to_all | solution.py:304
  19.7 185.9 %collective-permute-start = (f32[4,512]{1,0:T(4,128)S(1)}, f32[4,512]{1,0:T(4,128)S(1)}, u32[]{:S(2)}, u32[]{:S(2)}) collective-permute-start(f32[4,512]{1,0:T(4,128)S(1)} %get-tuple-element.215), channel_id=1, source_target_pairs={{0,1},{1,2},{2,3},{3,4},{4,5},{5,6},{6,7},{7,8},{8,9},{9,10},{10,1... | collective-permute-start | bytes 24584 | tf_op jit(solution)/shard_map/ppermute | solution.py:33
  73.2 14.9 %collective-permute-start.2 = (f32[2,1,16,2048]{3,2,1,0:T(8,128)S(1)}, f32[2,1,16,2048]{3,2,1,0:T(8,128)S(1)}, u32[]{:S(2)}, u32[]{:S(2)}) collective-permute-start(f32[2,1,16,2048]{3,2,1,0:T(8,128)S(1)} %get-tuple-element.208), channel_id=1, source_target_pairs={{16,0},{32,16},{48,32},{64,48},{80,64},{96,80},{112,96},{17,1},{33... | collective-permute-start | bytes 786440 | tf_op jit(solution)/shard_map/ppermute | solution.py:229
  75.1 12.9 %collective-permute-start.3 = (f32[2,1,16,2048]{3,2,1,0:T(8,128)S(1)}, f32[2,1,16,2048]{3,2,1,0:T(8,128)S(1)}, u32[]{:S(2)}, u32[]{:S(2)}) collective-permute-start(f32[2,1,16,2048]{3,2,1,0:T(8,128)S(1)} %get-tuple-element.207), channel_id=1, source_target_pairs={{0,16},{16,32},{32,48},{48,64},{64,80},{80,96},{96,112},{1,17},{17... | collective-permute-start | bytes 786440 | tf_op jit(solution)/shard_map/ppermute | solution.py:228
  77.6 6.9 %collective-permute-start.4 = (f32[2,8,1,2048]{3,1,2,0:T(8,128)S(1)}, f32[2,8,1,2048]{3,1,2,0:T(8,128)S(1)}, u32[]{:S(2)}, u32[]{:S(2)}) collective-permute-start(f32[2,8,1,2048]{3,1,2,0:T(8,128)S(1)} %copy.38), channel_id=1, source_target_pairs={{1,0},{2,1},{3,2},{4,3},{5,4},{6,5},{7,6},{8,7},{9,8},{10,9},{11,1... | collective-permute-start | bytes 393224 | tf_op jit(solution)/shard_map/ppermute | solution.py:229
  81.0 7.0 %copy-start.4 = (f32[2]{0:T(128)S(1)}, f32[2]{0:T(128)}, u32[]{:S(2)}) copy-start(f32[2]{0:T(128)} %constant.184.clone) | copy-start | bytes 28
  81.0 7.0 %copy-start.5 = (f32[2]{0:T(128)S(1)}, f32[2]{0:T(128)}, u32[]{:S(2)}) copy-start(f32[2]{0:T(128)} %constant.185.clone) | copy-start | bytes 28
  81.1 6.9 %collective-permute-start.5 = (f32[2,8,1,2048]{3,1,2,0:T(8,128)S(1)}, f32[2,8,1,2048]{3,1,2,0:T(8,128)S(1)}, u32[]{:S(2)}, u32[]{:S(2)}) collective-permute-start(f32[2,8,1,2048]{3,1,2,0:T(8,128)S(1)} %copy.40), channel_id=1, source_target_pairs={{0,1},{1,2},{2,3},{3,4},{4,5},{5,6},{6,7},{7,8},{8,9},{9,10},{10,1... | collective-permute-start | bytes 393224 | tf_op jit(solution)/shard_map/ppermute | solution.py:228
  91.0 14.0 %collective-permute-start.6 = (f32[2,1,16,2048]{3,2,1,0:T(8,128)S(1)}, f32[2,1,16,2048]{3,2,1,0:T(8,128)S(1)}, u32[]{:S(2)}, u32[]{:S(2)}) collective-permute-start(f32[2,1,16,2048]{3,2,1,0:T(8,128)S(1)} %get-tuple-element.200), channel_id=1, source_target_pairs={{16,0},{32,16},{48,32},{64,48},{80,64},{96,80},{112,96},{17,1},{33... | collective-permute-start | bytes 786440 | tf_op jit(solution)/shard_map/ppermute | solution.py:229
  94.1 11.0 %collective-permute-start.7 = (f32[2,1,16,2048]{3,2,1,0:T(8,128)S(1)}, f32[2,1,16,2048]{3,2,1,0:T(8,128)S(1)}, u32[]{:S(2)}, u32[]{:S(2)}) collective-permute-start(f32[2,1,16,2048]{3,2,1,0:T(8,128)S(1)} %get-tuple-element.199), channel_id=1, source_target_pairs={{0,16},{16,32},{32,48},{48,64},{64,80},{80,96},{96,112},{1,17},{17... | collective-permute-start | bytes 786440 | tf_op jit(solution)/shard_map/ppermute | solution.py:228
  96.0 6.9 %collective-permute-start.8 = (f32[2,8,1,2048]{3,1,2,0:T(8,128)S(1)}, f32[2,8,1,2048]{3,1,2,0:T(8,128)S(1)}, u32[]{:S(2)}, u32[]{:S(2)}) collective-permute-start(f32[2,8,1,2048]{3,1,2,0:T(8,128)S(1)} %copy.42), channel_id=1, source_target_pairs={{1,0},{2,1},{3,2},{4,3},{5,4},{6,5},{7,6},{8,7},{9,8},{10,9},{11,1... | collective-permute-start | bytes 393224 | tf_op jit(solution)/shard_map/ppermute | solution.py:229
  98.0 6.9 %collective-permute-start.9 = (f32[2,8,1,2048]{3,1,2,0:T(8,128)S(1)}, f32[2,8,1,2048]{3,1,2,0:T(8,128)S(1)}, u32[]{:S(2)}, u32[]{:S(2)}) collective-permute-start(f32[2,8,1,2048]{3,1,2,0:T(8,128)S(1)} %copy.44), channel_id=1, source_target_pairs={{0,1},{1,2},{2,3},{3,4},{4,5},{5,6},{6,7},{7,8},{8,9},{9,10},{10,1... | collective-permute-start | bytes 393224 | tf_op jit(solution)/shard_map/ppermute | solution.py:228
  107.9 15.1 %collective-permute-start.10 = (f32[2,1,16,2048]{3,2,1,0:T(8,128)S(1)}, f32[2,1,16,2048]{3,2,1,0:T(8,128)S(1)}, u32[]{:S(2)}, u32[]{:S(2)}) collective-permute-start(f32[2,1,16,2048]{3,2,1,0:T(8,128)S(1)} %get-tuple-element.192), channel_id=1, source_target_pairs={{16,0},{32,16},{48,32},{64,48},{80,64},{96,80},{112,96},{17,1},{33... | collective-permute-start | bytes 786440 | tf_op jit(solution)/shard_map/ppermute | solution.py:229
  112.1 11.0 %collective-permute-start.11 = (f32[2,1,16,2048]{3,2,1,0:T(8,128)S(1)}, f32[2,1,16,2048]{3,2,1,0:T(8,128)S(1)}, u32[]{:S(2)}, u32[]{:S(2)}) collective-permute-start(f32[2,1,16,2048]{3,2,1,0:T(8,128)S(1)} %get-tuple-element.191), channel_id=1, source_target_pairs={{0,16},{16,32},{32,48},{48,64},{64,80},{80,96},{96,112},{1,17},{17... | collective-permute-start | bytes 786440 | tf_op jit(solution)/shard_map/ppermute | solution.py:228
  114.1 6.9 %collective-permute-start.12 = (f32[2,8,1,2048]{3,1,2,0:T(8,128)S(1)}, f32[2,8,1,2048]{3,1,2,0:T(8,128)S(1)}, u32[]{:S(2)}, u32[]{:S(2)}) collective-permute-start(f32[2,8,1,2048]{3,1,2,0:T(8,128)S(1)} %copy.46), channel_id=1, source_target_pairs={{1,0},{2,1},{3,2},{4,3},{5,4},{6,5},{7,6},{8,7},{9,8},{10,9},{11,1... | collective-permute-start | bytes 393224 | tf_op jit(solution)/shard_map/ppermute | solution.py:229
  116.0 6.9 %collective-permute-start.13 = (f32[2,8,1,2048]{3,1,2,0:T(8,128)S(1)}, f32[2,8,1,2048]{3,1,2,0:T(8,128)S(1)}, u32[]{:S(2)}, u32[]{:S(2)}) collective-permute-start(f32[2,8,1,2048]{3,1,2,0:T(8,128)S(1)} %copy.48), channel_id=1, source_target_pairs={{0,1},{1,2},{2,3},{3,4},{4,5},{5,6},{6,7},{7,8},{8,9},{9,10},{10,1... | collective-permute-start | bytes 393224 | tf_op jit(solution)/shard_map/ppermute | solution.py:228
  126.0 14.8 %collective-permute-start.14 = (f32[2,1,16,2048]{3,2,1,0:T(8,128)S(1)}, f32[2,1,16,2048]{3,2,1,0:T(8,128)S(1)}, u32[]{:S(2)}, u32[]{:S(2)}) collective-permute-start(f32[2,1,16,2048]{3,2,1,0:T(8,128)S(1)} %get-tuple-element.184), channel_id=1, source_target_pairs={{16,0},{32,16},{48,32},{64,48},{80,64},{96,80},{112,96},{17,1},{33... | collective-permute-start | bytes 786440 | tf_op jit(solution)/shard_map/ppermute | solution.py:229
  129.5 11.3 %collective-permute-start.15 = (f32[2,1,16,2048]{3,2,1,0:T(8,128)S(1)}, f32[2,1,16,2048]{3,2,1,0:T(8,128)S(1)}, u32[]{:S(2)}, u32[]{:S(2)}) collective-permute-start(f32[2,1,16,2048]{3,2,1,0:T(8,128)S(1)} %get-tuple-element.183), channel_id=1, source_target_pairs={{0,16},{16,32},{32,48},{48,64},{64,80},{80,96},{96,112},{1,17},{17... | collective-permute-start | bytes 786440 | tf_op jit(solution)/shard_map/ppermute | solution.py:228
  131.5 7.1 %collective-permute-start.16 = (f32[2,8,1,2048]{3,1,2,0:T(8,128)S(1)}, f32[2,8,1,2048]{3,1,2,0:T(8,128)S(1)}, u32[]{:S(2)}, u32[]{:S(2)}) collective-permute-start(f32[2,8,1,2048]{3,1,2,0:T(8,128)S(1)} %copy.50), channel_id=1, source_target_pairs={{1,0},{2,1},{3,2},{4,3},{5,4},{6,5},{7,6},{8,7},{9,8},{10,9},{11,1... | collective-permute-start | bytes 393224 | tf_op jit(solution)/shard_map/ppermute | solution.py:229
  133.4 7.1 %collective-permute-start.17 = (f32[2,8,1,2048]{3,1,2,0:T(8,128)S(1)}, f32[2,8,1,2048]{3,1,2,0:T(8,128)S(1)}, u32[]{:S(2)}, u32[]{:S(2)}) collective-permute-start(f32[2,8,1,2048]{3,1,2,0:T(8,128)S(1)} %copy.52), channel_id=1, source_target_pairs={{0,1},{1,2},{2,3},{3,4},{4,5},{5,6},{6,7},{7,8},{8,9},{9,10},{10,1... | collective-permute-start | bytes 393224 | tf_op jit(solution)/shard_map/ppermute | solution.py:228
  138.5 67.1 %collective-permute-start.1 = (f32[4,512]{1,0:T(4,128)S(1)}, f32[4,512]{1,0:T(4,128)S(1)}, u32[]{:S(2)}, u32[]{:S(2)}) collective-permute-start(f32[4,512]{1,0:T(4,128)S(1)} %get-tuple-element.216), channel_id=1, source_target_pairs={{1,0},{2,1},{3,2},{4,3},{5,4},{6,5},{7,6},{8,7},{9,8},{10,9},{11,1... | collective-permute-start | bytes 24584 | tf_op jit(solution)/shard_map/ppermute | solution.py:36
  142.9 1.3 copy-start
  144.6 11.9 %collective-permute-start.20 = (f32[8,1,2048]{2,1,0:T(1,128)S(1)}, f32[8,1,2048]{2,1,0:T(1,128)S(1)}, u32[]{:S(2)}, u32[]{:S(2)}) collective-permute-start(f32[8,1,2048]{2,1,0:T(1,128)S(1)} %get-tuple-element.212), channel_id=1, source_target_pairs={{1,0},{2,1},{3,2},{4,3},{5,4},{6,5},{7,6},{8,7},{9,8},{10,9},{11,1... | collective-permute-start | bytes 196616 | tf_op jit(solution)/shard_map/ppermute | solution.py:229
  146.5 12.2 %collective-permute-start.21 = (f32[8,1,2048]{2,1,0:T(1,128)S(1)}, f32[8,1,2048]{2,1,0:T(1,128)S(1)}, u32[]{:S(2)}, u32[]{:S(2)}) collective-permute-start(f32[8,1,2048]{2,1,0:T(1,128)S(1)} %get-tuple-element.211), channel_id=1, source_target_pairs={{0,1},{1,2},{2,3},{3,4},{4,5},{5,6},{6,7},{7,8},{8,9},{9,10},{10,1... | collective-permute-start | bytes 196616 | tf_op jit(solution)/shard_map/ppermute | solution.py:228
  153.6 5.4 %collective-permute-start.18 = (f32[1,16,2048]{2,1,0:T(8,128)S(1)}, f32[1,16,2048]{2,1,0:T(8,128)S(1)}, u32[]{:S(2)}, u32[]{:S(2)}) collective-permute-start(f32[1,16,2048]{2,1,0:T(8,128)S(1)} %get-tuple-element.176), channel_id=1, source_target_pairs={{16,0},{32,16},{48,32},{64,48},{80,64},{96,80},{112,96},{17,1},{33... | collective-permute-start | bytes 393224 | tf_op jit(solution)/shard_map/ppermute | solution.py:229
  156.6 6.3 %collective-permute-start.19 = (f32[1,16,2048]{2,1,0:T(8,128)S(1)}, f32[1,16,2048]{2,1,0:T(8,128)S(1)}, u32[]{:S(2)}, u32[]{:S(2)}) collective-permute-start(f32[1,16,2048]{2,1,0:T(8,128)S(1)} %get-tuple-element.175), channel_id=1, source_target_pairs={{0,16},{16,32},{32,48},{48,64},{64,80},{80,96},{96,112},{1,17},{17... | collective-permute-start | bytes 393224 | tf_op jit(solution)/shard_map/ppermute | solution.py:228
  193.9 27.5 %all-to-all-start.1 = ((f32[3,16,256]{2,0,1:T(4,128)}), f32[3,16,256]{2,0,1:T(4,128)S(1)}, u32[]{:S(2)}, u32[]{:S(2)}) async-start(f32[3,16,256]{2,0,1:T(4,128)} %bitcast.30), calls=%async_computation.1 | async-start | bytes 131072 | tf_op jit(solution)/shard_map/all_to_all | solution.py:325
  205.7 3.8 %copy-start.1 = (f32[24,4,128]{2,1,0:T(4,128)}, f32[24,4,128]{2,1,0:T(4,128)S(1)}, u32[]{:S(2)}) copy-start(f32[24,4,128]{2,1,0:T(4,128)S(1)} %maximum_bitcast_fusion.rows_ref) | copy-start | bytes 147460
  221.4 0.7 copy-start.13
  221.4 1.1 copy-start.11
  221.9 1.1 copy-start.9
  226.1 0.8 copy-start.3

commit v7 on v5

--- a/solution.py
+++ b/solution.py
@@ -235,7 +235,7 @@
     rows = starts.shape[0]
     padded = jnp.pad(values, ((0, 0), (0, length)))
     held = jnp.broadcast_to(padded[:, None, :], (channels, rows, width))
-    for bit in range(bits_of(width)):
+    for bit in range(bits_of(cells)):
         step = 1 << bit
         take = ((starts >> bit) & 1 == 1)[None, :, None]
         held = jnp.where(take, jnp.roll(held, -step, axis=2), held)
@@ -246,7 +246,7 @@
     channels, rows, length = windows.shape
     width = cells + length
     held = jnp.pad(windows, ((0, 0), (0, 0), (0, width - length)))
-    for bit in range(bits_of(width)):
+    for bit in range(bits_of(cells)):
         step = 1 << bit
         take = ((starts >> bit) & 1 == 1)[None, :, None]
         held = jnp.where(take, jnp.roll(held, step, axis=2), held)

time: 225 us -> 224 us (level)
  transfers between devices with their start and end apart: 24 -> 24, of which waited for: 9 -> 8; matrix products, arithmetic and copies ran while one was open for 42% -> 42% of each run, Pallas kernels for 5% -> 5%
where the time goes in v7:
time: 224 us; the launch traced here: 223 us
  starting transfers between devices  84.9 us (38%)
  matrix products  63.3 us (28%)
  other arithmetic  25.3 us (11%)
  local copies, waits for them, and re-layouts  21.9 us (10%)
  waiting for transfers between devices  12.7 us (6%)
  Pallas kernels  11.9 us (5%)
  between operations  2.41 us (1%)
    ppermute x10, starting transfers between devices, neighbours(): lax.ppermute(lax.slice_in_dim(block, block.shape[dim] - 1, None, axis=dim...  32.1 us
    ppermute x10, starting transfers between devices, neighbours(): high = lax.ppermute(lax.slice_in_dim(block, 0, 1, axis=dim), axis, backward)  26.6 us
    dot_general x8, matrix products, one_piece(): jnp.einsum('srx,mx->srm', fields, column_hot, precision=lax.Precision.HIG...  25.4 us
    dot_general x8, matrix products, add_piece(): jnp.einsum('smr,mx->srx', weighted, column_hot, precision=lax.Precision.H...  24.1 us
    dot_general x4, matrix products, one_piece(): jnp.einsum('psrx,mx->psrm', parts, column_hot, preferred_element_type=jnp...  13.8 us
    all_to_all x1, starting transfers between devices, local(): lax.all_to_all(slopes, 'tile', split_axis=1, concat_axis=1, tiled=True)  12.5 us
    pallas_call x1, Pallas kernels, pair_forces(): pl.pallas_call(force_kernel, out_shape=jax.ShapeDtypeStruct((blocks, 3, l...  11.9 us
    ppermute x10, waiting for transfers between devices, neighbours(): lax.ppermute(lax.slice_in_dim(block, block.shape[dim] - 1, None, axis=dim...  10.6 us
  transfers between devices with their start and end apart: 24, of which 8 were waited for; matrix products, arithmetic and copies ran while one was open for 42% of the time, Pallas kernels for 5%

profile of v7, /device:TPU:26, one launch (start us, length us, event | category | flops | bytes accessed | tf_op | source)
XLA Modules:
  0.0 223.1 jit_solution(7284028354411181093)
XLA Ops:
  1.3 0.7 pad_maximum_fusion.4
  2.0 0.8 fusion.84
  2.8 0.7 copy.71
  9.7 0.7 fusion.80
  10.4 8.3 %all-to-all-start = ((f32[2,16,256]{2,0,1:T(2,128)}), f32[2,16,256]{2,0,1:T(2,128)S(1)}, u32[]{:S(2)}, u32[]{:S(2)}) async-start(f32[2,16,256]{2,0,1:T(2,128)} %fusion.80), calls=%async_computation | async-start | bytes 65536 | tf_op jit(solution)/shard_map/all_to_all | solution.py:278
  19.4 3.4 %collective-permute-start = (f32[4,512]{1,0:T(4,128)S(1)}, f32[4,512]{1,0:T(4,128)S(1)}, u32[]{:S(2)}, u32[]{:S(2)}) collective-permute-start(f32[4,512]{1,0:T(4,128)S(1)} %get-tuple-element.269), channel_id=1, source_target_pairs={{0,1},{1,2},{2,3},{3,4},{4,5},{5,6},{6,7},{7,8},{8,9},{9,10},{10,1... | collective-permute-start | bytes 24584 | tf_op jit(solution)/shard_map/ppermute | solution.py:33
  23.1 1.3 pad_maximum_fusion.1
  25.2 14.7 %while.37 = (s32[]{:T(128)}, f32[4,1,1024]{2,1,0:T(1,128)S(1)}, s32[4,1024]{1,0:T(4,128)S(1)}, bf16[3,1,128,2048]{3,2,0,1:T(8,128)(2,1)}, s32[]{:T(128)}) while((s32[]{:T(128)}, f32[4,1,1024]{2,1,0:T(1,128)S(1)}, s32[4,1024]{1,0:T(4,128)S(1)}, bf16[3,1,128,2048]{3,2,0,1:T(8,128)(2,1)}, s32[]{:T(128)}) %tuple.121), condition=%wide.region_3.4_spmd, body=%wide.region_1.3_spmd.sunk | while | flops 1613645824 | bytes 4759621 | solution.py:104
  25.2 3.5 %fusion.118 = f32[3,128,1024]{2,1,0:T(8,128)S(1)} fusion(bf16[3,1,128,2048]{3,2,0,1:T(8,128)(2,1)} %get-tuple-element.383, s32[1024]{0:T(1024)S(1)} %get-tuple-element.356), kind=kOutput, calls=%fused_computation.5.clone.1 | convolution fusion | flops 1612709888 | bytes 3149824 | tf_op jit(solution)/shard_map/while/body/eval_jaxpr/psrx,mx->psrm/dot_general | solution.py:98
  28.9 3.5 %fusion.118 = f32[3,128,1024]{2,1,0:T(8,128)S(1)} fusion(bf16[3,1,128,2048]{3,2,0,1:T(8,128)(2,1)} %get-tuple-element.383, s32[1024]{0:T(1024)S(1)} %get-tuple-element.356), kind=kOutput, calls=%fused_computation.5.clone.1 | convolution fusion | flops 1612709888 | bytes 3149824 | tf_op jit(solution)/shard_map/while/body/eval_jaxpr/psrx,mx->psrm/dot_general | solution.py:98
  32.6 3.5 %fusion.118 = f32[3,128,1024]{2,1,0:T(8,128)S(1)} fusion(bf16[3,1,128,2048]{3,2,0,1:T(8,128)(2,1)} %get-tuple-element.383, s32[1024]{0:T(1024)S(1)} %get-tuple-element.356), kind=kOutput, calls=%fused_computation.5.clone.1 | convolution fusion | flops 1612709888 | bytes 3149824 | tf_op jit(solution)/shard_map/while/body/eval_jaxpr/psrx,mx->psrm/dot_general | solution.py:98
  36.3 3.5 %fusion.118 = f32[3,128,1024]{2,1,0:T(8,128)S(1)} fusion(bf16[3,1,128,2048]{3,2,0,1:T(8,128)(2,1)} %get-tuple-element.383, s32[1024]{0:T(1024)S(1)} %get-tuple-element.356), kind=kOutput, calls=%fused_computation.5.clone.1 | convolution fusion | flops 1612709888 | bytes 3149824 | tf_op jit(solution)/shard_map/while/body/eval_jaxpr/psrx,mx->psrm/dot_general | solution.py:98
  40.1 25.0 %while.39 = (s32[]{:T(128)}, f32[2,128,2048]{2,1,0:T(8,128)S(1)}, f32[8,2,512]{2,0,1:T(8,128)S(1)}, s32[8,512]{1,0:T(8,128)S(1)}, s32[]{:T(128)}, /*index=5*/s32[]{:T(128)}) while((s32[]{:T(128)}, f32[2,128,2048]{2,1,0:T(8,128)S(1)}, f32[8,2,512]{2,0,1:T(8,128)S(1)}, s32[8,512]{1,0:T(8,128)S(1)}, s32[]{:T(128)}, ...), condition=%wide.region_5.6_spmd.clone, body=%wide.region_4.5_spmd.clone.sunk | while | flops 3223594496 | bytes 4753495 | solution.py:137
  40.2 3.0 %fusion.127 = f32[2,128,2048]{2,1,0:T(8,128)S(1)} fusion(f32[2,128,2048]{2,1,0:T(8,128)S(1)} %get-tuple-element.392, s32[512]{0:T(512)S(1)} %get-tuple-element.368, pred[]{:T(512)S(6)} %compare.53, f32[512,128]{0,1:T(8,128)S(1)} %fusion.126, f32[2,512]{1,0:T(2,128)S(1)} %bitcast.141), kind=kOutput, calls=%fused_computation.44.clone.1 | convolution fusion | flops 3223453696 | bytes 4462593 | tf_op jit(solution)/shard_map/while/body/eval_jaxpr/smr,mx->srx/dot_general | solution.py:132
  43.3 3.0 %fusion.127 = f32[2,128,2048]{2,1,0:T(8,128)S(1)} fusion(f32[2,128,2048]{2,1,0:T(8,128)S(1)} %get-tuple-element.392, s32[512]{0:T(512)S(1)} %get-tuple-element.368, pred[]{:T(512)S(6)} %compare.53, f32[512,128]{0,1:T(8,128)S(1)} %fusion.126, f32[2,512]{1,0:T(2,128)S(1)} %bitcast.141), kind=kOutput, calls=%fused_computation.44.clone.1 | convolution fusion | flops 3223453696 | bytes 4462593 | tf_op jit(solution)/shard_map/while/body/eval_jaxpr/smr,mx->srx/dot_general | solution.py:132
  46.5 3.0 %fusion.127 = f32[2,128,2048]{2,1,0:T(8,128)S(1)} fusion(f32[2,128,2048]{2,1,0:T(8,128)S(1)} %get-tuple-element.392, s32[512]{0:T(512)S(1)} %get-tuple-element.368, pred[]{:T(512)S(6)} %compare.53, f32[512,128]{0,1:T(8,128)S(1)} %fusion.126, f32[2,512]{1,0:T(2,128)S(1)} %bitcast.141), kind=kOutput, calls=%fused_computation.44.clone.1 | convolution fusion | flops 3223453696 | bytes 4462593 | tf_op jit(solution)/shard_map/while/body/eval_jaxpr/smr,mx->srx/dot_general | solution.py:132
  49.6 3.0 %fusion.127 = f32[2,128,2048]{2,1,0:T(8,128)S(1)} fusion(f32[2,128,2048]{2,1,0:T(8,128)S(1)} %get-tuple-element.392, s32[512]{0:T(512)S(1)} %get-tuple-element.368, pred[]{:T(512)S(6)} %compare.53, f32[512,128]{0,1:T(8,128)S(1)} %fusion.126, f32[2,512]{1,0:T(2,128)S(1)} %bitcast.141), kind=kOutput, calls=%fused_computation.44.clone.1 | convolution fusion | flops 3223453696 | bytes 4462593 | tf_op jit(solution)/shard_map/while/body/eval_jaxpr/smr,mx->srx/dot_general | solution.py:132
  52.7 3.0 %fusion.127 = f32[2,128,2048]{2,1,0:T(8,128)S(1)} fusion(f32[2,128,2048]{2,1,0:T(8,128)S(1)} %get-tuple-element.392, s32[512]{0:T(512)S(1)} %get-tuple-element.368, pred[]{:T(512)S(6)} %compare.53, f32[512,128]{0,1:T(8,128)S(1)} %fusion.126, f32[2,512]{1,0:T(2,128)S(1)} %bitcast.141), kind=kOutput, calls=%fused_computation.44.clone.1 | convolution fusion | flops 3223453696 | bytes 4462593 | tf_op jit(solution)/shard_map/while/body/eval_jaxpr/smr,mx->srx/dot_general | solution.py:132
  55.9 3.0 %fusion.127 = f32[2,128,2048]{2,1,0:T(8,128)S(1)} fusion(f32[2,128,2048]{2,1,0:T(8,128)S(1)} %get-tuple-element.392, s32[512]{0:T(512)S(1)} %get-tuple-element.368, pred[]{:T(512)S(6)} %compare.53, f32[512,128]{0,1:T(8,128)S(1)} %fusion.126, f32[2,512]{1,0:T(2,128)S(1)} %bitcast.141), kind=kOutput, calls=%fused_computation.44.clone.1 | convolution fusion | flops 3223453696 | bytes 4462593 | tf_op jit(solution)/shard_map/while/body/eval_jaxpr/smr,mx->srx/dot_general | solution.py:132
  59.0 3.0 %fusion.127 = f32[2,128,2048]{2,1,0:T(8,128)S(1)} fusion(f32[2,128,2048]{2,1,0:T(8,128)S(1)} %get-tuple-element.392, s32[512]{0:T(512)S(1)} %get-tuple-element.368, pred[]{:T(512)S(6)} %compare.53, f32[512,128]{0,1:T(8,128)S(1)} %fusion.126, f32[2,512]{1,0:T(2,128)S(1)} %bitcast.141), kind=kOutput, calls=%fused_computation.44.clone.1 | convolution fusion | flops 3223453696 | bytes 4462593 | tf_op jit(solution)/shard_map/while/body/eval_jaxpr/smr,mx->srx/dot_general | solution.py:132
  62.1 3.0 %fusion.127 = f32[2,128,2048]{2,1,0:T(8,128)S(1)} fusion(f32[2,128,2048]{2,1,0:T(8,128)S(1)} %get-tuple-element.392, s32[512]{0:T(512)S(1)} %get-tuple-element.368, pred[]{:T(512)S(6)} %compare.53, f32[512,128]{0,1:T(8,128)S(1)} %fusion.126, f32[2,512]{1,0:T(2,128)S(1)} %bitcast.141), kind=kOutput, calls=%fused_computation.44.clone.1 | convolution fusion | flops 3223453696 | bytes 4462593 | tf_op jit(solution)/shard_map/while/body/eval_jaxpr/smr,mx->srx/dot_general | solution.py:132
  65.2 1.8 add.225
  67.7 2.1 collective-permute-start.2
  69.8 2.4 %collective-permute-start.3 = (f32[2,1,16,2048]{3,2,1,0:T(8,128)S(1)}, f32[2,1,16,2048]{3,2,1,0:T(8,128)S(1)}, u32[]{:S(2)}, u32[]{:S(2)}) collective-permute-start(f32[2,1,16,2048]{3,2,1,0:T(8,128)S(1)} %get-tuple-element.258), channel_id=1, source_target_pairs={{0,16},{16,32},{32,48},{48,64},{64,80},{80,96},{96,112},{1,17},{17... | collective-permute-start | bytes 786440 | tf_op jit(solution)/shard_map/ppermute | solution.py:202
  72.3 3.2 %collective-permute-start.4 = (f32[2,8,1,2048]{3,1,2,0:T(8,128)S(1)}, f32[2,8,1,2048]{3,1,2,0:T(8,128)S(1)}, u32[]{:S(2)}, u32[]{:S(2)}) collective-permute-start(f32[2,8,1,2048]{3,1,2,0:T(8,128)S(1)} %copy.75), channel_id=1, source_target_pairs={{1,0},{2,1},{3,2},{4,3},{5,4},{6,5},{7,6},{8,7},{9,8},{10,9},{11,1... | collective-permute-start | bytes 393224 | tf_op jit(solution)/shard_map/ppermute | solution.py:203
  75.6 2.6 %collective-permute-start.5 = (f32[2,8,1,2048]{3,1,2,0:T(8,128)S(1)}, f32[2,8,1,2048]{3,1,2,0:T(8,128)S(1)}, u32[]{:S(2)}, u32[]{:S(2)}) collective-permute-start(f32[2,8,1,2048]{3,1,2,0:T(8,128)S(1)} %copy.77), channel_id=1, source_target_pairs={{0,1},{1,2},{2,3},{3,4},{4,5},{5,6},{6,7},{7,8},{8,9},{9,10},{10,1... | collective-permute-start | bytes 393224 | tf_op jit(solution)/shard_map/ppermute | solution.py:202
  79.3 3.2 %collective-permute-done.5 = f32[2,8,1,2048]{3,1,2,0:T(8,128)S(1)} collective-permute-done((f32[2,8,1,2048]{3,1,2,0:T(8,128)S(1)}, f32[2,8,1,2048]{3,1,2,0:T(8,128)S(1)}, u32[]{:S(2)}, u32[]{:S(2)}) %collective-permute-start.5) | collective-permute-done | bytes 131104 | tf_op jit(solution)/shard_map/ppermute | solution.py:202
  82.6 2.2 fusion.47
  85.5 3.1 %collective-permute-start.6 = (f32[2,1,16,2048]{3,2,1,0:T(8,128)S(1)}, f32[2,1,16,2048]{3,2,1,0:T(8,128)S(1)}, u32[]{:S(2)}, u32[]{:S(2)}) collective-permute-start(f32[2,1,16,2048]{3,2,1,0:T(8,128)S(1)} %get-tuple-element.251), channel_id=1, source_target_pairs={{16,0},{32,16},{48,32},{64,48},{80,64},{96,80},{112,96},{17,1},{33... | collective-permute-start | bytes 786440 | tf_op jit(solution)/shard_map/ppermute | solution.py:203
  88.6 1.9 collective-permute-start.7
  90.6 1.9 collective-permute-start.8
  92.6 3.9 %collective-permute-start.9 = (f32[2,8,1,2048]{3,1,2,0:T(8,128)S(1)}, f32[2,8,1,2048]{3,1,2,0:T(8,128)S(1)}, u32[]{:S(2)}, u32[]{:S(2)}) collective-permute-start(f32[2,8,1,2048]{3,1,2,0:T(8,128)S(1)} %copy.81), channel_id=1, source_target_pairs={{0,1},{1,2},{2,3},{3,4},{4,5},{5,6},{6,7},{7,8},{8,9},{9,10},{10,1... | collective-permute-start | bytes 393224 | tf_op jit(solution)/shard_map/ppermute | solution.py:202
  97.6 1.8 collective-permute-done.9
  99.6 2.2 fusion.53
  102.5 4.1 %collective-permute-start.10 = (f32[2,1,16,2048]{3,2,1,0:T(8,128)S(1)}, f32[2,1,16,2048]{3,2,1,0:T(8,128)S(1)}, u32[]{:S(2)}, u32[]{:S(2)}) collective-permute-start(f32[2,1,16,2048]{3,2,1,0:T(8,128)S(1)} %get-tuple-element.243), channel_id=1, source_target_pairs={{16,0},{32,16},{48,32},{64,48},{80,64},{96,80},{112,96},{17,1},{33... | collective-permute-start | bytes 786440 | tf_op jit(solution)/shard_map/ppermute | solution.py:203
  106.6 1.9 collective-permute-start.11
  108.6 1.9 collective-permute-start.12
  110.6 3.9 %collective-permute-start.13 = (f32[2,8,1,2048]{3,1,2,0:T(8,128)S(1)}, f32[2,8,1,2048]{3,1,2,0:T(8,128)S(1)}, u32[]{:S(2)}, u32[]{:S(2)}) collective-permute-start(f32[2,8,1,2048]{3,1,2,0:T(8,128)S(1)} %copy.85), channel_id=1, source_target_pairs={{0,1},{1,2},{2,3},{3,4},{4,5},{5,6},{6,7},{7,8},{8,9},{9,10},{10,1... | collective-permute-start | bytes 393224 | tf_op jit(solution)/shard_map/ppermute | solution.py:202
  115.6 1.8 collective-permute-done.13
  117.6 2.2 fusion.59
  120.5 3.5 %collective-permute-start.14 = (f32[2,1,16,2048]{3,2,1,0:T(8,128)S(1)}, f32[2,1,16,2048]{3,2,1,0:T(8,128)S(1)}, u32[]{:S(2)}, u32[]{:S(2)}) collective-permute-start(f32[2,1,16,2048]{3,2,1,0:T(8,128)S(1)} %get-tuple-element.235), channel_id=1, source_target_pairs={{16,0},{32,16},{48,32},{64,48},{80,64},{96,80},{112,96},{17,1},{33... | collective-permute-start | bytes 786440 | tf_op jit(solution)/shard_map/ppermute | solution.py:203
  124.0 1.9 collective-permute-start.15
  126.0 1.9 collective-permute-start.16
  128.0 4.8 %collective-permute-start.17 = (f32[2,8,1,2048]{3,1,2,0:T(8,128)S(1)}, f32[2,8,1,2048]{3,1,2,0:T(8,128)S(1)}, u32[]{:S(2)}, u32[]{:S(2)}) collective-permute-start(f32[2,8,1,2048]{3,1,2,0:T(8,128)S(1)} %copy.89), channel_id=1, source_target_pairs={{0,1},{1,2},{2,3},{3,4},{4,5},{5,6},{6,7},{7,8},{8,9},{9,10},{10,1... | collective-permute-start | bytes 393224 | tf_op jit(solution)/shard_map/ppermute | solution.py:202
  133.8 1.9 collective-permute-start.1
  136.0 2.2 fusion.65
  138.4 1.1 copy-done
  139.9 1.9 collective-permute-start.20
  141.8 6.5 %collective-permute-start.21 = (f32[8,1,2048]{2,1,0:T(1,128)S(1)}, f32[8,1,2048]{2,1,0:T(1,128)S(1)}, u32[]{:S(2)}, u32[]{:S(2)}) collective-permute-start(f32[8,1,2048]{2,1,0:T(1,128)S(1)} %get-tuple-element.262), channel_id=1, source_target_pairs={{0,1},{1,2},{2,3},{3,4},{4,5},{5,6},{6,7},{7,8},{8,9},{9,10},{10,1... | collective-permute-start | bytes 196616 | tf_op jit(solution)/shard_map/ppermute | solution.py:202
  148.9 2.9 %collective-permute-start.18 = (f32[1,16,2048]{2,1,0:T(8,128)S(1)}, f32[1,16,2048]{2,1,0:T(8,128)S(1)}, u32[]{:S(2)}, u32[]{:S(2)}) collective-permute-start(f32[1,16,2048]{2,1,0:T(8,128)S(1)} %get-tuple-element.227), channel_id=1, source_target_pairs={{16,0},{32,16},{48,32},{64,48},{80,64},{96,80},{112,96},{17,1},{33... | collective-permute-start | bytes 393224 | tf_op jit(solution)/shard_map/ppermute | solution.py:203
  151.9 2.1 collective-permute-start.19
  154.3 3.8 %collective-permute-done.19 = f32[1,16,2048]{2,1,0:T(8,128)S(1)} collective-permute-done((f32[1,16,2048]{2,1,0:T(8,128)S(1)}, f32[1,16,2048]{2,1,0:T(8,128)S(1)}, u32[]{:S(2)}, u32[]{:S(2)}) %collective-permute-start.19) | collective-permute-done | bytes 131104 | tf_op jit(solution)/shard_map/ppermute | solution.py:202
  158.5 30.7 %while.38 = (s32[]{:T(128)}, f32[8,3,512]{2,1,0:T(4,128)}, s32[8,512]{1,0:T(8,128)S(1)}, f32[3,128,2048]{2,1,0:T(8,128)S(1)}, s32[]{:T(128)}) while((s32[]{:T(128)}, f32[8,3,512]{2,1,0:T(4,128)}, s32[8,512]{1,0:T(8,128)S(1)}, f32[3,128,2048]{2,1,0:T(8,128)S(1)}, s32[]{:T(128)}) %tuple.130), condition=%wide.region_8.9_spmd, body=%wide.region_6.8_spmd.sunk | while | flops 4833419264 | bytes 3705409 | solution.py:117
  158.6 3.2 %fusion.123 = f32[3,512]{1,0:T(4,128)S(1)} fusion(f32[3,128,2048]{2,1,0:T(8,128)S(1)} %get-tuple-element.416, s32[512]{0:T(512)S(1)} %get-tuple-element.362, f32[128,512]{1,0:T(8,128)S(1)} %fusion.122), kind=kOutput, calls=%fused_computation.28.clone.1 | convolution fusion | flops 4833278464 | bytes 3416064 | tf_op jit(solution)/shard_map/while/body/eval_jaxpr/srx,mx->srm/dot_general | solution.py:114
  162.4 3.2 %fusion.123 = f32[3,512]{1,0:T(4,128)S(1)} fusion(f32[3,128,2048]{2,1,0:T(8,128)S(1)} %get-tuple-element.416, s32[512]{0:T(512)S(1)} %get-tuple-element.362, f32[128,512]{1,0:T(8,128)S(1)} %fusion.122), kind=kOutput, calls=%fused_computation.28.clone.1 | convolution fusion | flops 4833278464 | bytes 3416064 | tf_op jit(solution)/shard_map/while/body/eval_jaxpr/srx,mx->srm/dot_general | solution.py:114
  166.2 3.2 %fusion.123 = f32[3,512]{1,0:T(4,128)S(1)} fusion(f32[3,128,2048]{2,1,0:T(8,128)S(1)} %get-tuple-element.416, s32[512]{0:T(512)S(1)} %get-tuple-element.362, f32[128,512]{1,0:T(8,128)S(1)} %fusion.122), kind=kOutput, calls=%fused_computation.28.clone.1 | convolution fusion | flops 4833278464 | bytes 3416064 | tf_op jit(solution)/shard_map/while/body/eval_jaxpr/srx,mx->srm/dot_general | solution.py:114
  170.1 3.2 %fusion.123 = f32[3,512]{1,0:T(4,128)S(1)} fusion(f32[3,128,2048]{2,1,0:T(8,128)S(1)} %get-tuple-element.416, s32[512]{0:T(512)S(1)} %get-tuple-element.362, f32[128,512]{1,0:T(8,128)S(1)} %fusion.122), kind=kOutput, calls=%fused_computation.28.clone.1 | convolution fusion | flops 4833278464 | bytes 3416064 | tf_op jit(solution)/shard_map/while/body/eval_jaxpr/srx,mx->srm/dot_general | solution.py:114
  173.9 3.2 %fusion.123 = f32[3,512]{1,0:T(4,128)S(1)} fusion(f32[3,128,2048]{2,1,0:T(8,128)S(1)} %get-tuple-element.416, s32[512]{0:T(512)S(1)} %get-tuple-element.362, f32[128,512]{1,0:T(8,128)S(1)} %fusion.122), kind=kOutput, calls=%fused_computation.28.clone.1 | convolution fusion | flops 4833278464 | bytes 3416064 | tf_op jit(solution)/shard_map/while/body/eval_jaxpr/srx,mx->srm/dot_general | solution.py:114
  177.8 3.2 %fusion.123 = f32[3,512]{1,0:T(4,128)S(1)} fusion(f32[3,128,2048]{2,1,0:T(8,128)S(1)} %get-tuple-element.416, s32[512]{0:T(512)S(1)} %get-tuple-element.362, f32[128,512]{1,0:T(8,128)S(1)} %fusion.122), kind=kOutput, calls=%fused_computation.28.clone.1 | convolution fusion | flops 4833278464 | bytes 3416064 | tf_op jit(solution)/shard_map/while/body/eval_jaxpr/srx,mx->srm/dot_general | solution.py:114
  181.6 3.2 %fusion.123 = f32[3,512]{1,0:T(4,128)S(1)} fusion(f32[3,128,2048]{2,1,0:T(8,128)S(1)} %get-tuple-element.416, s32[512]{0:T(512)S(1)} %get-tuple-element.362, f32[128,512]{1,0:T(8,128)S(1)} %fusion.122), kind=kOutput, calls=%fused_computation.28.clone.1 | convolution fusion | flops 4833278464 | bytes 3416064 | tf_op jit(solution)/shard_map/while/body/eval_jaxpr/srx,mx->srm/dot_general | solution.py:114
  185.4 3.2 %fusion.123 = f32[3,512]{1,0:T(4,128)S(1)} fusion(f32[3,128,2048]{2,1,0:T(8,128)S(1)} %get-tuple-element.416, s32[512]{0:T(512)S(1)} %get-tuple-element.362, f32[128,512]{1,0:T(8,128)S(1)} %fusion.122), kind=kOutput, calls=%fused_computation.28.clone.1 | convolution fusion | flops 4833278464 | bytes 3416064 | tf_op jit(solution)/shard_map/while/body/eval_jaxpr/srx,mx->srm/dot_general | solution.py:114
  189.2 12.5 %all-to-all-start.1 = ((f32[3,16,256]{2,0,1:T(4,128)}), f32[3,16,256]{2,0,1:T(4,128)S(1)}, u32[]{:S(2)}, u32[]{:S(2)}) async-start(f32[3,16,256]{2,0,1:T(4,128)} %bitcast.41), calls=%async_computation.1 | async-start | bytes 131072 | tf_op jit(solution)/shard_map/all_to_all | solution.py:303
  201.8 3.8 %broadcast_in_dim.243.cols_ref = f32[24,4,128,128]{3,2,1,0:T(8,128)} broadcast(f32[24,4,128]{2,1,0:T(4,128)S(1)} %maximum_bitcast_fusion.rows_ref), dimensions={0,1,2} | broadcast | bytes 6340608 | tf_op jit(solution)/shard_map/broadcast_in_dim | solution.py:180
  205.6 11.9 %shard_map.167 = f32[16,3,128]{2,1,0:T(4,128)} custom-call(s32[128]{0:T(128)} %reshape.806.chosen_ref, f32[24,4,128]{2,1,0:T(4,128)} %copy-done.1, f32[24,4,128,128]{3,2,1,0:T(8,128)} %broadcast_in_dim.243.cols_ref), custom_call_target="tpu_custom_call" | custom-call | flops 54525952 | bytes 6291456 | tf_op jit(solution)/shard_map/pallas_call | solution.py:182
  (254 shorter events, 29.5 us)
Async XLA Ops:
  8.7 0.9 copy-start.7
  9.0 10.4 %copy-start.6 = (f32[2048]{0:T(1024)S(1)}, f32[2048]{0:T(1024)}, u32[]{:S(2)}) copy-start(f32[2048]{0:T(1024)} %param.23) | copy-start | bytes 24580
  9.0 10.4 %copy-start.2 = (f32[3,2048]{1,0:T(4,128)S(1)}, f32[3,2048]{1,0:T(4,128)}, u32[]{:S(2)}) copy-start(f32[3,2048]{1,0:T(4,128)} %param.22) | copy-start | bytes 73732
  9.3 13.5 %slice-start = ((f32[2,8,16,2048]{3,2,1,0:T(8,128)}), f32[1,8,16,2048]{3,2,1,0:T(8,128)S(1)}, s32[]{:S(2)}) async-start(f32[2,8,16,2048]{3,2,1,0:T(8,128)} %param.29), calls=%async_computation.2 | async-start | bytes 2097152 | tf_op jit(solution)/shard_map/slice | solution.py:283
  10.4 14.7 %all-to-all-start = ((f32[2,16,256]{2,0,1:T(2,128)}), f32[2,16,256]{2,0,1:T(2,128)S(1)}, u32[]{:S(2)}, u32[]{:S(2)}) async-start(f32[2,16,256]{2,0,1:T(2,128)} %fusion.80), calls=%async_computation | async-start | bytes 65536 | tf_op jit(solution)/shard_map/all_to_all | solution.py:278
  19.4 182.3 %collective-permute-start = (f32[4,512]{1,0:T(4,128)S(1)}, f32[4,512]{1,0:T(4,128)S(1)}, u32[]{:S(2)}, u32[]{:S(2)}) collective-permute-start(f32[4,512]{1,0:T(4,128)S(1)} %get-tuple-element.269), channel_id=1, source_target_pairs={{0,1},{1,2},{2,3},{3,4},{4,5},{5,6},{6,7},{7,8},{8,9},{9,10},{10,1... | collective-permute-start | bytes 24584 | tf_op jit(solution)/shard_map/ppermute | solution.py:33
  23.0 1.3 copy-start.8
  67.7 14.9 %collective-permute-start.2 = (f32[2,1,16,2048]{3,2,1,0:T(8,128)S(1)}, f32[2,1,16,2048]{3,2,1,0:T(8,128)S(1)}, u32[]{:S(2)}, u32[]{:S(2)}) collective-permute-start(f32[2,1,16,2048]{3,2,1,0:T(8,128)S(1)} %get-tuple-element.259), channel_id=1, source_target_pairs={{16,0},{32,16},{48,32},{64,48},{80,64},{96,80},{112,96},{17,1},{33... | collective-permute-start | bytes 786440 | tf_op jit(solution)/shard_map/ppermute | solution.py:203
  69.8 12.8 %collective-permute-start.3 = (f32[2,1,16,2048]{3,2,1,0:T(8,128)S(1)}, f32[2,1,16,2048]{3,2,1,0:T(8,128)S(1)}, u32[]{:S(2)}, u32[]{:S(2)}) collective-permute-start(f32[2,1,16,2048]{3,2,1,0:T(8,128)S(1)} %get-tuple-element.258), channel_id=1, source_target_pairs={{0,16},{16,32},{32,48},{48,64},{64,80},{80,96},{96,112},{1,17},{17... | collective-permute-start | bytes 786440 | tf_op jit(solution)/shard_map/ppermute | solution.py:202
  72.3 6.9 %collective-permute-start.4 = (f32[2,8,1,2048]{3,1,2,0:T(8,128)S(1)}, f32[2,8,1,2048]{3,1,2,0:T(8,128)S(1)}, u32[]{:S(2)}, u32[]{:S(2)}) collective-permute-start(f32[2,8,1,2048]{3,1,2,0:T(8,128)S(1)} %copy.75), channel_id=1, source_target_pairs={{1,0},{2,1},{3,2},{4,3},{5,4},{6,5},{7,6},{8,7},{9,8},{10,9},{11,1... | collective-permute-start | bytes 393224 | tf_op jit(solution)/shard_map/ppermute | solution.py:203
  75.6 7.0 %copy-start.4 = (f32[2]{0:T(128)S(1)}, f32[2]{0:T(128)}, u32[]{:S(2)}) copy-start(f32[2]{0:T(128)} %constant.224.clone) | copy-start | bytes 28
  75.6 7.0 %copy-start.5 = (f32[2]{0:T(128)S(1)}, f32[2]{0:T(128)}, u32[]{:S(2)}) copy-start(f32[2]{0:T(128)} %constant.225.clone) | copy-start | bytes 28
  75.6 6.9 %collective-permute-start.5 = (f32[2,8,1,2048]{3,1,2,0:T(8,128)S(1)}, f32[2,8,1,2048]{3,1,2,0:T(8,128)S(1)}, u32[]{:S(2)}, u32[]{:S(2)}) collective-permute-start(f32[2,8,1,2048]{3,1,2,0:T(8,128)S(1)} %copy.77), channel_id=1, source_target_pairs={{0,1},{1,2},{2,3},{3,4},{4,5},{5,6},{6,7},{7,8},{8,9},{9,10},{10,1... | collective-permute-start | bytes 393224 | tf_op jit(solution)/shard_map/ppermute | solution.py:202
  85.5 14.0 %collective-permute-start.6 = (f32[2,1,16,2048]{3,2,1,0:T(8,128)S(1)}, f32[2,1,16,2048]{3,2,1,0:T(8,128)S(1)}, u32[]{:S(2)}, u32[]{:S(2)}) collective-permute-start(f32[2,1,16,2048]{3,2,1,0:T(8,128)S(1)} %get-tuple-element.251), channel_id=1, source_target_pairs={{16,0},{32,16},{48,32},{64,48},{80,64},{96,80},{112,96},{17,1},{33... | collective-permute-start | bytes 786440 | tf_op jit(solution)/shard_map/ppermute | solution.py:203
  88.6 11.0 %collective-permute-start.7 = (f32[2,1,16,2048]{3,2,1,0:T(8,128)S(1)}, f32[2,1,16,2048]{3,2,1,0:T(8,128)S(1)}, u32[]{:S(2)}, u32[]{:S(2)}) collective-permute-start(f32[2,1,16,2048]{3,2,1,0:T(8,128)S(1)} %get-tuple-element.250), channel_id=1, source_target_pairs={{0,16},{16,32},{32,48},{48,64},{64,80},{80,96},{96,112},{1,17},{17... | collective-permute-start | bytes 786440 | tf_op jit(solution)/shard_map/ppermute | solution.py:202
  90.6 6.9 %collective-permute-start.8 = (f32[2,8,1,2048]{3,1,2,0:T(8,128)S(1)}, f32[2,8,1,2048]{3,1,2,0:T(8,128)S(1)}, u32[]{:S(2)}, u32[]{:S(2)}) collective-permute-start(f32[2,8,1,2048]{3,1,2,0:T(8,128)S(1)} %copy.79), channel_id=1, source_target_pairs={{1,0},{2,1},{3,2},{4,3},{5,4},{6,5},{7,6},{8,7},{9,8},{10,9},{11,1... | collective-permute-start | bytes 393224 | tf_op jit(solution)/shard_map/ppermute | solution.py:203
  92.6 6.9 %collective-permute-start.9 = (f32[2,8,1,2048]{3,1,2,0:T(8,128)S(1)}, f32[2,8,1,2048]{3,1,2,0:T(8,128)S(1)}, u32[]{:S(2)}, u32[]{:S(2)}) collective-permute-start(f32[2,8,1,2048]{3,1,2,0:T(8,128)S(1)} %copy.81), channel_id=1, source_target_pairs={{0,1},{1,2},{2,3},{3,4},{4,5},{5,6},{6,7},{7,8},{8,9},{9,10},{10,1... | collective-permute-start | bytes 393224 | tf_op jit(solution)/shard_map/ppermute | solution.py:202
  102.5 15.1 %collective-permute-start.10 = (f32[2,1,16,2048]{3,2,1,0:T(8,128)S(1)}, f32[2,1,16,2048]{3,2,1,0:T(8,128)S(1)}, u32[]{:S(2)}, u32[]{:S(2)}) collective-permute-start(f32[2,1,16,2048]{3,2,1,0:T(8,128)S(1)} %get-tuple-element.243), channel_id=1, source_target_pairs={{16,0},{32,16},{48,32},{64,48},{80,64},{96,80},{112,96},{17,1},{33... | collective-permute-start | bytes 786440 | tf_op jit(solution)/shard_map/ppermute | solution.py:203
  106.6 11.0 %collective-permute-start.11 = (f32[2,1,16,2048]{3,2,1,0:T(8,128)S(1)}, f32[2,1,16,2048]{3,2,1,0:T(8,128)S(1)}, u32[]{:S(2)}, u32[]{:S(2)}) collective-permute-start(f32[2,1,16,2048]{3,2,1,0:T(8,128)S(1)} %get-tuple-element.242), channel_id=1, source_target_pairs={{0,16},{16,32},{32,48},{48,64},{64,80},{80,96},{96,112},{1,17},{17... | collective-permute-start | bytes 786440 | tf_op jit(solution)/shard_map/ppermute | solution.py:202
  108.6 6.9 %collective-permute-start.12 = (f32[2,8,1,2048]{3,1,2,0:T(8,128)S(1)}, f32[2,8,1,2048]{3,1,2,0:T(8,128)S(1)}, u32[]{:S(2)}, u32[]{:S(2)}) collective-permute-start(f32[2,8,1,2048]{3,1,2,0:T(8,128)S(1)} %copy.83), channel_id=1, source_target_pairs={{1,0},{2,1},{3,2},{4,3},{5,4},{6,5},{7,6},{8,7},{9,8},{10,9},{11,1... | collective-permute-start | bytes 393224 | tf_op jit(solution)/shard_map/ppermute | solution.py:203
  110.6 6.9 %collective-permute-start.13 = (f32[2,8,1,2048]{3,1,2,0:T(8,128)S(1)}, f32[2,8,1,2048]{3,1,2,0:T(8,128)S(1)}, u32[]{:S(2)}, u32[]{:S(2)}) collective-permute-start(f32[2,8,1,2048]{3,1,2,0:T(8,128)S(1)} %copy.85), channel_id=1, source_target_pairs={{0,1},{1,2},{2,3},{3,4},{4,5},{5,6},{6,7},{7,8},{8,9},{9,10},{10,1... | collective-permute-start | bytes 393224 | tf_op jit(solution)/shard_map/ppermute | solution.py:202
  120.5 15.5 %collective-permute-start.14 = (f32[2,1,16,2048]{3,2,1,0:T(8,128)S(1)}, f32[2,1,16,2048]{3,2,1,0:T(8,128)S(1)}, u32[]{:S(2)}, u32[]{:S(2)}) collective-permute-start(f32[2,1,16,2048]{3,2,1,0:T(8,128)S(1)} %get-tuple-element.235), channel_id=1, source_target_pairs={{16,0},{32,16},{48,32},{64,48},{80,64},{96,80},{112,96},{17,1},{33... | collective-permute-start | bytes 786440 | tf_op jit(solution)/shard_map/ppermute | solution.py:203
  124.0 12.0 %collective-permute-start.15 = (f32[2,1,16,2048]{3,2,1,0:T(8,128)S(1)}, f32[2,1,16,2048]{3,2,1,0:T(8,128)S(1)}, u32[]{:S(2)}, u32[]{:S(2)}) collective-permute-start(f32[2,1,16,2048]{3,2,1,0:T(8,128)S(1)} %get-tuple-element.234), channel_id=1, source_target_pairs={{0,16},{16,32},{32,48},{48,64},{64,80},{80,96},{96,112},{1,17},{17... | collective-permute-start | bytes 786440 | tf_op jit(solution)/shard_map/ppermute | solution.py:202
  126.0 7.8 %collective-permute-start.16 = (f32[2,8,1,2048]{3,1,2,0:T(8,128)S(1)}, f32[2,8,1,2048]{3,1,2,0:T(8,128)S(1)}, u32[]{:S(2)}, u32[]{:S(2)}) collective-permute-start(f32[2,8,1,2048]{3,1,2,0:T(8,128)S(1)} %copy.87), channel_id=1, source_target_pairs={{1,0},{2,1},{3,2},{4,3},{5,4},{6,5},{7,6},{8,7},{9,8},{10,9},{11,1... | collective-permute-start | bytes 393224 | tf_op jit(solution)/shard_map/ppermute | solution.py:203
  128.0 7.8 %collective-permute-start.17 = (f32[2,8,1,2048]{3,1,2,0:T(8,128)S(1)}, f32[2,8,1,2048]{3,1,2,0:T(8,128)S(1)}, u32[]{:S(2)}, u32[]{:S(2)}) collective-permute-start(f32[2,8,1,2048]{3,1,2,0:T(8,128)S(1)} %copy.89), channel_id=1, source_target_pairs={{0,1},{1,2},{2,3},{3,4},{4,5},{5,6},{6,7},{7,8},{8,9},{9,10},{10,1... | collective-permute-start | bytes 393224 | tf_op jit(solution)/shard_map/ppermute | solution.py:202
  133.8 68.0 %collective-permute-start.1 = (f32[4,512]{1,0:T(4,128)S(1)}, f32[4,512]{1,0:T(4,128)S(1)}, u32[]{:S(2)}, u32[]{:S(2)}) collective-permute-start(f32[4,512]{1,0:T(4,128)S(1)} %get-tuple-element.270), channel_id=1, source_target_pairs={{1,0},{2,1},{3,2},{4,3},{5,4},{6,5},{7,6},{8,7},{9,8},{10,9},{11,1... | collective-permute-start | bytes 24584 | tf_op jit(solution)/shard_map/ppermute | solution.py:36
  138.2 1.3 copy-start
  139.9 12.0 %collective-permute-start.20 = (f32[8,1,2048]{2,1,0:T(1,128)S(1)}, f32[8,1,2048]{2,1,0:T(1,128)S(1)}, u32[]{:S(2)}, u32[]{:S(2)}) collective-permute-start(f32[8,1,2048]{2,1,0:T(1,128)S(1)} %get-tuple-element.263), channel_id=1, source_target_pairs={{1,0},{2,1},{3,2},{4,3},{5,4},{6,5},{7,6},{8,7},{9,8},{10,9},{11,1... | collective-permute-start | bytes 196616 | tf_op jit(solution)/shard_map/ppermute | solution.py:203
  141.8 12.2 %collective-permute-start.21 = (f32[8,1,2048]{2,1,0:T(1,128)S(1)}, f32[8,1,2048]{2,1,0:T(1,128)S(1)}, u32[]{:S(2)}, u32[]{:S(2)}) collective-permute-start(f32[8,1,2048]{2,1,0:T(1,128)S(1)} %get-tuple-element.262), channel_id=1, source_target_pairs={{0,1},{1,2},{2,3},{3,4},{4,5},{5,6},{6,7},{7,8},{8,9},{9,10},{10,1... | collective-permute-start | bytes 196616 | tf_op jit(solution)/shard_map/ppermute | solution.py:202
  148.9 5.4 %collective-permute-start.18 = (f32[1,16,2048]{2,1,0:T(8,128)S(1)}, f32[1,16,2048]{2,1,0:T(8,128)S(1)}, u32[]{:S(2)}, u32[]{:S(2)}) collective-permute-start(f32[1,16,2048]{2,1,0:T(8,128)S(1)} %get-tuple-element.227), channel_id=1, source_target_pairs={{16,0},{32,16},{48,32},{64,48},{80,64},{96,80},{112,96},{17,1},{33... | collective-permute-start | bytes 393224 | tf_op jit(solution)/shard_map/ppermute | solution.py:203
  151.9 6.3 %collective-permute-start.19 = (f32[1,16,2048]{2,1,0:T(8,128)S(1)}, f32[1,16,2048]{2,1,0:T(8,128)S(1)}, u32[]{:S(2)}, u32[]{:S(2)}) collective-permute-start(f32[1,16,2048]{2,1,0:T(8,128)S(1)} %get-tuple-element.226), channel_id=1, source_target_pairs={{0,16},{16,32},{32,48},{48,64},{64,80},{80,96},{96,112},{1,17},{17... | collective-permute-start | bytes 393224 | tf_op jit(solution)/shard_map/ppermute | solution.py:202
  189.2 28.3 %all-to-all-start.1 = ((f32[3,16,256]{2,0,1:T(4,128)}), f32[3,16,256]{2,0,1:T(4,128)S(1)}, u32[]{:S(2)}, u32[]{:S(2)}) async-start(f32[3,16,256]{2,0,1:T(4,128)} %bitcast.41), calls=%async_computation.1 | async-start | bytes 131072 | tf_op jit(solution)/shard_map/all_to_all | solution.py:303
  201.8 3.8 %copy-start.1 = (f32[24,4,128]{2,1,0:T(4,128)}, f32[24,4,128]{2,1,0:T(4,128)S(1)}, u32[]{:S(2)}) copy-start(f32[24,4,128]{2,1,0:T(4,128)S(1)} %maximum_bitcast_fusion.rows_ref) | copy-start | bytes 147460
  221.8 0.8 copy-start.3

commit v8 on v7

--- a/solution.py
+++ b/solution.py
@@ -142,7 +142,7 @@
     blocks = out_ref.shape[0]
     picks = chosen_ref.shape[0] // blocks
     chunks = cols_ref.shape[2] // 8
-    shape = (8, cols_ref.shape[3])
+    shape = (8, rows_ref.shape[2])
 
     def one_block(block, carry):
         own = rows_ref[block + HB]
@@ -153,12 +153,12 @@
             totals = list(totals)
             for chunk in range(chunks):
                 part = pl.ds(chunk * 8, 8)
-                offset = [mine[axis] - cols_ref[other, axis, part, :] for axis in range(3)]
+                offset = [mine[axis] - jnp.broadcast_to(cols_ref[other, axis, part, :], shape) for axis in range(3)]
                 distance = offset[0] * offset[0] + offset[1] * offset[1] + offset[2] * offset[2]
                 strength = REPULSION * jnp.exp(-distance / REPEL_RANGE) - ADHESION * jnp.exp(
                     -distance / ADHERE_RANGE
                 )
-                weight = mine[3] * cols_ref[other, 3, part, :] * strength
+                weight = mine[3] * jnp.broadcast_to(cols_ref[other, 3, part, :], shape) * strength
                 for axis in range(3):
                     totals[axis] = totals[axis] + offset[axis] * weight
             return tuple(totals)
@@ -177,7 +177,7 @@
     coords, span, lanes = extended.shape
     blocks, picks = neighbor_blocks.shape
     rows = jnp.transpose(extended, (1, 0, 2))
-    cols = jnp.broadcast_to(rows[:, :, :, None], (span, coords, lanes, lanes))
+    cols = rows[:, :, :, None]
     pairs = blocks * picks * lanes * lanes
     out = pl.pallas_call(
         force_kernel,

time: 224 us -> 240 us (1.071)
  Pallas kernels: 11.9 us -> 22.3 us
  waiting for transfers between devices: 12.7 us -> 17.2 us
    pallas_call x1, Pallas kernels: 11.9 us -> 22.3 us  [pair_forces(): pl.pallas_call(force_kernel, out_shape=jax.ShapeDtypeStruct((blocks, 3, l...]
    ppermute x10, waiting for transfers between devices: 2.03 us -> 6.45 us  [neighbours(): high = lax.ppermute(lax.slice_in_dim(block, 0, 1, axis=dim), axis, backward)]
  transfers between devices with their start and end apart: 24 -> 24, of which waited for: 8 -> 9; matrix products, arithmetic and copies ran while one was open for 42% -> 40% of each run, Pallas kernels for 5% -> 9%
where the time goes in v8:
time: 240 us; the launch traced here: 238 us
  starting transfers between devices  84.3 us (35%)
  matrix products  63.3 us (26%)
  other arithmetic  25.9 us (11%)
  Pallas kernels  22.3 us (9%)
  local copies, waits for them, and re-layouts  22.1 us (9%)
  waiting for transfers between devices  17.2 us (7%)
    ppermute x10, starting transfers between devices, neighbours(): lax.ppermute(lax.slice_in_dim(block, block.shape[dim] - 1, None, axis=dim...  31.8 us
    ppermute x10, starting transfers between devices, neighbours(): high = lax.ppermute(lax.slice_in_dim(block, 0, 1, axis=dim), axis, backward)  26.9 us
    dot_general x8, matrix products, one_piece(): jnp.einsum('srx,mx->srm', fields, column_hot, precision=lax.Precision.HIG...  25.4 us
    dot_general x8, matrix products, add_piece(): jnp.einsum('smr,mx->srx', weighted, column_hot, precision=lax.Precision.H...  24.1 us
    pallas_call x1, Pallas kernels, pair_forces(): pl.pallas_call(force_kernel, out_shape=jax.ShapeDtypeStruct((blocks, 3, l...  22.3 us
    dot_general x4, matrix products, one_piece(): jnp.einsum('psrx,mx->psrm', parts, column_hot, preferred_element_type=jnp...  13.8 us
    all_to_all x1, starting transfers between devices, local(): lax.all_to_all(slopes, 'tile', split_axis=1, concat_axis=1, tiled=True)  12.1 us
    ppermute x10, waiting for transfers between devices, neighbours(): lax.ppermute(lax.slice_in_dim(block, block.shape[dim] - 1, None, axis=dim...  10.7 us
  transfers between devices with their start and end apart: 24, of which 9 were waited for; matrix products, arithmetic and copies ran while one was open for 40% of the time, Pallas kernels for 9%

profile of v8, /device:TPU:26, one launch (start us, length us, event | category | flops | bytes accessed | tf_op | source)
XLA Modules:
  0.0 238.3 jit_solution(11398147470619307111)
XLA Ops:
  1.3 0.7 pad_maximum_fusion.5
  2.0 0.8 fusion.86
  2.8 0.7 copy.81
  10.4 8.3 %all-to-all-start = ((f32[2,16,256]{2,0,1:T(2,128)}), f32[2,16,256]{2,0,1:T(2,128)S(1)}, u32[]{:S(2)}, u32[]{:S(2)}) async-start(f32[2,16,256]{2,0,1:T(2,128)} %fusion.80), calls=%async_computation | async-start | bytes 65536 | tf_op jit(solution)/shard_map/all_to_all | solution.py:278
  19.4 3.4 %collective-permute-start = (f32[4,512]{1,0:T(4,128)S(1)}, f32[4,512]{1,0:T(4,128)S(1)}, u32[]{:S(2)}, u32[]{:S(2)}) collective-permute-start(f32[4,512]{1,0:T(4,128)S(1)} %get-tuple-element.271), channel_id=1, source_target_pairs={{0,1},{1,2},{2,3},{3,4},{4,5},{5,6},{6,7},{7,8},{8,9},{9,10},{10,1... | collective-permute-start | bytes 24584 | tf_op jit(solution)/shard_map/ppermute | solution.py:33
  23.1 1.3 pad_maximum_fusion.1
  25.2 14.7 %while.37 = (s32[]{:T(128)}, f32[4,1,1024]{2,1,0:T(1,128)S(1)}, s32[4,1024]{1,0:T(4,128)S(1)}, bf16[3,1,128,2048]{3,2,0,1:T(8,128)(2,1)}, s32[]{:T(128)}) while((s32[]{:T(128)}, f32[4,1,1024]{2,1,0:T(1,128)S(1)}, s32[4,1024]{1,0:T(4,128)S(1)}, bf16[3,1,128,2048]{3,2,0,1:T(8,128)(2,1)}, s32[]{:T(128)}) %tuple.122), condition=%wide.region_3.4_spmd, body=%wide.region_1.3_spmd.sunk | while | flops 1613645824 | bytes 4759621 | solution.py:104
  25.2 3.5 %fusion.120 = f32[3,128,1024]{2,1,0:T(8,128)S(1)} fusion(bf16[3,1,128,2048]{3,2,0,1:T(8,128)(2,1)} %get-tuple-element.385, s32[1024]{0:T(1024)S(1)} %get-tuple-element.358), kind=kOutput, calls=%fused_computation.5.clone.1 | convolution fusion | flops 1612709888 | bytes 3149824 | tf_op jit(solution)/shard_map/while/body/eval_jaxpr/psrx,mx->psrm/dot_general | solution.py:98
  28.9 3.5 %fusion.120 = f32[3,128,1024]{2,1,0:T(8,128)S(1)} fusion(bf16[3,1,128,2048]{3,2,0,1:T(8,128)(2,1)} %get-tuple-element.385, s32[1024]{0:T(1024)S(1)} %get-tuple-element.358), kind=kOutput, calls=%fused_computation.5.clone.1 | convolution fusion | flops 1612709888 | bytes 3149824 | tf_op jit(solution)/shard_map/while/body/eval_jaxpr/psrx,mx->psrm/dot_general | solution.py:98
  32.6 3.5 %fusion.120 = f32[3,128,1024]{2,1,0:T(8,128)S(1)} fusion(bf16[3,1,128,2048]{3,2,0,1:T(8,128)(2,1)} %get-tuple-element.385, s32[1024]{0:T(1024)S(1)} %get-tuple-element.358), kind=kOutput, calls=%fused_computation.5.clone.1 | convolution fusion | flops 1612709888 | bytes 3149824 | tf_op jit(solution)/shard_map/while/body/eval_jaxpr/psrx,mx->psrm/dot_general | solution.py:98
  36.3 3.5 %fusion.120 = f32[3,128,1024]{2,1,0:T(8,128)S(1)} fusion(bf16[3,1,128,2048]{3,2,0,1:T(8,128)(2,1)} %get-tuple-element.385, s32[1024]{0:T(1024)S(1)} %get-tuple-element.358), kind=kOutput, calls=%fused_computation.5.clone.1 | convolution fusion | flops 1612709888 | bytes 3149824 | tf_op jit(solution)/shard_map/while/body/eval_jaxpr/psrx,mx->psrm/dot_general | solution.py:98
  40.1 25.0 %while.39 = (s32[]{:T(128)}, f32[2,128,2048]{2,1,0:T(8,128)S(1)}, f32[8,2,512]{2,0,1:T(8,128)S(1)}, s32[8,512]{1,0:T(8,128)S(1)}, s32[]{:T(128)}, /*index=5*/s32[]{:T(128)}) while((s32[]{:T(128)}, f32[2,128,2048]{2,1,0:T(8,128)S(1)}, f32[8,2,512]{2,0,1:T(8,128)S(1)}, s32[8,512]{1,0:T(8,128)S(1)}, s32[]{:T(128)}, ...), condition=%wide.region_5.6_spmd.clone, body=%wide.region_4.5_spmd.clone.sunk | while | flops 3223594496 | bytes 4753495 | solution.py:137
  40.2 3.0 %fusion.129 = f32[2,128,2048]{2,1,0:T(8,128)S(1)} fusion(f32[2,128,2048]{2,1,0:T(8,128)S(1)} %get-tuple-element.394, s32[512]{0:T(512)S(1)} %get-tuple-element.370, pred[]{:T(512)S(6)} %compare.53, f32[512,128]{0,1:T(8,128)S(1)} %fusion.128, f32[2,512]{1,0:T(2,128)S(1)} %bitcast.144), kind=kOutput, calls=%fused_computation.44.clone.1 | convolution fusion | flops 3223453696 | bytes 4462593 | tf_op jit(solution)/shard_map/while/body/eval_jaxpr/smr,mx->srx/dot_general | solution.py:132
  43.3 3.0 %fusion.129 = f32[2,128,2048]{2,1,0:T(8,128)S(1)} fusion(f32[2,128,2048]{2,1,0:T(8,128)S(1)} %get-tuple-element.394, s32[512]{0:T(512)S(1)} %get-tuple-element.370, pred[]{:T(512)S(6)} %compare.53, f32[512,128]{0,1:T(8,128)S(1)} %fusion.128, f32[2,512]{1,0:T(2,128)S(1)} %bitcast.144), kind=kOutput, calls=%fused_computation.44.clone.1 | convolution fusion | flops 3223453696 | bytes 4462593 | tf_op jit(solution)/shard_map/while/body/eval_jaxpr/smr,mx->srx/dot_general | solution.py:132
  46.5 3.0 %fusion.129 = f32[2,128,2048]{2,1,0:T(8,128)S(1)} fusion(f32[2,128,2048]{2,1,0:T(8,128)S(1)} %get-tuple-element.394, s32[512]{0:T(512)S(1)} %get-tuple-element.370, pred[]{:T(512)S(6)} %compare.53, f32[512,128]{0,1:T(8,128)S(1)} %fusion.128, f32[2,512]{1,0:T(2,128)S(1)} %bitcast.144), kind=kOutput, calls=%fused_computation.44.clone.1 | convolution fusion | flops 3223453696 | bytes 4462593 | tf_op jit(solution)/shard_map/while/body/eval_jaxpr/smr,mx->srx/dot_general | solution.py:132
  49.6 3.0 %fusion.129 = f32[2,128,2048]{2,1,0:T(8,128)S(1)} fusion(f32[2,128,2048]{2,1,0:T(8,128)S(1)} %get-tuple-element.394, s32[512]{0:T(512)S(1)} %get-tuple-element.370, pred[]{:T(512)S(6)} %compare.53, f32[512,128]{0,1:T(8,128)S(1)} %fusion.128, f32[2,512]{1,0:T(2,128)S(1)} %bitcast.144), kind=kOutput, calls=%fused_computation.44.clone.1 | convolution fusion | flops 3223453696 | bytes 4462593 | tf_op jit(solution)/shard_map/while/body/eval_jaxpr/smr,mx->srx/dot_general | solution.py:132
  52.7 3.0 %fusion.129 = f32[2,128,2048]{2,1,0:T(8,128)S(1)} fusion(f32[2,128,2048]{2,1,0:T(8,128)S(1)} %get-tuple-element.394, s32[512]{0:T(512)S(1)} %get-tuple-element.370, pred[]{:T(512)S(6)} %compare.53, f32[512,128]{0,1:T(8,128)S(1)} %fusion.128, f32[2,512]{1,0:T(2,128)S(1)} %bitcast.144), kind=kOutput, calls=%fused_computation.44.clone.1 | convolution fusion | flops 3223453696 | bytes 4462593 | tf_op jit(solution)/shard_map/while/body/eval_jaxpr/smr,mx->srx/dot_general | solution.py:132
  55.9 3.0 %fusion.129 = f32[2,128,2048]{2,1,0:T(8,128)S(1)} fusion(f32[2,128,2048]{2,1,0:T(8,128)S(1)} %get-tuple-element.394, s32[512]{0:T(512)S(1)} %get-tuple-element.370, pred[]{:T(512)S(6)} %compare.53, f32[512,128]{0,1:T(8,128)S(1)} %fusion.128, f32[2,512]{1,0:T(2,128)S(1)} %bitcast.144), kind=kOutput, calls=%fused_computation.44.clone.1 | convolution fusion | flops 3223453696 | bytes 4462593 | tf_op jit(solution)/shard_map/while/body/eval_jaxpr/smr,mx->srx/dot_general | solution.py:132
  59.0 3.0 %fusion.129 = f32[2,128,2048]{2,1,0:T(8,128)S(1)} fusion(f32[2,128,2048]{2,1,0:T(8,128)S(1)} %get-tuple-element.394, s32[512]{0:T(512)S(1)} %get-tuple-element.370, pred[]{:T(512)S(6)} %compare.53, f32[512,128]{0,1:T(8,128)S(1)} %fusion.128, f32[2,512]{1,0:T(2,128)S(1)} %bitcast.144), kind=kOutput, calls=%fused_computation.44.clone.1 | convolution fusion | flops 3223453696 | bytes 4462593 | tf_op jit(solution)/shard_map/while/body/eval_jaxpr/smr,mx->srx/dot_general | solution.py:132
  62.1 3.0 %fusion.129 = f32[2,128,2048]{2,1,0:T(8,128)S(1)} fusion(f32[2,128,2048]{2,1,0:T(8,128)S(1)} %get-tuple-element.394, s32[512]{0:T(512)S(1)} %get-tuple-element.370, pred[]{:T(512)S(6)} %compare.53, f32[512,128]{0,1:T(8,128)S(1)} %fusion.128, f32[2,512]{1,0:T(2,128)S(1)} %bitcast.144), kind=kOutput, calls=%fused_computation.44.clone.1 | convolution fusion | flops 3223453696 | bytes 4462593 | tf_op jit(solution)/shard_map/while/body/eval_jaxpr/smr,mx->srx/dot_general | solution.py:132
  65.2 1.8 add.225
  67.7 2.1 collective-permute-start.2
  69.8 2.4 %collective-permute-start.3 = (f32[2,1,16,2048]{3,2,1,0:T(8,128)S(1)}, f32[2,1,16,2048]{3,2,1,0:T(8,128)S(1)}, u32[]{:S(2)}, u32[]{:S(2)}) collective-permute-start(f32[2,1,16,2048]{3,2,1,0:T(8,128)S(1)} %get-tuple-element.258), channel_id=1, source_target_pairs={{0,16},{16,32},{32,48},{48,64},{64,80},{80,96},{96,112},{1,17},{17... | collective-permute-start | bytes 786440 | tf_op jit(solution)/shard_map/ppermute | solution.py:202
  72.3 3.2 %collective-permute-start.4 = (f32[2,8,1,2048]{3,1,2,0:T(8,128)S(1)}, f32[2,8,1,2048]{3,1,2,0:T(8,128)S(1)}, u32[]{:S(2)}, u32[]{:S(2)}) collective-permute-start(f32[2,8,1,2048]{3,1,2,0:T(8,128)S(1)} %copy.85), channel_id=1, source_target_pairs={{1,0},{2,1},{3,2},{4,3},{5,4},{6,5},{7,6},{8,7},{9,8},{10,9},{11,1... | collective-permute-start | bytes 393224 | tf_op jit(solution)/shard_map/ppermute | solution.py:203
  75.6 2.6 %collective-permute-start.5 = (f32[2,8,1,2048]{3,1,2,0:T(8,128)S(1)}, f32[2,8,1,2048]{3,1,2,0:T(8,128)S(1)}, u32[]{:S(2)}, u32[]{:S(2)}) collective-permute-start(f32[2,8,1,2048]{3,1,2,0:T(8,128)S(1)} %copy.87), channel_id=1, source_target_pairs={{0,1},{1,2},{2,3},{3,4},{4,5},{5,6},{6,7},{7,8},{8,9},{9,10},{10,1... | collective-permute-start | bytes 393224 | tf_op jit(solution)/shard_map/ppermute | solution.py:202
  79.3 3.2 %collective-permute-done.5 = f32[2,8,1,2048]{3,1,2,0:T(8,128)S(1)} collective-permute-done((f32[2,8,1,2048]{3,1,2,0:T(8,128)S(1)}, f32[2,8,1,2048]{3,1,2,0:T(8,128)S(1)}, u32[]{:S(2)}, u32[]{:S(2)}) %collective-permute-start.5) | collective-permute-done | bytes 131104 | tf_op jit(solution)/shard_map/ppermute | solution.py:202
  82.6 2.2 fusion.47
  85.5 3.1 %collective-permute-start.6 = (f32[2,1,16,2048]{3,2,1,0:T(8,128)S(1)}, f32[2,1,16,2048]{3,2,1,0:T(8,128)S(1)}, u32[]{:S(2)}, u32[]{:S(2)}) collective-permute-start(f32[2,1,16,2048]{3,2,1,0:T(8,128)S(1)} %get-tuple-element.251), channel_id=1, source_target_pairs={{16,0},{32,16},{48,32},{64,48},{80,64},{96,80},{112,96},{17,1},{33... | collective-permute-start | bytes 786440 | tf_op jit(solution)/shard_map/ppermute | solution.py:203
  88.6 1.9 collective-permute-start.7
  90.6 1.9 collective-permute-start.8
  92.6 3.9 %collective-permute-start.9 = (f32[2,8,1,2048]{3,1,2,0:T(8,128)S(1)}, f32[2,8,1,2048]{3,1,2,0:T(8,128)S(1)}, u32[]{:S(2)}, u32[]{:S(2)}) collective-permute-start(f32[2,8,1,2048]{3,1,2,0:T(8,128)S(1)} %copy.91), channel_id=1, source_target_pairs={{0,1},{1,2},{2,3},{3,4},{4,5},{5,6},{6,7},{7,8},{8,9},{9,10},{10,1... | collective-permute-start | bytes 393224 | tf_op jit(solution)/shard_map/ppermute | solution.py:202
  97.6 1.8 collective-permute-done.9
  99.6 2.2 fusion.53
  102.5 4.1 %collective-permute-start.10 = (f32[2,1,16,2048]{3,2,1,0:T(8,128)S(1)}, f32[2,1,16,2048]{3,2,1,0:T(8,128)S(1)}, u32[]{:S(2)}, u32[]{:S(2)}) collective-permute-start(f32[2,1,16,2048]{3,2,1,0:T(8,128)S(1)} %get-tuple-element.243), channel_id=1, source_target_pairs={{16,0},{32,16},{48,32},{64,48},{80,64},{96,80},{112,96},{17,1},{33... | collective-permute-start | bytes 786440 | tf_op jit(solution)/shard_map/ppermute | solution.py:203
  106.6 1.9 collective-permute-start.11
  108.6 1.9 collective-permute-start.12
  110.6 3.9 %collective-permute-start.13 = (f32[2,8,1,2048]{3,1,2,0:T(8,128)S(1)}, f32[2,8,1,2048]{3,1,2,0:T(8,128)S(1)}, u32[]{:S(2)}, u32[]{:S(2)}) collective-permute-start(f32[2,8,1,2048]{3,1,2,0:T(8,128)S(1)} %copy.95), channel_id=1, source_target_pairs={{0,1},{1,2},{2,3},{3,4},{4,5},{5,6},{6,7},{7,8},{8,9},{9,10},{10,1... | collective-permute-start | bytes 393224 | tf_op jit(solution)/shard_map/ppermute | solution.py:202
  115.6 1.8 collective-permute-done.13
  117.6 2.2 fusion.59
  120.5 3.5 %collective-permute-start.14 = (f32[2,1,16,2048]{3,2,1,0:T(8,128)S(1)}, f32[2,1,16,2048]{3,2,1,0:T(8,128)S(1)}, u32[]{:S(2)}, u32[]{:S(2)}) collective-permute-start(f32[2,1,16,2048]{3,2,1,0:T(8,128)S(1)} %get-tuple-element.235), channel_id=1, source_target_pairs={{16,0},{32,16},{48,32},{64,48},{80,64},{96,80},{112,96},{17,1},{33... | collective-permute-start | bytes 786440 | tf_op jit(solution)/shard_map/ppermute | solution.py:203
  124.0 1.9 collective-permute-start.15
  126.0 4.8 %collective-permute-start.17 = (f32[2,8,1,2048]{3,1,2,0:T(8,128)S(1)}, f32[2,8,1,2048]{3,1,2,0:T(8,128)S(1)}, u32[]{:S(2)}, u32[]{:S(2)}) collective-permute-start(f32[2,8,1,2048]{3,1,2,0:T(8,128)S(1)} %copy.99), channel_id=1, source_target_pairs={{0,1},{1,2},{2,3},{3,4},{4,5},{5,6},{6,7},{7,8},{8,9},{9,10},{10,1... | collective-permute-start | bytes 393224 | tf_op jit(solution)/shard_map/ppermute | solution.py:202
  130.9 1.9 collective-permute-start.16
  133.3 1.9 collective-permute-start.1
  135.4 4.9 %collective-permute-done.16 = f32[2,8,1,2048]{3,1,2,0:T(8,128)S(1)} collective-permute-done((f32[2,8,1,2048]{3,1,2,0:T(8,128)S(1)}, f32[2,8,1,2048]{3,1,2,0:T(8,128)S(1)}, u32[]{:S(2)}, u32[]{:S(2)}) %collective-permute-start.16) | collective-permute-done | bytes 131104 | tf_op jit(solution)/shard_map/ppermute | solution.py:203
  140.5 2.2 fusion.65
  142.9 1.1 copy-done
  144.3 1.9 collective-permute-start.20
  146.3 6.2 %collective-permute-start.21 = (f32[8,1,2048]{2,1,0:T(1,128)S(1)}, f32[8,1,2048]{2,1,0:T(1,128)S(1)}, u32[]{:S(2)}, u32[]{:S(2)}) collective-permute-start(f32[8,1,2048]{2,1,0:T(1,128)S(1)} %get-tuple-element.262), channel_id=1, source_target_pairs={{0,1},{1,2},{2,3},{3,4},{4,5},{5,6},{6,7},{7,8},{8,9},{9,10},{10,1... | collective-permute-start | bytes 196616 | tf_op jit(solution)/shard_map/ppermute | solution.py:202
  153.1 3.1 %collective-permute-start.18 = (f32[1,16,2048]{2,1,0:T(8,128)S(1)}, f32[1,16,2048]{2,1,0:T(8,128)S(1)}, u32[]{:S(2)}, u32[]{:S(2)}) collective-permute-start(f32[1,16,2048]{2,1,0:T(8,128)S(1)} %get-tuple-element.227), channel_id=1, source_target_pairs={{16,0},{32,16},{48,32},{64,48},{80,64},{96,80},{112,96},{17,1},{33... | collective-permute-start | bytes 393224 | tf_op jit(solution)/shard_map/ppermute | solution.py:203
  156.3 2.1 collective-permute-start.19
  158.7 3.8 %collective-permute-done.19 = f32[1,16,2048]{2,1,0:T(8,128)S(1)} collective-permute-done((f32[1,16,2048]{2,1,0:T(8,128)S(1)}, f32[1,16,2048]{2,1,0:T(8,128)S(1)}, u32[]{:S(2)}, u32[]{:S(2)}) %collective-permute-start.19) | collective-permute-done | bytes 131104 | tf_op jit(solution)/shard_map/ppermute | solution.py:202
  162.9 30.7 %while.38 = (s32[]{:T(128)}, f32[8,3,512]{2,1,0:T(4,128)}, s32[8,512]{1,0:T(8,128)S(1)}, f32[3,128,2048]{2,1,0:T(8,128)S(1)}, s32[]{:T(128)}) while((s32[]{:T(128)}, f32[8,3,512]{2,1,0:T(4,128)}, s32[8,512]{1,0:T(8,128)S(1)}, f32[3,128,2048]{2,1,0:T(8,128)S(1)}, s32[]{:T(128)}) %tuple.131), condition=%wide.region_8.9_spmd, body=%wide.region_6.8_spmd.sunk | while | flops 4833419264 | bytes 3705409 | solution.py:117
  163.0 3.2 %fusion.125 = f32[3,512]{1,0:T(4,128)S(1)} fusion(f32[3,128,2048]{2,1,0:T(8,128)S(1)} %get-tuple-element.418, s32[512]{0:T(512)S(1)} %get-tuple-element.364, f32[128,512]{1,0:T(8,128)S(1)} %fusion.124), kind=kOutput, calls=%fused_computation.28.clone.1 | convolution fusion | flops 4833278464 | bytes 3416064 | tf_op jit(solution)/shard_map/while/body/eval_jaxpr/srx,mx->srm/dot_general | solution.py:114
  166.8 3.2 %fusion.125 = f32[3,512]{1,0:T(4,128)S(1)} fusion(f32[3,128,2048]{2,1,0:T(8,128)S(1)} %get-tuple-element.418, s32[512]{0:T(512)S(1)} %get-tuple-element.364, f32[128,512]{1,0:T(8,128)S(1)} %fusion.124), kind=kOutput, calls=%fused_computation.28.clone.1 | convolution fusion | flops 4833278464 | bytes 3416064 | tf_op jit(solution)/shard_map/while/body/eval_jaxpr/srx,mx->srm/dot_general | solution.py:114
  170.6 3.2 %fusion.125 = f32[3,512]{1,0:T(4,128)S(1)} fusion(f32[3,128,2048]{2,1,0:T(8,128)S(1)} %get-tuple-element.418, s32[512]{0:T(512)S(1)} %get-tuple-element.364, f32[128,512]{1,0:T(8,128)S(1)} %fusion.124), kind=kOutput, calls=%fused_computation.28.clone.1 | convolution fusion | flops 4833278464 | bytes 3416064 | tf_op jit(solution)/shard_map/while/body/eval_jaxpr/srx,mx->srm/dot_general | solution.py:114
  174.5 3.2 %fusion.125 = f32[3,512]{1,0:T(4,128)S(1)} fusion(f32[3,128,2048]{2,1,0:T(8,128)S(1)} %get-tuple-element.418, s32[512]{0:T(512)S(1)} %get-tuple-element.364, f32[128,512]{1,0:T(8,128)S(1)} %fusion.124), kind=kOutput, calls=%fused_computation.28.clone.1 | convolution fusion | flops 4833278464 | bytes 3416064 | tf_op jit(solution)/shard_map/while/body/eval_jaxpr/srx,mx->srm/dot_general | solution.py:114
  178.3 3.2 %fusion.125 = f32[3,512]{1,0:T(4,128)S(1)} fusion(f32[3,128,2048]{2,1,0:T(8,128)S(1)} %get-tuple-element.418, s32[512]{0:T(512)S(1)} %get-tuple-element.364, f32[128,512]{1,0:T(8,128)S(1)} %fusion.124), kind=kOutput, calls=%fused_computation.28.clone.1 | convolution fusion | flops 4833278464 | bytes 3416064 | tf_op jit(solution)/shard_map/while/body/eval_jaxpr/srx,mx->srm/dot_general | solution.py:114
  182.2 3.2 %fusion.125 = f32[3,512]{1,0:T(4,128)S(1)} fusion(f32[3,128,2048]{2,1,0:T(8,128)S(1)} %get-tuple-element.418, s32[512]{0:T(512)S(1)} %get-tuple-element.364, f32[128,512]{1,0:T(8,128)S(1)} %fusion.124), kind=kOutput, calls=%fused_computation.28.clone.1 | convolution fusion | flops 4833278464 | bytes 3416064 | tf_op jit(solution)/shard_map/while/body/eval_jaxpr/srx,mx->srm/dot_general | solution.py:114
  186.0 3.2 %fusion.125 = f32[3,512]{1,0:T(4,128)S(1)} fusion(f32[3,128,2048]{2,1,0:T(8,128)S(1)} %get-tuple-element.418, s32[512]{0:T(512)S(1)} %get-tuple-element.364, f32[128,512]{1,0:T(8,128)S(1)} %fusion.124), kind=kOutput, calls=%fused_computation.28.clone.1 | convolution fusion | flops 4833278464 | bytes 3416064 | tf_op jit(solution)/shard_map/while/body/eval_jaxpr/srx,mx->srm/dot_general | solution.py:114
  189.8 3.2 %fusion.125 = f32[3,512]{1,0:T(4,128)S(1)} fusion(f32[3,128,2048]{2,1,0:T(8,128)S(1)} %get-tuple-element.418, s32[512]{0:T(512)S(1)} %get-tuple-element.364, f32[128,512]{1,0:T(8,128)S(1)} %fusion.124), kind=kOutput, calls=%fused_computation.28.clone.1 | convolution fusion | flops 4833278464 | bytes 3416064 | tf_op jit(solution)/shard_map/while/body/eval_jaxpr/srx,mx->srm/dot_general | solution.py:114
  193.6 12.1 %all-to-all-start.1 = ((f32[3,16,256]{2,0,1:T(4,128)}), f32[3,16,256]{2,0,1:T(4,128)S(1)}, u32[]{:S(2)}, u32[]{:S(2)}) async-start(f32[3,16,256]{2,0,1:T(4,128)} %bitcast.42), calls=%async_computation.1 | async-start | bytes 131072 | tf_op jit(solution)/shard_map/all_to_all | solution.py:303
  206.3 4.0 %copy.80.cols_ref = f32[24,4,128,1]{3,2,1,0:T(8,128)} copy(f32[24,4,128,1]{2,1,0,3:T(4,128)S(1)} %get-tuple-element.269) | data formatting | bytes 98304 | tf_op jit(solution)/shard_map/broadcast_in_dim | solution.py:180
  210.4 22.3 %shard_map.167 = f32[16,3,128]{2,1,0:T(4,128)} custom-call(s32[128]{0:T(128)} %reshape.805.chosen_ref, f32[24,4,128]{2,1,0:T(4,128)} %get-tuple-element.270.rows_ref, f32[24,4,128,1]{3,2,1,0:T(8,128)} %copy.80.cols_ref), custom_call_target="tpu_custom_call" | custom-call | flops 54525952 | bytes 49152 | tf_op jit(solution)/shard_map/pallas_call | solution.py:182
  (252 shorter events, 30.4 us)
Async XLA Ops:
  8.7 0.9 copy-start.6
  9.0 10.4 %copy-start.5 = (f32[2048]{0:T(1024)S(1)}, f32[2048]{0:T(1024)}, u32[]{:S(2)}) copy-start(f32[2048]{0:T(1024)} %param.23) | copy-start | bytes 24580
  9.0 10.4 %copy-start.1 = (f32[3,2048]{1,0:T(4,128)S(1)}, f32[3,2048]{1,0:T(4,128)}, u32[]{:S(2)}) copy-start(f32[3,2048]{1,0:T(4,128)} %param.22) | copy-start | bytes 73732
  9.3 13.5 %slice-start = ((f32[2,8,16,2048]{3,2,1,0:T(8,128)}), f32[1,8,16,2048]{3,2,1,0:T(8,128)S(1)}, s32[]{:S(2)}) async-start(f32[2,8,16,2048]{3,2,1,0:T(8,128)} %param.29), calls=%async_computation.2 | async-start | bytes 2097152 | tf_op jit(solution)/shard_map/slice | solution.py:283
  10.4 14.7 %all-to-all-start = ((f32[2,16,256]{2,0,1:T(2,128)}), f32[2,16,256]{2,0,1:T(2,128)S(1)}, u32[]{:S(2)}, u32[]{:S(2)}) async-start(f32[2,16,256]{2,0,1:T(2,128)} %fusion.80), calls=%async_computation | async-start | bytes 65536 | tf_op jit(solution)/shard_map/all_to_all | solution.py:278
  19.4 186.3 %collective-permute-start = (f32[4,512]{1,0:T(4,128)S(1)}, f32[4,512]{1,0:T(4,128)S(1)}, u32[]{:S(2)}, u32[]{:S(2)}) collective-permute-start(f32[4,512]{1,0:T(4,128)S(1)} %get-tuple-element.271), channel_id=1, source_target_pairs={{0,1},{1,2},{2,3},{3,4},{4,5},{5,6},{6,7},{7,8},{8,9},{9,10},{10,1... | collective-permute-start | bytes 24584 | tf_op jit(solution)/shard_map/ppermute | solution.py:33
  23.0 1.3 copy-start.7
  67.7 14.9 %collective-permute-start.2 = (f32[2,1,16,2048]{3,2,1,0:T(8,128)S(1)}, f32[2,1,16,2048]{3,2,1,0:T(8,128)S(1)}, u32[]{:S(2)}, u32[]{:S(2)}) collective-permute-start(f32[2,1,16,2048]{3,2,1,0:T(8,128)S(1)} %get-tuple-element.259), channel_id=1, source_target_pairs={{16,0},{32,16},{48,32},{64,48},{80,64},{96,80},{112,96},{17,1},{33... | collective-permute-start | bytes 786440 | tf_op jit(solution)/shard_map/ppermute | solution.py:203
  69.8 12.8 %collective-permute-start.3 = (f32[2,1,16,2048]{3,2,1,0:T(8,128)S(1)}, f32[2,1,16,2048]{3,2,1,0:T(8,128)S(1)}, u32[]{:S(2)}, u32[]{:S(2)}) collective-permute-start(f32[2,1,16,2048]{3,2,1,0:T(8,128)S(1)} %get-tuple-element.258), channel_id=1, source_target_pairs={{0,16},{16,32},{32,48},{48,64},{64,80},{80,96},{96,112},{1,17},{17... | collective-permute-start | bytes 786440 | tf_op jit(solution)/shard_map/ppermute | solution.py:202
  72.3 6.9 %collective-permute-start.4 = (f32[2,8,1,2048]{3,1,2,0:T(8,128)S(1)}, f32[2,8,1,2048]{3,1,2,0:T(8,128)S(1)}, u32[]{:S(2)}, u32[]{:S(2)}) collective-permute-start(f32[2,8,1,2048]{3,1,2,0:T(8,128)S(1)} %copy.85), channel_id=1, source_target_pairs={{1,0},{2,1},{3,2},{4,3},{5,4},{6,5},{7,6},{8,7},{9,8},{10,9},{11,1... | collective-permute-start | bytes 393224 | tf_op jit(solution)/shard_map/ppermute | solution.py:203
  75.6 7.0 %copy-start.3 = (f32[2]{0:T(128)S(1)}, f32[2]{0:T(128)}, u32[]{:S(2)}) copy-start(f32[2]{0:T(128)} %constant.224.clone) | copy-start | bytes 28
  75.6 7.0 %copy-start.4 = (f32[2]{0:T(128)S(1)}, f32[2]{0:T(128)}, u32[]{:S(2)}) copy-start(f32[2]{0:T(128)} %constant.225.clone) | copy-start | bytes 28
  75.6 6.9 %collective-permute-start.5 = (f32[2,8,1,2048]{3,1,2,0:T(8,128)S(1)}, f32[2,8,1,2048]{3,1,2,0:T(8,128)S(1)}, u32[]{:S(2)}, u32[]{:S(2)}) collective-permute-start(f32[2,8,1,2048]{3,1,2,0:T(8,128)S(1)} %copy.87), channel_id=1, source_target_pairs={{0,1},{1,2},{2,3},{3,4},{4,5},{5,6},{6,7},{7,8},{8,9},{9,10},{10,1... | collective-permute-start | bytes 393224 | tf_op jit(solution)/shard_map/ppermute | solution.py:202
  85.5 14.0 %collective-permute-start.6 = (f32[2,1,16,2048]{3,2,1,0:T(8,128)S(1)}, f32[2,1,16,2048]{3,2,1,0:T(8,128)S(1)}, u32[]{:S(2)}, u32[]{:S(2)}) collective-permute-start(f32[2,1,16,2048]{3,2,1,0:T(8,128)S(1)} %get-tuple-element.251), channel_id=1, source_target_pairs={{16,0},{32,16},{48,32},{64,48},{80,64},{96,80},{112,96},{17,1},{33... | collective-permute-start | bytes 786440 | tf_op jit(solution)/shard_map/ppermute | solution.py:203
  88.6 11.0 %collective-permute-start.7 = (f32[2,1,16,2048]{3,2,1,0:T(8,128)S(1)}, f32[2,1,16,2048]{3,2,1,0:T(8,128)S(1)}, u32[]{:S(2)}, u32[]{:S(2)}) collective-permute-start(f32[2,1,16,2048]{3,2,1,0:T(8,128)S(1)} %get-tuple-element.250), channel_id=1, source_target_pairs={{0,16},{16,32},{32,48},{48,64},{64,80},{80,96},{96,112},{1,17},{17... | collective-permute-start | bytes 786440 | tf_op jit(solution)/shard_map/ppermute | solution.py:202
  90.6 6.9 %collective-permute-start.8 = (f32[2,8,1,2048]{3,1,2,0:T(8,128)S(1)}, f32[2,8,1,2048]{3,1,2,0:T(8,128)S(1)}, u32[]{:S(2)}, u32[]{:S(2)}) collective-permute-start(f32[2,8,1,2048]{3,1,2,0:T(8,128)S(1)} %copy.89), channel_id=1, source_target_pairs={{1,0},{2,1},{3,2},{4,3},{5,4},{6,5},{7,6},{8,7},{9,8},{10,9},{11,1... | collective-permute-start | bytes 393224 | tf_op jit(solution)/shard_map/ppermute | solution.py:203
  92.6 6.9 %collective-permute-start.9 = (f32[2,8,1,2048]{3,1,2,0:T(8,128)S(1)}, f32[2,8,1,2048]{3,1,2,0:T(8,128)S(1)}, u32[]{:S(2)}, u32[]{:S(2)}) collective-permute-start(f32[2,8,1,2048]{3,1,2,0:T(8,128)S(1)} %copy.91), channel_id=1, source_target_pairs={{0,1},{1,2},{2,3},{3,4},{4,5},{5,6},{6,7},{7,8},{8,9},{9,10},{10,1... | collective-permute-start | bytes 393224 | tf_op jit(solution)/shard_map/ppermute | solution.py:202
  102.5 15.1 %collective-permute-start.10 = (f32[2,1,16,2048]{3,2,1,0:T(8,128)S(1)}, f32[2,1,16,2048]{3,2,1,0:T(8,128)S(1)}, u32[]{:S(2)}, u32[]{:S(2)}) collective-permute-start(f32[2,1,16,2048]{3,2,1,0:T(8,128)S(1)} %get-tuple-element.243), channel_id=1, source_target_pairs={{16,0},{32,16},{48,32},{64,48},{80,64},{96,80},{112,96},{17,1},{33... | collective-permute-start | bytes 786440 | tf_op jit(solution)/shard_map/ppermute | solution.py:203
  106.6 11.0 %collective-permute-start.11 = (f32[2,1,16,2048]{3,2,1,0:T(8,128)S(1)}, f32[2,1,16,2048]{3,2,1,0:T(8,128)S(1)}, u32[]{:S(2)}, u32[]{:S(2)}) collective-permute-start(f32[2,1,16,2048]{3,2,1,0:T(8,128)S(1)} %get-tuple-element.242), channel_id=1, source_target_pairs={{0,16},{16,32},{32,48},{48,64},{64,80},{80,96},{96,112},{1,17},{17... | collective-permute-start | bytes 786440 | tf_op jit(solution)/shard_map/ppermute | solution.py:202
  108.6 6.9 %collective-permute-start.12 = (f32[2,8,1,2048]{3,1,2,0:T(8,128)S(1)}, f32[2,8,1,2048]{3,1,2,0:T(8,128)S(1)}, u32[]{:S(2)}, u32[]{:S(2)}) collective-permute-start(f32[2,8,1,2048]{3,1,2,0:T(8,128)S(1)} %copy.93), channel_id=1, source_target_pairs={{1,0},{2,1},{3,2},{4,3},{5,4},{6,5},{7,6},{8,7},{9,8},{10,9},{11,1... | collective-permute-start | bytes 393224 | tf_op jit(solution)/shard_map/ppermute | solution.py:203
  110.6 6.9 %collective-permute-start.13 = (f32[2,8,1,2048]{3,1,2,0:T(8,128)S(1)}, f32[2,8,1,2048]{3,1,2,0:T(8,128)S(1)}, u32[]{:S(2)}, u32[]{:S(2)}) collective-permute-start(f32[2,8,1,2048]{3,1,2,0:T(8,128)S(1)} %copy.95), channel_id=1, source_target_pairs={{0,1},{1,2},{2,3},{3,4},{4,5},{5,6},{6,7},{7,8},{8,9},{9,10},{10,1... | collective-permute-start | bytes 393224 | tf_op jit(solution)/shard_map/ppermute | solution.py:202
  120.5 20.0 %collective-permute-start.14 = (f32[2,1,16,2048]{3,2,1,0:T(8,128)S(1)}, f32[2,1,16,2048]{3,2,1,0:T(8,128)S(1)}, u32[]{:S(2)}, u32[]{:S(2)}) collective-permute-start(f32[2,1,16,2048]{3,2,1,0:T(8,128)S(1)} %get-tuple-element.235), channel_id=1, source_target_pairs={{16,0},{32,16},{48,32},{64,48},{80,64},{96,80},{112,96},{17,1},{33... | collective-permute-start | bytes 786440 | tf_op jit(solution)/shard_map/ppermute | solution.py:203
  124.0 16.4 %collective-permute-start.15 = (f32[2,1,16,2048]{3,2,1,0:T(8,128)S(1)}, f32[2,1,16,2048]{3,2,1,0:T(8,128)S(1)}, u32[]{:S(2)}, u32[]{:S(2)}) collective-permute-start(f32[2,1,16,2048]{3,2,1,0:T(8,128)S(1)} %get-tuple-element.234), channel_id=1, source_target_pairs={{0,16},{16,32},{32,48},{48,64},{64,80},{80,96},{96,112},{1,17},{17... | collective-permute-start | bytes 786440 | tf_op jit(solution)/shard_map/ppermute | solution.py:202
  126.0 7.3 %collective-permute-start.17 = (f32[2,8,1,2048]{3,1,2,0:T(8,128)S(1)}, f32[2,8,1,2048]{3,1,2,0:T(8,128)S(1)}, u32[]{:S(2)}, u32[]{:S(2)}) collective-permute-start(f32[2,8,1,2048]{3,1,2,0:T(8,128)S(1)} %copy.99), channel_id=1, source_target_pairs={{0,1},{1,2},{2,3},{3,4},{4,5},{5,6},{6,7},{7,8},{8,9},{9,10},{10,1... | collective-permute-start | bytes 393224 | tf_op jit(solution)/shard_map/ppermute | solution.py:202
  130.9 9.4 %collective-permute-start.16 = (f32[2,8,1,2048]{3,1,2,0:T(8,128)S(1)}, f32[2,8,1,2048]{3,1,2,0:T(8,128)S(1)}, u32[]{:S(2)}, u32[]{:S(2)}) collective-permute-start(f32[2,8,1,2048]{3,1,2,0:T(8,128)S(1)} %copy.97), channel_id=1, source_target_pairs={{1,0},{2,1},{3,2},{4,3},{5,4},{6,5},{7,6},{8,7},{9,8},{10,9},{11,1... | collective-permute-start | bytes 393224 | tf_op jit(solution)/shard_map/ppermute | solution.py:203
  133.3 72.4 %collective-permute-start.1 = (f32[4,512]{1,0:T(4,128)S(1)}, f32[4,512]{1,0:T(4,128)S(1)}, u32[]{:S(2)}, u32[]{:S(2)}) collective-permute-start(f32[4,512]{1,0:T(4,128)S(1)} %get-tuple-element.272), channel_id=1, source_target_pairs={{1,0},{2,1},{3,2},{4,3},{5,4},{6,5},{7,6},{8,7},{9,8},{10,9},{11,1... | collective-permute-start | bytes 24584 | tf_op jit(solution)/shard_map/ppermute | solution.py:36
  142.7 1.3 copy-start
  144.3 11.9 %collective-permute-start.20 = (f32[8,1,2048]{2,1,0:T(1,128)S(1)}, f32[8,1,2048]{2,1,0:T(1,128)S(1)}, u32[]{:S(2)}, u32[]{:S(2)}) collective-permute-start(f32[8,1,2048]{2,1,0:T(1,128)S(1)} %get-tuple-element.263), channel_id=1, source_target_pairs={{1,0},{2,1},{3,2},{4,3},{5,4},{6,5},{7,6},{8,7},{9,8},{10,9},{11,1... | collective-permute-start | bytes 196616 | tf_op jit(solution)/shard_map/ppermute | solution.py:203
  146.3 12.1 %collective-permute-start.21 = (f32[8,1,2048]{2,1,0:T(1,128)S(1)}, f32[8,1,2048]{2,1,0:T(1,128)S(1)}, u32[]{:S(2)}, u32[]{:S(2)}) collective-permute-start(f32[8,1,2048]{2,1,0:T(1,128)S(1)} %get-tuple-element.262), channel_id=1, source_target_pairs={{0,1},{1,2},{2,3},{3,4},{4,5},{5,6},{6,7},{7,8},{8,9},{9,10},{10,1... | collective-permute-start | bytes 196616 | tf_op jit(solution)/shard_map/ppermute | solution.py:202
  153.1 5.7 %collective-permute-start.18 = (f32[1,16,2048]{2,1,0:T(8,128)S(1)}, f32[1,16,2048]{2,1,0:T(8,128)S(1)}, u32[]{:S(2)}, u32[]{:S(2)}) collective-permute-start(f32[1,16,2048]{2,1,0:T(8,128)S(1)} %get-tuple-element.227), channel_id=1, source_target_pairs={{16,0},{32,16},{48,32},{64,48},{80,64},{96,80},{112,96},{17,1},{33... | collective-permute-start | bytes 393224 | tf_op jit(solution)/shard_map/ppermute | solution.py:203
  156.3 6.3 %collective-permute-start.19 = (f32[1,16,2048]{2,1,0:T(8,128)S(1)}, f32[1,16,2048]{2,1,0:T(8,128)S(1)}, u32[]{:S(2)}, u32[]{:S(2)}) collective-permute-start(f32[1,16,2048]{2,1,0:T(8,128)S(1)} %get-tuple-element.226), channel_id=1, source_target_pairs={{0,16},{16,32},{32,48},{48,64},{64,80},{80,96},{96,112},{1,17},{17... | collective-permute-start | bytes 393224 | tf_op jit(solution)/shard_map/ppermute | solution.py:202
  193.6 39.1 %all-to-all-start.1 = ((f32[3,16,256]{2,0,1:T(4,128)}), f32[3,16,256]{2,0,1:T(4,128)S(1)}, u32[]{:S(2)}, u32[]{:S(2)}) async-start(f32[3,16,256]{2,0,1:T(4,128)} %bitcast.42), calls=%async_computation.1 | async-start | bytes 131072 | tf_op jit(solution)/shard_map/all_to_all | solution.py:303
  236.9 0.8 copy-start.2

commit v9 on v7

--- a/solution.py
+++ b/solution.py
@@ -22,7 +22,7 @@
 ADHERE_RANGE = 4.0
 FORCE_SCALE = 0.08
 CHEMOTAXIS = 1.5
-SLOT_BLOCK = 512
+SLOT_BLOCK = 256
 
 
 def with_halo(block, sides, width):
@@ -281,7 +281,7 @@
     species, depth, rows, columns = field.shape
     planes = depth * rows
     oxygen_rows = field[0].reshape(1, planes, columns)
-    oxygen = pick_exact(oxygen_rows, reached, 2 * SLOT_BLOCK)[0]
+    oxygen = pick_exact(oxygen_rows, reached, 4 * SLOT_BLOCK)[0]
     consume = rates * oxygen / (MICHAELIS_HALF + oxygen)
     secrete = SECRETION * rates * HYPOXIA_HALF / (HYPOXIA_HALF + oxygen)
     amounts = jnp.stack([-STEP_TIME * consume, STEP_TIME * secrete])

time: 224 us -> 241 us (1.076)
  matrix products: 63.3 us -> 74.9 us
  local copies, waits for them, and re-layouts: 21.9 us -> 26.8 us
    dot_general x8 -> x16, matrix products: 24.1 us -> 30.1 us  [add_piece(): jnp.einsum('smr,mx->srx', weighted, column_hot, precision=lax.Precision.H...]
    dot_general x8 -> x16, matrix products: 25.4 us -> 31 us  [one_piece(): jnp.einsum('srx,mx->srm', fields, column_hot, precision=lax.Precision.HIG...]
    dynamic_update_slice x8 -> x16, local copies, waits for them, and re-layouts: 4.81 us -> 9.55 us  [pick_voxels(): found = lax.map(one_piece, pieces)]
  transfers between devices with their start and end apart: 24 -> 24, of which waited for: 8 -> 8; matrix products, arithmetic and copies ran while one was open for 42% -> 46% of each run, Pallas kernels for 5% -> 5%
where the time goes in v9:
time: 241 us; the launch traced here: 240 us
  starting transfers between devices  84.9 us (35%)
  matrix products  74.9 us (31%)
  local copies, waits for them, and re-layouts  26.8 us (11%)
  other arithmetic  25.6 us (11%)
  waiting for transfers between devices  12.5 us (5%)
  Pallas kernels  11.9 us (5%)
    ppermute x10, starting transfers between devices, neighbours(): lax.ppermute(lax.slice_in_dim(block, block.shape[dim] - 1, None, axis=dim...  32.3 us
    dot_general x16, matrix products, one_piece(): jnp.einsum('srx,mx->srm', fields, column_hot, precision=lax.Precision.HIG...  31 us
    dot_general x16, matrix products, add_piece(): jnp.einsum('smr,mx->srx', weighted, column_hot, precision=lax.Precision.H...  30.1 us
    ppermute x10, starting transfers between devices, neighbours(): high = lax.ppermute(lax.slice_in_dim(block, 0, 1, axis=dim), axis, backward)  26.4 us
    dot_general x4, matrix products, one_piece(): jnp.einsum('psrx,mx->psrm', parts, column_hot, preferred_element_type=jnp...  13.8 us
    all_to_all x1, starting transfers between devices, local(): lax.all_to_all(slopes, 'tile', split_axis=1, concat_axis=1, tiled=True)  12.6 us
    pallas_call x1, Pallas kernels, pair_forces(): pl.pallas_call(force_kernel, out_shape=jax.ShapeDtypeStruct((blocks, 3, l...  11.9 us
    ppermute x10, waiting for transfers between devices, neighbours(): lax.ppermute(lax.slice_in_dim(block, block.shape[dim] - 1, None, axis=dim...  10.6 us
  transfers between devices with their start and end apart: 24, of which 8 were waited for; matrix products, arithmetic and copies ran while one was open for 46% of the time, Pallas kernels for 5%

profile of v9, /device:TPU:26, one launch (start us, length us, event | category | flops | bytes accessed | tf_op | source)
XLA Modules:
  0.0 240.2 jit_solution(16862167049658917612)
XLA Ops:
  10.4 8.3 %all-to-all-start = ((f32[2,16,256]{2,0,1:T(2,128)}), f32[2,16,256]{2,0,1:T(2,128)S(1)}, u32[]{:S(2)}, u32[]{:S(2)}) async-start(f32[2,16,256]{2,0,1:T(2,128)} %fusion.74), calls=%async_computation | async-start | bytes 65536 | tf_op jit(solution)/shard_map/all_to_all | solution.py:278
  19.4 3.4 %collective-permute-start = (f32[4,512]{1,0:T(4,128)S(1)}, f32[4,512]{1,0:T(4,128)S(1)}, u32[]{:S(2)}, u32[]{:S(2)}) collective-permute-start(f32[4,512]{1,0:T(4,128)S(1)} %get-tuple-element.279), channel_id=1, source_target_pairs={{0,1},{1,2},{2,3},{3,4},{4,5},{5,6},{6,7},{7,8},{8,9},{9,10},{10,1... | collective-permute-start | bytes 24584 | tf_op jit(solution)/shard_map/ppermute | solution.py:33
  25.2 14.7 %while.37 = (s32[]{:T(128)}, f32[4,1,1024]{2,1,0:T(1,128)S(1)}, s32[4,1024]{1,0:T(4,128)S(1)}, bf16[3,1,128,2048]{3,2,0,1:T(8,128)(2,1)}, s32[]{:T(128)}) while((s32[]{:T(128)}, f32[4,1,1024]{2,1,0:T(1,128)S(1)}, s32[4,1024]{1,0:T(4,128)S(1)}, bf16[3,1,128,2048]{3,2,0,1:T(8,128)(2,1)}, s32[]{:T(128)}) %tuple.124), condition=%wide.region_3.4_spmd, body=%wide.region_1.3_spmd.sunk | while | flops 1613645824 | bytes 4759621 | solution.py:104
  25.2 3.5 %fusion.113 = f32[3,128,1024]{2,1,0:T(8,128)S(1)} fusion(bf16[3,1,128,2048]{3,2,0,1:T(8,128)(2,1)} %get-tuple-element.392, s32[1024]{0:T(1024)S(1)} %get-tuple-element.365), kind=kOutput, calls=%fused_computation.5.clone.1 | convolution fusion | flops 1612709888 | bytes 3149824 | tf_op jit(solution)/shard_map/while/body/eval_jaxpr/psrx,mx->psrm/dot_general | solution.py:98
  28.9 3.5 %fusion.113 = f32[3,128,1024]{2,1,0:T(8,128)S(1)} fusion(bf16[3,1,128,2048]{3,2,0,1:T(8,128)(2,1)} %get-tuple-element.392, s32[1024]{0:T(1024)S(1)} %get-tuple-element.365), kind=kOutput, calls=%fused_computation.5.clone.1 | convolution fusion | flops 1612709888 | bytes 3149824 | tf_op jit(solution)/shard_map/while/body/eval_jaxpr/psrx,mx->psrm/dot_general | solution.py:98
  32.6 3.5 %fusion.113 = f32[3,128,1024]{2,1,0:T(8,128)S(1)} fusion(bf16[3,1,128,2048]{3,2,0,1:T(8,128)(2,1)} %get-tuple-element.392, s32[1024]{0:T(1024)S(1)} %get-tuple-element.365), kind=kOutput, calls=%fused_computation.5.clone.1 | convolution fusion | flops 1612709888 | bytes 3149824 | tf_op jit(solution)/shard_map/while/body/eval_jaxpr/psrx,mx->psrm/dot_general | solution.py:98
  36.3 3.5 %fusion.113 = f32[3,128,1024]{2,1,0:T(8,128)S(1)} fusion(bf16[3,1,128,2048]{3,2,0,1:T(8,128)(2,1)} %get-tuple-element.392, s32[1024]{0:T(1024)S(1)} %get-tuple-element.365), kind=kOutput, calls=%fused_computation.5.clone.1 | convolution fusion | flops 1612709888 | bytes 3149824 | tf_op jit(solution)/shard_map/while/body/eval_jaxpr/psrx,mx->psrm/dot_general | solution.py:98
  40.1 31.8 %while.39 = (s32[]{:T(128)}, f32[2,128,2048]{2,1,0:T(8,128)S(1)}, f32[16,2,256]{2,1,0:T(2,128)S(1)}, s32[16,256]{1,0:T(8,128)S(1)}, s32[]{:T(128)}, /*index=5*/s32[]{:T(128)}) while((s32[]{:T(128)}, f32[2,128,2048]{2,1,0:T(8,128)S(1)}, f32[16,2,256]{2,1,0:T(2,128)S(1)}, s32[16,256]{1,0:T(8,128)S(1)}, s32[]{:T(128)}, ...), condition=%wide.region_5.6_spmd.clone, body=%wide.region_4.5_spmd.clone.sunk | while | flops 1612321536 | bytes 4469847 | solution.py:137
  42.2 1.9 convolution_add_fusion.2
  44.1 1.9 convolution_add_fusion.2
  48.1 1.9 convolution_add_fusion.2
  50.1 1.9 convolution_add_fusion.2
  54.1 1.9 convolution_add_fusion.2
  56.0 1.9 convolution_add_fusion.2
  60.0 1.9 convolution_add_fusion.2
  62.0 1.9 convolution_add_fusion.2
  66.0 1.9 convolution_add_fusion.2
  74.4 1.9 collective-permute-start.2
  76.3 2.4 %collective-permute-start.3 = (f32[2,1,16,2048]{3,2,1,0:T(8,128)S(1)}, f32[2,1,16,2048]{3,2,1,0:T(8,128)S(1)}, u32[]{:S(2)}, u32[]{:S(2)}) collective-permute-start(f32[2,1,16,2048]{3,2,1,0:T(8,128)S(1)} %get-tuple-element.266), channel_id=1, source_target_pairs={{0,16},{16,32},{32,48},{48,64},{64,80},{80,96},{96,112},{1,17},{17... | collective-permute-start | bytes 786440 | tf_op jit(solution)/shard_map/ppermute | solution.py:202
  78.8 3.2 %collective-permute-start.4 = (f32[2,8,1,2048]{3,1,2,0:T(8,128)S(1)}, f32[2,8,1,2048]{3,1,2,0:T(8,128)S(1)}, u32[]{:S(2)}, u32[]{:S(2)}) collective-permute-start(f32[2,8,1,2048]{3,1,2,0:T(8,128)S(1)} %copy.47), channel_id=1, source_target_pairs={{1,0},{2,1},{3,2},{4,3},{5,4},{6,5},{7,6},{8,7},{9,8},{10,9},{11,1... | collective-permute-start | bytes 393224 | tf_op jit(solution)/shard_map/ppermute | solution.py:203
  82.1 2.8 %collective-permute-start.5 = (f32[2,8,1,2048]{3,1,2,0:T(8,128)S(1)}, f32[2,8,1,2048]{3,1,2,0:T(8,128)S(1)}, u32[]{:S(2)}, u32[]{:S(2)}) collective-permute-start(f32[2,8,1,2048]{3,1,2,0:T(8,128)S(1)} %copy.49), channel_id=1, source_target_pairs={{0,1},{1,2},{2,3},{3,4},{4,5},{5,6},{6,7},{7,8},{8,9},{9,10},{10,1... | collective-permute-start | bytes 393224 | tf_op jit(solution)/shard_map/ppermute | solution.py:202
  85.8 3.1 %collective-permute-done.5 = f32[2,8,1,2048]{3,1,2,0:T(8,128)S(1)} collective-permute-done((f32[2,8,1,2048]{3,1,2,0:T(8,128)S(1)}, f32[2,8,1,2048]{3,1,2,0:T(8,128)S(1)}, u32[]{:S(2)}, u32[]{:S(2)}) %collective-permute-start.5) | collective-permute-done | bytes 131104 | tf_op jit(solution)/shard_map/ppermute | solution.py:202
  89.1 2.2 fusion.41
  92.0 3.1 %collective-permute-start.6 = (f32[2,1,16,2048]{3,2,1,0:T(8,128)S(1)}, f32[2,1,16,2048]{3,2,1,0:T(8,128)S(1)}, u32[]{:S(2)}, u32[]{:S(2)}) collective-permute-start(f32[2,1,16,2048]{3,2,1,0:T(8,128)S(1)} %get-tuple-element.259), channel_id=1, source_target_pairs={{16,0},{32,16},{48,32},{64,48},{80,64},{96,80},{112,96},{17,1},{33... | collective-permute-start | bytes 786440 | tf_op jit(solution)/shard_map/ppermute | solution.py:203
  95.1 1.9 collective-permute-start.7
  97.1 1.9 collective-permute-start.8
  99.0 3.9 %collective-permute-start.9 = (f32[2,8,1,2048]{3,1,2,0:T(8,128)S(1)}, f32[2,8,1,2048]{3,1,2,0:T(8,128)S(1)}, u32[]{:S(2)}, u32[]{:S(2)}) collective-permute-start(f32[2,8,1,2048]{3,1,2,0:T(8,128)S(1)} %copy.53), channel_id=1, source_target_pairs={{0,1},{1,2},{2,3},{3,4},{4,5},{5,6},{6,7},{7,8},{8,9},{9,10},{10,1... | collective-permute-start | bytes 393224 | tf_op jit(solution)/shard_map/ppermute | solution.py:202
  106.1 2.2 fusion.47
  109.0 4.1 %collective-permute-start.10 = (f32[2,1,16,2048]{3,2,1,0:T(8,128)S(1)}, f32[2,1,16,2048]{3,2,1,0:T(8,128)S(1)}, u32[]{:S(2)}, u32[]{:S(2)}) collective-permute-start(f32[2,1,16,2048]{3,2,1,0:T(8,128)S(1)} %get-tuple-element.251), channel_id=1, source_target_pairs={{16,0},{32,16},{48,32},{64,48},{80,64},{96,80},{112,96},{17,1},{33... | collective-permute-start | bytes 786440 | tf_op jit(solution)/shard_map/ppermute | solution.py:203
  113.1 1.9 collective-permute-start.11
  115.1 1.9 collective-permute-start.12
  117.1 3.9 %collective-permute-start.13 = (f32[2,8,1,2048]{3,1,2,0:T(8,128)S(1)}, f32[2,8,1,2048]{3,1,2,0:T(8,128)S(1)}, u32[]{:S(2)}, u32[]{:S(2)}) collective-permute-start(f32[2,8,1,2048]{3,1,2,0:T(8,128)S(1)} %copy.57), channel_id=1, source_target_pairs={{0,1},{1,2},{2,3},{3,4},{4,5},{5,6},{6,7},{7,8},{8,9},{9,10},{10,1... | collective-permute-start | bytes 393224 | tf_op jit(solution)/shard_map/ppermute | solution.py:202
  124.1 2.2 fusion.53
  127.0 3.5 %collective-permute-start.14 = (f32[2,1,16,2048]{3,2,1,0:T(8,128)S(1)}, f32[2,1,16,2048]{3,2,1,0:T(8,128)S(1)}, u32[]{:S(2)}, u32[]{:S(2)}) collective-permute-start(f32[2,1,16,2048]{3,2,1,0:T(8,128)S(1)} %get-tuple-element.243), channel_id=1, source_target_pairs={{16,0},{32,16},{48,32},{64,48},{80,64},{96,80},{112,96},{17,1},{33... | collective-permute-start | bytes 786440 | tf_op jit(solution)/shard_map/ppermute | solution.py:203
  130.5 1.9 collective-permute-start.15
  132.5 1.9 collective-permute-start.16
  134.5 4.8 %collective-permute-start.17 = (f32[2,8,1,2048]{3,1,2,0:T(8,128)S(1)}, f32[2,8,1,2048]{3,1,2,0:T(8,128)S(1)}, u32[]{:S(2)}, u32[]{:S(2)}) collective-permute-start(f32[2,8,1,2048]{3,1,2,0:T(8,128)S(1)} %copy.61), channel_id=1, source_target_pairs={{0,1},{1,2},{2,3},{3,4},{4,5},{5,6},{6,7},{7,8},{8,9},{9,10},{10,1... | collective-permute-start | bytes 393224 | tf_op jit(solution)/shard_map/ppermute | solution.py:202
  140.3 1.9 collective-permute-start.1
  142.5 2.2 fusion.59
  146.4 1.9 collective-permute-start.20
  148.3 6.5 %collective-permute-start.21 = (f32[8,1,2048]{2,1,0:T(1,128)S(1)}, f32[8,1,2048]{2,1,0:T(1,128)S(1)}, u32[]{:S(2)}, u32[]{:S(2)}) collective-permute-start(f32[8,1,2048]{2,1,0:T(1,128)S(1)} %get-tuple-element.270), channel_id=1, source_target_pairs={{0,1},{1,2},{2,3},{3,4},{4,5},{5,6},{6,7},{7,8},{8,9},{9,10},{10,1... | collective-permute-start | bytes 196616 | tf_op jit(solution)/shard_map/ppermute | solution.py:202
  155.4 2.9 %collective-permute-start.18 = (f32[1,16,2048]{2,1,0:T(8,128)S(1)}, f32[1,16,2048]{2,1,0:T(8,128)S(1)}, u32[]{:S(2)}, u32[]{:S(2)}) collective-permute-start(f32[1,16,2048]{2,1,0:T(8,128)S(1)} %get-tuple-element.235), channel_id=1, source_target_pairs={{16,0},{32,16},{48,32},{64,48},{80,64},{96,80},{112,96},{17,1},{33... | collective-permute-start | bytes 393224 | tf_op jit(solution)/shard_map/ppermute | solution.py:203
  158.3 2.1 collective-permute-start.19
  160.8 3.8 %collective-permute-done.19 = f32[1,16,2048]{2,1,0:T(8,128)S(1)} collective-permute-done((f32[1,16,2048]{2,1,0:T(8,128)S(1)}, f32[1,16,2048]{2,1,0:T(8,128)S(1)}, u32[]{:S(2)}, u32[]{:S(2)}) %collective-permute-start.19) | collective-permute-done | bytes 131104 | tf_op jit(solution)/shard_map/ppermute | solution.py:202
  165.0 41.3 %while.38 = (s32[]{:T(128)}, f32[16,3,256]{2,1,0:T(4,128)}, s32[16,256]{1,0:T(8,128)S(1)}, f32[3,128,2048]{2,1,0:T(8,128)S(1)}, s32[]{:T(128)}) while((s32[]{:T(128)}, f32[16,3,256]{2,1,0:T(4,128)}, s32[16,256]{1,0:T(8,128)S(1)}, f32[3,128,2048]{2,1,0:T(8,128)S(1)}, s32[]{:T(128)}) %tuple.134), condition=%wide.region_8.9_spmd, body=%wide.region_6.8_spmd.sunk | while | flops 2416709632 | bytes 3425857 | solution.py:117
  165.0 1.9 fusion.118
  167.6 1.9 fusion.118
  170.2 1.9 fusion.118
  172.8 1.9 fusion.118
  175.4 1.9 fusion.118
  177.9 1.9 fusion.118
  180.5 1.9 fusion.118
  183.1 1.9 fusion.118
  185.7 1.9 fusion.118
  188.2 1.9 fusion.118
  190.8 1.9 fusion.118
  193.4 1.9 fusion.118
  196.0 1.9 fusion.118
  198.6 1.9 fusion.118
  201.1 1.9 fusion.118
  203.7 1.9 fusion.118
  206.2 12.6 %all-to-all-start.1 = ((f32[3,16,256]{2,0,1:T(4,128)}), f32[3,16,256]{2,0,1:T(4,128)S(1)}, u32[]{:S(2)}, u32[]{:S(2)}) async-start(f32[3,16,256]{2,0,1:T(4,128)} %bitcast.41), calls=%async_computation.1 | async-start | bytes 131072 | tf_op jit(solution)/shard_map/all_to_all | solution.py:303
  218.9 3.8 %broadcast_in_dim.243.cols_ref = f32[24,4,128,128]{3,2,1,0:T(8,128)} broadcast(f32[24,4,128]{2,1,0:T(4,128)S(1)} %maximum_bitcast_fusion.rows_ref), dimensions={0,1,2} | broadcast | bytes 6340608 | tf_op jit(solution)/shard_map/broadcast_in_dim | solution.py:180
  222.7 11.9 %shard_map.167 = f32[16,3,128]{2,1,0:T(4,128)} custom-call(s32[128]{0:T(128)} %reshape.768.chosen_ref, f32[24,4,128]{2,1,0:T(4,128)} %copy-done.1, f32[24,4,128,128]{3,2,1,0:T(8,128)} %broadcast_in_dim.243.cols_ref), custom_call_target="tpu_custom_call" | custom-call | flops 54525952 | bytes 6291456 | tf_op jit(solution)/shard_map/pallas_call | solution.py:182
  (322 shorter events, 58.6 us)
Async XLA Ops:
  8.7 0.9 copy-start.7
  9.0 10.4 %copy-start.6 = (f32[2048]{0:T(1024)S(1)}, f32[2048]{0:T(1024)}, u32[]{:S(2)}) copy-start(f32[2048]{0:T(1024)} %param.23) | copy-start | bytes 24580
  9.0 10.4 %copy-start.2 = (f32[3,2048]{1,0:T(4,128)S(1)}, f32[3,2048]{1,0:T(4,128)}, u32[]{:S(2)}) copy-start(f32[3,2048]{1,0:T(4,128)} %param.22) | copy-start | bytes 73732
  9.3 13.5 %slice-start = ((f32[2,8,16,2048]{3,2,1,0:T(8,128)}), f32[1,8,16,2048]{3,2,1,0:T(8,128)S(1)}, s32[]{:S(2)}) async-start(f32[2,8,16,2048]{3,2,1,0:T(8,128)} %param.29), calls=%async_computation.2 | async-start | bytes 2097152 | tf_op jit(solution)/shard_map/slice | solution.py:283
  10.4 14.7 %all-to-all-start = ((f32[2,16,256]{2,0,1:T(2,128)}), f32[2,16,256]{2,0,1:T(2,128)S(1)}, u32[]{:S(2)}, u32[]{:S(2)}) async-start(f32[2,16,256]{2,0,1:T(2,128)} %fusion.74), calls=%async_computation | async-start | bytes 65536 | tf_op jit(solution)/shard_map/all_to_all | solution.py:278
  19.4 199.4 %collective-permute-start = (f32[4,512]{1,0:T(4,128)S(1)}, f32[4,512]{1,0:T(4,128)S(1)}, u32[]{:S(2)}, u32[]{:S(2)}) collective-permute-start(f32[4,512]{1,0:T(4,128)S(1)} %get-tuple-element.279), channel_id=1, source_target_pairs={{0,1},{1,2},{2,3},{3,4},{4,5},{5,6},{6,7},{7,8},{8,9},{9,10},{10,1... | collective-permute-start | bytes 24584 | tf_op jit(solution)/shard_map/ppermute | solution.py:33
  23.0 1.3 copy-start.8
  74.4 14.7 %collective-permute-start.2 = (f32[2,1,16,2048]{3,2,1,0:T(8,128)S(1)}, f32[2,1,16,2048]{3,2,1,0:T(8,128)S(1)}, u32[]{:S(2)}, u32[]{:S(2)}) collective-permute-start(f32[2,1,16,2048]{3,2,1,0:T(8,128)S(1)} %get-tuple-element.267), channel_id=1, source_target_pairs={{16,0},{32,16},{48,32},{64,48},{80,64},{96,80},{112,96},{17,1},{33... | collective-permute-start | bytes 786440 | tf_op jit(solution)/shard_map/ppermute | solution.py:203
  76.3 12.8 %collective-permute-start.3 = (f32[2,1,16,2048]{3,2,1,0:T(8,128)S(1)}, f32[2,1,16,2048]{3,2,1,0:T(8,128)S(1)}, u32[]{:S(2)}, u32[]{:S(2)}) collective-permute-start(f32[2,1,16,2048]{3,2,1,0:T(8,128)S(1)} %get-tuple-element.266), channel_id=1, source_target_pairs={{0,16},{16,32},{32,48},{48,64},{64,80},{80,96},{96,112},{1,17},{17... | collective-permute-start | bytes 786440 | tf_op jit(solution)/shard_map/ppermute | solution.py:202
  78.8 6.9 %collective-permute-start.4 = (f32[2,8,1,2048]{3,1,2,0:T(8,128)S(1)}, f32[2,8,1,2048]{3,1,2,0:T(8,128)S(1)}, u32[]{:S(2)}, u32[]{:S(2)}) collective-permute-start(f32[2,8,1,2048]{3,1,2,0:T(8,128)S(1)} %copy.47), channel_id=1, source_target_pairs={{1,0},{2,1},{3,2},{4,3},{5,4},{6,5},{7,6},{8,7},{9,8},{10,9},{11,1... | collective-permute-start | bytes 393224 | tf_op jit(solution)/shard_map/ppermute | solution.py:203
  82.0 7.0 %copy-start.4 = (f32[2]{0:T(128)S(1)}, f32[2]{0:T(128)}, u32[]{:S(2)}) copy-start(f32[2]{0:T(128)} %constant.224.clone) | copy-start | bytes 28
  82.1 7.0 %copy-start.5 = (f32[2]{0:T(128)S(1)}, f32[2]{0:T(128)}, u32[]{:S(2)}) copy-start(f32[2]{0:T(128)} %constant.225.clone) | copy-start | bytes 28
  82.1 6.9 %collective-permute-start.5 = (f32[2,8,1,2048]{3,1,2,0:T(8,128)S(1)}, f32[2,8,1,2048]{3,1,2,0:T(8,128)S(1)}, u32[]{:S(2)}, u32[]{:S(2)}) collective-permute-start(f32[2,8,1,2048]{3,1,2,0:T(8,128)S(1)} %copy.49), channel_id=1, source_target_pairs={{0,1},{1,2},{2,3},{3,4},{4,5},{5,6},{6,7},{7,8},{8,9},{9,10},{10,1... | collective-permute-start | bytes 393224 | tf_op jit(solution)/shard_map/ppermute | solution.py:202
  92.0 14.0 %collective-permute-start.6 = (f32[2,1,16,2048]{3,2,1,0:T(8,128)S(1)}, f32[2,1,16,2048]{3,2,1,0:T(8,128)S(1)}, u32[]{:S(2)}, u32[]{:S(2)}) collective-permute-start(f32[2,1,16,2048]{3,2,1,0:T(8,128)S(1)} %get-tuple-element.259), channel_id=1, source_target_pairs={{16,0},{32,16},{48,32},{64,48},{80,64},{96,80},{112,96},{17,1},{33... | collective-permute-start | bytes 786440 | tf_op jit(solution)/shard_map/ppermute | solution.py:203
  95.1 11.0 %collective-permute-start.7 = (f32[2,1,16,2048]{3,2,1,0:T(8,128)S(1)}, f32[2,1,16,2048]{3,2,1,0:T(8,128)S(1)}, u32[]{:S(2)}, u32[]{:S(2)}) collective-permute-start(f32[2,1,16,2048]{3,2,1,0:T(8,128)S(1)} %get-tuple-element.258), channel_id=1, source_target_pairs={{0,16},{16,32},{32,48},{48,64},{64,80},{80,96},{96,112},{1,17},{17... | collective-permute-start | bytes 786440 | tf_op jit(solution)/shard_map/ppermute | solution.py:202
  97.1 6.9 %collective-permute-start.8 = (f32[2,8,1,2048]{3,1,2,0:T(8,128)S(1)}, f32[2,8,1,2048]{3,1,2,0:T(8,128)S(1)}, u32[]{:S(2)}, u32[]{:S(2)}) collective-permute-start(f32[2,8,1,2048]{3,1,2,0:T(8,128)S(1)} %copy.51), channel_id=1, source_target_pairs={{1,0},{2,1},{3,2},{4,3},{5,4},{6,5},{7,6},{8,7},{9,8},{10,9},{11,1... | collective-permute-start | bytes 393224 | tf_op jit(solution)/shard_map/ppermute | solution.py:203
  99.0 6.9 %collective-permute-start.9 = (f32[2,8,1,2048]{3,1,2,0:T(8,128)S(1)}, f32[2,8,1,2048]{3,1,2,0:T(8,128)S(1)}, u32[]{:S(2)}, u32[]{:S(2)}) collective-permute-start(f32[2,8,1,2048]{3,1,2,0:T(8,128)S(1)} %copy.53), channel_id=1, source_target_pairs={{0,1},{1,2},{2,3},{3,4},{4,5},{5,6},{6,7},{7,8},{8,9},{9,10},{10,1... | collective-permute-start | bytes 393224 | tf_op jit(solution)/shard_map/ppermute | solution.py:202
  109.0 15.1 %collective-permute-start.10 = (f32[2,1,16,2048]{3,2,1,0:T(8,128)S(1)}, f32[2,1,16,2048]{3,2,1,0:T(8,128)S(1)}, u32[]{:S(2)}, u32[]{:S(2)}) collective-permute-start(f32[2,1,16,2048]{3,2,1,0:T(8,128)S(1)} %get-tuple-element.251), channel_id=1, source_target_pairs={{16,0},{32,16},{48,32},{64,48},{80,64},{96,80},{112,96},{17,1},{33... | collective-permute-start | bytes 786440 | tf_op jit(solution)/shard_map/ppermute | solution.py:203
  113.1 11.0 %collective-permute-start.11 = (f32[2,1,16,2048]{3,2,1,0:T(8,128)S(1)}, f32[2,1,16,2048]{3,2,1,0:T(8,128)S(1)}, u32[]{:S(2)}, u32[]{:S(2)}) collective-permute-start(f32[2,1,16,2048]{3,2,1,0:T(8,128)S(1)} %get-tuple-element.250), channel_id=1, source_target_pairs={{0,16},{16,32},{32,48},{48,64},{64,80},{80,96},{96,112},{1,17},{17... | collective-permute-start | bytes 786440 | tf_op jit(solution)/shard_map/ppermute | solution.py:202
  115.1 6.9 %collective-permute-start.12 = (f32[2,8,1,2048]{3,1,2,0:T(8,128)S(1)}, f32[2,8,1,2048]{3,1,2,0:T(8,128)S(1)}, u32[]{:S(2)}, u32[]{:S(2)}) collective-permute-start(f32[2,8,1,2048]{3,1,2,0:T(8,128)S(1)} %copy.55), channel_id=1, source_target_pairs={{1,0},{2,1},{3,2},{4,3},{5,4},{6,5},{7,6},{8,7},{9,8},{10,9},{11,1... | collective-permute-start | bytes 393224 | tf_op jit(solution)/shard_map/ppermute | solution.py:203
  117.1 6.9 %collective-permute-start.13 = (f32[2,8,1,2048]{3,1,2,0:T(8,128)S(1)}, f32[2,8,1,2048]{3,1,2,0:T(8,128)S(1)}, u32[]{:S(2)}, u32[]{:S(2)}) collective-permute-start(f32[2,8,1,2048]{3,1,2,0:T(8,128)S(1)} %copy.57), channel_id=1, source_target_pairs={{0,1},{1,2},{2,3},{3,4},{4,5},{5,6},{6,7},{7,8},{8,9},{9,10},{10,1... | collective-permute-start | bytes 393224 | tf_op jit(solution)/shard_map/ppermute | solution.py:202
  127.0 15.5 %collective-permute-start.14 = (f32[2,1,16,2048]{3,2,1,0:T(8,128)S(1)}, f32[2,1,16,2048]{3,2,1,0:T(8,128)S(1)}, u32[]{:S(2)}, u32[]{:S(2)}) collective-permute-start(f32[2,1,16,2048]{3,2,1,0:T(8,128)S(1)} %get-tuple-element.243), channel_id=1, source_target_pairs={{16,0},{32,16},{48,32},{64,48},{80,64},{96,80},{112,96},{17,1},{33... | collective-permute-start | bytes 786440 | tf_op jit(solution)/shard_map/ppermute | solution.py:203
  130.5 12.0 %collective-permute-start.15 = (f32[2,1,16,2048]{3,2,1,0:T(8,128)S(1)}, f32[2,1,16,2048]{3,2,1,0:T(8,128)S(1)}, u32[]{:S(2)}, u32[]{:S(2)}) collective-permute-start(f32[2,1,16,2048]{3,2,1,0:T(8,128)S(1)} %get-tuple-element.242), channel_id=1, source_target_pairs={{0,16},{16,32},{32,48},{48,64},{64,80},{80,96},{96,112},{1,17},{17... | collective-permute-start | bytes 786440 | tf_op jit(solution)/shard_map/ppermute | solution.py:202
  132.5 7.8 %collective-permute-start.16 = (f32[2,8,1,2048]{3,1,2,0:T(8,128)S(1)}, f32[2,8,1,2048]{3,1,2,0:T(8,128)S(1)}, u32[]{:S(2)}, u32[]{:S(2)}) collective-permute-start(f32[2,8,1,2048]{3,1,2,0:T(8,128)S(1)} %copy.59), channel_id=1, source_target_pairs={{1,0},{2,1},{3,2},{4,3},{5,4},{6,5},{7,6},{8,7},{9,8},{10,9},{11,1... | collective-permute-start | bytes 393224 | tf_op jit(solution)/shard_map/ppermute | solution.py:203
  134.5 7.9 %collective-permute-start.17 = (f32[2,8,1,2048]{3,1,2,0:T(8,128)S(1)}, f32[2,8,1,2048]{3,1,2,0:T(8,128)S(1)}, u32[]{:S(2)}, u32[]{:S(2)}) collective-permute-start(f32[2,8,1,2048]{3,1,2,0:T(8,128)S(1)} %copy.61), channel_id=1, source_target_pairs={{0,1},{1,2},{2,3},{3,4},{4,5},{5,6},{6,7},{7,8},{8,9},{9,10},{10,1... | collective-permute-start | bytes 393224 | tf_op jit(solution)/shard_map/ppermute | solution.py:202
  140.3 78.6 %collective-permute-start.1 = (f32[4,512]{1,0:T(4,128)S(1)}, f32[4,512]{1,0:T(4,128)S(1)}, u32[]{:S(2)}, u32[]{:S(2)}) collective-permute-start(f32[4,512]{1,0:T(4,128)S(1)} %get-tuple-element.280), channel_id=1, source_target_pairs={{1,0},{2,1},{3,2},{4,3},{5,4},{6,5},{7,6},{8,7},{9,8},{10,9},{11,1... | collective-permute-start | bytes 24584 | tf_op jit(solution)/shard_map/ppermute | solution.py:36
  144.7 1.3 copy-start
  146.4 12.0 %collective-permute-start.20 = (f32[8,1,2048]{2,1,0:T(1,128)S(1)}, f32[8,1,2048]{2,1,0:T(1,128)S(1)}, u32[]{:S(2)}, u32[]{:S(2)}) collective-permute-start(f32[8,1,2048]{2,1,0:T(1,128)S(1)} %get-tuple-element.271), channel_id=1, source_target_pairs={{1,0},{2,1},{3,2},{4,3},{5,4},{6,5},{7,6},{8,7},{9,8},{10,9},{11,1... | collective-permute-start | bytes 196616 | tf_op jit(solution)/shard_map/ppermute | solution.py:203
  148.3 12.2 %collective-permute-start.21 = (f32[8,1,2048]{2,1,0:T(1,128)S(1)}, f32[8,1,2048]{2,1,0:T(1,128)S(1)}, u32[]{:S(2)}, u32[]{:S(2)}) collective-permute-start(f32[8,1,2048]{2,1,0:T(1,128)S(1)} %get-tuple-element.270), channel_id=1, source_target_pairs={{0,1},{1,2},{2,3},{3,4},{4,5},{5,6},{6,7},{7,8},{8,9},{9,10},{10,1... | collective-permute-start | bytes 196616 | tf_op jit(solution)/shard_map/ppermute | solution.py:202
  155.4 5.4 %collective-permute-start.18 = (f32[1,16,2048]{2,1,0:T(8,128)S(1)}, f32[1,16,2048]{2,1,0:T(8,128)S(1)}, u32[]{:S(2)}, u32[]{:S(2)}) collective-permute-start(f32[1,16,2048]{2,1,0:T(8,128)S(1)} %get-tuple-element.235), channel_id=1, source_target_pairs={{16,0},{32,16},{48,32},{64,48},{80,64},{96,80},{112,96},{17,1},{33... | collective-permute-start | bytes 393224 | tf_op jit(solution)/shard_map/ppermute | solution.py:203
  158.3 6.3 %collective-permute-start.19 = (f32[1,16,2048]{2,1,0:T(8,128)S(1)}, f32[1,16,2048]{2,1,0:T(8,128)S(1)}, u32[]{:S(2)}, u32[]{:S(2)}) collective-permute-start(f32[1,16,2048]{2,1,0:T(8,128)S(1)} %get-tuple-element.234), channel_id=1, source_target_pairs={{0,16},{16,32},{32,48},{48,64},{64,80},{80,96},{96,112},{1,17},{17... | collective-permute-start | bytes 393224 | tf_op jit(solution)/shard_map/ppermute | solution.py:202
  206.2 28.3 %all-to-all-start.1 = ((f32[3,16,256]{2,0,1:T(4,128)}), f32[3,16,256]{2,0,1:T(4,128)S(1)}, u32[]{:S(2)}, u32[]{:S(2)}) async-start(f32[3,16,256]{2,0,1:T(4,128)} %bitcast.41), calls=%async_computation.1 | async-start | bytes 131072 | tf_op jit(solution)/shard_map/all_to_all | solution.py:303
  218.9 3.8 %copy-start.1 = (f32[24,4,128]{2,1,0:T(4,128)}, f32[24,4,128]{2,1,0:T(4,128)S(1)}, u32[]{:S(2)}) copy-start(f32[24,4,128]{2,1,0:T(4,128)S(1)} %maximum_bitcast_fusion.rows_ref) | copy-start | bytes 147460
  238.8 0.8 copy-start.3

commit v10 on v7

--- a/solution.py
+++ b/solution.py
@@ -23,6 +23,7 @@
 FORCE_SCALE = 0.08
 CHEMOTAXIS = 1.5
 SLOT_BLOCK = 512
+RADIX_BITS = 2
 
 
 def with_halo(block, sides, width):
@@ -235,10 +236,12 @@
     rows = starts.shape[0]
     padded = jnp.pad(values, ((0, 0), (0, length)))
     held = jnp.broadcast_to(padded[:, None, :], (channels, rows, width))
-    for bit in range(bits_of(cells)):
-        step = 1 << bit
-        take = ((starts >> bit) & 1 == 1)[None, :, None]
-        held = jnp.where(take, jnp.roll(held, -step, axis=2), held)
+    for bit in range(0, bits_of(cells), RADIX_BITS):
+        digit = ((starts >> bit) & ((1 << RADIX_BITS) - 1))[None, :, None]
+        moved = held
+        for value in range(1, 1 << RADIX_BITS):
+            moved = jnp.where(digit == value, jnp.roll(held, -(value << bit), axis=2), moved)
+        held = moved
     return held[:, :, :length]
 
 
@@ -246,10 +249,12 @@
     channels, rows, length = windows.shape
     width = cells + length
     held = jnp.pad(windows, ((0, 0), (0, 0), (0, width - length)))
-    for bit in range(bits_of(cells)):
-        step = 1 << bit
-        take = ((starts >> bit) & 1 == 1)[None, :, None]
-        held = jnp.where(take, jnp.roll(held, step, axis=2), held)
+    for bit in range(0, bits_of(cells), RADIX_BITS):
+        digit = ((starts >> bit) & ((1 << RADIX_BITS) - 1))[None, :, None]
+        moved = held
+        for value in range(1, 1 << RADIX_BITS):
+            moved = jnp.where(digit == value, jnp.roll(held, value << bit, axis=2), moved)
+        held = moved
     return jnp.sum(held[:, :, :cells], axis=1)
 
 

time: 224 us -> 231 us (1.031)
  other arithmetic: 25.3 us -> 29.1 us
    select_n x20 -> x10, other arithmetic: 5.8 us -> 8.15 us  [the longest x5 4.69 us: scatter_windows(): jnp.where(digit == value, jnp.roll(held, value << bit, axis=2), moved)]
    slice x36 -> x59, local copies, waits for them, and re-layouts: 3.45 us -> 5.26 us  [the longest x33 3.45 us: gather_windows(): jnp.roll(held, -(value << bit), axis=2)]
  transfers between devices with their start and end apart: 24 -> 24, of which waited for: 8 -> 9; matrix products, arithmetic and copies ran while one was open for 42% -> 41% of each run, Pallas kernels for 5% -> 5%
where the time goes in v10:
time: 231 us; the launch traced here: 229 us
  starting transfers between devices  85.1 us (37%)
  matrix products  63.3 us (27%)
  other arithmetic  29.1 us (13%)
  local copies, waits for them, and re-layouts  23.9 us (10%)
  waiting for transfers between devices  12.7 us (5%)
  Pallas kernels  11.9 us (5%)
  between operations  2.57 us (1%)
    ppermute x10, starting transfers between devices, neighbours(): lax.ppermute(lax.slice_in_dim(block, block.shape[dim] - 1, None, axis=dim...  32.5 us
    ppermute x10, starting transfers between devices, neighbours(): high = lax.ppermute(lax.slice_in_dim(block, 0, 1, axis=dim), axis, backward)  26.2 us
    dot_general x8, matrix products, one_piece(): jnp.einsum('srx,mx->srm', fields, column_hot, precision=lax.Precision.HIG...  25.4 us
    dot_general x8, matrix products, add_piece(): jnp.einsum('smr,mx->srx', weighted, column_hot, precision=lax.Precision.H...  24.1 us
    dot_general x4, matrix products, one_piece(): jnp.einsum('psrx,mx->psrm', parts, column_hot, preferred_element_type=jnp...  13.8 us
    all_to_all x1, starting transfers between devices, local(): lax.all_to_all(slopes, 'tile', split_axis=1, concat_axis=1, tiled=True)  12.6 us
    pallas_call x1, Pallas kernels, pair_forces(): pl.pallas_call(force_kernel, out_shape=jax.ShapeDtypeStruct((blocks, 3, l...  11.9 us
    ppermute x10, waiting for transfers between devices, neighbours(): lax.ppermute(lax.slice_in_dim(block, block.shape[dim] - 1, None, axis=dim...  10.5 us
  transfers between devices with their start and end apart: 24, of which 9 were waited for; matrix products, arithmetic and copies ran while one was open for 41% of the time, Pallas kernels for 5%

profile of v10, /device:TPU:26, one launch (start us, length us, event | category | flops | bytes accessed | tf_op | source)
XLA Modules:
  0.0 229.4 jit_solution(9822203078628144774)
XLA Ops:
  7.9 1.7 maximum_select_fusion.15
  14.1 8.3 %all-to-all-start = ((f32[2,16,256]{2,0,1:T(2,128)}), f32[2,16,256]{2,0,1:T(2,128)S(1)}, u32[]{:S(2)}, u32[]{:S(2)}) async-start(f32[2,16,256]{2,0,1:T(2,128)} %fusion.85), calls=%async_computation | async-start | bytes 65536 | tf_op jit(solution)/shard_map/all_to_all | solution.py:283
  23.1 3.6 %collective-permute-start = (f32[4,512]{1,0:T(4,128)S(1)}, f32[4,512]{1,0:T(4,128)S(1)}, u32[]{:S(2)}, u32[]{:S(2)}) collective-permute-start(f32[4,512]{1,0:T(4,128)S(1)} %get-tuple-element.269), channel_id=1, source_target_pairs={{0,1},{1,2},{2,3},{3,4},{4,5},{5,6},{6,7},{7,8},{8,9},{9,10},{10,1... | collective-permute-start | bytes 24584 | tf_op jit(solution)/shard_map/ppermute | solution.py:34
  27.0 1.3 pad_maximum_fusion.1
  29.1 14.8 %while.37 = (s32[]{:T(128)}, f32[4,1,1024]{2,1,0:T(1,128)S(1)}, s32[4,1024]{1,0:T(4,128)S(1)}, bf16[3,1,128,2048]{3,2,0,1:T(8,128)(2,1)}, s32[]{:T(128)}) while((s32[]{:T(128)}, f32[4,1,1024]{2,1,0:T(1,128)S(1)}, s32[4,1024]{1,0:T(4,128)S(1)}, bf16[3,1,128,2048]{3,2,0,1:T(8,128)(2,1)}, s32[]{:T(128)}) %tuple.128), condition=%wide.region_3.4_spmd, body=%wide.region_1.3_spmd.sunk | while | flops 1613645824 | bytes 4759621 | solution.py:105
  29.1 3.5 %fusion.126 = f32[3,128,1024]{2,1,0:T(8,128)S(1)} fusion(bf16[3,1,128,2048]{3,2,0,1:T(8,128)(2,1)} %get-tuple-element.390, s32[1024]{0:T(1024)S(1)} %get-tuple-element.363), kind=kOutput, calls=%fused_computation.5.clone.1 | convolution fusion | flops 1612709888 | bytes 3149824 | tf_op jit(solution)/shard_map/while/body/eval_jaxpr/psrx,mx->psrm/dot_general | solution.py:99
  32.8 3.5 %fusion.126 = f32[3,128,1024]{2,1,0:T(8,128)S(1)} fusion(bf16[3,1,128,2048]{3,2,0,1:T(8,128)(2,1)} %get-tuple-element.390, s32[1024]{0:T(1024)S(1)} %get-tuple-element.363), kind=kOutput, calls=%fused_computation.5.clone.1 | convolution fusion | flops 1612709888 | bytes 3149824 | tf_op jit(solution)/shard_map/while/body/eval_jaxpr/psrx,mx->psrm/dot_general | solution.py:99
  36.5 3.5 %fusion.126 = f32[3,128,1024]{2,1,0:T(8,128)S(1)} fusion(bf16[3,1,128,2048]{3,2,0,1:T(8,128)(2,1)} %get-tuple-element.390, s32[1024]{0:T(1024)S(1)} %get-tuple-element.363), kind=kOutput, calls=%fused_computation.5.clone.1 | convolution fusion | flops 1612709888 | bytes 3149824 | tf_op jit(solution)/shard_map/while/body/eval_jaxpr/psrx,mx->psrm/dot_general | solution.py:99
  40.2 3.5 %fusion.126 = f32[3,128,1024]{2,1,0:T(8,128)S(1)} fusion(bf16[3,1,128,2048]{3,2,0,1:T(8,128)(2,1)} %get-tuple-element.390, s32[1024]{0:T(1024)S(1)} %get-tuple-element.363), kind=kOutput, calls=%fused_computation.5.clone.1 | convolution fusion | flops 1612709888 | bytes 3149824 | tf_op jit(solution)/shard_map/while/body/eval_jaxpr/psrx,mx->psrm/dot_general | solution.py:99
  44.0 25.0 %while.39 = (s32[]{:T(128)}, f32[2,128,2048]{2,1,0:T(8,128)S(1)}, f32[8,2,512]{2,0,1:T(8,128)S(1)}, s32[8,512]{1,0:T(8,128)S(1)}, s32[]{:T(128)}, /*index=5*/s32[]{:T(128)}) while((s32[]{:T(128)}, f32[2,128,2048]{2,1,0:T(8,128)S(1)}, f32[8,2,512]{2,0,1:T(8,128)S(1)}, s32[8,512]{1,0:T(8,128)S(1)}, s32[]{:T(128)}, ...), condition=%wide.region_5.6_spmd.clone, body=%wide.region_4.5_spmd.clone.sunk | while | flops 3223594496 | bytes 4753495 | solution.py:138
  44.1 3.0 %fusion.135 = f32[2,128,2048]{2,1,0:T(8,128)S(1)} fusion(f32[2,128,2048]{2,1,0:T(8,128)S(1)} %get-tuple-element.399, s32[512]{0:T(512)S(1)} %get-tuple-element.375, pred[]{:T(512)S(6)} %compare.55, f32[512,128]{0,1:T(8,128)S(1)} %fusion.134, f32[2,512]{1,0:T(2,128)S(1)} %bitcast.143), kind=kOutput, calls=%fused_computation.44.clone.1 | convolution fusion | flops 3223453696 | bytes 4462593 | tf_op jit(solution)/shard_map/while/body/eval_jaxpr/smr,mx->srx/dot_general | solution.py:133
  47.2 3.0 %fusion.135 = f32[2,128,2048]{2,1,0:T(8,128)S(1)} fusion(f32[2,128,2048]{2,1,0:T(8,128)S(1)} %get-tuple-element.399, s32[512]{0:T(512)S(1)} %get-tuple-element.375, pred[]{:T(512)S(6)} %compare.55, f32[512,128]{0,1:T(8,128)S(1)} %fusion.134, f32[2,512]{1,0:T(2,128)S(1)} %bitcast.143), kind=kOutput, calls=%fused_computation.44.clone.1 | convolution fusion | flops 3223453696 | bytes 4462593 | tf_op jit(solution)/shard_map/while/body/eval_jaxpr/smr,mx->srx/dot_general | solution.py:133
  50.4 3.0 %fusion.135 = f32[2,128,2048]{2,1,0:T(8,128)S(1)} fusion(f32[2,128,2048]{2,1,0:T(8,128)S(1)} %get-tuple-element.399, s32[512]{0:T(512)S(1)} %get-tuple-element.375, pred[]{:T(512)S(6)} %compare.55, f32[512,128]{0,1:T(8,128)S(1)} %fusion.134, f32[2,512]{1,0:T(2,128)S(1)} %bitcast.143), kind=kOutput, calls=%fused_computation.44.clone.1 | convolution fusion | flops 3223453696 | bytes 4462593 | tf_op jit(solution)/shard_map/while/body/eval_jaxpr/smr,mx->srx/dot_general | solution.py:133
  53.5 3.0 %fusion.135 = f32[2,128,2048]{2,1,0:T(8,128)S(1)} fusion(f32[2,128,2048]{2,1,0:T(8,128)S(1)} %get-tuple-element.399, s32[512]{0:T(512)S(1)} %get-tuple-element.375, pred[]{:T(512)S(6)} %compare.55, f32[512,128]{0,1:T(8,128)S(1)} %fusion.134, f32[2,512]{1,0:T(2,128)S(1)} %bitcast.143), kind=kOutput, calls=%fused_computation.44.clone.1 | convolution fusion | flops 3223453696 | bytes 4462593 | tf_op jit(solution)/shard_map/while/body/eval_jaxpr/smr,mx->srx/dot_general | solution.py:133
  56.6 3.0 %fusion.135 = f32[2,128,2048]{2,1,0:T(8,128)S(1)} fusion(f32[2,128,2048]{2,1,0:T(8,128)S(1)} %get-tuple-element.399, s32[512]{0:T(512)S(1)} %get-tuple-element.375, pred[]{:T(512)S(6)} %compare.55, f32[512,128]{0,1:T(8,128)S(1)} %fusion.134, f32[2,512]{1,0:T(2,128)S(1)} %bitcast.143), kind=kOutput, calls=%fused_computation.44.clone.1 | convolution fusion | flops 3223453696 | bytes 4462593 | tf_op jit(solution)/shard_map/while/body/eval_jaxpr/smr,mx->srx/dot_general | solution.py:133
  59.8 3.0 %fusion.135 = f32[2,128,2048]{2,1,0:T(8,128)S(1)} fusion(f32[2,128,2048]{2,1,0:T(8,128)S(1)} %get-tuple-element.399, s32[512]{0:T(512)S(1)} %get-tuple-element.375, pred[]{:T(512)S(6)} %compare.55, f32[512,128]{0,1:T(8,128)S(1)} %fusion.134, f32[2,512]{1,0:T(2,128)S(1)} %bitcast.143), kind=kOutput, calls=%fused_computation.44.clone.1 | convolution fusion | flops 3223453696 | bytes 4462593 | tf_op jit(solution)/shard_map/while/body/eval_jaxpr/smr,mx->srx/dot_general | solution.py:133
  62.9 3.0 %fusion.135 = f32[2,128,2048]{2,1,0:T(8,128)S(1)} fusion(f32[2,128,2048]{2,1,0:T(8,128)S(1)} %get-tuple-element.399, s32[512]{0:T(512)S(1)} %get-tuple-element.375, pred[]{:T(512)S(6)} %compare.55, f32[512,128]{0,1:T(8,128)S(1)} %fusion.134, f32[2,512]{1,0:T(2,128)S(1)} %bitcast.143), kind=kOutput, calls=%fused_computation.44.clone.1 | convolution fusion | flops 3223453696 | bytes 4462593 | tf_op jit(solution)/shard_map/while/body/eval_jaxpr/smr,mx->srx/dot_general | solution.py:133
  66.0 3.0 %fusion.135 = f32[2,128,2048]{2,1,0:T(8,128)S(1)} fusion(f32[2,128,2048]{2,1,0:T(8,128)S(1)} %get-tuple-element.399, s32[512]{0:T(512)S(1)} %get-tuple-element.375, pred[]{:T(512)S(6)} %compare.55, f32[512,128]{0,1:T(8,128)S(1)} %fusion.134, f32[2,512]{1,0:T(2,128)S(1)} %bitcast.143), kind=kOutput, calls=%fused_computation.44.clone.1 | convolution fusion | flops 3223453696 | bytes 4462593 | tf_op jit(solution)/shard_map/while/body/eval_jaxpr/smr,mx->srx/dot_general | solution.py:133
  69.0 1.8 add.229
  71.6 1.9 collective-permute-start.2
  73.5 2.4 %collective-permute-start.3 = (f32[2,1,16,2048]{3,2,1,0:T(8,128)S(1)}, f32[2,1,16,2048]{3,2,1,0:T(8,128)S(1)}, u32[]{:S(2)}, u32[]{:S(2)}) collective-permute-start(f32[2,1,16,2048]{3,2,1,0:T(8,128)S(1)} %get-tuple-element.258), channel_id=1, source_target_pairs={{0,16},{16,32},{32,48},{48,64},{64,80},{80,96},{96,112},{1,17},{17... | collective-permute-start | bytes 786440 | tf_op jit(solution)/shard_map/ppermute | solution.py:203
  76.0 3.0 %collective-permute-start.4 = (f32[2,8,1,2048]{3,1,2,0:T(8,128)S(1)}, f32[2,8,1,2048]{3,1,2,0:T(8,128)S(1)}, u32[]{:S(2)}, u32[]{:S(2)}) collective-permute-start(f32[2,8,1,2048]{3,1,2,0:T(8,128)S(1)} %copy.79), channel_id=1, source_target_pairs={{1,0},{2,1},{3,2},{4,3},{5,4},{6,5},{7,6},{8,7},{9,8},{10,9},{11,1... | collective-permute-start | bytes 393224 | tf_op jit(solution)/shard_map/ppermute | solution.py:204
  79.1 2.8 %collective-permute-start.5 = (f32[2,8,1,2048]{3,1,2,0:T(8,128)S(1)}, f32[2,8,1,2048]{3,1,2,0:T(8,128)S(1)}, u32[]{:S(2)}, u32[]{:S(2)}) collective-permute-start(f32[2,8,1,2048]{3,1,2,0:T(8,128)S(1)} %copy.81), channel_id=1, source_target_pairs={{0,1},{1,2},{2,3},{3,4},{4,5},{5,6},{6,7},{7,8},{8,9},{9,10},{10,1... | collective-permute-start | bytes 393224 | tf_op jit(solution)/shard_map/ppermute | solution.py:203
  83.0 3.0 %collective-permute-done.5 = f32[2,8,1,2048]{3,1,2,0:T(8,128)S(1)} collective-permute-done((f32[2,8,1,2048]{3,1,2,0:T(8,128)S(1)}, f32[2,8,1,2048]{3,1,2,0:T(8,128)S(1)}, u32[]{:S(2)}, u32[]{:S(2)}) %collective-permute-start.5) | collective-permute-done | bytes 131104 | tf_op jit(solution)/shard_map/ppermute | solution.py:203
  86.2 2.2 fusion.47
  89.1 3.1 %collective-permute-start.6 = (f32[2,1,16,2048]{3,2,1,0:T(8,128)S(1)}, f32[2,1,16,2048]{3,2,1,0:T(8,128)S(1)}, u32[]{:S(2)}, u32[]{:S(2)}) collective-permute-start(f32[2,1,16,2048]{3,2,1,0:T(8,128)S(1)} %get-tuple-element.251), channel_id=1, source_target_pairs={{16,0},{32,16},{48,32},{64,48},{80,64},{96,80},{112,96},{17,1},{33... | collective-permute-start | bytes 786440 | tf_op jit(solution)/shard_map/ppermute | solution.py:204
  92.1 1.9 collective-permute-start.7
  94.1 1.9 collective-permute-start.8
  96.1 3.9 %collective-permute-start.9 = (f32[2,8,1,2048]{3,1,2,0:T(8,128)S(1)}, f32[2,8,1,2048]{3,1,2,0:T(8,128)S(1)}, u32[]{:S(2)}, u32[]{:S(2)}) collective-permute-start(f32[2,8,1,2048]{3,1,2,0:T(8,128)S(1)} %copy.85), channel_id=1, source_target_pairs={{0,1},{1,2},{2,3},{3,4},{4,5},{5,6},{6,7},{7,8},{8,9},{9,10},{10,1... | collective-permute-start | bytes 393224 | tf_op jit(solution)/shard_map/ppermute | solution.py:203
  101.1 1.8 collective-permute-done.9
  103.1 2.2 fusion.53
  106.0 4.1 %collective-permute-start.10 = (f32[2,1,16,2048]{3,2,1,0:T(8,128)S(1)}, f32[2,1,16,2048]{3,2,1,0:T(8,128)S(1)}, u32[]{:S(2)}, u32[]{:S(2)}) collective-permute-start(f32[2,1,16,2048]{3,2,1,0:T(8,128)S(1)} %get-tuple-element.243), channel_id=1, source_target_pairs={{16,0},{32,16},{48,32},{64,48},{80,64},{96,80},{112,96},{17,1},{33... | collective-permute-start | bytes 786440 | tf_op jit(solution)/shard_map/ppermute | solution.py:204
  110.2 2.1 collective-permute-start.11
  112.4 1.9 collective-permute-start.12
  114.3 3.9 %collective-permute-start.13 = (f32[2,8,1,2048]{3,1,2,0:T(8,128)S(1)}, f32[2,8,1,2048]{3,1,2,0:T(8,128)S(1)}, u32[]{:S(2)}, u32[]{:S(2)}) collective-permute-start(f32[2,8,1,2048]{3,1,2,0:T(8,128)S(1)} %copy.89), channel_id=1, source_target_pairs={{0,1},{1,2},{2,3},{3,4},{4,5},{5,6},{6,7},{7,8},{8,9},{9,10},{10,1... | collective-permute-start | bytes 393224 | tf_op jit(solution)/shard_map/ppermute | solution.py:203
  119.4 1.8 collective-permute-done.13
  121.4 2.2 fusion.59
  124.3 3.5 %collective-permute-start.14 = (f32[2,1,16,2048]{3,2,1,0:T(8,128)S(1)}, f32[2,1,16,2048]{3,2,1,0:T(8,128)S(1)}, u32[]{:S(2)}, u32[]{:S(2)}) collective-permute-start(f32[2,1,16,2048]{3,2,1,0:T(8,128)S(1)} %get-tuple-element.235), channel_id=1, source_target_pairs={{16,0},{32,16},{48,32},{64,48},{80,64},{96,80},{112,96},{17,1},{33... | collective-permute-start | bytes 786440 | tf_op jit(solution)/shard_map/ppermute | solution.py:204
  127.8 1.9 collective-permute-start.15
  129.8 1.9 collective-permute-start.16
  131.7 5.0 %collective-permute-start.17 = (f32[2,8,1,2048]{3,1,2,0:T(8,128)S(1)}, f32[2,8,1,2048]{3,1,2,0:T(8,128)S(1)}, u32[]{:S(2)}, u32[]{:S(2)}) collective-permute-start(f32[2,8,1,2048]{3,1,2,0:T(8,128)S(1)} %copy.93), channel_id=1, source_target_pairs={{0,1},{1,2},{2,3},{3,4},{4,5},{5,6},{6,7},{7,8},{8,9},{9,10},{10,1... | collective-permute-start | bytes 393224 | tf_op jit(solution)/shard_map/ppermute | solution.py:203
  137.7 1.9 collective-permute-start.1
  139.9 2.2 fusion.65
  142.4 1.1 copy-done
  143.8 1.9 collective-permute-start.20
  145.7 6.5 %collective-permute-start.21 = (f32[8,1,2048]{2,1,0:T(1,128)S(1)}, f32[8,1,2048]{2,1,0:T(1,128)S(1)}, u32[]{:S(2)}, u32[]{:S(2)}) collective-permute-start(f32[8,1,2048]{2,1,0:T(1,128)S(1)} %get-tuple-element.262), channel_id=1, source_target_pairs={{0,1},{1,2},{2,3},{3,4},{4,5},{5,6},{6,7},{7,8},{8,9},{9,10},{10,1... | collective-permute-start | bytes 196616 | tf_op jit(solution)/shard_map/ppermute | solution.py:203
  152.8 2.9 %collective-permute-start.18 = (f32[1,16,2048]{2,1,0:T(8,128)S(1)}, f32[1,16,2048]{2,1,0:T(8,128)S(1)}, u32[]{:S(2)}, u32[]{:S(2)}) collective-permute-start(f32[1,16,2048]{2,1,0:T(8,128)S(1)} %get-tuple-element.227), channel_id=1, source_target_pairs={{16,0},{32,16},{48,32},{64,48},{80,64},{96,80},{112,96},{17,1},{33... | collective-permute-start | bytes 393224 | tf_op jit(solution)/shard_map/ppermute | solution.py:204
  155.8 1.9 collective-permute-start.19
  158.3 3.8 %collective-permute-done.19 = f32[1,16,2048]{2,1,0:T(8,128)S(1)} collective-permute-done((f32[1,16,2048]{2,1,0:T(8,128)S(1)}, f32[1,16,2048]{2,1,0:T(8,128)S(1)}, u32[]{:S(2)}, u32[]{:S(2)}) %collective-permute-start.19) | collective-permute-done | bytes 131104 | tf_op jit(solution)/shard_map/ppermute | solution.py:203
  162.4 30.7 %while.38 = (s32[]{:T(128)}, f32[8,3,512]{2,1,0:T(4,128)}, s32[8,512]{1,0:T(8,128)S(1)}, f32[3,128,2048]{2,1,0:T(8,128)S(1)}, s32[]{:T(128)}) while((s32[]{:T(128)}, f32[8,3,512]{2,1,0:T(4,128)}, s32[8,512]{1,0:T(8,128)S(1)}, f32[3,128,2048]{2,1,0:T(8,128)S(1)}, s32[]{:T(128)}) %tuple.137), condition=%wide.region_8.9_spmd, body=%wide.region_6.8_spmd.sunk | while | flops 4833419264 | bytes 3705409 | solution.py:118
  162.5 3.2 %fusion.131 = f32[3,512]{1,0:T(4,128)S(1)} fusion(f32[3,128,2048]{2,1,0:T(8,128)S(1)} %get-tuple-element.423, s32[512]{0:T(512)S(1)} %get-tuple-element.369, f32[128,512]{1,0:T(8,128)S(1)} %fusion.130), kind=kOutput, calls=%fused_computation.28.clone.1 | convolution fusion | flops 4833278464 | bytes 3416064 | tf_op jit(solution)/shard_map/while/body/eval_jaxpr/srx,mx->srm/dot_general | solution.py:115
  166.3 3.2 %fusion.131 = f32[3,512]{1,0:T(4,128)S(1)} fusion(f32[3,128,2048]{2,1,0:T(8,128)S(1)} %get-tuple-element.423, s32[512]{0:T(512)S(1)} %get-tuple-element.369, f32[128,512]{1,0:T(8,128)S(1)} %fusion.130), kind=kOutput, calls=%fused_computation.28.clone.1 | convolution fusion | flops 4833278464 | bytes 3416064 | tf_op jit(solution)/shard_map/while/body/eval_jaxpr/srx,mx->srm/dot_general | solution.py:115
  170.2 3.2 %fusion.131 = f32[3,512]{1,0:T(4,128)S(1)} fusion(f32[3,128,2048]{2,1,0:T(8,128)S(1)} %get-tuple-element.423, s32[512]{0:T(512)S(1)} %get-tuple-element.369, f32[128,512]{1,0:T(8,128)S(1)} %fusion.130), kind=kOutput, calls=%fused_computation.28.clone.1 | convolution fusion | flops 4833278464 | bytes 3416064 | tf_op jit(solution)/shard_map/while/body/eval_jaxpr/srx,mx->srm/dot_general | solution.py:115
  174.0 3.2 %fusion.131 = f32[3,512]{1,0:T(4,128)S(1)} fusion(f32[3,128,2048]{2,1,0:T(8,128)S(1)} %get-tuple-element.423, s32[512]{0:T(512)S(1)} %get-tuple-element.369, f32[128,512]{1,0:T(8,128)S(1)} %fusion.130), kind=kOutput, calls=%fused_computation.28.clone.1 | convolution fusion | flops 4833278464 | bytes 3416064 | tf_op jit(solution)/shard_map/while/body/eval_jaxpr/srx,mx->srm/dot_general | solution.py:115
  177.8 3.2 %fusion.131 = f32[3,512]{1,0:T(4,128)S(1)} fusion(f32[3,128,2048]{2,1,0:T(8,128)S(1)} %get-tuple-element.423, s32[512]{0:T(512)S(1)} %get-tuple-element.369, f32[128,512]{1,0:T(8,128)S(1)} %fusion.130), kind=kOutput, calls=%fused_computation.28.clone.1 | convolution fusion | flops 4833278464 | bytes 3416064 | tf_op jit(solution)/shard_map/while/body/eval_jaxpr/srx,mx->srm/dot_general | solution.py:115
  181.7 3.2 %fusion.131 = f32[3,512]{1,0:T(4,128)S(1)} fusion(f32[3,128,2048]{2,1,0:T(8,128)S(1)} %get-tuple-element.423, s32[512]{0:T(512)S(1)} %get-tuple-element.369, f32[128,512]{1,0:T(8,128)S(1)} %fusion.130), kind=kOutput, calls=%fused_computation.28.clone.1 | convolution fusion | flops 4833278464 | bytes 3416064 | tf_op jit(solution)/shard_map/while/body/eval_jaxpr/srx,mx->srm/dot_general | solution.py:115
  185.5 3.2 %fusion.131 = f32[3,512]{1,0:T(4,128)S(1)} fusion(f32[3,128,2048]{2,1,0:T(8,128)S(1)} %get-tuple-element.423, s32[512]{0:T(512)S(1)} %get-tuple-element.369, f32[128,512]{1,0:T(8,128)S(1)} %fusion.130), kind=kOutput, calls=%fused_computation.28.clone.1 | convolution fusion | flops 4833278464 | bytes 3416064 | tf_op jit(solution)/shard_map/while/body/eval_jaxpr/srx,mx->srm/dot_general | solution.py:115
  189.3 3.2 %fusion.131 = f32[3,512]{1,0:T(4,128)S(1)} fusion(f32[3,128,2048]{2,1,0:T(8,128)S(1)} %get-tuple-element.423, s32[512]{0:T(512)S(1)} %get-tuple-element.369, f32[128,512]{1,0:T(8,128)S(1)} %fusion.130), kind=kOutput, calls=%fused_computation.28.clone.1 | convolution fusion | flops 4833278464 | bytes 3416064 | tf_op jit(solution)/shard_map/while/body/eval_jaxpr/srx,mx->srm/dot_general | solution.py:115
  193.1 12.6 %all-to-all-start.1 = ((f32[3,16,256]{2,0,1:T(4,128)}), f32[3,16,256]{2,0,1:T(4,128)S(1)}, u32[]{:S(2)}, u32[]{:S(2)}) async-start(f32[3,16,256]{2,0,1:T(4,128)} %bitcast.41), calls=%async_computation.1 | async-start | bytes 131072 | tf_op jit(solution)/shard_map/all_to_all | solution.py:308
  205.7 3.8 %broadcast_in_dim.311.cols_ref = f32[24,4,128,128]{3,2,1,0:T(8,128)} broadcast(f32[24,4,128]{2,1,0:T(4,128)S(1)} %maximum_bitcast_fusion.rows_ref), dimensions={0,1,2} | broadcast | bytes 6340608 | tf_op jit(solution)/shard_map/broadcast_in_dim | solution.py:181
  209.6 11.9 %shard_map.167 = f32[16,3,128]{2,1,0:T(4,128)} custom-call(s32[128]{0:T(128)} %reshape.863.chosen_ref, f32[24,4,128]{2,1,0:T(4,128)} %copy-done.1, f32[24,4,128,128]{3,2,1,0:T(8,128)} %broadcast_in_dim.311.cols_ref), custom_call_target="tpu_custom_call" | custom-call | flops 54525952 | bytes 6291456 | tf_op jit(solution)/shard_map/pallas_call | solution.py:183
  221.8 1.1 fusion.80
  223.1 1.1 maximum_select_fusion
  224.4 1.1 maximum_select_fusion.3
  (273 shorter events, 33.6 us)
Async XLA Ops:
  12.5 0.7 copy-start.7
  12.6 10.4 %copy-start.6 = (f32[2048]{0:T(1024)S(1)}, f32[2048]{0:T(1024)}, u32[]{:S(2)}) copy-start(f32[2048]{0:T(1024)} %param.23) | copy-start | bytes 24580
  12.6 10.5 %copy-start.2 = (f32[3,2048]{1,0:T(4,128)S(1)}, f32[3,2048]{1,0:T(4,128)}, u32[]{:S(2)}) copy-start(f32[3,2048]{1,0:T(4,128)} %param.22) | copy-start | bytes 73732
  13.2 13.5 %slice-start = ((f32[2,8,16,2048]{3,2,1,0:T(8,128)}), f32[1,8,16,2048]{3,2,1,0:T(8,128)S(1)}, s32[]{:S(2)}) async-start(f32[2,8,16,2048]{3,2,1,0:T(8,128)} %param.29), calls=%async_computation.2 | async-start | bytes 2097152 | tf_op jit(solution)/shard_map/slice | solution.py:288
  14.1 14.9 %all-to-all-start = ((f32[2,16,256]{2,0,1:T(2,128)}), f32[2,16,256]{2,0,1:T(2,128)S(1)}, u32[]{:S(2)}, u32[]{:S(2)}) async-start(f32[2,16,256]{2,0,1:T(2,128)} %fusion.85), calls=%async_computation | async-start | bytes 65536 | tf_op jit(solution)/shard_map/all_to_all | solution.py:283
  23.1 182.6 %collective-permute-start = (f32[4,512]{1,0:T(4,128)S(1)}, f32[4,512]{1,0:T(4,128)S(1)}, u32[]{:S(2)}, u32[]{:S(2)}) collective-permute-start(f32[4,512]{1,0:T(4,128)S(1)} %get-tuple-element.269), channel_id=1, source_target_pairs={{0,1},{1,2},{2,3},{3,4},{4,5},{5,6},{6,7},{7,8},{8,9},{9,10},{10,1... | collective-permute-start | bytes 24584 | tf_op jit(solution)/shard_map/ppermute | solution.py:34
  26.9 1.3 copy-start.8
  71.6 14.5 %collective-permute-start.2 = (f32[2,1,16,2048]{3,2,1,0:T(8,128)S(1)}, f32[2,1,16,2048]{3,2,1,0:T(8,128)S(1)}, u32[]{:S(2)}, u32[]{:S(2)}) collective-permute-start(f32[2,1,16,2048]{3,2,1,0:T(8,128)S(1)} %get-tuple-element.259), channel_id=1, source_target_pairs={{16,0},{32,16},{48,32},{64,48},{80,64},{96,80},{112,96},{17,1},{33... | collective-permute-start | bytes 786440 | tf_op jit(solution)/shard_map/ppermute | solution.py:204
  73.5 12.6 %collective-permute-start.3 = (f32[2,1,16,2048]{3,2,1,0:T(8,128)S(1)}, f32[2,1,16,2048]{3,2,1,0:T(8,128)S(1)}, u32[]{:S(2)}, u32[]{:S(2)}) collective-permute-start(f32[2,1,16,2048]{3,2,1,0:T(8,128)S(1)} %get-tuple-element.258), channel_id=1, source_target_pairs={{0,16},{16,32},{32,48},{48,64},{64,80},{80,96},{96,112},{1,17},{17... | collective-permute-start | bytes 786440 | tf_op jit(solution)/shard_map/ppermute | solution.py:203
  76.0 6.9 %collective-permute-start.4 = (f32[2,8,1,2048]{3,1,2,0:T(8,128)S(1)}, f32[2,8,1,2048]{3,1,2,0:T(8,128)S(1)}, u32[]{:S(2)}, u32[]{:S(2)}) collective-permute-start(f32[2,8,1,2048]{3,1,2,0:T(8,128)S(1)} %copy.79), channel_id=1, source_target_pairs={{1,0},{2,1},{3,2},{4,3},{5,4},{6,5},{7,6},{8,7},{9,8},{10,9},{11,1... | collective-permute-start | bytes 393224 | tf_op jit(solution)/shard_map/ppermute | solution.py:204
  79.1 7.0 %copy-start.4 = (f32[2]{0:T(128)S(1)}, f32[2]{0:T(128)}, u32[]{:S(2)}) copy-start(f32[2]{0:T(128)} %constant.220.clone) | copy-start | bytes 28
  79.1 7.0 %copy-start.5 = (f32[2]{0:T(128)S(1)}, f32[2]{0:T(128)}, u32[]{:S(2)}) copy-start(f32[2]{0:T(128)} %constant.221.clone) | copy-start | bytes 28
  79.1 6.9 %collective-permute-start.5 = (f32[2,8,1,2048]{3,1,2,0:T(8,128)S(1)}, f32[2,8,1,2048]{3,1,2,0:T(8,128)S(1)}, u32[]{:S(2)}, u32[]{:S(2)}) collective-permute-start(f32[2,8,1,2048]{3,1,2,0:T(8,128)S(1)} %copy.81), channel_id=1, source_target_pairs={{0,1},{1,2},{2,3},{3,4},{4,5},{5,6},{6,7},{7,8},{8,9},{9,10},{10,1... | collective-permute-start | bytes 393224 | tf_op jit(solution)/shard_map/ppermute | solution.py:203
  89.1 14.0 %collective-permute-start.6 = (f32[2,1,16,2048]{3,2,1,0:T(8,128)S(1)}, f32[2,1,16,2048]{3,2,1,0:T(8,128)S(1)}, u32[]{:S(2)}, u32[]{:S(2)}) collective-permute-start(f32[2,1,16,2048]{3,2,1,0:T(8,128)S(1)} %get-tuple-element.251), channel_id=1, source_target_pairs={{16,0},{32,16},{48,32},{64,48},{80,64},{96,80},{112,96},{17,1},{33... | collective-permute-start | bytes 786440 | tf_op jit(solution)/shard_map/ppermute | solution.py:204
  92.1 11.0 %collective-permute-start.7 = (f32[2,1,16,2048]{3,2,1,0:T(8,128)S(1)}, f32[2,1,16,2048]{3,2,1,0:T(8,128)S(1)}, u32[]{:S(2)}, u32[]{:S(2)}) collective-permute-start(f32[2,1,16,2048]{3,2,1,0:T(8,128)S(1)} %get-tuple-element.250), channel_id=1, source_target_pairs={{0,16},{16,32},{32,48},{48,64},{64,80},{80,96},{96,112},{1,17},{17... | collective-permute-start | bytes 786440 | tf_op jit(solution)/shard_map/ppermute | solution.py:203
  94.1 6.9 %collective-permute-start.8 = (f32[2,8,1,2048]{3,1,2,0:T(8,128)S(1)}, f32[2,8,1,2048]{3,1,2,0:T(8,128)S(1)}, u32[]{:S(2)}, u32[]{:S(2)}) collective-permute-start(f32[2,8,1,2048]{3,1,2,0:T(8,128)S(1)} %copy.83), channel_id=1, source_target_pairs={{1,0},{2,1},{3,2},{4,3},{5,4},{6,5},{7,6},{8,7},{9,8},{10,9},{11,1... | collective-permute-start | bytes 393224 | tf_op jit(solution)/shard_map/ppermute | solution.py:204
  96.1 6.9 %collective-permute-start.9 = (f32[2,8,1,2048]{3,1,2,0:T(8,128)S(1)}, f32[2,8,1,2048]{3,1,2,0:T(8,128)S(1)}, u32[]{:S(2)}, u32[]{:S(2)}) collective-permute-start(f32[2,8,1,2048]{3,1,2,0:T(8,128)S(1)} %copy.85), channel_id=1, source_target_pairs={{0,1},{1,2},{2,3},{3,4},{4,5},{5,6},{6,7},{7,8},{8,9},{9,10},{10,1... | collective-permute-start | bytes 393224 | tf_op jit(solution)/shard_map/ppermute | solution.py:203
  106.0 15.3 %collective-permute-start.10 = (f32[2,1,16,2048]{3,2,1,0:T(8,128)S(1)}, f32[2,1,16,2048]{3,2,1,0:T(8,128)S(1)}, u32[]{:S(2)}, u32[]{:S(2)}) collective-permute-start(f32[2,1,16,2048]{3,2,1,0:T(8,128)S(1)} %get-tuple-element.243), channel_id=1, source_target_pairs={{16,0},{32,16},{48,32},{64,48},{80,64},{96,80},{112,96},{17,1},{33... | collective-permute-start | bytes 786440 | tf_op jit(solution)/shard_map/ppermute | solution.py:204
  110.2 11.2 %collective-permute-start.11 = (f32[2,1,16,2048]{3,2,1,0:T(8,128)S(1)}, f32[2,1,16,2048]{3,2,1,0:T(8,128)S(1)}, u32[]{:S(2)}, u32[]{:S(2)}) collective-permute-start(f32[2,1,16,2048]{3,2,1,0:T(8,128)S(1)} %get-tuple-element.242), channel_id=1, source_target_pairs={{0,16},{16,32},{32,48},{48,64},{64,80},{80,96},{96,112},{1,17},{17... | collective-permute-start | bytes 786440 | tf_op jit(solution)/shard_map/ppermute | solution.py:203
  112.4 6.9 %collective-permute-start.12 = (f32[2,8,1,2048]{3,1,2,0:T(8,128)S(1)}, f32[2,8,1,2048]{3,1,2,0:T(8,128)S(1)}, u32[]{:S(2)}, u32[]{:S(2)}) collective-permute-start(f32[2,8,1,2048]{3,1,2,0:T(8,128)S(1)} %copy.87), channel_id=1, source_target_pairs={{1,0},{2,1},{3,2},{4,3},{5,4},{6,5},{7,6},{8,7},{9,8},{10,9},{11,1... | collective-permute-start | bytes 393224 | tf_op jit(solution)/shard_map/ppermute | solution.py:204
  114.3 6.9 %collective-permute-start.13 = (f32[2,8,1,2048]{3,1,2,0:T(8,128)S(1)}, f32[2,8,1,2048]{3,1,2,0:T(8,128)S(1)}, u32[]{:S(2)}, u32[]{:S(2)}) collective-permute-start(f32[2,8,1,2048]{3,1,2,0:T(8,128)S(1)} %copy.89), channel_id=1, source_target_pairs={{0,1},{1,2},{2,3},{3,4},{4,5},{5,6},{6,7},{7,8},{8,9},{9,10},{10,1... | collective-permute-start | bytes 393224 | tf_op jit(solution)/shard_map/ppermute | solution.py:203
  124.3 15.7 %collective-permute-start.14 = (f32[2,1,16,2048]{3,2,1,0:T(8,128)S(1)}, f32[2,1,16,2048]{3,2,1,0:T(8,128)S(1)}, u32[]{:S(2)}, u32[]{:S(2)}) collective-permute-start(f32[2,1,16,2048]{3,2,1,0:T(8,128)S(1)} %get-tuple-element.235), channel_id=1, source_target_pairs={{16,0},{32,16},{48,32},{64,48},{80,64},{96,80},{112,96},{17,1},{33... | collective-permute-start | bytes 786440 | tf_op jit(solution)/shard_map/ppermute | solution.py:204
  127.8 12.1 %collective-permute-start.15 = (f32[2,1,16,2048]{3,2,1,0:T(8,128)S(1)}, f32[2,1,16,2048]{3,2,1,0:T(8,128)S(1)}, u32[]{:S(2)}, u32[]{:S(2)}) collective-permute-start(f32[2,1,16,2048]{3,2,1,0:T(8,128)S(1)} %get-tuple-element.234), channel_id=1, source_target_pairs={{0,16},{16,32},{32,48},{48,64},{64,80},{80,96},{96,112},{1,17},{17... | collective-permute-start | bytes 786440 | tf_op jit(solution)/shard_map/ppermute | solution.py:203
  129.8 7.9 %collective-permute-start.16 = (f32[2,8,1,2048]{3,1,2,0:T(8,128)S(1)}, f32[2,8,1,2048]{3,1,2,0:T(8,128)S(1)}, u32[]{:S(2)}, u32[]{:S(2)}) collective-permute-start(f32[2,8,1,2048]{3,1,2,0:T(8,128)S(1)} %copy.91), channel_id=1, source_target_pairs={{1,0},{2,1},{3,2},{4,3},{5,4},{6,5},{7,6},{8,7},{9,8},{10,9},{11,1... | collective-permute-start | bytes 393224 | tf_op jit(solution)/shard_map/ppermute | solution.py:204
  131.7 8.0 %collective-permute-start.17 = (f32[2,8,1,2048]{3,1,2,0:T(8,128)S(1)}, f32[2,8,1,2048]{3,1,2,0:T(8,128)S(1)}, u32[]{:S(2)}, u32[]{:S(2)}) collective-permute-start(f32[2,8,1,2048]{3,1,2,0:T(8,128)S(1)} %copy.93), channel_id=1, source_target_pairs={{0,1},{1,2},{2,3},{3,4},{4,5},{5,6},{6,7},{7,8},{8,9},{9,10},{10,1... | collective-permute-start | bytes 393224 | tf_op jit(solution)/shard_map/ppermute | solution.py:203
  137.7 68.0 %collective-permute-start.1 = (f32[4,512]{1,0:T(4,128)S(1)}, f32[4,512]{1,0:T(4,128)S(1)}, u32[]{:S(2)}, u32[]{:S(2)}) collective-permute-start(f32[4,512]{1,0:T(4,128)S(1)} %get-tuple-element.270), channel_id=1, source_target_pairs={{1,0},{2,1},{3,2},{4,3},{5,4},{6,5},{7,6},{8,7},{9,8},{10,9},{11,1... | collective-permute-start | bytes 24584 | tf_op jit(solution)/shard_map/ppermute | solution.py:37
  142.1 1.3 copy-start
  143.8 12.0 %collective-permute-start.20 = (f32[8,1,2048]{2,1,0:T(1,128)S(1)}, f32[8,1,2048]{2,1,0:T(1,128)S(1)}, u32[]{:S(2)}, u32[]{:S(2)}) collective-permute-start(f32[8,1,2048]{2,1,0:T(1,128)S(1)} %get-tuple-element.263), channel_id=1, source_target_pairs={{1,0},{2,1},{3,2},{4,3},{5,4},{6,5},{7,6},{8,7},{9,8},{10,9},{11,1... | collective-permute-start | bytes 196616 | tf_op jit(solution)/shard_map/ppermute | solution.py:204
  145.7 12.0 %collective-permute-start.21 = (f32[8,1,2048]{2,1,0:T(1,128)S(1)}, f32[8,1,2048]{2,1,0:T(1,128)S(1)}, u32[]{:S(2)}, u32[]{:S(2)}) collective-permute-start(f32[8,1,2048]{2,1,0:T(1,128)S(1)} %get-tuple-element.262), channel_id=1, source_target_pairs={{0,1},{1,2},{2,3},{3,4},{4,5},{5,6},{6,7},{7,8},{8,9},{9,10},{10,1... | collective-permute-start | bytes 196616 | tf_op jit(solution)/shard_map/ppermute | solution.py:203
  152.8 5.4 %collective-permute-start.18 = (f32[1,16,2048]{2,1,0:T(8,128)S(1)}, f32[1,16,2048]{2,1,0:T(8,128)S(1)}, u32[]{:S(2)}, u32[]{:S(2)}) collective-permute-start(f32[1,16,2048]{2,1,0:T(8,128)S(1)} %get-tuple-element.227), channel_id=1, source_target_pairs={{16,0},{32,16},{48,32},{64,48},{80,64},{96,80},{112,96},{17,1},{33... | collective-permute-start | bytes 393224 | tf_op jit(solution)/shard_map/ppermute | solution.py:204
  155.8 6.3 %collective-permute-start.19 = (f32[1,16,2048]{2,1,0:T(8,128)S(1)}, f32[1,16,2048]{2,1,0:T(8,128)S(1)}, u32[]{:S(2)}, u32[]{:S(2)}) collective-permute-start(f32[1,16,2048]{2,1,0:T(8,128)S(1)} %get-tuple-element.226), channel_id=1, source_target_pairs={{0,16},{16,32},{32,48},{48,64},{64,80},{80,96},{96,112},{1,17},{17... | collective-permute-start | bytes 393224 | tf_op jit(solution)/shard_map/ppermute | solution.py:203
  193.1 28.4 %all-to-all-start.1 = ((f32[3,16,256]{2,0,1:T(4,128)}), f32[3,16,256]{2,0,1:T(4,128)S(1)}, u32[]{:S(2)}, u32[]{:S(2)}) async-start(f32[3,16,256]{2,0,1:T(4,128)} %bitcast.41), calls=%async_computation.1 | async-start | bytes 131072 | tf_op jit(solution)/shard_map/all_to_all | solution.py:308
  205.7 3.8 %copy-start.1 = (f32[24,4,128]{2,1,0:T(4,128)}, f32[24,4,128]{2,1,0:T(4,128)S(1)}, u32[]{:S(2)}) copy-start(f32[24,4,128]{2,1,0:T(4,128)S(1)} %maximum_bitcast_fusion.rows_ref) | copy-start | bytes 147460
  228.0 0.8 copy-start.3

commit v11 on v7

--- a/solution.py
+++ b/solution.py
@@ -158,7 +158,7 @@
                 strength = REPULSION * jnp.exp(-distance / REPEL_RANGE) - ADHESION * jnp.exp(
                     -distance / ADHERE_RANGE
                 )
-                weight = mine[3] * cols_ref[other, 3, part, :] * strength
+                weight = cols_ref[other, 3, part, :] * strength
                 for axis in range(3):
                     totals[axis] = totals[axis] + offset[axis] * weight
             return tuple(totals)
@@ -166,7 +166,7 @@
         zero = jnp.zeros(shape, jnp.float32)
         totals = lax.fori_loop(0, picks, one_pick, (zero, zero, zero))
         out_ref[block] = jnp.concatenate(
-            [jnp.sum(total, axis=0, keepdims=True) for total in totals], axis=0
+            [own[3:4, :] * jnp.sum(total, axis=0, keepdims=True) for total in totals], axis=0
         )
         return carry
 

time: 224 us -> 224 us (level)
  no operation moved by 1% of the time
where the time goes in v11:
time: 224 us; the launch traced here: 223 us
  starting transfers between devices  84.9 us (38%)
  matrix products  63.3 us (28%)
  other arithmetic  25.3 us (11%)
  local copies, waits for them, and re-layouts  21.9 us (10%)
  waiting for transfers between devices  12.7 us (6%)
  Pallas kernels  11.6 us (5%)
  between operations  2.41 us (1%)
    ppermute x10, starting transfers between devices, neighbours(): lax.ppermute(lax.slice_in_dim(block, block.shape[dim] - 1, None, axis=dim...  32.1 us
    ppermute x10, starting transfers between devices, neighbours(): high = lax.ppermute(lax.slice_in_dim(block, 0, 1, axis=dim), axis, backward)  26.6 us
    dot_general x8, matrix products, one_piece(): jnp.einsum('srx,mx->srm', fields, column_hot, precision=lax.Precision.HIG...  25.4 us
    dot_general x8, matrix products, add_piece(): jnp.einsum('smr,mx->srx', weighted, column_hot, precision=lax.Precision.H...  24.1 us
    dot_general x4, matrix products, one_piece(): jnp.einsum('psrx,mx->psrm', parts, column_hot, preferred_element_type=jnp...  13.8 us
    all_to_all x1, starting transfers between devices, local(): lax.all_to_all(slopes, 'tile', split_axis=1, concat_axis=1, tiled=True)  12.5 us
    pallas_call x1, Pallas kernels, pair_forces(): pl.pallas_call(force_kernel, out_shape=jax.ShapeDtypeStruct((blocks, 3, l...  11.6 us
    ppermute x10, waiting for transfers between devices, neighbours(): lax.ppermute(lax.slice_in_dim(block, block.shape[dim] - 1, None, axis=dim...  10.6 us
  transfers between devices with their start and end apart: 24, of which 8 were waited for; matrix products, arithmetic and copies ran while one was open for 42% of the time, Pallas kernels for 5%

profile of v11, /device:TPU:26, one launch (start us, length us, event | category | flops | bytes accessed | tf_op | source)
XLA Modules:
  0.0 222.8 jit_solution(9381131161515974648)
XLA Ops:
  1.3 0.7 pad_maximum_fusion.4
  2.0 0.8 fusion.84
  2.8 0.7 copy.71
  9.7 0.7 fusion.80
  10.4 8.3 %all-to-all-start = ((f32[2,16,256]{2,0,1:T(2,128)}), f32[2,16,256]{2,0,1:T(2,128)S(1)}, u32[]{:S(2)}, u32[]{:S(2)}) async-start(f32[2,16,256]{2,0,1:T(2,128)} %fusion.80), calls=%async_computation | async-start | bytes 65536 | tf_op jit(solution)/shard_map/all_to_all | solution.py:278
  19.4 3.4 %collective-permute-start = (f32[4,512]{1,0:T(4,128)S(1)}, f32[4,512]{1,0:T(4,128)S(1)}, u32[]{:S(2)}, u32[]{:S(2)}) collective-permute-start(f32[4,512]{1,0:T(4,128)S(1)} %get-tuple-element.269), channel_id=1, source_target_pairs={{0,1},{1,2},{2,3},{3,4},{4,5},{5,6},{6,7},{7,8},{8,9},{9,10},{10,1... | collective-permute-start | bytes 24584 | tf_op jit(solution)/shard_map/ppermute | solution.py:33
  23.1 1.3 pad_maximum_fusion.1
  25.2 14.7 %while.37 = (s32[]{:T(128)}, f32[4,1,1024]{2,1,0:T(1,128)S(1)}, s32[4,1024]{1,0:T(4,128)S(1)}, bf16[3,1,128,2048]{3,2,0,1:T(8,128)(2,1)}, s32[]{:T(128)}) while((s32[]{:T(128)}, f32[4,1,1024]{2,1,0:T(1,128)S(1)}, s32[4,1024]{1,0:T(4,128)S(1)}, bf16[3,1,128,2048]{3,2,0,1:T(8,128)(2,1)}, s32[]{:T(128)}) %tuple.121), condition=%wide.region_3.4_spmd, body=%wide.region_1.3_spmd.sunk | while | flops 1613645824 | bytes 4759621 | solution.py:104
  25.2 3.5 %fusion.118 = f32[3,128,1024]{2,1,0:T(8,128)S(1)} fusion(bf16[3,1,128,2048]{3,2,0,1:T(8,128)(2,1)} %get-tuple-element.383, s32[1024]{0:T(1024)S(1)} %get-tuple-element.356), kind=kOutput, calls=%fused_computation.5.clone.1 | convolution fusion | flops 1612709888 | bytes 3149824 | tf_op jit(solution)/shard_map/while/body/eval_jaxpr/psrx,mx->psrm/dot_general | solution.py:98
  28.9 3.5 %fusion.118 = f32[3,128,1024]{2,1,0:T(8,128)S(1)} fusion(bf16[3,1,128,2048]{3,2,0,1:T(8,128)(2,1)} %get-tuple-element.383, s32[1024]{0:T(1024)S(1)} %get-tuple-element.356), kind=kOutput, calls=%fused_computation.5.clone.1 | convolution fusion | flops 1612709888 | bytes 3149824 | tf_op jit(solution)/shard_map/while/body/eval_jaxpr/psrx,mx->psrm/dot_general | solution.py:98
  32.6 3.5 %fusion.118 = f32[3,128,1024]{2,1,0:T(8,128)S(1)} fusion(bf16[3,1,128,2048]{3,2,0,1:T(8,128)(2,1)} %get-tuple-element.383, s32[1024]{0:T(1024)S(1)} %get-tuple-element.356), kind=kOutput, calls=%fused_computation.5.clone.1 | convolution fusion | flops 1612709888 | bytes 3149824 | tf_op jit(solution)/shard_map/while/body/eval_jaxpr/psrx,mx->psrm/dot_general | solution.py:98
  36.3 3.5 %fusion.118 = f32[3,128,1024]{2,1,0:T(8,128)S(1)} fusion(bf16[3,1,128,2048]{3,2,0,1:T(8,128)(2,1)} %get-tuple-element.383, s32[1024]{0:T(1024)S(1)} %get-tuple-element.356), kind=kOutput, calls=%fused_computation.5.clone.1 | convolution fusion | flops 1612709888 | bytes 3149824 | tf_op jit(solution)/shard_map/while/body/eval_jaxpr/psrx,mx->psrm/dot_general | solution.py:98
  40.1 25.0 %while.39 = (s32[]{:T(128)}, f32[2,128,2048]{2,1,0:T(8,128)S(1)}, f32[8,2,512]{2,0,1:T(8,128)S(1)}, s32[8,512]{1,0:T(8,128)S(1)}, s32[]{:T(128)}, /*index=5*/s32[]{:T(128)}) while((s32[]{:T(128)}, f32[2,128,2048]{2,1,0:T(8,128)S(1)}, f32[8,2,512]{2,0,1:T(8,128)S(1)}, s32[8,512]{1,0:T(8,128)S(1)}, s32[]{:T(128)}, ...), condition=%wide.region_5.6_spmd.clone, body=%wide.region_4.5_spmd.clone.sunk | while | flops 3223594496 | bytes 4753495 | solution.py:137
  40.2 3.0 %fusion.127 = f32[2,128,2048]{2,1,0:T(8,128)S(1)} fusion(f32[2,128,2048]{2,1,0:T(8,128)S(1)} %get-tuple-element.392, s32[512]{0:T(512)S(1)} %get-tuple-element.368, pred[]{:T(512)S(6)} %compare.53, f32[512,128]{0,1:T(8,128)S(1)} %fusion.126, f32[2,512]{1,0:T(2,128)S(1)} %bitcast.141), kind=kOutput, calls=%fused_computation.44.clone.1 | convolution fusion | flops 3223453696 | bytes 4462593 | tf_op jit(solution)/shard_map/while/body/eval_jaxpr/smr,mx->srx/dot_general | solution.py:132
  43.3 3.0 %fusion.127 = f32[2,128,2048]{2,1,0:T(8,128)S(1)} fusion(f32[2,128,2048]{2,1,0:T(8,128)S(1)} %get-tuple-element.392, s32[512]{0:T(512)S(1)} %get-tuple-element.368, pred[]{:T(512)S(6)} %compare.53, f32[512,128]{0,1:T(8,128)S(1)} %fusion.126, f32[2,512]{1,0:T(2,128)S(1)} %bitcast.141), kind=kOutput, calls=%fused_computation.44.clone.1 | convolution fusion | flops 3223453696 | bytes 4462593 | tf_op jit(solution)/shard_map/while/body/eval_jaxpr/smr,mx->srx/dot_general | solution.py:132
  46.5 3.0 %fusion.127 = f32[2,128,2048]{2,1,0:T(8,128)S(1)} fusion(f32[2,128,2048]{2,1,0:T(8,128)S(1)} %get-tuple-element.392, s32[512]{0:T(512)S(1)} %get-tuple-element.368, pred[]{:T(512)S(6)} %compare.53, f32[512,128]{0,1:T(8,128)S(1)} %fusion.126, f32[2,512]{1,0:T(2,128)S(1)} %bitcast.141), kind=kOutput, calls=%fused_computation.44.clone.1 | convolution fusion | flops 3223453696 | bytes 4462593 | tf_op jit(solution)/shard_map/while/body/eval_jaxpr/smr,mx->srx/dot_general | solution.py:132
  49.6 3.0 %fusion.127 = f32[2,128,2048]{2,1,0:T(8,128)S(1)} fusion(f32[2,128,2048]{2,1,0:T(8,128)S(1)} %get-tuple-element.392, s32[512]{0:T(512)S(1)} %get-tuple-element.368, pred[]{:T(512)S(6)} %compare.53, f32[512,128]{0,1:T(8,128)S(1)} %fusion.126, f32[2,512]{1,0:T(2,128)S(1)} %bitcast.141), kind=kOutput, calls=%fused_computation.44.clone.1 | convolution fusion | flops 3223453696 | bytes 4462593 | tf_op jit(solution)/shard_map/while/body/eval_jaxpr/smr,mx->srx/dot_general | solution.py:132
  52.7 3.0 %fusion.127 = f32[2,128,2048]{2,1,0:T(8,128)S(1)} fusion(f32[2,128,2048]{2,1,0:T(8,128)S(1)} %get-tuple-element.392, s32[512]{0:T(512)S(1)} %get-tuple-element.368, pred[]{:T(512)S(6)} %compare.53, f32[512,128]{0,1:T(8,128)S(1)} %fusion.126, f32[2,512]{1,0:T(2,128)S(1)} %bitcast.141), kind=kOutput, calls=%fused_computation.44.clone.1 | convolution fusion | flops 3223453696 | bytes 4462593 | tf_op jit(solution)/shard_map/while/body/eval_jaxpr/smr,mx->srx/dot_general | solution.py:132
  55.9 3.0 %fusion.127 = f32[2,128,2048]{2,1,0:T(8,128)S(1)} fusion(f32[2,128,2048]{2,1,0:T(8,128)S(1)} %get-tuple-element.392, s32[512]{0:T(512)S(1)} %get-tuple-element.368, pred[]{:T(512)S(6)} %compare.53, f32[512,128]{0,1:T(8,128)S(1)} %fusion.126, f32[2,512]{1,0:T(2,128)S(1)} %bitcast.141), kind=kOutput, calls=%fused_computation.44.clone.1 | convolution fusion | flops 3223453696 | bytes 4462593 | tf_op jit(solution)/shard_map/while/body/eval_jaxpr/smr,mx->srx/dot_general | solution.py:132
  59.0 3.0 %fusion.127 = f32[2,128,2048]{2,1,0:T(8,128)S(1)} fusion(f32[2,128,2048]{2,1,0:T(8,128)S(1)} %get-tuple-element.392, s32[512]{0:T(512)S(1)} %get-tuple-element.368, pred[]{:T(512)S(6)} %compare.53, f32[512,128]{0,1:T(8,128)S(1)} %fusion.126, f32[2,512]{1,0:T(2,128)S(1)} %bitcast.141), kind=kOutput, calls=%fused_computation.44.clone.1 | convolution fusion | flops 3223453696 | bytes 4462593 | tf_op jit(solution)/shard_map/while/body/eval_jaxpr/smr,mx->srx/dot_general | solution.py:132
  62.1 3.0 %fusion.127 = f32[2,128,2048]{2,1,0:T(8,128)S(1)} fusion(f32[2,128,2048]{2,1,0:T(8,128)S(1)} %get-tuple-element.392, s32[512]{0:T(512)S(1)} %get-tuple-element.368, pred[]{:T(512)S(6)} %compare.53, f32[512,128]{0,1:T(8,128)S(1)} %fusion.126, f32[2,512]{1,0:T(2,128)S(1)} %bitcast.141), kind=kOutput, calls=%fused_computation.44.clone.1 | convolution fusion | flops 3223453696 | bytes 4462593 | tf_op jit(solution)/shard_map/while/body/eval_jaxpr/smr,mx->srx/dot_general | solution.py:132
  65.2 1.8 add.225
  67.7 2.1 collective-permute-start.2
  69.8 2.4 %collective-permute-start.3 = (f32[2,1,16,2048]{3,2,1,0:T(8,128)S(1)}, f32[2,1,16,2048]{3,2,1,0:T(8,128)S(1)}, u32[]{:S(2)}, u32[]{:S(2)}) collective-permute-start(f32[2,1,16,2048]{3,2,1,0:T(8,128)S(1)} %get-tuple-element.258), channel_id=1, source_target_pairs={{0,16},{16,32},{32,48},{48,64},{64,80},{80,96},{96,112},{1,17},{17... | collective-permute-start | bytes 786440 | tf_op jit(solution)/shard_map/ppermute | solution.py:202
  72.3 3.2 %collective-permute-start.4 = (f32[2,8,1,2048]{3,1,2,0:T(8,128)S(1)}, f32[2,8,1,2048]{3,1,2,0:T(8,128)S(1)}, u32[]{:S(2)}, u32[]{:S(2)}) collective-permute-start(f32[2,8,1,2048]{3,1,2,0:T(8,128)S(1)} %copy.75), channel_id=1, source_target_pairs={{1,0},{2,1},{3,2},{4,3},{5,4},{6,5},{7,6},{8,7},{9,8},{10,9},{11,1... | collective-permute-start | bytes 393224 | tf_op jit(solution)/shard_map/ppermute | solution.py:203
  75.6 2.6 %collective-permute-start.5 = (f32[2,8,1,2048]{3,1,2,0:T(8,128)S(1)}, f32[2,8,1,2048]{3,1,2,0:T(8,128)S(1)}, u32[]{:S(2)}, u32[]{:S(2)}) collective-permute-start(f32[2,8,1,2048]{3,1,2,0:T(8,128)S(1)} %copy.77), channel_id=1, source_target_pairs={{0,1},{1,2},{2,3},{3,4},{4,5},{5,6},{6,7},{7,8},{8,9},{9,10},{10,1... | collective-permute-start | bytes 393224 | tf_op jit(solution)/shard_map/ppermute | solution.py:202
  79.3 3.2 %collective-permute-done.5 = f32[2,8,1,2048]{3,1,2,0:T(8,128)S(1)} collective-permute-done((f32[2,8,1,2048]{3,1,2,0:T(8,128)S(1)}, f32[2,8,1,2048]{3,1,2,0:T(8,128)S(1)}, u32[]{:S(2)}, u32[]{:S(2)}) %collective-permute-start.5) | collective-permute-done | bytes 131104 | tf_op jit(solution)/shard_map/ppermute | solution.py:202
  82.6 2.2 fusion.47
  85.5 3.1 %collective-permute-start.6 = (f32[2,1,16,2048]{3,2,1,0:T(8,128)S(1)}, f32[2,1,16,2048]{3,2,1,0:T(8,128)S(1)}, u32[]{:S(2)}, u32[]{:S(2)}) collective-permute-start(f32[2,1,16,2048]{3,2,1,0:T(8,128)S(1)} %get-tuple-element.251), channel_id=1, source_target_pairs={{16,0},{32,16},{48,32},{64,48},{80,64},{96,80},{112,96},{17,1},{33... | collective-permute-start | bytes 786440 | tf_op jit(solution)/shard_map/ppermute | solution.py:203
  88.6 1.9 collective-permute-start.7
  90.6 1.9 collective-permute-start.8
  92.6 3.9 %collective-permute-start.9 = (f32[2,8,1,2048]{3,1,2,0:T(8,128)S(1)}, f32[2,8,1,2048]{3,1,2,0:T(8,128)S(1)}, u32[]{:S(2)}, u32[]{:S(2)}) collective-permute-start(f32[2,8,1,2048]{3,1,2,0:T(8,128)S(1)} %copy.81), channel_id=1, source_target_pairs={{0,1},{1,2},{2,3},{3,4},{4,5},{5,6},{6,7},{7,8},{8,9},{9,10},{10,1... | collective-permute-start | bytes 393224 | tf_op jit(solution)/shard_map/ppermute | solution.py:202
  97.6 1.8 collective-permute-done.9
  99.6 2.2 fusion.53
  102.5 4.1 %collective-permute-start.10 = (f32[2,1,16,2048]{3,2,1,0:T(8,128)S(1)}, f32[2,1,16,2048]{3,2,1,0:T(8,128)S(1)}, u32[]{:S(2)}, u32[]{:S(2)}) collective-permute-start(f32[2,1,16,2048]{3,2,1,0:T(8,128)S(1)} %get-tuple-element.243), channel_id=1, source_target_pairs={{16,0},{32,16},{48,32},{64,48},{80,64},{96,80},{112,96},{17,1},{33... | collective-permute-start | bytes 786440 | tf_op jit(solution)/shard_map/ppermute | solution.py:203
  106.6 1.9 collective-permute-start.11
  108.6 1.9 collective-permute-start.12
  110.6 3.9 %collective-permute-start.13 = (f32[2,8,1,2048]{3,1,2,0:T(8,128)S(1)}, f32[2,8,1,2048]{3,1,2,0:T(8,128)S(1)}, u32[]{:S(2)}, u32[]{:S(2)}) collective-permute-start(f32[2,8,1,2048]{3,1,2,0:T(8,128)S(1)} %copy.85), channel_id=1, source_target_pairs={{0,1},{1,2},{2,3},{3,4},{4,5},{5,6},{6,7},{7,8},{8,9},{9,10},{10,1... | collective-permute-start | bytes 393224 | tf_op jit(solution)/shard_map/ppermute | solution.py:202
  115.6 1.8 collective-permute-done.13
  117.6 2.2 fusion.59
  120.5 3.5 %collective-permute-start.14 = (f32[2,1,16,2048]{3,2,1,0:T(8,128)S(1)}, f32[2,1,16,2048]{3,2,1,0:T(8,128)S(1)}, u32[]{:S(2)}, u32[]{:S(2)}) collective-permute-start(f32[2,1,16,2048]{3,2,1,0:T(8,128)S(1)} %get-tuple-element.235), channel_id=1, source_target_pairs={{16,0},{32,16},{48,32},{64,48},{80,64},{96,80},{112,96},{17,1},{33... | collective-permute-start | bytes 786440 | tf_op jit(solution)/shard_map/ppermute | solution.py:203
  124.0 1.9 collective-permute-start.15
  126.0 1.9 collective-permute-start.16
  128.0 4.8 %collective-permute-start.17 = (f32[2,8,1,2048]{3,1,2,0:T(8,128)S(1)}, f32[2,8,1,2048]{3,1,2,0:T(8,128)S(1)}, u32[]{:S(2)}, u32[]{:S(2)}) collective-permute-start(f32[2,8,1,2048]{3,1,2,0:T(8,128)S(1)} %copy.89), channel_id=1, source_target_pairs={{0,1},{1,2},{2,3},{3,4},{4,5},{5,6},{6,7},{7,8},{8,9},{9,10},{10,1... | collective-permute-start | bytes 393224 | tf_op jit(solution)/shard_map/ppermute | solution.py:202
  133.8 1.9 collective-permute-start.1
  136.0 2.2 fusion.65
  138.4 1.1 copy-done
  139.9 1.9 collective-permute-start.20
  141.8 6.5 %collective-permute-start.21 = (f32[8,1,2048]{2,1,0:T(1,128)S(1)}, f32[8,1,2048]{2,1,0:T(1,128)S(1)}, u32[]{:S(2)}, u32[]{:S(2)}) collective-permute-start(f32[8,1,2048]{2,1,0:T(1,128)S(1)} %get-tuple-element.262), channel_id=1, source_target_pairs={{0,1},{1,2},{2,3},{3,4},{4,5},{5,6},{6,7},{7,8},{8,9},{9,10},{10,1... | collective-permute-start | bytes 196616 | tf_op jit(solution)/shard_map/ppermute | solution.py:202
  148.9 2.9 %collective-permute-start.18 = (f32[1,16,2048]{2,1,0:T(8,128)S(1)}, f32[1,16,2048]{2,1,0:T(8,128)S(1)}, u32[]{:S(2)}, u32[]{:S(2)}) collective-permute-start(f32[1,16,2048]{2,1,0:T(8,128)S(1)} %get-tuple-element.227), channel_id=1, source_target_pairs={{16,0},{32,16},{48,32},{64,48},{80,64},{96,80},{112,96},{17,1},{33... | collective-permute-start | bytes 393224 | tf_op jit(solution)/shard_map/ppermute | solution.py:203
  151.9 2.1 collective-permute-start.19
  154.3 3.8 %collective-permute-done.19 = f32[1,16,2048]{2,1,0:T(8,128)S(1)} collective-permute-done((f32[1,16,2048]{2,1,0:T(8,128)S(1)}, f32[1,16,2048]{2,1,0:T(8,128)S(1)}, u32[]{:S(2)}, u32[]{:S(2)}) %collective-permute-start.19) | collective-permute-done | bytes 131104 | tf_op jit(solution)/shard_map/ppermute | solution.py:202
  158.5 30.7 %while.38 = (s32[]{:T(128)}, f32[8,3,512]{2,1,0:T(4,128)}, s32[8,512]{1,0:T(8,128)S(1)}, f32[3,128,2048]{2,1,0:T(8,128)S(1)}, s32[]{:T(128)}) while((s32[]{:T(128)}, f32[8,3,512]{2,1,0:T(4,128)}, s32[8,512]{1,0:T(8,128)S(1)}, f32[3,128,2048]{2,1,0:T(8,128)S(1)}, s32[]{:T(128)}) %tuple.130), condition=%wide.region_8.9_spmd, body=%wide.region_6.8_spmd.sunk | while | flops 4833419264 | bytes 3705409 | solution.py:117
  158.6 3.2 %fusion.123 = f32[3,512]{1,0:T(4,128)S(1)} fusion(f32[3,128,2048]{2,1,0:T(8,128)S(1)} %get-tuple-element.416, s32[512]{0:T(512)S(1)} %get-tuple-element.362, f32[128,512]{1,0:T(8,128)S(1)} %fusion.122), kind=kOutput, calls=%fused_computation.28.clone.1 | convolution fusion | flops 4833278464 | bytes 3416064 | tf_op jit(solution)/shard_map/while/body/eval_jaxpr/srx,mx->srm/dot_general | solution.py:114
  162.4 3.2 %fusion.123 = f32[3,512]{1,0:T(4,128)S(1)} fusion(f32[3,128,2048]{2,1,0:T(8,128)S(1)} %get-tuple-element.416, s32[512]{0:T(512)S(1)} %get-tuple-element.362, f32[128,512]{1,0:T(8,128)S(1)} %fusion.122), kind=kOutput, calls=%fused_computation.28.clone.1 | convolution fusion | flops 4833278464 | bytes 3416064 | tf_op jit(solution)/shard_map/while/body/eval_jaxpr/srx,mx->srm/dot_general | solution.py:114
  166.2 3.2 %fusion.123 = f32[3,512]{1,0:T(4,128)S(1)} fusion(f32[3,128,2048]{2,1,0:T(8,128)S(1)} %get-tuple-element.416, s32[512]{0:T(512)S(1)} %get-tuple-element.362, f32[128,512]{1,0:T(8,128)S(1)} %fusion.122), kind=kOutput, calls=%fused_computation.28.clone.1 | convolution fusion | flops 4833278464 | bytes 3416064 | tf_op jit(solution)/shard_map/while/body/eval_jaxpr/srx,mx->srm/dot_general | solution.py:114
  170.1 3.2 %fusion.123 = f32[3,512]{1,0:T(4,128)S(1)} fusion(f32[3,128,2048]{2,1,0:T(8,128)S(1)} %get-tuple-element.416, s32[512]{0:T(512)S(1)} %get-tuple-element.362, f32[128,512]{1,0:T(8,128)S(1)} %fusion.122), kind=kOutput, calls=%fused_computation.28.clone.1 | convolution fusion | flops 4833278464 | bytes 3416064 | tf_op jit(solution)/shard_map/while/body/eval_jaxpr/srx,mx->srm/dot_general | solution.py:114
  173.9 3.2 %fusion.123 = f32[3,512]{1,0:T(4,128)S(1)} fusion(f32[3,128,2048]{2,1,0:T(8,128)S(1)} %get-tuple-element.416, s32[512]{0:T(512)S(1)} %get-tuple-element.362, f32[128,512]{1,0:T(8,128)S(1)} %fusion.122), kind=kOutput, calls=%fused_computation.28.clone.1 | convolution fusion | flops 4833278464 | bytes 3416064 | tf_op jit(solution)/shard_map/while/body/eval_jaxpr/srx,mx->srm/dot_general | solution.py:114
  177.8 3.2 %fusion.123 = f32[3,512]{1,0:T(4,128)S(1)} fusion(f32[3,128,2048]{2,1,0:T(8,128)S(1)} %get-tuple-element.416, s32[512]{0:T(512)S(1)} %get-tuple-element.362, f32[128,512]{1,0:T(8,128)S(1)} %fusion.122), kind=kOutput, calls=%fused_computation.28.clone.1 | convolution fusion | flops 4833278464 | bytes 3416064 | tf_op jit(solution)/shard_map/while/body/eval_jaxpr/srx,mx->srm/dot_general | solution.py:114
  181.6 3.2 %fusion.123 = f32[3,512]{1,0:T(4,128)S(1)} fusion(f32[3,128,2048]{2,1,0:T(8,128)S(1)} %get-tuple-element.416, s32[512]{0:T(512)S(1)} %get-tuple-element.362, f32[128,512]{1,0:T(8,128)S(1)} %fusion.122), kind=kOutput, calls=%fused_computation.28.clone.1 | convolution fusion | flops 4833278464 | bytes 3416064 | tf_op jit(solution)/shard_map/while/body/eval_jaxpr/srx,mx->srm/dot_general | solution.py:114
  185.4 3.2 %fusion.123 = f32[3,512]{1,0:T(4,128)S(1)} fusion(f32[3,128,2048]{2,1,0:T(8,128)S(1)} %get-tuple-element.416, s32[512]{0:T(512)S(1)} %get-tuple-element.362, f32[128,512]{1,0:T(8,128)S(1)} %fusion.122), kind=kOutput, calls=%fused_computation.28.clone.1 | convolution fusion | flops 4833278464 | bytes 3416064 | tf_op jit(solution)/shard_map/while/body/eval_jaxpr/srx,mx->srm/dot_general | solution.py:114
  189.2 12.5 %all-to-all-start.1 = ((f32[3,16,256]{2,0,1:T(4,128)}), f32[3,16,256]{2,0,1:T(4,128)S(1)}, u32[]{:S(2)}, u32[]{:S(2)}) async-start(f32[3,16,256]{2,0,1:T(4,128)} %bitcast.41), calls=%async_computation.1 | async-start | bytes 131072 | tf_op jit(solution)/shard_map/all_to_all | solution.py:303
  201.8 3.8 %broadcast_in_dim.243.cols_ref = f32[24,4,128,128]{3,2,1,0:T(8,128)} broadcast(f32[24,4,128]{2,1,0:T(4,128)S(1)} %maximum_bitcast_fusion.rows_ref), dimensions={0,1,2} | broadcast | bytes 6340608 | tf_op jit(solution)/shard_map/broadcast_in_dim | solution.py:180
  205.6 11.6 %shard_map.167 = f32[16,3,128]{2,1,0:T(4,128)} custom-call(s32[128]{0:T(128)} %reshape.806.chosen_ref, f32[24,4,128]{2,1,0:T(4,128)} %copy-done.1, f32[24,4,128,128]{3,2,1,0:T(8,128)} %broadcast_in_dim.243.cols_ref), custom_call_target="tpu_custom_call" | custom-call | flops 54525952 | bytes 6291456 | tf_op jit(solution)/shard_map/pallas_call | solution.py:182
  (254 shorter events, 29.5 us)
Async XLA Ops:
  8.7 0.9 copy-start.7
  9.0 10.4 %copy-start.6 = (f32[2048]{0:T(1024)S(1)}, f32[2048]{0:T(1024)}, u32[]{:S(2)}) copy-start(f32[2048]{0:T(1024)} %param.23) | copy-start | bytes 24580
  9.0 10.4 %copy-start.2 = (f32[3,2048]{1,0:T(4,128)S(1)}, f32[3,2048]{1,0:T(4,128)}, u32[]{:S(2)}) copy-start(f32[3,2048]{1,0:T(4,128)} %param.22) | copy-start | bytes 73732
  9.3 13.5 %slice-start = ((f32[2,8,16,2048]{3,2,1,0:T(8,128)}), f32[1,8,16,2048]{3,2,1,0:T(8,128)S(1)}, s32[]{:S(2)}) async-start(f32[2,8,16,2048]{3,2,1,0:T(8,128)} %param.29), calls=%async_computation.2 | async-start | bytes 2097152 | tf_op jit(solution)/shard_map/slice | solution.py:283
  10.4 14.7 %all-to-all-start = ((f32[2,16,256]{2,0,1:T(2,128)}), f32[2,16,256]{2,0,1:T(2,128)S(1)}, u32[]{:S(2)}, u32[]{:S(2)}) async-start(f32[2,16,256]{2,0,1:T(2,128)} %fusion.80), calls=%async_computation | async-start | bytes 65536 | tf_op jit(solution)/shard_map/all_to_all | solution.py:278
  19.4 182.3 %collective-permute-start = (f32[4,512]{1,0:T(4,128)S(1)}, f32[4,512]{1,0:T(4,128)S(1)}, u32[]{:S(2)}, u32[]{:S(2)}) collective-permute-start(f32[4,512]{1,0:T(4,128)S(1)} %get-tuple-element.269), channel_id=1, source_target_pairs={{0,1},{1,2},{2,3},{3,4},{4,5},{5,6},{6,7},{7,8},{8,9},{9,10},{10,1... | collective-permute-start | bytes 24584 | tf_op jit(solution)/shard_map/ppermute | solution.py:33
  23.0 1.3 copy-start.8
  67.7 14.9 %collective-permute-start.2 = (f32[2,1,16,2048]{3,2,1,0:T(8,128)S(1)}, f32[2,1,16,2048]{3,2,1,0:T(8,128)S(1)}, u32[]{:S(2)}, u32[]{:S(2)}) collective-permute-start(f32[2,1,16,2048]{3,2,1,0:T(8,128)S(1)} %get-tuple-element.259), channel_id=1, source_target_pairs={{16,0},{32,16},{48,32},{64,48},{80,64},{96,80},{112,96},{17,1},{33... | collective-permute-start | bytes 786440 | tf_op jit(solution)/shard_map/ppermute | solution.py:203
  69.8 12.8 %collective-permute-start.3 = (f32[2,1,16,2048]{3,2,1,0:T(8,128)S(1)}, f32[2,1,16,2048]{3,2,1,0:T(8,128)S(1)}, u32[]{:S(2)}, u32[]{:S(2)}) collective-permute-start(f32[2,1,16,2048]{3,2,1,0:T(8,128)S(1)} %get-tuple-element.258), channel_id=1, source_target_pairs={{0,16},{16,32},{32,48},{48,64},{64,80},{80,96},{96,112},{1,17},{17... | collective-permute-start | bytes 786440 | tf_op jit(solution)/shard_map/ppermute | solution.py:202
  72.3 6.9 %collective-permute-start.4 = (f32[2,8,1,2048]{3,1,2,0:T(8,128)S(1)}, f32[2,8,1,2048]{3,1,2,0:T(8,128)S(1)}, u32[]{:S(2)}, u32[]{:S(2)}) collective-permute-start(f32[2,8,1,2048]{3,1,2,0:T(8,128)S(1)} %copy.75), channel_id=1, source_target_pairs={{1,0},{2,1},{3,2},{4,3},{5,4},{6,5},{7,6},{8,7},{9,8},{10,9},{11,1... | collective-permute-start | bytes 393224 | tf_op jit(solution)/shard_map/ppermute | solution.py:203
  75.6 7.0 %copy-start.4 = (f32[2]{0:T(128)S(1)}, f32[2]{0:T(128)}, u32[]{:S(2)}) copy-start(f32[2]{0:T(128)} %constant.224.clone) | copy-start | bytes 28
  75.6 7.0 %copy-start.5 = (f32[2]{0:T(128)S(1)}, f32[2]{0:T(128)}, u32[]{:S(2)}) copy-start(f32[2]{0:T(128)} %constant.225.clone) | copy-start | bytes 28
  75.6 6.9 %collective-permute-start.5 = (f32[2,8,1,2048]{3,1,2,0:T(8,128)S(1)}, f32[2,8,1,2048]{3,1,2,0:T(8,128)S(1)}, u32[]{:S(2)}, u32[]{:S(2)}) collective-permute-start(f32[2,8,1,2048]{3,1,2,0:T(8,128)S(1)} %copy.77), channel_id=1, source_target_pairs={{0,1},{1,2},{2,3},{3,4},{4,5},{5,6},{6,7},{7,8},{8,9},{9,10},{10,1... | collective-permute-start | bytes 393224 | tf_op jit(solution)/shard_map/ppermute | solution.py:202
  85.5 14.0 %collective-permute-start.6 = (f32[2,1,16,2048]{3,2,1,0:T(8,128)S(1)}, f32[2,1,16,2048]{3,2,1,0:T(8,128)S(1)}, u32[]{:S(2)}, u32[]{:S(2)}) collective-permute-start(f32[2,1,16,2048]{3,2,1,0:T(8,128)S(1)} %get-tuple-element.251), channel_id=1, source_target_pairs={{16,0},{32,16},{48,32},{64,48},{80,64},{96,80},{112,96},{17,1},{33... | collective-permute-start | bytes 786440 | tf_op jit(solution)/shard_map/ppermute | solution.py:203
  88.6 11.0 %collective-permute-start.7 = (f32[2,1,16,2048]{3,2,1,0:T(8,128)S(1)}, f32[2,1,16,2048]{3,2,1,0:T(8,128)S(1)}, u32[]{:S(2)}, u32[]{:S(2)}) collective-permute-start(f32[2,1,16,2048]{3,2,1,0:T(8,128)S(1)} %get-tuple-element.250), channel_id=1, source_target_pairs={{0,16},{16,32},{32,48},{48,64},{64,80},{80,96},{96,112},{1,17},{17... | collective-permute-start | bytes 786440 | tf_op jit(solution)/shard_map/ppermute | solution.py:202
  90.6 6.9 %collective-permute-start.8 = (f32[2,8,1,2048]{3,1,2,0:T(8,128)S(1)}, f32[2,8,1,2048]{3,1,2,0:T(8,128)S(1)}, u32[]{:S(2)}, u32[]{:S(2)}) collective-permute-start(f32[2,8,1,2048]{3,1,2,0:T(8,128)S(1)} %copy.79), channel_id=1, source_target_pairs={{1,0},{2,1},{3,2},{4,3},{5,4},{6,5},{7,6},{8,7},{9,8},{10,9},{11,1... | collective-permute-start | bytes 393224 | tf_op jit(solution)/shard_map/ppermute | solution.py:203
  92.6 6.9 %collective-permute-start.9 = (f32[2,8,1,2048]{3,1,2,0:T(8,128)S(1)}, f32[2,8,1,2048]{3,1,2,0:T(8,128)S(1)}, u32[]{:S(2)}, u32[]{:S(2)}) collective-permute-start(f32[2,8,1,2048]{3,1,2,0:T(8,128)S(1)} %copy.81), channel_id=1, source_target_pairs={{0,1},{1,2},{2,3},{3,4},{4,5},{5,6},{6,7},{7,8},{8,9},{9,10},{10,1... | collective-permute-start | bytes 393224 | tf_op jit(solution)/shard_map/ppermute | solution.py:202
  102.5 15.1 %collective-permute-start.10 = (f32[2,1,16,2048]{3,2,1,0:T(8,128)S(1)}, f32[2,1,16,2048]{3,2,1,0:T(8,128)S(1)}, u32[]{:S(2)}, u32[]{:S(2)}) collective-permute-start(f32[2,1,16,2048]{3,2,1,0:T(8,128)S(1)} %get-tuple-element.243), channel_id=1, source_target_pairs={{16,0},{32,16},{48,32},{64,48},{80,64},{96,80},{112,96},{17,1},{33... | collective-permute-start | bytes 786440 | tf_op jit(solution)/shard_map/ppermute | solution.py:203
  106.6 11.0 %collective-permute-start.11 = (f32[2,1,16,2048]{3,2,1,0:T(8,128)S(1)}, f32[2,1,16,2048]{3,2,1,0:T(8,128)S(1)}, u32[]{:S(2)}, u32[]{:S(2)}) collective-permute-start(f32[2,1,16,2048]{3,2,1,0:T(8,128)S(1)} %get-tuple-element.242), channel_id=1, source_target_pairs={{0,16},{16,32},{32,48},{48,64},{64,80},{80,96},{96,112},{1,17},{17... | collective-permute-start | bytes 786440 | tf_op jit(solution)/shard_map/ppermute | solution.py:202
  108.6 6.9 %collective-permute-start.12 = (f32[2,8,1,2048]{3,1,2,0:T(8,128)S(1)}, f32[2,8,1,2048]{3,1,2,0:T(8,128)S(1)}, u32[]{:S(2)}, u32[]{:S(2)}) collective-permute-start(f32[2,8,1,2048]{3,1,2,0:T(8,128)S(1)} %copy.83), channel_id=1, source_target_pairs={{1,0},{2,1},{3,2},{4,3},{5,4},{6,5},{7,6},{8,7},{9,8},{10,9},{11,1... | collective-permute-start | bytes 393224 | tf_op jit(solution)/shard_map/ppermute | solution.py:203
  110.6 6.9 %collective-permute-start.13 = (f32[2,8,1,2048]{3,1,2,0:T(8,128)S(1)}, f32[2,8,1,2048]{3,1,2,0:T(8,128)S(1)}, u32[]{:S(2)}, u32[]{:S(2)}) collective-permute-start(f32[2,8,1,2048]{3,1,2,0:T(8,128)S(1)} %copy.85), channel_id=1, source_target_pairs={{0,1},{1,2},{2,3},{3,4},{4,5},{5,6},{6,7},{7,8},{8,9},{9,10},{10,1... | collective-permute-start | bytes 393224 | tf_op jit(solution)/shard_map/ppermute | solution.py:202
  120.5 15.5 %collective-permute-start.14 = (f32[2,1,16,2048]{3,2,1,0:T(8,128)S(1)}, f32[2,1,16,2048]{3,2,1,0:T(8,128)S(1)}, u32[]{:S(2)}, u32[]{:S(2)}) collective-permute-start(f32[2,1,16,2048]{3,2,1,0:T(8,128)S(1)} %get-tuple-element.235), channel_id=1, source_target_pairs={{16,0},{32,16},{48,32},{64,48},{80,64},{96,80},{112,96},{17,1},{33... | collective-permute-start | bytes 786440 | tf_op jit(solution)/shard_map/ppermute | solution.py:203
  124.0 12.0 %collective-permute-start.15 = (f32[2,1,16,2048]{3,2,1,0:T(8,128)S(1)}, f32[2,1,16,2048]{3,2,1,0:T(8,128)S(1)}, u32[]{:S(2)}, u32[]{:S(2)}) collective-permute-start(f32[2,1,16,2048]{3,2,1,0:T(8,128)S(1)} %get-tuple-element.234), channel_id=1, source_target_pairs={{0,16},{16,32},{32,48},{48,64},{64,80},{80,96},{96,112},{1,17},{17... | collective-permute-start | bytes 786440 | tf_op jit(solution)/shard_map/ppermute | solution.py:202
  126.0 7.8 %collective-permute-start.16 = (f32[2,8,1,2048]{3,1,2,0:T(8,128)S(1)}, f32[2,8,1,2048]{3,1,2,0:T(8,128)S(1)}, u32[]{:S(2)}, u32[]{:S(2)}) collective-permute-start(f32[2,8,1,2048]{3,1,2,0:T(8,128)S(1)} %copy.87), channel_id=1, source_target_pairs={{1,0},{2,1},{3,2},{4,3},{5,4},{6,5},{7,6},{8,7},{9,8},{10,9},{11,1... | collective-permute-start | bytes 393224 | tf_op jit(solution)/shard_map/ppermute | solution.py:203
  128.0 7.8 %collective-permute-start.17 = (f32[2,8,1,2048]{3,1,2,0:T(8,128)S(1)}, f32[2,8,1,2048]{3,1,2,0:T(8,128)S(1)}, u32[]{:S(2)}, u32[]{:S(2)}) collective-permute-start(f32[2,8,1,2048]{3,1,2,0:T(8,128)S(1)} %copy.89), channel_id=1, source_target_pairs={{0,1},{1,2},{2,3},{3,4},{4,5},{5,6},{6,7},{7,8},{8,9},{9,10},{10,1... | collective-permute-start | bytes 393224 | tf_op jit(solution)/shard_map/ppermute | solution.py:202
  133.8 68.0 %collective-permute-start.1 = (f32[4,512]{1,0:T(4,128)S(1)}, f32[4,512]{1,0:T(4,128)S(1)}, u32[]{:S(2)}, u32[]{:S(2)}) collective-permute-start(f32[4,512]{1,0:T(4,128)S(1)} %get-tuple-element.270), channel_id=1, source_target_pairs={{1,0},{2,1},{3,2},{4,3},{5,4},{6,5},{7,6},{8,7},{9,8},{10,9},{11,1... | collective-permute-start | bytes 24584 | tf_op jit(solution)/shard_map/ppermute | solution.py:36
  138.2 1.3 copy-start
  139.9 12.0 %collective-permute-start.20 = (f32[8,1,2048]{2,1,0:T(1,128)S(1)}, f32[8,1,2048]{2,1,0:T(1,128)S(1)}, u32[]{:S(2)}, u32[]{:S(2)}) collective-permute-start(f32[8,1,2048]{2,1,0:T(1,128)S(1)} %get-tuple-element.263), channel_id=1, source_target_pairs={{1,0},{2,1},{3,2},{4,3},{5,4},{6,5},{7,6},{8,7},{9,8},{10,9},{11,1... | collective-permute-start | bytes 196616 | tf_op jit(solution)/shard_map/ppermute | solution.py:203
  141.8 12.2 %collective-permute-start.21 = (f32[8,1,2048]{2,1,0:T(1,128)S(1)}, f32[8,1,2048]{2,1,0:T(1,128)S(1)}, u32[]{:S(2)}, u32[]{:S(2)}) collective-permute-start(f32[8,1,2048]{2,1,0:T(1,128)S(1)} %get-tuple-element.262), channel_id=1, source_target_pairs={{0,1},{1,2},{2,3},{3,4},{4,5},{5,6},{6,7},{7,8},{8,9},{9,10},{10,1... | collective-permute-start | bytes 196616 | tf_op jit(solution)/shard_map/ppermute | solution.py:202
  148.9 5.4 %collective-permute-start.18 = (f32[1,16,2048]{2,1,0:T(8,128)S(1)}, f32[1,16,2048]{2,1,0:T(8,128)S(1)}, u32[]{:S(2)}, u32[]{:S(2)}) collective-permute-start(f32[1,16,2048]{2,1,0:T(8,128)S(1)} %get-tuple-element.227), channel_id=1, source_target_pairs={{16,0},{32,16},{48,32},{64,48},{80,64},{96,80},{112,96},{17,1},{33... | collective-permute-start | bytes 393224 | tf_op jit(solution)/shard_map/ppermute | solution.py:203
  151.9 6.3 %collective-permute-start.19 = (f32[1,16,2048]{2,1,0:T(8,128)S(1)}, f32[1,16,2048]{2,1,0:T(8,128)S(1)}, u32[]{:S(2)}, u32[]{:S(2)}) collective-permute-start(f32[1,16,2048]{2,1,0:T(8,128)S(1)} %get-tuple-element.226), channel_id=1, source_target_pairs={{0,16},{16,32},{32,48},{48,64},{64,80},{80,96},{96,112},{1,17},{17... | collective-permute-start | bytes 393224 | tf_op jit(solution)/shard_map/ppermute | solution.py:202
  189.2 28.0 %all-to-all-start.1 = ((f32[3,16,256]{2,0,1:T(4,128)}), f32[3,16,256]{2,0,1:T(4,128)S(1)}, u32[]{:S(2)}, u32[]{:S(2)}) async-start(f32[3,16,256]{2,0,1:T(4,128)} %bitcast.41), calls=%async_computation.1 | async-start | bytes 131072 | tf_op jit(solution)/shard_map/all_to_all | solution.py:303
  201.8 3.8 %copy-start.1 = (f32[24,4,128]{2,1,0:T(4,128)}, f32[24,4,128]{2,1,0:T(4,128)S(1)}, u32[]{:S(2)}) copy-start(f32[24,4,128]{2,1,0:T(4,128)S(1)} %maximum_bitcast_fusion.rows_ref) | copy-start | bytes 147460
  221.5 0.8 copy-start.3
